TPU v7x, 512 devices: a whole 4x4x16 slice. The times are simulated.
512 devices in a mesh: ctx: 32 (over y_hi, z), fsdp: 16 (over y_lo, x, core).
Axes of the slice: x: 4, y: 4 (y_hi: 2, y_lo: 2; y = y_hi * 2 + y_lo), z: 16, core: 2. Of those that a mesh axis runs over, the one named last changes fastest.
Arguments:
- latents: bfloat16 [10240, 3072], P('ctx'), may hold values from -6 to 6, as said below
- timestep: int32 [1], replicated, may hold values from 0 to 999
- offsets: int32 [64], replicated, may hold values from 0 to 63, as said below
- qkv_weight: bfloat16 [3072, 16, 384], P('ctx', 'fsdp'), may hold values from -2 to 2
- mod_weight: bfloat16 [3072, 2, 256], P('ctx'), may hold values from -0.375 to 0.375
- gate_weight: bfloat16 [256, 3072], P(None, 'fsdp'), may hold values from -0.375 to 0.375
- out_weight: bfloat16 [3072, 16, 128], P('ctx', 'fsdp'), may hold values from -0.125 to 0.125
- conv_weight: bfloat16 [3, 3, 3, 3072], P(None, None, None, 'fsdp'), may hold values from -1.25 to 1.25
Outputs:
- mixed: bfloat16 [10240, 3072], P('ctx', 'fsdp')
Inputs may be any that keep to these rules, and one draw needn't show every extreme that they name: `latents`: tokens in order of frame, then row, then column. offsets[f] is at most f; the last frame's offset is exactly 63.
All inputs are finite; a program needn't handle non-finite values.
Results may differ from a plain program's by a relative error of at most 0.0095.
Values may be sent and summed in bfloat16 or wider, within the bound.
No kernel may reach another device: no remote copies, remote signals or barrier semaphores. Data moves between devices by JAX's collectives and lax.ppermute only.
A program may use at most 64 MiB of HBM per device.

v0:
```python
import math

import jax
import jax.numpy as jnp
from jax import lax
from jax.sharding import PartitionSpec as P

HH = 10
WW = 16


EPS = 1e-06
NEG = -1e30


def passed_along(block, axis, distance):
    devices = range(lax.axis_size(axis))
    route = [(i - distance, i) for i in devices if i - distance in devices]
    return lax.ppermute(block, axis, route)


def time_features(timestep, embed_width):
    half_width = embed_width // 2
    freqs = jnp.exp(-math.log(10000.0) * jnp.arange(half_width, dtype=jnp.float32) / half_width)
    angles = timestep[0].astype(jnp.float32) * freqs
    embed = jnp.concatenate([jnp.cos(angles), jnp.sin(angles)])
    return jax.nn.silu(embed).astype(jnp.bfloat16)


def attend_piece(
    state_now, kv_piece, first_key, queries, query_frame, query_first, frame_size, head_dim
):
    run_max, run_sum, accumulated = state_now
    key_count = kv_piece.shape[0]
    key_part = kv_piece[:, :, :head_dim]
    value_part = kv_piece[:, :, head_dim:]
    scores = jnp.einsum(
        "nhe,mhe->nhm", queries, key_part, preferred_element_type=jnp.float32
    ) * head_dim ** (-0.5)
    key_frame = (first_key + jnp.arange(key_count, dtype=jnp.int32)) // frame_size
    allowed = (key_frame[None, :] <= query_frame[:, None]) & (
        key_frame[None, :] >= query_first[:, None]
    )
    masked = jnp.where(allowed[:, None, :], scores, NEG)
    new_max = jnp.maximum(run_max, masked.max(-1))
    exponent = jnp.where(allowed[:, None, :], jnp.exp(masked - new_max[..., None]), 0.0)
    factor = jnp.exp(run_max - new_max)
    run_sum = run_sum * factor + exponent.sum(-1)
    accumulated = accumulated * factor[..., None] + jnp.einsum(
        "nhm,mhe->nhe",
        exponent.astype(jnp.bfloat16),
        value_part,
        preferred_element_type=jnp.float32,
    )
    return (new_max, run_sum, accumulated)


def fold_blocks(state_now, kv_piece, step_fn, block_rows):
    key_count = kv_piece.shape[0]
    split_rows = kv_piece.reshape(
        key_count // block_rows, block_rows, kv_piece.shape[1], kv_piece.shape[2]
    )

    def visit_block(state_in, block_item):
        block_no, block_rows_kv = block_item
        return (step_fn(state_in, block_rows_kv, block_no * block_rows), None)

    block_ids = jnp.arange(key_count // block_rows, dtype=jnp.int32)
    state_out, _ = lax.scan(visit_block, state_now, (block_ids, split_rows))
    return state_out


def per_device(
    latents, timestep, offsets, qkv_weight, mod_weight, gate_weight, out_weight, conv_weight
):
    tok_rows = latents.shape[0]
    heads_here = qkv_weight.shape[1]
    head_dim = out_weight.shape[2]
    chan_here = gate_weight.shape[1]
    frame_size = HH * WW
    frames_here = tok_rows // frame_size
    position = lax.axis_index("ctx")
    column = lax.axis_index("fsdp")
    time_act = time_features(timestep, gate_weight.shape[0])
    gate_vec = jnp.dot(time_act, gate_weight, preferred_element_type=jnp.float32)
    float_rows = latents.astype(jnp.float32)
    centred = float_rows - float_rows.mean(-1, keepdims=True)
    variance = (centred * centred).mean(-1, keepdims=True)
    normed = centred * lax.rsqrt(variance + EPS)
    w_piece = lax.all_gather(qkv_weight, "ctx", axis=0, tiled=True)
    m_piece = lax.all_gather(mod_weight, "ctx", axis=0, tiled=True)
    shares = jnp.einsum("rjt,t->rj", m_piece, time_act, preferred_element_type=jnp.float32)
    modulated = (normed * (1.0 + shares[:, 1]) + shares[:, 0]).astype(jnp.bfloat16)
    projected_qkv = jnp.einsum(
        "nr,rhc->nhc", modulated, w_piece, preferred_element_type=jnp.float32
    ).astype(jnp.bfloat16)
    queries = projected_qkv[:, :, :head_dim]
    packed = projected_qkv[:, :, head_dim:]
    query_frame = position * frames_here + jnp.arange(tok_rows, dtype=jnp.int32) // frame_size
    local_first = lax.dynamic_slice_in_dim(offsets, position * frames_here, frames_here, 0)
    query_first = jnp.repeat(local_first, frame_size)
    start_state = (
        jnp.full((tok_rows, heads_here), NEG, jnp.float32),
        jnp.zeros((tok_rows, heads_here), jnp.float32),
        jnp.zeros((tok_rows, heads_here, head_dim), jnp.float32),
    )
    block_rows = 2 * tok_rows

    def attend(state_now, kv_piece, first_key):
        return attend_piece(
            state_now, kv_piece, first_key, queries, query_frame, query_first, frame_size, head_dim
        )

    run_max, run_sum, accumulated = fold_blocks(
        start_state, lax.all_gather(packed, "ctx", axis=0, tiled=True), attend, block_rows
    )
    attended = (accumulated / run_sum[..., None]).astype(jnp.bfloat16)
    partial_out = jnp.einsum(
        "nhe,rhe->nr",
        attended,
        lax.all_gather(out_weight, "ctx", axis=0, tiled=True),
        preferred_element_type=jnp.float32,
    )
    head_total = lax.psum_scatter(
        partial_out.astype(jnp.bfloat16), "fsdp", scatter_dimension=1, tiled=True
    ).astype(jnp.float32)
    own_chan = lax.dynamic_slice_in_dim(latents, column * chan_here, chan_here, 1)
    before = passed_along(own_chan, "ctx", 1)
    stacked = (
        jnp.concatenate([before, own_chan], 0)
        .astype(jnp.float32)
        .reshape(frames_here + 2, HH, WW, chan_here)
    )
    padded = jnp.pad(stacked, ((0, 0), (1, 1), (1, 1), (0, 0)))
    convolved = jnp.zeros((frames_here, HH, WW, chan_here), jnp.float32)
    for time_lag in range(3):
        for row_shift in range(3):
            for col_shift in range(3):
                tap = conv_weight[time_lag, row_shift, col_shift].astype(jnp.float32)
                convolved = (
                    convolved
                    + tap
                    * padded[
                        2 - time_lag : 2 - time_lag + frames_here,
                        row_shift : row_shift + HH,
                        col_shift : col_shift + WW,
                    ]
                )
    residual = own_chan.astype(jnp.float32)
    mixed = residual + gate_vec * head_total + convolved.reshape(tok_rows, chan_here)
    return mixed.astype(jnp.bfloat16)


def solution(mesh):
    in_specs = (
        P("ctx", None),
        P(),
        P(),
        P("ctx", "fsdp", None),
        P("ctx", None, None),
        P(None, "fsdp"),
        P("ctx", "fsdp", None),
        P(None, None, None, "fsdp"),
    )
    out_specs = P("ctx", "fsdp")
    return jax.shard_map(
        per_device, mesh=mesh, in_specs=in_specs, out_specs=out_specs, check_vma=False
    )
```

profile of v0, /device:TPU:1, one launch (start us, length us, event | category | flops | bytes accessed | tf_op | source)
XLA Modules:
  0.0 628.4 jit_solution(11266354992504720666)
XLA Ops:
  8.8 1.9 convert_reduce_fusion
  11.4 152.3 %all-gather.4.cloned.1.call-done = bf16[3072,2,256]{2,1,0:T(2,128)(2,1)} async-done(((bf16[96,2,256]{2,1,0:T(2,128)(2,1)}), bf16[3072,2,256]{2,1,0:T(2,128)(2,1)}) %all-gather.4.cloned.1.call-update) | async-done | bytes 3145744 | tf_op jit(solution)/shard_map/all_gather | solution.py:91
  163.7 33.1 %multiply_reduce_fusion = f32[3072,2]{1,0:T(8,128)S(1)} fusion(f32[256]{0:T(256)S(1)} %get-tuple-element.206, bf16[3072,2,256]{2,1,0:T(2,128)(2,1)} %all-gather.4.cloned.1.call-done), kind=kLoop, calls=%fused_computation.43 | loop fusion | flops 4712448 | bytes 3171328
  196.8 2.2 slice_add_fusion
  198.9 1.9 copy.34
  200.8 1.9 copy.33
  202.7 110.9 %all-gather.6.cloned.1.call-done = bf16[3072,1,384]{2,0,1:T(8,128)(2,1)} async-done(((bf16[96,1,384]{2,0,1:T(8,128)(2,1)}), bf16[3072,1,384]{2,0,1:T(8,128)(2,1)}) %all-gather.6.cloned.1.call-update) | async-done | bytes 2359312 | tf_op jit(solution)/shard_map/all_gather | solution.py:90
  313.6 2.9 fusion.44
  317.4 69.1 %all_gather.15 = bf16[3072,1,128]{2,0,1:T(8,128)(2,1)} all-gather(bf16[96,1,128]{2,0,1:T(8,128)(2,1)S(1)} %copy-done.3), channel_id=1, replica_groups=mesh['ctx'=32,'fsdp'=16] {'ctx'}, dimensions={0}, use_global_device_ids=true | all-gather | bytes 811008 | tf_op jit(solution)/shard_map/all_gather | solution.py:121
  386.5 98.3 %all-gather.8.cloned.1.call-done = bf16[10240,1,256]{2,0,1:T(8,128)(2,1)} async-done(((bf16[320,1,256]{2,0,1:T(8,128)(2,1)}), bf16[10240,1,256]{2,0,1:T(8,128)(2,1)}) %all-gather.8.cloned.1.call-update) | async-done | bytes 5242896 | tf_op jit(solution)/shard_map/all_gather | solution.py:115
  484.8 60.1 %while.17 = (s32[]{:T(128)}, f32[320,1]{0,1:T(1,128)S(1)}, f32[320,1]{0,1:T(1,128)S(1)}, f32[320,1,128]{2,0,1:T(8,128)S(1)}, s32[16]{0:T(128)S(1)}, /*index=5*/b...) while((s32[]{:T(128)}, f32[320,1]{0,1:T(1,128)S(1)}, ...), condition=%wide.region_5.6_spmd.clone, body=%wide.region_2.5_spmd.clone.sunk | while | flops 108677440 | bytes 3902893 | solution.py:69
  486.1 1.0 dynamic-slice_bitcast_fusion.2
  489.8 1.0 dynamic-slice_bitcast_fusion.2
  493.6 1.0 dynamic-slice_bitcast_fusion.2
  497.3 1.0 dynamic-slice_bitcast_fusion.2
  501.1 1.0 dynamic-slice_bitcast_fusion.2
  504.9 1.0 dynamic-slice_bitcast_fusion.2
  508.6 1.0 dynamic-slice_bitcast_fusion.2
  512.4 1.0 dynamic-slice_bitcast_fusion.2
  516.1 1.0 dynamic-slice_bitcast_fusion.2
  519.9 1.0 dynamic-slice_bitcast_fusion.2
  523.6 1.0 dynamic-slice_bitcast_fusion.2
  527.4 1.0 dynamic-slice_bitcast_fusion.2
  531.1 1.0 dynamic-slice_bitcast_fusion.2
  534.9 1.0 dynamic-slice_bitcast_fusion.2
  538.7 1.0 dynamic-slice_bitcast_fusion.2
  542.4 1.0 dynamic-slice_bitcast_fusion.2
  544.9 3.4 convolution_convert_fusion
  548.6 3.1 collective-permute-start
  551.9 1.8 collective-permute-done
  555.8 64.4 %reduce-scatter.2.cloned.1.call-done = bf16[320,192]{0,1:T(8,128)(2,1)} async-done(((bf16[320,3072]{0,1:T(8,128)(2,1)}), bf16[320,192]{0,1:T(8,128)(2,1)}) %reduce-scatter.2.cloned.1.call-update) | async-done | bytes 122896 | tf_op jit(solution)/shard_map/reduce_scatter | solution.py:124
  620.1 1.7 add_convert_fusion
  (221 shorter events, 38.6 us)
Async XLA Ops:
  6.5 545.2 %copy-start = (bf16[256,192]{0,1:T(8,128)(2,1)S(1)}, bf16[256,192]{0,1:T(8,128)(2,1)}, u32[]{:S(2)}) copy-start(bf16[256,192]{0,1:T(8,128)(2,1)} %param.15) | copy-start | bytes 294916
  6.5 4.2 copy-start.1
  6.5 157.2 %all-gather.4.cloned.1.call-start = ((), (), s32[]{:S(2)}) async-start(), calls=%async_computation.1 | async-start | bytes 3244032 | tf_op jit(solution)/shard_map/all_gather | solution.py:91
  7.3 306.3 %all-gather.6.cloned.1.call-start = ((), (), s32[]{:S(2)}) async-start(), calls=%async_computation.2 | async-start | bytes 2433024 | tf_op jit(solution)/shard_map/all_gather | solution.py:90
  8.0 476.8 %all-gather.8.cloned.1.call-start = ((), (), s32[]{:S(2)}) async-start(), calls=%async_computation.3 | async-start | bytes 5406720 | tf_op jit(solution)/shard_map/all_gather | solution.py:115
  313.6 3.7 copy-start.4
  313.6 3.8 copy-start.3
  317.2 302.9 %reduce-scatter.2.cloned.1.call-start = ((), (), s32[]{:S(2)}) async-start(), calls=%async_computation.4 | async-start | bytes 2506752 | tf_op jit(solution)/shard_map/reduce_scatter | solution.py:124
  548.3 3.4 copy-start.2
  548.6 5.2 collective-permute-start
Sparse Core Ops, SparseCore 0:
  10.5 153.2 all-gather.3
  166.8 146.7 all-gather.5
  317.3 167.4 all-gather.7
  548.5 71.6 reduce-scatter.1
where the time goes:
time: 631 us; the launch traced here: 628 us
  waiting for transfers between devices  429 us (68%)
  blocking collectives  69.1 us (11%)
  other arithmetic  47.8 us (8%)
  local copies, waits for them, and re-layouts  34.2 us (5%)
  matrix products  20 us (3%)
  between operations  14 us (2%)
  loops' own time  11 us (2%)
    all_gather x1, waiting for transfers between devices, per_device(): m_piece = lax.all_gather(mod_weight, 'ctx', axis=0, tiled=True)  152 us
    all_gather x1, waiting for transfers between devices, per_device(): w_piece = lax.all_gather(qkv_weight, 'ctx', axis=0, tiled=True)  111 us
    all_gather x1, waiting for transfers between devices, per_device(): lax.all_gather(packed, 'ctx', axis=0, tiled=True)  98.3 us
    all_gather x1, blocking collectives, per_device(): lax.all_gather(out_weight, 'ctx', axis=0, tiled=True)  69.1 us
    reduce_scatter x1, waiting for transfers between devices, per_device(): lax.psum_scatter(partial_out.astype(jnp.bfloat16), 'fsdp', scatter_dimens...  64.4 us
    unnamed x5, other arithmetic  33.1 us
    squeeze x16, local copies, waits for them, and re-layouts, fold_blocks(): state_out, _ = lax.scan(visit_block, state_now, (block_ids, split_rows))  16 us
  transfers between devices with their start and end apart: 5, of which 5 were waited for; matrix products, arithmetic and copies ran while one was open for 7% of the time, Pallas kernels for 0%

commit v1 on v0

--- a/solution.py
+++ b/solution.py
@@ -87,9 +87,30 @@
     centred = float_rows - float_rows.mean(-1, keepdims=True)
     variance = (centred * centred).mean(-1, keepdims=True)
     normed = centred * lax.rsqrt(variance + EPS)
-    w_piece = lax.all_gather(qkv_weight, "ctx", axis=0, tiled=True)
-    m_piece = lax.all_gather(mod_weight, "ctx", axis=0, tiled=True)
-    shares = jnp.einsum("rjt,t->rj", m_piece, time_act, preferred_element_type=jnp.float32)
+    rows_here = qkv_weight.shape[0]
+    qkv_width = qkv_weight.shape[2]
+    local_shares = jnp.einsum(
+        "rjt,t->rj", mod_weight, time_act, preferred_element_type=jnp.float32
+    )
+    shares_hi = local_shares.astype(jnp.bfloat16)
+    shares_lo = (local_shares - shares_hi.astype(jnp.float32)).astype(jnp.bfloat16)
+    bundle = jnp.concatenate(
+        [
+            qkv_weight.reshape(rows_here, heads_here * qkv_width),
+            out_weight.reshape(rows_here, heads_here * head_dim),
+            shares_hi,
+            shares_lo,
+        ],
+        axis=1,
+    )
+    gathered = lax.all_gather(bundle, "ctx", axis=0, tiled=True)
+    full_rows = gathered.shape[0]
+    qkv_cols = heads_here * qkv_width
+    out_cols = heads_here * head_dim
+    w_piece = gathered[:, :qkv_cols].reshape(full_rows, heads_here, qkv_width)
+    o_piece = gathered[:, qkv_cols : qkv_cols + out_cols].reshape(full_rows, heads_here, head_dim)
+    share_bits = gathered[:, qkv_cols + out_cols :].astype(jnp.float32)
+    shares = share_bits[:, :2] + share_bits[:, 2:]
     modulated = (normed * (1.0 + shares[:, 1]) + shares[:, 0]).astype(jnp.bfloat16)
     projected_qkv = jnp.einsum(
         "nr,rhc->nhc", modulated, w_piece, preferred_element_type=jnp.float32
@@ -118,7 +139,7 @@
     partial_out = jnp.einsum(
         "nhe,rhe->nr",
         attended,
-        lax.all_gather(out_weight, "ctx", axis=0, tiled=True),
+        o_piece,
         preferred_element_type=jnp.float32,
     )
     head_total = lax.psum_scatter(

time: 631 us -> 487 us (0.77)
  blocking collectives: 69.1 us -> 0 us
  waiting for transfers between devices: 429 us -> 390 us
  other arithmetic: 47.8 us -> 17.3 us
    all_gather x2 -> x1, waiting for transfers between devices: 263 us -> 158 us  [per_device(): gathered = lax.all_gather(bundle, 'ctx', axis=0, tiled=True)]
    all_gather x1 -> x0, blocking collectives: 69.1 us -> none  [per_device(): lax.all_gather(out_weight, 'ctx', axis=0, tiled=True)]
    all_gather x1, waiting for transfers between devices: 98.3 us -> 166 us  [per_device(): lax.all_gather(packed, 'ctx', axis=0, tiled=True)]
    unnamed x5 -> x3, other arithmetic: 33.1 us -> 0.01 us
  transfers between devices with their start and end apart: 5 -> 4, of which waited for: 5 -> 4; matrix products, arithmetic and copies ran while one was open for 7% -> 1% of each run, Pallas kernels for 0% -> 0%
where the time goes in v1:
time: 487 us; the launch traced here: 484 us
  waiting for transfers between devices  390 us (80%)
  local copies, waits for them, and re-layouts  30.7 us (6%)
  matrix products  18.5 us (4%)
  other arithmetic  17.3 us (4%)
  between operations  14.2 us (3%)
  loops' own time  10 us (2%)
    all_gather x1, waiting for transfers between devices, per_device(): lax.all_gather(packed, 'ctx', axis=0, tiled=True)  166 us
    all_gather x1, waiting for transfers between devices, per_device(): gathered = lax.all_gather(bundle, 'ctx', axis=0, tiled=True)  158 us
    reduce_scatter x1, waiting for transfers between devices, per_device(): lax.psum_scatter(partial_out.astype(jnp.bfloat16), 'fsdp', scatter_dimens...  64.2 us
    squeeze x16, local copies, waits for them, and re-layouts, fold_blocks(): state_out, _ = lax.scan(visit_block, state_now, (block_ids, split_rows))  16 us
    another operation x1, loops' own time, fold_blocks(): state_out, _ = lax.scan(visit_block, state_now, (block_ids, split_rows))  10 us
  transfers between devices with their start and end apart: 4, of which 4 were waited for; matrix products, arithmetic and copies ran while one was open for 1% of the time, Pallas kernels for 0%

profile of v1, /device:TPU:1, one launch (start us, length us, event | category | flops | bytes accessed | tf_op | source)
XLA Modules:
  0.0 483.9 jit_solution(17367744901689047)
XLA Ops:
  7.9 1.6 pad_maximum_fusion
  9.6 1.9 convert_reduce_fusion
  11.5 0.7 fusion.28
  12.2 158.1 %all-gather.3.cloned.1.call-done = bf16[3072,516]{1,0:T(8,128)(2,1)} async-done(((bf16[96,516]{1,0:T(8,128)(2,1)}), bf16[3072,516]{1,0:T(8,128)(2,1)}) %all-gather.3.cloned.1.call-update) | async-done | bytes 3170320 | tf_op jit(solution)/shard_map/all_gather | solution.py:106
  170.3 1.2 slice_convert_fusion
  172.0 1.3 fusion.39
  173.7 1.3 fusion.45
  174.9 0.7 slice.289
  175.8 165.8 %all-gather.5.cloned.1.call-done = bf16[10240,1,256]{2,0,1:T(8,128)(2,1)} async-done(((bf16[320,1,256]{2,0,1:T(8,128)(2,1)}), bf16[10240,1,256]{2,0,1:T(8,128)(2,1)}) %all-gather.5.cloned.1.call-update) | async-done | bytes 5242896 | tf_op jit(solution)/shard_map/all_gather | solution.py:136
  341.7 58.9 %while.17 = (s32[]{:T(128)}, f32[320,1]{0,1:T(1,128)S(1)}, f32[320,1]{0,1:T(1,128)S(1)}, f32[320,1,128]{2,0,1:T(8,128)S(1)}, s32[16]{0:T(128)S(1)}, /*index=5*/b...) while((s32[]{:T(128)}, f32[320,1]{0,1:T(1,128)S(1)}, ...), condition=%wide.region_5.6_spmd.clone, body=%wide.region_2.5_spmd.clone.sunk | while | flops 108677440 | bytes 3902893 | solution.py:69
  342.9 1.0 dynamic-slice_bitcast_fusion.2
  346.5 1.0 dynamic-slice_bitcast_fusion.2
  350.2 1.0 dynamic-slice_bitcast_fusion.2
  353.9 1.0 dynamic-slice_bitcast_fusion.2
  357.6 1.0 dynamic-slice_bitcast_fusion.2
  361.3 1.0 dynamic-slice_bitcast_fusion.2
  364.9 1.0 dynamic-slice_bitcast_fusion.2
  368.6 1.0 dynamic-slice_bitcast_fusion.2
  372.3 1.0 dynamic-slice_bitcast_fusion.2
  376.0 1.0 dynamic-slice_bitcast_fusion.2
  379.7 1.0 dynamic-slice_bitcast_fusion.2
  383.3 1.0 dynamic-slice_bitcast_fusion.2
  387.0 1.0 dynamic-slice_bitcast_fusion.2
  390.7 1.0 dynamic-slice_bitcast_fusion.2
  394.4 1.0 dynamic-slice_bitcast_fusion.2
  398.1 1.0 dynamic-slice_bitcast_fusion.2
  400.6 3.4 convolution_convert_fusion
  404.3 3.1 collective-permute-start
  407.6 1.8 collective-permute-done
  410.5 0.8 fusion.96
  411.4 64.2 %reduce-scatter.2.cloned.1.call-done = bf16[320,192]{0,1:T(8,128)(2,1)} async-done(((bf16[320,3072]{0,1:T(8,128)(2,1)}), bf16[320,192]{0,1:T(8,128)(2,1)}) %reduce-scatter.2.cloned.1.call-update) | async-done | bytes 122896 | tf_op jit(solution)/shard_map/reduce_scatter | solution.py:145
  475.6 1.7 add_convert_fusion
  (224 shorter events, 36.0 us)
Async XLA Ops:
  6.5 0.9 copy-start
  6.5 5.0 %copy-start.1 = (bf16[320,3072]{1,0:T(8,128)(2,1)S(1)}, bf16[320,3072]{1,0:T(8,128)(2,1)}, u32[]{:S(2)}) copy-start(bf16[320,3072]{1,0:T(8,128)(2,1)} %param.10) | copy-start | bytes 5898244
  6.5 163.8 %all-gather.3.cloned.1.call-start = ((), (), s32[]{:S(2)}) async-start(), calls=%async_computation.1 | async-start | bytes 4055040 | tf_op jit(solution)/shard_map/all_gather | solution.py:106
  9.5 332.1 %all-gather.5.cloned.1.call-start = ((), (), s32[]{:S(2)}) async-start(), calls=%async_computation.2 | async-start | bytes 5406720 | tf_op jit(solution)/shard_map/all_gather | solution.py:136
  171.6 2.1 copy-start.2
  173.7 2.1 copy-start.5
  175.6 300.0 %reduce-scatter.2.cloned.1.call-start = ((), (), s32[]{:S(2)}) async-start(), calls=%async_computation.3 | async-start | bytes 2506752 | tf_op jit(solution)/shard_map/reduce_scatter | solution.py:145
  404.0 3.4 copy-start.4
  404.0 3.4 copy-start.3
  404.3 5.2 %collective-permute-start = (bf16[320,192]{0,1:T(8,128)(2,1)S(1)}, bf16[320,192]{0,1:T(8,128)(2,1)S(1)}, u32[]{:S(2)}, u32[]{:S(2)}) collective-permute-start(bf16[320,192]{0,1:T(8,128)(2,1)S(1)} %copy.30), channel_id=1, source_target_pairs={{0,16},{16,32},{32,48},{48,64},{64,80},{80,96},{96,112},{112,128},... | collective-permute-start | bytes 368648 | tf_op jit(solution)/shard_map/ppermute | solution.py:19
Sparse Core Ops, SparseCore 0:
  10.5 159.8 all-gather.2
  175.8 165.8 all-gather.4
  404.1 71.4 reduce-scatter.1

commit v2 on v1

--- a/solution.py
+++ b/solution.py
@@ -27,17 +27,69 @@
     return jax.nn.silu(embed).astype(jnp.bfloat16)
 
 
-def attend_piece(
-    state_now, kv_piece, first_key, queries, query_frame, query_first, frame_size, head_dim
-):
+def ring_pieces(block, axis):
+    size = lax.axis_size(axis)
+    ring = size // 2
+    position = lax.axis_index(axis)
+    partner = lax.ppermute(block, axis, [(i, (i + ring) % size) for i in range(size)])
+    pair = jnp.where(
+        position // ring == 0, jnp.stack([block, partner]), jnp.stack([partner, block])
+    )
+    ring_pos = position % ring
+    forward = [(y * ring + a, y * ring + (a + 1) % ring) for y in range(2) for a in range(ring)]
+    backward = [(y * ring + a, y * ring + (a - 1) % ring) for y in range(2) for a in range(ring)]
+    pieces = [(pair, ring_pos)]
+    ahead = pair
+    behind = pair
+    for step in range(1, ring // 2 + 1):
+        ahead = lax.ppermute(ahead, axis, forward)
+        pieces.append((ahead, (ring_pos - step) % ring))
+        if step < ring - ring // 2:
+            behind = lax.ppermute(behind, axis, backward)
+            pieces.append((behind, (ring_pos + step) % ring))
+    return pieces, ring
+
+
+def ring_gather(block, axis):
+    pieces, ring = ring_pieces(block, axis)
+    gathered = jnp.zeros((ring,) + pieces[0][0].shape, block.dtype)
+    for piece, source in pieces:
+        gathered = lax.dynamic_update_index_in_dim(gathered, piece, source, 0)
+    gathered = jnp.swapaxes(gathered, 0, 1)
+    return gathered.reshape((2 * ring * block.shape[0],) + block.shape[1:])
+
+
+def halving_scatter(partial, axis):
+    size = lax.axis_size(axis)
+    bits = size.bit_length() - 1
+    position = lax.axis_index(axis)
+    rows, cols = partial.shape
+    width = cols // size
+    state = partial.reshape((rows,) + (2,) * bits + (width,))
+    axis_bits = [bits - 1 - a for a in range(bits)]
+    order = [0] + ([bits - 1] if bits > 1 else []) + list(range(1, bits - 1))
+    for bit in order:
+        dim = 1 + axis_bits.index(bit)
+        mine = (position >> bit) & 1
+        low = lax.index_in_dim(state, 0, dim, keepdims=False)
+        high = lax.index_in_dim(state, 1, dim, keepdims=False)
+        keep = jnp.where(mine == 0, low, high)
+        send = jnp.where(mine == 0, high, low)
+        got = lax.ppermute(
+            send.astype(jnp.bfloat16), axis, [(i, i ^ (1 << bit)) for i in range(size)]
+        )
+        state = keep + got.astype(jnp.float32)
+        axis_bits.remove(bit)
+    return state.reshape(rows, width)
+
+
+def attend_piece(state_now, kv_piece, key_frame, queries, query_frame, query_first, head_dim):
     run_max, run_sum, accumulated = state_now
-    key_count = kv_piece.shape[0]
     key_part = kv_piece[:, :, :head_dim]
     value_part = kv_piece[:, :, head_dim:]
     scores = jnp.einsum(
         "nhe,mhe->nhm", queries, key_part, preferred_element_type=jnp.float32
     ) * head_dim ** (-0.5)
-    key_frame = (first_key + jnp.arange(key_count, dtype=jnp.int32)) // frame_size
     allowed = (key_frame[None, :] <= query_frame[:, None]) & (
         key_frame[None, :] >= query_first[:, None]
     )
@@ -53,21 +105,6 @@
         preferred_element_type=jnp.float32,
     )
     return (new_max, run_sum, accumulated)
-
-
-def fold_blocks(state_now, kv_piece, step_fn, block_rows):
-    key_count = kv_piece.shape[0]
-    split_rows = kv_piece.reshape(
-        key_count // block_rows, block_rows, kv_piece.shape[1], kv_piece.shape[2]
-    )
-
-    def visit_block(state_in, block_item):
-        block_no, block_rows_kv = block_item
-        return (step_fn(state_in, block_rows_kv, block_no * block_rows), None)
-
-    block_ids = jnp.arange(key_count // block_rows, dtype=jnp.int32)
-    state_out, _ = lax.scan(visit_block, state_now, (block_ids, split_rows))
-    return state_out
 
 
 def per_device(
@@ -87,30 +124,50 @@
     centred = float_rows - float_rows.mean(-1, keepdims=True)
     variance = (centred * centred).mean(-1, keepdims=True)
     normed = centred * lax.rsqrt(variance + EPS)
+
     rows_here = qkv_weight.shape[0]
     qkv_width = qkv_weight.shape[2]
+    qkv_cols = heads_here * qkv_width
+    out_cols = heads_here * head_dim
+    width = qkv_cols + out_cols
     local_shares = jnp.einsum(
         "rjt,t->rj", mod_weight, time_act, preferred_element_type=jnp.float32
     )
     shares_hi = local_shares.astype(jnp.bfloat16)
     shares_lo = (local_shares - shares_hi.astype(jnp.float32)).astype(jnp.bfloat16)
+    share_count = 4 * rows_here
+    extra_rows = 16 * ((share_count + 16 * width - 1) // (16 * width))
+    share_block = jnp.zeros((extra_rows * width,), jnp.bfloat16)
+    share_block = share_block.at[:share_count].set(
+        jnp.concatenate([shares_hi, shares_lo], axis=1).reshape(share_count)
+    )
     bundle = jnp.concatenate(
         [
-            qkv_weight.reshape(rows_here, heads_here * qkv_width),
-            out_weight.reshape(rows_here, heads_here * head_dim),
-            shares_hi,
-            shares_lo,
+            jnp.concatenate(
+                [
+                    qkv_weight.reshape(rows_here, qkv_cols),
+                    out_weight.reshape(rows_here, out_cols),
+                ],
+                axis=1,
+            ),
+            share_block.reshape(extra_rows, width),
         ],
-        axis=1,
-    )
-    gathered = lax.all_gather(bundle, "ctx", axis=0, tiled=True)
-    full_rows = gathered.shape[0]
-    qkv_cols = heads_here * qkv_width
-    out_cols = heads_here * head_dim
-    w_piece = gathered[:, :qkv_cols].reshape(full_rows, heads_here, qkv_width)
-    o_piece = gathered[:, qkv_cols : qkv_cols + out_cols].reshape(full_rows, heads_here, head_dim)
-    share_bits = gathered[:, qkv_cols + out_cols :].astype(jnp.float32)
+        axis=0,
+    )
+    gathered = ring_gather(bundle, "ctx")
+    blocks = gathered.shape[0] // bundle.shape[0]
+    gathered = gathered.reshape(blocks, rows_here + extra_rows, width)
+    full_rows = blocks * rows_here
+    w_piece = gathered[:, :rows_here, :qkv_cols].reshape(full_rows, heads_here, qkv_width)
+    o_piece = gathered[:, :rows_here, qkv_cols:].reshape(full_rows, heads_here, head_dim)
+    share_bits = (
+        gathered[:, rows_here:, :]
+        .reshape(blocks, extra_rows * width)[:, :share_count]
+        .reshape(full_rows, 4)
+        .astype(jnp.float32)
+    )
     shares = share_bits[:, :2] + share_bits[:, 2:]
+
     modulated = (normed * (1.0 + shares[:, 1]) + shares[:, 0]).astype(jnp.bfloat16)
     projected_qkv = jnp.einsum(
         "nr,rhc->nhc", modulated, w_piece, preferred_element_type=jnp.float32
@@ -120,21 +177,30 @@
     query_frame = position * frames_here + jnp.arange(tok_rows, dtype=jnp.int32) // frame_size
     local_first = lax.dynamic_slice_in_dim(offsets, position * frames_here, frames_here, 0)
     query_first = jnp.repeat(local_first, frame_size)
-    start_state = (
+    state = (
         jnp.full((tok_rows, heads_here), NEG, jnp.float32),
         jnp.zeros((tok_rows, heads_here), jnp.float32),
         jnp.zeros((tok_rows, heads_here, head_dim), jnp.float32),
     )
-    block_rows = 2 * tok_rows
-
-    def attend(state_now, kv_piece, first_key):
-        return attend_piece(
-            state_now, kv_piece, first_key, queries, query_frame, query_first, frame_size, head_dim
+    kv_pieces, ring = ring_pieces(packed, "ctx")
+    token_ids = jnp.arange(tok_rows, dtype=jnp.int32)
+    for piece, source in kv_pieces:
+        key_frame = (
+            jnp.concatenate(
+                [source * tok_rows + token_ids, (ring + source) * tok_rows + token_ids]
+            )
+            // frame_size
         )
-
-    run_max, run_sum, accumulated = fold_blocks(
-        start_state, lax.all_gather(packed, "ctx", axis=0, tiled=True), attend, block_rows
-    )
+        state = attend_piece(
+            state,
+            piece.reshape((2 * tok_rows,) + piece.shape[2:]),
+            key_frame,
+            queries,
+            query_frame,
+            query_first,
+            head_dim,
+        )
+    run_max, run_sum, accumulated = state
     attended = (accumulated / run_sum[..., None]).astype(jnp.bfloat16)
     partial_out = jnp.einsum(
         "nhe,rhe->nr",
@@ -142,9 +208,7 @@
         o_piece,
         preferred_element_type=jnp.float32,
     )
-    head_total = lax.psum_scatter(
-        partial_out.astype(jnp.bfloat16), "fsdp", scatter_dimension=1, tiled=True
-    ).astype(jnp.float32)
+    head_total = halving_scatter(partial_out, "fsdp")
     own_chan = lax.dynamic_slice_in_dim(latents, column * chan_here, chan_here, 1)
     before = passed_along(own_chan, "ctx", 1)
     stacked = (

time: 487 us -> 275 us (0.56)
  waiting for transfers between devices: 390 us -> 68.9 us
  starting transfers between devices: 3.17 us -> 144 us
  local copies, waits for them, and re-layouts: 30.7 us -> 11.8 us
  between operations: 14.2 us -> 2.35 us
  other arithmetic: 17.3 us -> 29.1 us
  loops' own time: 10 us -> 0 us
    all_gather x2 -> x0, waiting for transfers between devices: 324 us -> none  [the longest x1 166 us: per_device(): lax.all_gather(packed, 'ctx', axis=0, tiled=True)]
    ppermute x0 -> x36, starting transfers between devices: none -> 142 us  [the longest x14 68.2 us: ring_pieces(): behind = lax.ppermute(behind, axis, backward)]
    ppermute x0 -> x36, waiting for transfers between devices: none -> 68.9 us  [the longest x16 33.7 us: ring_pieces(): ahead = lax.ppermute(ahead, axis, forward)]
    reduce_scatter x1 -> x0, waiting for transfers between devices: 64.2 us -> none  [per_device(): lax.psum_scatter(partial_out.astype(jnp.bfloat16), 'fsdp', scatter_dimens...]
    squeeze x16 -> x0, local copies, waits for them, and re-layouts: 16 us -> none  [fold_blocks(): state_out, _ = lax.scan(visit_block, state_now, (block_ids, split_rows))]
    another operation x1 -> x0, loops' own time: 10 us -> none  [fold_blocks(): state_out, _ = lax.scan(visit_block, state_now, (block_ids, split_rows))]
    dynamic_slice x16 -> x0, local copies, waits for them, and re-layouts: 9.46 us -> none  [fold_blocks(): state_out, _ = lax.scan(visit_block, state_now, (block_ids, split_rows))]
    add x0 -> x19, other arithmetic: none -> 5.41 us  [the longest x3 5.35 us: halving_scatter(): state = keep + got.astype(jnp.float32)]
  transfers between devices with their start and end apart: 4 -> 37, of which waited for: 4 -> 19; matrix products, arithmetic and copies ran while one was open for 1% -> 10% of each run, Pallas kernels for 0% -> 0%
where the time goes in v2:
time: 275 us; the launch traced here: 274 us
  starting transfers between devices  144 us (52%)
  waiting for transfers between devices  68.9 us (25%)
  other arithmetic  29.1 us (11%)
  matrix products  18 us (7%)
  local copies, waits for them, and re-layouts  11.8 us (4%)
    ppermute x14, starting transfers between devices, ring_pieces(): behind = lax.ppermute(behind, axis, backward)  68.2 us
    ppermute x16, starting transfers between devices, ring_pieces(): ahead = lax.ppermute(ahead, axis, forward)  33.9 us
    ppermute x16, waiting for transfers between devices, ring_pieces(): ahead = lax.ppermute(ahead, axis, forward)  33.7 us
    ppermute x4, starting transfers between devices, halving_scatter(): lax.ppermute(send.astype(jnp.bfloat16), axis, [(i, i ^ 1 << bit) for i in...  30.5 us
    ppermute x4, waiting for transfers between devices, halving_scatter(): lax.ppermute(send.astype(jnp.bfloat16), axis, [(i, i ^ 1 << bit) for i in...  22 us
    ppermute x14, waiting for transfers between devices, ring_pieces(): behind = lax.ppermute(behind, axis, backward)  10.1 us
    ppermute x2, starting transfers between devices, ring_pieces(): lax.ppermute(block, axis, [(i, (i + ring) % size) for i in range(size)])  9.79 us
    dot_general x16, matrix products, attend_piece(): jnp.einsum('nhe,mhe->nhm', queries, key_part, preferred_element_type=jnp....  7.02 us
  transfers between devices with their start and end apart: 37, of which 19 were waited for; matrix products, arithmetic and copies ran while one was open for 10% of the time, Pallas kernels for 0%

profile of v2, /device:TPU:1, one launch (start us, length us, event | category | flops | bytes accessed | tf_op | source)
XLA Modules:
  0.0 273.8 jit_solution(9020960068116728213)
XLA Ops:
  2.3 5.7 %collective-permute-start = (bf16[112,512]{1,0:T(8,128)(2,1)S(1)}, bf16[112,512]{1,0:T(8,128)(2,1)S(1)}, u32[]{:S(2)}, u32[]{:S(2)}) collective-permute-start(bf16[112,512]{1,0:T(8,128)(2,1)S(1)} %get-tuple-element.74), channel_id=1, source_target_pairs={{0,256},{16,272},{32,288},{48,304},{64,320},{80,336},{96,352},{112... | collective-permute-start | bytes 344072 | tf_op jit(solution)/shard_map/ppermute | solution.py:34
  12.4 3.5 %collective-permute-start.1 = (bf16[2,112,512]{2,1,0:T(8,128)(2,1)S(1)}, bf16[2,112,512]{2,1,0:T(8,128)(2,1)S(1)}, u32[]{:S(2)}, u32[]{:S(2)}) collective-permute-start(bf16[2,112,512]{2,1,0:T(8,128)(2,1)S(1)} %maximum_select_fusion.2), channel_id=1, source_target_pairs={{0,16},{16,32},{32,48},{48,64},{64,80},{80,96},{96,112},{112,128},... | collective-permute-start | bytes 688136 | tf_op jit(solution)/shard_map/ppermute | solution.py:45
  16.0 9.5 %collective-permute-start.2 = (bf16[2,112,512]{2,1,0:T(8,128)(2,1)S(1)}, bf16[2,112,512]{2,1,0:T(8,128)(2,1)S(1)}, u32[]{:S(2)}, u32[]{:S(2)}) collective-permute-start(bf16[2,112,512]{2,1,0:T(8,128)(2,1)S(1)} %maximum_select_fusion.2), channel_id=1, source_target_pairs={{0,240},{16,0},{32,16},{48,32},{64,48},{80,64},{96,80},{112,96},{1... | collective-permute-start | bytes 688136 | tf_op jit(solution)/shard_map/ppermute | solution.py:48
  26.0 2.5 collective-permute-done.1
  30.5 4.6 %collective-permute-start.4 = (bf16[2,112,512]{2,1,0:T(8,128)(2,1)S(1)}, bf16[2,112,512]{2,1,0:T(8,128)(2,1)S(1)}, u32[]{:S(2)}, u32[]{:S(2)}) collective-permute-start(bf16[2,112,512]{2,1,0:T(8,128)(2,1)S(1)} %collective-permute-done.2), channel_id=1, source_target_pairs={{0,240},{16,0},{32,16},{48,32},{64,48},{80,64},{96,80},{112,96},{1... | collective-permute-start | bytes 688136 | tf_op jit(solution)/shard_map/ppermute | solution.py:48
  39.1 4.6 %collective-permute-start.6 = (bf16[2,112,512]{2,1,0:T(8,128)(2,1)S(1)}, bf16[2,112,512]{2,1,0:T(8,128)(2,1)S(1)}, u32[]{:S(2)}, u32[]{:S(2)}) collective-permute-start(bf16[2,112,512]{2,1,0:T(8,128)(2,1)S(1)} %collective-permute-done.4), channel_id=1, source_target_pairs={{0,240},{16,0},{32,16},{48,32},{64,48},{80,64},{96,80},{112,96},{1... | collective-permute-start | bytes 688136 | tf_op jit(solution)/shard_map/ppermute | solution.py:48
  47.1 4.6 %collective-permute-start.8 = (bf16[2,112,512]{2,1,0:T(8,128)(2,1)S(1)}, bf16[2,112,512]{2,1,0:T(8,128)(2,1)S(1)}, u32[]{:S(2)}, u32[]{:S(2)}) collective-permute-start(bf16[2,112,512]{2,1,0:T(8,128)(2,1)S(1)} %collective-permute-done.6), channel_id=1, source_target_pairs={{0,240},{16,0},{32,16},{48,32},{64,48},{80,64},{96,80},{112,96},{1... | collective-permute-start | bytes 688136 | tf_op jit(solution)/shard_map/ppermute | solution.py:48
  55.1 4.6 %collective-permute-start.10 = (bf16[2,112,512]{2,1,0:T(8,128)(2,1)S(1)}, bf16[2,112,512]{2,1,0:T(8,128)(2,1)S(1)}, u32[]{:S(2)}, u32[]{:S(2)}) collective-permute-start(bf16[2,112,512]{2,1,0:T(8,128)(2,1)S(1)} %collective-permute-done.8), channel_id=1, source_target_pairs={{0,240},{16,0},{32,16},{48,32},{64,48},{80,64},{96,80},{112,96},{1... | collective-permute-start | bytes 688136 | tf_op jit(solution)/shard_map/ppermute | solution.py:48
  63.0 4.6 %collective-permute-start.12 = (bf16[2,112,512]{2,1,0:T(8,128)(2,1)S(1)}, bf16[2,112,512]{2,1,0:T(8,128)(2,1)S(1)}, u32[]{:S(2)}, u32[]{:S(2)}) collective-permute-start(bf16[2,112,512]{2,1,0:T(8,128)(2,1)S(1)} %collective-permute-done.10), channel_id=1, source_target_pairs={{0,240},{16,0},{32,16},{48,32},{64,48},{80,64},{96,80},{112,96},{1... | collective-permute-start | bytes 688136 | tf_op jit(solution)/shard_map/ppermute | solution.py:48
  71.0 4.6 %collective-permute-start.14 = (bf16[2,112,512]{2,1,0:T(8,128)(2,1)S(1)}, bf16[2,112,512]{2,1,0:T(8,128)(2,1)S(1)}, u32[]{:S(2)}, u32[]{:S(2)}) collective-permute-start(bf16[2,112,512]{2,1,0:T(8,128)(2,1)S(1)} %collective-permute-done.12), channel_id=1, source_target_pairs={{0,240},{16,0},{32,16},{48,32},{64,48},{80,64},{96,80},{112,96},{1... | collective-permute-start | bytes 688136 | tf_op jit(solution)/shard_map/ppermute | solution.py:48
  80.2 7.6 %collective-permute-done.15 = bf16[2,112,512]{2,1,0:T(8,128)(2,1)S(1)} collective-permute-done((bf16[2,112,512]{2,1,0:T(8,128)(2,1)S(1)}, bf16[2,112,512]{2,1,0:T(8,128)(2,1)S(1)}, u32[]{:S(2)}, u32[]{:S(2)}) %collective-permute-start.15) | collective-permute-done | bytes 229408 | tf_op jit(solution)/shard_map/ppermute | solution.py:45
  95.9 4.1 %collective-permute-start.16 = (bf16[320,1,256]{2,0,1:T(8,128)(2,1)S(1)}, bf16[320,1,256]{2,0,1:T(8,128)(2,1)S(1)}, u32[]{:S(2)}, u32[]{:S(2)}) collective-permute-start(bf16[320,1,256]{2,0,1:T(8,128)(2,1)S(1)} %get-tuple-element.71), channel_id=1, source_target_pairs={{0,256},{16,272},{32,288},{48,304},{64,320},{80,336},{96,352},{112... | collective-permute-start | bytes 491528 | tf_op jit(solution)/shard_map/ppermute | solution.py:34
  100.4 3.1 %collective-permute-done.16 = bf16[320,1,256]{2,0,1:T(8,128)(2,1)S(1)} collective-permute-done((bf16[320,1,256]{2,0,1:T(8,128)(2,1)S(1)}, bf16[320,1,256]{2,0,1:T(8,128)(2,1)S(1)}, u32[]{:S(2)}, u32[]{:S(2)}) %collective-permute-start.16) | collective-permute-done | bytes 163872 | tf_op jit(solution)/shard_map/ppermute | solution.py:34
  105.4 3.4 %collective-permute-start.17 = (bf16[2,320,1,256]{3,1,2,0:T(8,128)(2,1)S(1)}, bf16[2,320,1,256]{3,1,2,0:T(8,128)(2,1)S(1)}, u32[]{:S(2)}, u32[]{:S(2)}) collective-permute-start(bf16[2,320,1,256]{3,1,2,0:T(8,128)(2,1)S(1)} %maximum_select_fusion), channel_id=1, source_target_pairs={{0,16},{16,32},{32,48},{48,64},{64,80},{80,96},{96,112},{112,128},... | collective-permute-start | bytes 983048 | tf_op jit(solution)/shard_map/ppermute | solution.py:45
  111.3 3.4 %collective-permute-start.20 = (bf16[2,320,1,256]{3,1,2,0:T(8,128)(2,1)S(1)}, bf16[2,320,1,256]{3,1,2,0:T(8,128)(2,1)S(1)}, u32[]{:S(2)}, u32[]{:S(2)}) collective-permute-start(bf16[2,320,1,256]{3,1,2,0:T(8,128)(2,1)S(1)} %collective-permute-done.18), channel_id=1, source_target_pairs={{0,240},{16,0},{32,16},{48,32},{64,48},{80,64},{96,80},{112,96},{1... | collective-permute-start | bytes 983048 | tf_op jit(solution)/shard_map/ppermute | solution.py:48
  117.5 3.3 %collective-permute-done.20 = bf16[2,320,1,256]{3,1,2,0:T(8,128)(2,1)S(1)} collective-permute-done((bf16[2,320,1,256]{3,1,2,0:T(8,128)(2,1)S(1)}, bf16[2,320,1,256]{3,1,2,0:T(8,128)(2,1)S(1)}, u32[]{:S(2)}, u32[]{:S(2)}) %collective-permute-start.20) | collective-permute-done | bytes 327712 | tf_op jit(solution)/shard_map/ppermute | solution.py:48
  120.8 5.3 %collective-permute-start.22 = (bf16[2,320,1,256]{3,1,2,0:T(8,128)(2,1)S(1)}, bf16[2,320,1,256]{3,1,2,0:T(8,128)(2,1)S(1)}, u32[]{:S(2)}, u32[]{:S(2)}) collective-permute-start(bf16[2,320,1,256]{3,1,2,0:T(8,128)(2,1)S(1)} %collective-permute-done.20), channel_id=1, source_target_pairs={{0,240},{16,0},{32,16},{48,32},{64,48},{80,64},{96,80},{112,96},{1... | collective-permute-start | bytes 983048 | tf_op jit(solution)/shard_map/ppermute | solution.py:48
  131.2 5.3 %collective-permute-start.24 = (bf16[2,320,1,256]{3,1,2,0:T(8,128)(2,1)S(1)}, bf16[2,320,1,256]{3,1,2,0:T(8,128)(2,1)S(1)}, u32[]{:S(2)}, u32[]{:S(2)}) collective-permute-start(bf16[2,320,1,256]{3,1,2,0:T(8,128)(2,1)S(1)} %collective-permute-done.22), channel_id=1, source_target_pairs={{0,240},{16,0},{32,16},{48,32},{64,48},{80,64},{96,80},{112,96},{1... | collective-permute-start | bytes 983048 | tf_op jit(solution)/shard_map/ppermute | solution.py:48
  140.8 5.3 %collective-permute-start.26 = (bf16[2,320,1,256]{3,1,2,0:T(8,128)(2,1)S(1)}, bf16[2,320,1,256]{3,1,2,0:T(8,128)(2,1)S(1)}, u32[]{:S(2)}, u32[]{:S(2)}) collective-permute-start(bf16[2,320,1,256]{3,1,2,0:T(8,128)(2,1)S(1)} %collective-permute-done.24), channel_id=1, source_target_pairs={{0,240},{16,0},{32,16},{48,32},{64,48},{80,64},{96,80},{112,96},{1... | collective-permute-start | bytes 983048 | tf_op jit(solution)/shard_map/ppermute | solution.py:48
  150.1 5.0 %collective-permute-start.28 = (bf16[2,320,1,256]{3,1,2,0:T(8,128)(2,1)S(1)}, bf16[2,320,1,256]{3,1,2,0:T(8,128)(2,1)S(1)}, u32[]{:S(2)}, u32[]{:S(2)}) collective-permute-start(bf16[2,320,1,256]{3,1,2,0:T(8,128)(2,1)S(1)} %collective-permute-done.26), channel_id=1, source_target_pairs={{0,240},{16,0},{32,16},{48,32},{64,48},{80,64},{96,80},{112,96},{1... | collective-permute-start | bytes 983048 | tf_op jit(solution)/shard_map/ppermute | solution.py:48
  159.1 5.0 %collective-permute-start.30 = (bf16[2,320,1,256]{3,1,2,0:T(8,128)(2,1)S(1)}, bf16[2,320,1,256]{3,1,2,0:T(8,128)(2,1)S(1)}, u32[]{:S(2)}, u32[]{:S(2)}) collective-permute-start(bf16[2,320,1,256]{3,1,2,0:T(8,128)(2,1)S(1)} %collective-permute-done.28), channel_id=1, source_target_pairs={{0,240},{16,0},{32,16},{48,32},{64,48},{80,64},{96,80},{112,96},{1... | collective-permute-start | bytes 983048 | tf_op jit(solution)/shard_map/ppermute | solution.py:48
  167.0 6.3 %collective-permute-done.29 = bf16[2,320,1,256]{3,1,2,0:T(8,128)(2,1)S(1)} collective-permute-done((bf16[2,320,1,256]{3,1,2,0:T(8,128)(2,1)S(1)}, bf16[2,320,1,256]{3,1,2,0:T(8,128)(2,1)S(1)}, u32[]{:S(2)}, u32[]{:S(2)}) %collective-permute-start.29) | collective-permute-done | bytes 327712 | tf_op jit(solution)/shard_map/ppermute | solution.py:45
  176.0 7.4 %collective-permute-done.31 = bf16[2,320,1,256]{3,1,2,0:T(8,128)(2,1)S(1)} collective-permute-done((bf16[2,320,1,256]{3,1,2,0:T(8,128)(2,1)S(1)}, bf16[2,320,1,256]{3,1,2,0:T(8,128)(2,1)S(1)}, u32[]{:S(2)}, u32[]{:S(2)}) %collective-permute-start.31) | collective-permute-done | bytes 327712 | tf_op jit(solution)/shard_map/ppermute | solution.py:45
  195.2 3.6 %fusion.89 = f32[320,2,2,2,2,192]{0,5,4,3,2,1:T(8,128)} fusion(bf16[2,2,2,2,192,128]{5,4,3,2,1,0:T(8,128)(2,1)S(1)} %bitcast.629, f32[320,1,128]{2,0,1:T(8,128)S(1)} %fusion.84, f32[320,1,640]{2,0,1:T(8,128)S(1)} %get-tuple-element.105, f32[320]{0:T(512)S(1)} %get-tuple-element.50, s32[640]{0:T(1024)S(1)} %add_select_fusion, s32[320]{0:T(512)S(1)} %ge.260, ...), kind=kOutput, calls=%fused_computation.181 | convolution fusion | flops 305438720 | bytes 5877760 | tf_op jit(solution)/shard_map/nhe,rhe->nr/dot_general | solution.py:205
  198.8 2.6 fusion.50
  201.5 20.5 %collective-permute-start.32 = (bf16[320,2,2,2,192]{0,4,3,2,1:T(8,128)(2,1)S(1)}, bf16[320,2,2,2,192]{0,4,3,2,1:T(8,128)(2,1)}, u32[]{:S(2)}, u32[]{:S(2)}) collective-permute-start(bf16[320,2,2,2,192]{0,4,3,2,1:T(8,128)(2,1)S(1)} %fusion.50), channel_id=1, source_target_pairs={{0,1},{1,0},{2,3},{3,2},{4,5},{5,4},{6,7},{7,6},{8,9},{9,8},{10,11... | collective-permute-start | bytes 2949128 | tf_op jit(solution)/shard_map/ppermute | solution.py:78
  224.7 3.1 %fusion.7 = f32[320,2,2,2,192]{0,4,3,2,1:T(8,128)S(1)} fusion(bf16[320,2,2,2,192]{0,4,3,2,1:T(8,128)(2,1)} %collective-permute-done.32, f32[320,2,2,2,2,192]{0,5,4,3,2,1:T(8,128)} %fusion.89, pred[]{:T(512)S(6)} %eq.56), kind=kLoop, calls=%fused_computation.34 | loop fusion | flops 1474560 | bytes 6881281 | tf_op jit(solution)/shard_map/add | solution.py:81
  232.2 15.5 %collective-permute-done.33 = bf16[320,2,2,192]{0,3,2,1:T(8,128)(2,1)} collective-permute-done((bf16[320,2,2,192]{0,3,2,1:T(8,128)(2,1)}, bf16[320,2,2,192]{0,3,2,1:T(8,128)(2,1)}, u32[]{:S(2)}, u32[]{:S(2)}) %collective-permute-start.33) | collective-permute-done | bytes 491552 | tf_op jit(solution)/shard_map/ppermute | solution.py:78
  250.7 3.2 %collective-permute-start.34 = (bf16[320,2,192]{0,2,1:T(8,128)(2,1)}, bf16[320,2,192]{0,2,1:T(8,128)(2,1)}, u32[]{:S(2)}, u32[]{:S(2)}) collective-permute-start(bf16[320,2,192]{0,2,1:T(8,128)(2,1)} %fusion.293), channel_id=1, source_target_pairs={{0,2},{1,3},{2,0},{3,1},{4,6},{5,7},{6,4},{7,5},{8,10},{9,11},{10,... | collective-permute-start | bytes 737288 | tf_op jit(solution)/shard_map/ppermute | solution.py:78
  254.6 6.5 %collective-permute-done.34 = bf16[320,2,192]{0,2,1:T(8,128)(2,1)} collective-permute-done((bf16[320,2,192]{0,2,1:T(8,128)(2,1)}, bf16[320,2,192]{0,2,1:T(8,128)(2,1)}, u32[]{:S(2)}, u32[]{:S(2)}) %collective-permute-start.34) | collective-permute-done | bytes 245792 | tf_op jit(solution)/shard_map/ppermute | solution.py:78
  262.2 4.7 %collective-permute-start.35 = (bf16[320,192]{0,1:T(8,128)(2,1)S(1)}, bf16[320,192]{0,1:T(8,128)(2,1)S(1)}, u32[]{:S(2)}, u32[]{:S(2)}) collective-permute-start(bf16[320,192]{0,1:T(8,128)(2,1)S(1)} %fusion.299), channel_id=1, source_target_pairs={{0,4},{1,5},{2,6},{3,7},{4,0},{5,1},{6,2},{7,3},{8,12},{9,13},{10,... | collective-permute-start | bytes 368648 | tf_op jit(solution)/shard_map/ppermute | solution.py:78
  266.9 6.0 %fusion.288 = f32[2,10,16,192]{3,2,1,0:T(8,128)S(1)} fusion(f32[4,10,16,192]{3,2,1,0:T(8,128)} %bitcast.630, f32[2,10,16,192]{3,2,1,0:T(8,128)S(1)} %bitcast.633, f32[2,10,16,192]{3,2,1,0:T(8,128)S(1)} %bitcast.634, f32[2,10,16,192]{3,2,1,0:T(8,128)S(1)} %bitcast.635, f32[192]{0:T(256)S(1)} %bitcast.672, f32[192]{0:T(256)S(1)} %bitcast.673, ...), kind=kLoop, calls=%fused_computation.360 | loop fusion | flops 3256320 | bytes 1495296 | tf_op jit(solution)/shard_map/add | solution.py:226
  (203 shorter events, 92.7 us)
Async XLA Ops:
  2.3 10.1 %collective-permute-start = (bf16[112,512]{1,0:T(8,128)(2,1)S(1)}, bf16[112,512]{1,0:T(8,128)(2,1)S(1)}, u32[]{:S(2)}, u32[]{:S(2)}) collective-permute-start(bf16[112,512]{1,0:T(8,128)(2,1)S(1)} %get-tuple-element.74), channel_id=1, source_target_pairs={{0,256},{16,272},{32,288},{48,304},{64,320},{80,336},{96,352},{112... | collective-permute-start | bytes 344072 | tf_op jit(solution)/shard_map/ppermute | solution.py:34
  12.4 16.1 %collective-permute-start.1 = (bf16[2,112,512]{2,1,0:T(8,128)(2,1)S(1)}, bf16[2,112,512]{2,1,0:T(8,128)(2,1)S(1)}, u32[]{:S(2)}, u32[]{:S(2)}) collective-permute-start(bf16[2,112,512]{2,1,0:T(8,128)(2,1)S(1)} %maximum_select_fusion.2), channel_id=1, source_target_pairs={{0,16},{16,32},{32,48},{48,64},{64,80},{80,96},{96,112},{112,128},... | collective-permute-start | bytes 688136 | tf_op jit(solution)/shard_map/ppermute | solution.py:45
  16.0 14.5 %collective-permute-start.2 = (bf16[2,112,512]{2,1,0:T(8,128)(2,1)S(1)}, bf16[2,112,512]{2,1,0:T(8,128)(2,1)S(1)}, u32[]{:S(2)}, u32[]{:S(2)}) collective-permute-start(bf16[2,112,512]{2,1,0:T(8,128)(2,1)S(1)} %maximum_select_fusion.2), channel_id=1, source_target_pairs={{0,240},{16,0},{32,16},{48,32},{64,48},{80,64},{96,80},{112,96},{1... | collective-permute-start | bytes 688136 | tf_op jit(solution)/shard_map/ppermute | solution.py:48
  28.6 8.6 %collective-permute-start.3 = (bf16[2,112,512]{2,1,0:T(8,128)(2,1)S(1)}, bf16[2,112,512]{2,1,0:T(8,128)(2,1)S(1)}, u32[]{:S(2)}, u32[]{:S(2)}) collective-permute-start(bf16[2,112,512]{2,1,0:T(8,128)(2,1)S(1)} %collective-permute-done.1), channel_id=1, source_target_pairs={{0,16},{16,32},{32,48},{48,64},{64,80},{80,96},{96,112},{112,128},... | collective-permute-start | bytes 688136 | tf_op jit(solution)/shard_map/ppermute | solution.py:45
  30.5 8.6 %collective-permute-start.4 = (bf16[2,112,512]{2,1,0:T(8,128)(2,1)S(1)}, bf16[2,112,512]{2,1,0:T(8,128)(2,1)S(1)}, u32[]{:S(2)}, u32[]{:S(2)}) collective-permute-start(bf16[2,112,512]{2,1,0:T(8,128)(2,1)S(1)} %collective-permute-done.2), channel_id=1, source_target_pairs={{0,240},{16,0},{32,16},{48,32},{64,48},{80,64},{96,80},{112,96},{1... | collective-permute-start | bytes 688136 | tf_op jit(solution)/shard_map/ppermute | solution.py:48
  37.2 8.0 %collective-permute-start.5 = (bf16[2,112,512]{2,1,0:T(8,128)(2,1)S(1)}, bf16[2,112,512]{2,1,0:T(8,128)(2,1)S(1)}, u32[]{:S(2)}, u32[]{:S(2)}) collective-permute-start(bf16[2,112,512]{2,1,0:T(8,128)(2,1)S(1)} %collective-permute-done.3), channel_id=1, source_target_pairs={{0,16},{16,32},{32,48},{48,64},{64,80},{80,96},{96,112},{112,128},... | collective-permute-start | bytes 688136 | tf_op jit(solution)/shard_map/ppermute | solution.py:45
  39.1 8.0 %collective-permute-start.6 = (bf16[2,112,512]{2,1,0:T(8,128)(2,1)S(1)}, bf16[2,112,512]{2,1,0:T(8,128)(2,1)S(1)}, u32[]{:S(2)}, u32[]{:S(2)}) collective-permute-start(bf16[2,112,512]{2,1,0:T(8,128)(2,1)S(1)} %collective-permute-done.4), channel_id=1, source_target_pairs={{0,240},{16,0},{32,16},{48,32},{64,48},{80,64},{96,80},{112,96},{1... | collective-permute-start | bytes 688136 | tf_op jit(solution)/shard_map/ppermute | solution.py:48
  45.2 8.0 %collective-permute-start.7 = (bf16[2,112,512]{2,1,0:T(8,128)(2,1)S(1)}, bf16[2,112,512]{2,1,0:T(8,128)(2,1)S(1)}, u32[]{:S(2)}, u32[]{:S(2)}) collective-permute-start(bf16[2,112,512]{2,1,0:T(8,128)(2,1)S(1)} %collective-permute-done.5), channel_id=1, source_target_pairs={{0,16},{16,32},{32,48},{48,64},{64,80},{80,96},{96,112},{112,128},... | collective-permute-start | bytes 688136 | tf_op jit(solution)/shard_map/ppermute | solution.py:45
  47.1 8.0 %collective-permute-start.8 = (bf16[2,112,512]{2,1,0:T(8,128)(2,1)S(1)}, bf16[2,112,512]{2,1,0:T(8,128)(2,1)S(1)}, u32[]{:S(2)}, u32[]{:S(2)}) collective-permute-start(bf16[2,112,512]{2,1,0:T(8,128)(2,1)S(1)} %collective-permute-done.6), channel_id=1, source_target_pairs={{0,240},{16,0},{32,16},{48,32},{64,48},{80,64},{96,80},{112,96},{1... | collective-permute-start | bytes 688136 | tf_op jit(solution)/shard_map/ppermute | solution.py:48
  53.1 8.0 %collective-permute-start.9 = (bf16[2,112,512]{2,1,0:T(8,128)(2,1)S(1)}, bf16[2,112,512]{2,1,0:T(8,128)(2,1)S(1)}, u32[]{:S(2)}, u32[]{:S(2)}) collective-permute-start(bf16[2,112,512]{2,1,0:T(8,128)(2,1)S(1)} %collective-permute-done.7), channel_id=1, source_target_pairs={{0,16},{16,32},{32,48},{48,64},{64,80},{80,96},{96,112},{112,128},... | collective-permute-start | bytes 688136 | tf_op jit(solution)/shard_map/ppermute | solution.py:45
  61.1 8.0 %collective-permute-start.11 = (bf16[2,112,512]{2,1,0:T(8,128)(2,1)S(1)}, bf16[2,112,512]{2,1,0:T(8,128)(2,1)S(1)}, u32[]{:S(2)}, u32[]{:S(2)}) collective-permute-start(bf16[2,112,512]{2,1,0:T(8,128)(2,1)S(1)} %collective-permute-done.9), channel_id=1, source_target_pairs={{0,16},{16,32},{32,48},{48,64},{64,80},{80,96},{96,112},{112,128},... | collective-permute-start | bytes 688136 | tf_op jit(solution)/shard_map/ppermute | solution.py:45
  69.1 8.8 %collective-permute-start.13 = (bf16[2,112,512]{2,1,0:T(8,128)(2,1)S(1)}, bf16[2,112,512]{2,1,0:T(8,128)(2,1)S(1)}, u32[]{:S(2)}, u32[]{:S(2)}) collective-permute-start(bf16[2,112,512]{2,1,0:T(8,128)(2,1)S(1)} %collective-permute-done.11), channel_id=1, source_target_pairs={{0,16},{16,32},{32,48},{48,64},{64,80},{80,96},{96,112},{112,128},... | collective-permute-start | bytes 688136 | tf_op jit(solution)/shard_map/ppermute | solution.py:45
  71.0 9.2 %collective-permute-start.14 = (bf16[2,112,512]{2,1,0:T(8,128)(2,1)S(1)}, bf16[2,112,512]{2,1,0:T(8,128)(2,1)S(1)}, u32[]{:S(2)}, u32[]{:S(2)}) collective-permute-start(bf16[2,112,512]{2,1,0:T(8,128)(2,1)S(1)} %collective-permute-done.12), channel_id=1, source_target_pairs={{0,240},{16,0},{32,16},{48,32},{64,48},{80,64},{96,80},{112,96},{1... | collective-permute-start | bytes 688136 | tf_op jit(solution)/shard_map/ppermute | solution.py:48
  78.2 9.6 %collective-permute-start.15 = (bf16[2,112,512]{2,1,0:T(8,128)(2,1)S(1)}, bf16[2,112,512]{2,1,0:T(8,128)(2,1)S(1)}, u32[]{:S(2)}, u32[]{:S(2)}) collective-permute-start(bf16[2,112,512]{2,1,0:T(8,128)(2,1)S(1)} %collective-permute-done.13), channel_id=1, source_target_pairs={{0,16},{16,32},{32,48},{48,64},{64,80},{80,96},{96,112},{112,128},... | collective-permute-start | bytes 688136 | tf_op jit(solution)/shard_map/ppermute | solution.py:45
  105.4 9.3 %collective-permute-start.17 = (bf16[2,320,1,256]{3,1,2,0:T(8,128)(2,1)S(1)}, bf16[2,320,1,256]{3,1,2,0:T(8,128)(2,1)S(1)}, u32[]{:S(2)}, u32[]{:S(2)}) collective-permute-start(bf16[2,320,1,256]{3,1,2,0:T(8,128)(2,1)S(1)} %maximum_select_fusion), channel_id=1, source_target_pairs={{0,16},{16,32},{32,48},{48,64},{64,80},{80,96},{96,112},{112,128},... | collective-permute-start | bytes 983048 | tf_op jit(solution)/shard_map/ppermute | solution.py:45
  111.3 9.5 %collective-permute-start.20 = (bf16[2,320,1,256]{3,1,2,0:T(8,128)(2,1)S(1)}, bf16[2,320,1,256]{3,1,2,0:T(8,128)(2,1)S(1)}, u32[]{:S(2)}, u32[]{:S(2)}) collective-permute-start(bf16[2,320,1,256]{3,1,2,0:T(8,128)(2,1)S(1)} %collective-permute-done.18), channel_id=1, source_target_pairs={{0,240},{16,0},{32,16},{48,32},{64,48},{80,64},{96,80},{112,96},{1... | collective-permute-start | bytes 983048 | tf_op jit(solution)/shard_map/ppermute | solution.py:48
  114.7 11.4 %collective-permute-start.19 = (bf16[2,320,1,256]{3,1,2,0:T(8,128)(2,1)S(1)}, bf16[2,320,1,256]{3,1,2,0:T(8,128)(2,1)S(1)}, u32[]{:S(2)}, u32[]{:S(2)}) collective-permute-start(bf16[2,320,1,256]{3,1,2,0:T(8,128)(2,1)S(1)} %collective-permute-done.17), channel_id=1, source_target_pairs={{0,16},{16,32},{32,48},{48,64},{64,80},{80,96},{96,112},{112,128},... | collective-permute-start | bytes 983048 | tf_op jit(solution)/shard_map/ppermute | solution.py:45
  120.8 10.5 %collective-permute-start.22 = (bf16[2,320,1,256]{3,1,2,0:T(8,128)(2,1)S(1)}, bf16[2,320,1,256]{3,1,2,0:T(8,128)(2,1)S(1)}, u32[]{:S(2)}, u32[]{:S(2)}) collective-permute-start(bf16[2,320,1,256]{3,1,2,0:T(8,128)(2,1)S(1)} %collective-permute-done.20), channel_id=1, source_target_pairs={{0,240},{16,0},{32,16},{48,32},{64,48},{80,64},{96,80},{112,96},{1... | collective-permute-start | bytes 983048 | tf_op jit(solution)/shard_map/ppermute | solution.py:48
  126.1 10.5 %collective-permute-start.21 = (bf16[2,320,1,256]{3,1,2,0:T(8,128)(2,1)S(1)}, bf16[2,320,1,256]{3,1,2,0:T(8,128)(2,1)S(1)}, u32[]{:S(2)}, u32[]{:S(2)}) collective-permute-start(bf16[2,320,1,256]{3,1,2,0:T(8,128)(2,1)S(1)} %collective-permute-done.19), channel_id=1, source_target_pairs={{0,16},{16,32},{32,48},{48,64},{64,80},{80,96},{96,112},{112,128},... | collective-permute-start | bytes 983048 | tf_op jit(solution)/shard_map/ppermute | solution.py:45
  131.2 9.6 %collective-permute-start.24 = (bf16[2,320,1,256]{3,1,2,0:T(8,128)(2,1)S(1)}, bf16[2,320,1,256]{3,1,2,0:T(8,128)(2,1)S(1)}, u32[]{:S(2)}, u32[]{:S(2)}) collective-permute-start(bf16[2,320,1,256]{3,1,2,0:T(8,128)(2,1)S(1)} %collective-permute-done.22), channel_id=1, source_target_pairs={{0,240},{16,0},{32,16},{48,32},{64,48},{80,64},{96,80},{112,96},{1... | collective-permute-start | bytes 983048 | tf_op jit(solution)/shard_map/ppermute | solution.py:48
  136.6 9.5 %collective-permute-start.23 = (bf16[2,320,1,256]{3,1,2,0:T(8,128)(2,1)S(1)}, bf16[2,320,1,256]{3,1,2,0:T(8,128)(2,1)S(1)}, u32[]{:S(2)}, u32[]{:S(2)}) collective-permute-start(bf16[2,320,1,256]{3,1,2,0:T(8,128)(2,1)S(1)} %collective-permute-done.21), channel_id=1, source_target_pairs={{0,16},{16,32},{32,48},{48,64},{64,80},{80,96},{96,112},{112,128},... | collective-permute-start | bytes 983048 | tf_op jit(solution)/shard_map/ppermute | solution.py:45
  140.8 9.3 %collective-permute-start.26 = (bf16[2,320,1,256]{3,1,2,0:T(8,128)(2,1)S(1)}, bf16[2,320,1,256]{3,1,2,0:T(8,128)(2,1)S(1)}, u32[]{:S(2)}, u32[]{:S(2)}) collective-permute-start(bf16[2,320,1,256]{3,1,2,0:T(8,128)(2,1)S(1)} %collective-permute-done.24), channel_id=1, source_target_pairs={{0,240},{16,0},{32,16},{48,32},{64,48},{80,64},{96,80},{112,96},{1... | collective-permute-start | bytes 983048 | tf_op jit(solution)/shard_map/ppermute | solution.py:48
  146.1 9.0 %collective-permute-start.25 = (bf16[2,320,1,256]{3,1,2,0:T(8,128)(2,1)S(1)}, bf16[2,320,1,256]{3,1,2,0:T(8,128)(2,1)S(1)}, u32[]{:S(2)}, u32[]{:S(2)}) collective-permute-start(bf16[2,320,1,256]{3,1,2,0:T(8,128)(2,1)S(1)} %collective-permute-done.23), channel_id=1, source_target_pairs={{0,16},{16,32},{32,48},{48,64},{64,80},{80,96},{96,112},{112,128},... | collective-permute-start | bytes 983048 | tf_op jit(solution)/shard_map/ppermute | solution.py:45
  150.1 9.0 %collective-permute-start.28 = (bf16[2,320,1,256]{3,1,2,0:T(8,128)(2,1)S(1)}, bf16[2,320,1,256]{3,1,2,0:T(8,128)(2,1)S(1)}, u32[]{:S(2)}, u32[]{:S(2)}) collective-permute-start(bf16[2,320,1,256]{3,1,2,0:T(8,128)(2,1)S(1)} %collective-permute-done.26), channel_id=1, source_target_pairs={{0,240},{16,0},{32,16},{48,32},{64,48},{80,64},{96,80},{112,96},{1... | collective-permute-start | bytes 983048 | tf_op jit(solution)/shard_map/ppermute | solution.py:48
  155.1 9.0 %collective-permute-start.27 = (bf16[2,320,1,256]{3,1,2,0:T(8,128)(2,1)S(1)}, bf16[2,320,1,256]{3,1,2,0:T(8,128)(2,1)S(1)}, u32[]{:S(2)}, u32[]{:S(2)}) collective-permute-start(bf16[2,320,1,256]{3,1,2,0:T(8,128)(2,1)S(1)} %collective-permute-done.25), channel_id=1, source_target_pairs={{0,16},{16,32},{32,48},{48,64},{64,80},{80,96},{96,112},{112,128},... | collective-permute-start | bytes 983048 | tf_op jit(solution)/shard_map/ppermute | solution.py:45
  159.1 16.0 %collective-permute-start.30 = (bf16[2,320,1,256]{3,1,2,0:T(8,128)(2,1)S(1)}, bf16[2,320,1,256]{3,1,2,0:T(8,128)(2,1)S(1)}, u32[]{:S(2)}, u32[]{:S(2)}) collective-permute-start(bf16[2,320,1,256]{3,1,2,0:T(8,128)(2,1)S(1)} %collective-permute-done.28), channel_id=1, source_target_pairs={{0,240},{16,0},{32,16},{48,32},{64,48},{80,64},{96,80},{112,96},{1... | collective-permute-start | bytes 983048 | tf_op jit(solution)/shard_map/ppermute | solution.py:48
  164.2 9.1 %collective-permute-start.29 = (bf16[2,320,1,256]{3,1,2,0:T(8,128)(2,1)S(1)}, bf16[2,320,1,256]{3,1,2,0:T(8,128)(2,1)S(1)}, u32[]{:S(2)}, u32[]{:S(2)}) collective-permute-start(bf16[2,320,1,256]{3,1,2,0:T(8,128)(2,1)S(1)} %collective-permute-done.27), channel_id=1, source_target_pairs={{0,16},{16,32},{32,48},{48,64},{64,80},{80,96},{96,112},{112,128},... | collective-permute-start | bytes 983048 | tf_op jit(solution)/shard_map/ppermute | solution.py:45
  173.2 10.2 %collective-permute-start.31 = (bf16[2,320,1,256]{3,1,2,0:T(8,128)(2,1)S(1)}, bf16[2,320,1,256]{3,1,2,0:T(8,128)(2,1)S(1)}, u32[]{:S(2)}, u32[]{:S(2)}) collective-permute-start(bf16[2,320,1,256]{3,1,2,0:T(8,128)(2,1)S(1)} %collective-permute-done.29), channel_id=1, source_target_pairs={{0,16},{16,32},{32,48},{48,64},{64,80},{80,96},{96,112},{112,128},... | collective-permute-start | bytes 983048 | tf_op jit(solution)/shard_map/ppermute | solution.py:45
  201.5 23.2 %collective-permute-start.32 = (bf16[320,2,2,2,192]{0,4,3,2,1:T(8,128)(2,1)S(1)}, bf16[320,2,2,2,192]{0,4,3,2,1:T(8,128)(2,1)}, u32[]{:S(2)}, u32[]{:S(2)}) collective-permute-start(bf16[320,2,2,2,192]{0,4,3,2,1:T(8,128)(2,1)S(1)} %fusion.50), channel_id=1, source_target_pairs={{0,1},{1,0},{2,3},{3,2},{4,5},{5,4},{6,7},{7,6},{8,9},{9,8},{10,11... | collective-permute-start | bytes 2949128 | tf_op jit(solution)/shard_map/ppermute | solution.py:78
  228.7 18.9 %collective-permute-start.33 = (bf16[320,2,2,192]{0,3,2,1:T(8,128)(2,1)}, bf16[320,2,2,192]{0,3,2,1:T(8,128)(2,1)}, u32[]{:S(2)}, u32[]{:S(2)}) collective-permute-start(bf16[320,2,2,192]{0,3,2,1:T(8,128)(2,1)} %fusion.90), channel_id=1, source_target_pairs={{0,8},{1,9},{2,10},{3,11},{4,12},{5,13},{6,14},{7,15},{8,0},{9,1},... | collective-permute-start | bytes 1474568 | tf_op jit(solution)/shard_map/ppermute | solution.py:78
  250.7 10.4 %collective-permute-start.34 = (bf16[320,2,192]{0,2,1:T(8,128)(2,1)}, bf16[320,2,192]{0,2,1:T(8,128)(2,1)}, u32[]{:S(2)}, u32[]{:S(2)}) collective-permute-start(bf16[320,2,192]{0,2,1:T(8,128)(2,1)} %fusion.293), channel_id=1, source_target_pairs={{0,2},{1,3},{2,0},{3,1},{4,6},{5,7},{6,4},{7,5},{8,10},{9,11},{10,... | collective-permute-start | bytes 737288 | tf_op jit(solution)/shard_map/ppermute | solution.py:78
  262.2 10.8 %collective-permute-start.35 = (bf16[320,192]{0,1:T(8,128)(2,1)S(1)}, bf16[320,192]{0,1:T(8,128)(2,1)S(1)}, u32[]{:S(2)}, u32[]{:S(2)}) collective-permute-start(bf16[320,192]{0,1:T(8,128)(2,1)S(1)} %fusion.299), channel_id=1, source_target_pairs={{0,4},{1,5},{2,6},{3,7},{4,0},{5,1},{6,2},{7,3},{8,12},{9,13},{10,... | collective-permute-start | bytes 368648 | tf_op jit(solution)/shard_map/ppermute | solution.py:78
  (15 other events, 105.5 us)

commit v3 on v2

--- a/solution.py
+++ b/solution.py
@@ -59,28 +59,27 @@
     return gathered.reshape((2 * ring * block.shape[0],) + block.shape[1:])
 
 
-def halving_scatter(partial, axis):
+def block_order(size, order):
+    bits = len(order)
+    return [
+        sum(((j >> order[s]) & 1) << (bits - 1 - s) for s in range(bits)) for j in range(size)
+    ]
+
+
+def halving_scatter(partial, axis, order):
     size = lax.axis_size(axis)
-    bits = size.bit_length() - 1
     position = lax.axis_index(axis)
-    rows, cols = partial.shape
-    width = cols // size
-    state = partial.reshape((rows,) + (2,) * bits + (width,))
-    axis_bits = [bits - 1 - a for a in range(bits)]
-    order = [0] + ([bits - 1] if bits > 1 else []) + list(range(1, bits - 1))
+    state = partial
     for bit in order:
-        dim = 1 + axis_bits.index(bit)
+        half = state.shape[1] // 2
         mine = (position >> bit) & 1
-        low = lax.index_in_dim(state, 0, dim, keepdims=False)
-        high = lax.index_in_dim(state, 1, dim, keepdims=False)
-        keep = jnp.where(mine == 0, low, high)
-        send = jnp.where(mine == 0, high, low)
+        keep = lax.dynamic_slice_in_dim(state, mine * half, half, 1)
+        send = lax.dynamic_slice_in_dim(state, (1 - mine) * half, half, 1)
         got = lax.ppermute(
             send.astype(jnp.bfloat16), axis, [(i, i ^ (1 << bit)) for i in range(size)]
         )
         state = keep + got.astype(jnp.float32)
-        axis_bits.remove(bit)
-    return state.reshape(rows, width)
+    return state
 
 
 def attend_piece(state_now, kv_piece, key_frame, queries, query_frame, query_first, head_dim):
@@ -200,15 +199,147 @@
             query_first,
             head_dim,
         )
+    run_max, run_sum, accumulated = state_now
+    key_part = kv_piece[:, :, :head_dim]
+    value_part = kv_piece[:, :, head_dim:]
+    scores = jnp.einsum(
+        "nhe,mhe->nhm", queries, key_part, preferred_element_type=jnp.float32
+    ) * head_dim ** (-0.5)
+    allowed = (key_frame[None, :] <= query_frame[:, None]) & (
+        key_frame[None, :] >= query_first[:, None]
+    )
+    masked = jnp.where(allowed[:, None, :], scores, NEG)
+    new_max = jnp.maximum(run_max, masked.max(-1))
+    exponent = jnp.where(allowed[:, None, :], jnp.exp(masked - new_max[..., None]), 0.0)
+    factor = jnp.exp(run_max - new_max)
+    run_sum = run_sum * factor + exponent.sum(-1)
+    accumulated = accumulated * factor[..., None] + jnp.einsum(
+        "nhm,mhe->nhe",
+        exponent.astype(jnp.bfloat16),
+        value_part,
+        preferred_element_type=jnp.float32,
+    )
+    return (new_max, run_sum, accumulated)
+
+
+def per_device(
+    latents, timestep, offsets, qkv_weight, mod_weight, gate_weight, out_weight, conv_weight
+):
+    tok_rows = latents.shape[0]
+    heads_here = qkv_weight.shape[1]
+    head_dim = out_weight.shape[2]
+    chan_here = gate_weight.shape[1]
+    frame_size = HH * WW
+    frames_here = tok_rows // frame_size
+    position = lax.axis_index("ctx")
+    column = lax.axis_index("fsdp")
+    time_act = time_features(timestep, gate_weight.shape[0])
+    gate_vec = jnp.dot(time_act, gate_weight, preferred_element_type=jnp.float32)
+    float_rows = latents.astype(jnp.float32)
+    centred = float_rows - float_rows.mean(-1, keepdims=True)
+    variance = (centred * centred).mean(-1, keepdims=True)
+    normed = centred * lax.rsqrt(variance + EPS)
+
+    rows_here = qkv_weight.shape[0]
+    qkv_width = qkv_weight.shape[2]
+    qkv_cols = heads_here * qkv_width
+    out_cols = heads_here * head_dim
+    width = qkv_cols + out_cols
+    local_shares = jnp.einsum(
+        "rjt,t->rj", mod_weight, time_act, preferred_element_type=jnp.float32
+    )
+    shares_hi = local_shares.astype(jnp.bfloat16)
+    shares_lo = (local_shares - shares_hi.astype(jnp.float32)).astype(jnp.bfloat16)
+    share_count = 4 * rows_here
+    extra_rows = 16 * ((share_count + 16 * width - 1) // (16 * width))
+    share_block = jnp.zeros((extra_rows * width,), jnp.bfloat16)
+    share_block = share_block.at[:share_count].set(
+        jnp.concatenate([shares_hi, shares_lo], axis=1).reshape(share_count)
+    )
+    bundle = jnp.concatenate(
+        [
+            jnp.concatenate(
+                [
+                    qkv_weight.reshape(rows_here, qkv_cols),
+                    out_weight.reshape(rows_here, out_cols),
+                ],
+                axis=1,
+            ),
+            share_block.reshape(extra_rows, width),
+        ],
+        axis=0,
+    )
+    gathered = ring_gather(bundle, "ctx")
+    blocks = gathered.shape[0] // bundle.shape[0]
+    gathered = gathered.reshape(blocks, rows_here + extra_rows, width)
+    full_rows = blocks * rows_here
+    w_piece = gathered[:, :rows_here, :qkv_cols].reshape(full_rows, heads_here, qkv_width)
+    o_piece = gathered[:, :rows_here, qkv_cols:].reshape(full_rows, heads_here, head_dim)
+    share_bits = (
+        gathered[:, rows_here:, :]
+        .reshape(blocks, extra_rows * width)[:, :share_count]
+        .reshape(full_rows, 4)
+        .astype(jnp.float32)
+    )
+    shares = share_bits[:, :2] + share_bits[:, 2:]
+
+    modulated = (normed * (1.0 + shares[:, 1]) + shares[:, 0]).astype(jnp.bfloat16)
+    projected_qkv = jnp.einsum(
+        "nr,rhc->nhc", modulated, w_piece, preferred_element_type=jnp.float32
+    ).astype(jnp.bfloat16)
+    queries = projected_qkv[:, :, :head_dim]
+    packed = projected_qkv[:, :, head_dim:]
+    query_frame = position * frames_here + jnp.arange(tok_rows, dtype=jnp.int32) // frame_size
+    local_first = lax.dynamic_slice_in_dim(offsets, position * frames_here, frames_here, 0)
+    query_first = jnp.repeat(local_first, frame_size)
+    state = (
+        jnp.full((tok_rows, heads_here), NEG, jnp.float32),
+        jnp.zeros((tok_rows, heads_here), jnp.float32),
+        jnp.zeros((tok_rows, heads_here, head_dim), jnp.float32),
+    )
+    kv_pieces, ring = ring_pieces(packed, "ctx")
+    token_ids = jnp.arange(tok_rows, dtype=jnp.int32)
+    step_groups = [kv_pieces[:1]] + [
+        kv_pieces[i : i + 2] for i in range(1, len(kv_pieces), 2)
+    ]
+    for group in step_groups:
+        key_frame = (
+            jnp.concatenate(
+                [
+                    jnp.concatenate(
+                        [source * tok_rows + token_ids, (ring + source) * tok_rows + token_ids]
+                    )
+                    for _, source in group
+                ]
+            )
+            // frame_size
+        )
+        keys_values = jnp.concatenate(
+            [piece.reshape((2 * tok_rows,) + piece.shape[2:]) for piece, _ in group]
+        )
+        state = attend_piece(
+            state, keys_values, key_frame, queries, query_frame, query_first, head_dim
+        )
     run_max, run_sum, accumulated = state
     attended = (accumulated / run_sum[..., None]).astype(jnp.bfloat16)
-    partial_out = jnp.einsum(
-        "nhe,rhe->nr",
-        attended,
-        o_piece,
-        preferred_element_type=jnp.float32,
-    )
-    head_total = halving_scatter(partial_out, "fsdp")
+    size = lax.axis_size("fsdp")
+    bits = size.bit_length() - 1
+    middle = list(range(1, bits - 1))
+    half_rows = tok_rows // 2
+    orders = [[0, bits - 1] + middle, [0] + middle + [bits - 1]]
+    head_parts = []
+    for part, order in enumerate(orders):
+        positions = block_order(size, order)
+        by_block = o_piece.reshape((size, full_rows // size) + o_piece.shape[1:])
+        permuted = jnp.stack([by_block[positions.index(q)] for q in range(size)])
+        partial_out = jnp.einsum(
+            "nhe,rhe->nr",
+            attended[part * half_rows : (part + 1) * half_rows],
+            permuted.reshape(o_piece.shape),
+            preferred_element_type=jnp.float32,
+        )
+        head_parts.append(halving_scatter(partial_out, "fsdp", order))
+    head_total = jnp.concatenate(head_parts, axis=0)
     own_chan = lax.dynamic_slice_in_dim(latents, column * chan_here, chan_here, 1)
     before = passed_along(own_chan, "ctx", 1)
     stacked = (

time: 275 us -> 256 us (0.931); the launches traced: 274 us -> 252 us
  waiting for transfers between devices: 68.9 us -> 55.6 us
  other arithmetic: 29.1 us -> 17.8 us
  starting transfers between devices: 144 us -> 152 us
  matrix products: 18 us -> 13.1 us
    ppermute x4 -> x8, waiting for transfers between devices: 22 us -> 6.74 us  [halving_scatter(): lax.ppermute(send.astype(jnp.bfloat16), axis, [(i, i ^ 1 << bit) for i in...]
    ppermute x4 -> x8, starting transfers between devices: 30.5 us -> 41.5 us  [halving_scatter(): lax.ppermute(send.astype(jnp.bfloat16), axis, [(i, i ^ 1 << bit) for i in...]
    ppermute x14, waiting for transfers between devices: 10.1 us -> 0.04 us  [ring_pieces(): behind = lax.ppermute(behind, axis, backward)]
    ppermute x16, waiting for transfers between devices: 33.7 us -> 43.2 us  [ring_pieces(): ahead = lax.ppermute(ahead, axis, forward)]
    add x3 -> x8, other arithmetic: 5.35 us -> 0.6 us  [halving_scatter(): state = keep + got.astype(jnp.float32)]
    convert_element_type x4 -> x0, other arithmetic: 4.41 us -> none  [halving_scatter(): send.astype(jnp.bfloat16)]
    add x1, other arithmetic: 5.96 us -> 1.56 us  [per_device(): convolved + tap * padded[2 - time_lag:2 - time_lag + frames_here, row_shi...]
    select_n x16 -> x9, other arithmetic: 1.37 us -> 4.42 us  [per_device(): jnp.concatenate([jnp.concatenate([source * tok_rows + token_ids, (ring +...]
  transfers between devices with their start and end apart: 37 -> 41, of which waited for: 19 -> 21; matrix products, arithmetic and copies ran while one was open for 10% -> 8% of each run, Pallas kernels for 0% -> 0%
where the time goes in v3:
time: 256 us; the launch traced here: 252 us
  starting transfers between devices  152 us (59%)
  waiting for transfers between devices  55.6 us (22%)
  other arithmetic  17.8 us (7%)
  matrix products  13.1 us (5%)
  local copies, waits for them, and re-layouts  10.4 us (4%)
    ppermute x14, starting transfers between devices, ring_pieces(): behind = lax.ppermute(behind, axis, backward)  67.5 us
    ppermute x16, waiting for transfers between devices, ring_pieces(): ahead = lax.ppermute(ahead, axis, forward)  43.2 us
    ppermute x8, starting transfers between devices, halving_scatter(): lax.ppermute(send.astype(jnp.bfloat16), axis, [(i, i ^ 1 << bit) for i in...  41.5 us
    ppermute x16, starting transfers between devices, ring_pieces(): ahead = lax.ppermute(ahead, axis, forward)  32.2 us
    ppermute x2, starting transfers between devices, ring_pieces(): lax.ppermute(block, axis, [(i, (i + ring) % size) for i in range(size)])  7.57 us
    ppermute x8, waiting for transfers between devices, halving_scatter(): lax.ppermute(send.astype(jnp.bfloat16), axis, [(i, i ^ 1 << bit) for i in...  6.74 us
    ppermute x2, waiting for transfers between devices, ring_pieces(): lax.ppermute(block, axis, [(i, (i + ring) % size) for i in range(size)])  5.59 us
    dot_general x9, matrix products, attend_piece(): jnp.einsum('nhe,mhe->nhm', queries, key_part, preferred_element_type=jnp....  5.25 us
  transfers between devices with their start and end apart: 41, of which 21 were waited for; matrix products, arithmetic and copies ran while one was open for 8% of the time, Pallas kernels for 0%

profile of v3, /device:TPU:1, one launch (start us, length us, event | category | flops | bytes accessed | tf_op | source)
XLA Modules:
  0.0 251.7 jit_solution(16263226459408781249)
XLA Ops:
  2.5 5.7 %collective-permute-start = (bf16[112,512]{1,0:T(8,128)(2,1)S(1)}, bf16[112,512]{1,0:T(8,128)(2,1)S(1)}, u32[]{:S(2)}, u32[]{:S(2)}) collective-permute-start(bf16[112,512]{1,0:T(8,128)(2,1)S(1)} %get-tuple-element.70), channel_id=1, source_target_pairs={{0,256},{16,272},{32,288},{48,304},{64,320},{80,336},{96,352},{112... | collective-permute-start | bytes 344072 | tf_op jit(solution)/shard_map/ppermute | solution.py:34
  9.2 3.6 %collective-permute-start.40 = (bf16[320,192]{1,0:T(8,128)(2,1)S(1)}, bf16[320,192]{1,0:T(8,128)(2,1)S(1)}, u32[]{:S(2)}, u32[]{:S(2)}) collective-permute-start(bf16[320,192]{1,0:T(8,128)(2,1)S(1)} %constant_dynamic-slice_fusion), channel_id=1, source_target_pairs={{0,16},{16,32},{32,48},{48,64},{64,80},{80,96},{96,112},{112,128},... | collective-permute-start | bytes 368648 | tf_op jit(solution)/shard_map/ppermute | solution.py:19
  23.7 3.5 %collective-permute-start.1 = (bf16[2,112,512]{2,1,0:T(8,128)(2,1)S(1)}, bf16[2,112,512]{2,1,0:T(8,128)(2,1)S(1)}, u32[]{:S(2)}, u32[]{:S(2)}) collective-permute-start(bf16[2,112,512]{2,1,0:T(8,128)(2,1)S(1)} %maximum_select_fusion.2), channel_id=1, source_target_pairs={{0,16},{16,32},{32,48},{48,64},{64,80},{80,96},{96,112},{112,128},... | collective-permute-start | bytes 688136 | tf_op jit(solution)/shard_map/ppermute | solution.py:45
  27.2 7.9 %collective-permute-start.2 = (bf16[2,112,512]{2,1,0:T(8,128)(2,1)S(1)}, bf16[2,112,512]{2,1,0:T(8,128)(2,1)S(1)}, u32[]{:S(2)}, u32[]{:S(2)}) collective-permute-start(bf16[2,112,512]{2,1,0:T(8,128)(2,1)S(1)} %maximum_select_fusion.2), channel_id=1, source_target_pairs={{0,240},{16,0},{32,16},{48,32},{64,48},{80,64},{96,80},{112,96},{1... | collective-permute-start | bytes 688136 | tf_op jit(solution)/shard_map/ppermute | solution.py:48
  40.1 4.6 %collective-permute-start.4 = (bf16[2,112,512]{2,1,0:T(8,128)(2,1)S(1)}, bf16[2,112,512]{2,1,0:T(8,128)(2,1)S(1)}, u32[]{:S(2)}, u32[]{:S(2)}) collective-permute-start(bf16[2,112,512]{2,1,0:T(8,128)(2,1)S(1)} %collective-permute-done.2), channel_id=1, source_target_pairs={{0,240},{16,0},{32,16},{48,32},{64,48},{80,64},{96,80},{112,96},{1... | collective-permute-start | bytes 688136 | tf_op jit(solution)/shard_map/ppermute | solution.py:48
  48.7 4.6 %collective-permute-start.6 = (bf16[2,112,512]{2,1,0:T(8,128)(2,1)S(1)}, bf16[2,112,512]{2,1,0:T(8,128)(2,1)S(1)}, u32[]{:S(2)}, u32[]{:S(2)}) collective-permute-start(bf16[2,112,512]{2,1,0:T(8,128)(2,1)S(1)} %collective-permute-done.4), channel_id=1, source_target_pairs={{0,240},{16,0},{32,16},{48,32},{64,48},{80,64},{96,80},{112,96},{1... | collective-permute-start | bytes 688136 | tf_op jit(solution)/shard_map/ppermute | solution.py:48
  56.7 4.6 %collective-permute-start.8 = (bf16[2,112,512]{2,1,0:T(8,128)(2,1)S(1)}, bf16[2,112,512]{2,1,0:T(8,128)(2,1)S(1)}, u32[]{:S(2)}, u32[]{:S(2)}) collective-permute-start(bf16[2,112,512]{2,1,0:T(8,128)(2,1)S(1)} %collective-permute-done.6), channel_id=1, source_target_pairs={{0,240},{16,0},{32,16},{48,32},{64,48},{80,64},{96,80},{112,96},{1... | collective-permute-start | bytes 688136 | tf_op jit(solution)/shard_map/ppermute | solution.py:48
  64.7 4.6 %collective-permute-start.10 = (bf16[2,112,512]{2,1,0:T(8,128)(2,1)S(1)}, bf16[2,112,512]{2,1,0:T(8,128)(2,1)S(1)}, u32[]{:S(2)}, u32[]{:S(2)}) collective-permute-start(bf16[2,112,512]{2,1,0:T(8,128)(2,1)S(1)} %collective-permute-done.8), channel_id=1, source_target_pairs={{0,240},{16,0},{32,16},{48,32},{64,48},{80,64},{96,80},{112,96},{1... | collective-permute-start | bytes 688136 | tf_op jit(solution)/shard_map/ppermute | solution.py:48
  72.6 4.6 %collective-permute-start.12 = (bf16[2,112,512]{2,1,0:T(8,128)(2,1)S(1)}, bf16[2,112,512]{2,1,0:T(8,128)(2,1)S(1)}, u32[]{:S(2)}, u32[]{:S(2)}) collective-permute-start(bf16[2,112,512]{2,1,0:T(8,128)(2,1)S(1)} %collective-permute-done.10), channel_id=1, source_target_pairs={{0,240},{16,0},{32,16},{48,32},{64,48},{80,64},{96,80},{112,96},{1... | collective-permute-start | bytes 688136 | tf_op jit(solution)/shard_map/ppermute | solution.py:48
  80.6 4.6 %collective-permute-start.14 = (bf16[2,112,512]{2,1,0:T(8,128)(2,1)S(1)}, bf16[2,112,512]{2,1,0:T(8,128)(2,1)S(1)}, u32[]{:S(2)}, u32[]{:S(2)}) collective-permute-start(bf16[2,112,512]{2,1,0:T(8,128)(2,1)S(1)} %collective-permute-done.12), channel_id=1, source_target_pairs={{0,240},{16,0},{32,16},{48,32},{64,48},{80,64},{96,80},{112,96},{1... | collective-permute-start | bytes 688136 | tf_op jit(solution)/shard_map/ppermute | solution.py:48
  89.5 7.9 %collective-permute-done.15 = bf16[2,112,512]{2,1,0:T(8,128)(2,1)S(1)} collective-permute-done((bf16[2,112,512]{2,1,0:T(8,128)(2,1)S(1)}, bf16[2,112,512]{2,1,0:T(8,128)(2,1)S(1)}, u32[]{:S(2)}, u32[]{:S(2)}) %collective-permute-start.15) | collective-permute-done | bytes 229408 | tf_op jit(solution)/shard_map/ppermute | solution.py:45
  107.9 5.6 %collective-permute-done.16 = bf16[320,1,256]{2,0,1:T(8,128)(2,1)S(1)} collective-permute-done((bf16[320,1,256]{2,0,1:T(8,128)(2,1)S(1)}, bf16[320,1,256]{2,0,1:T(8,128)(2,1)S(1)}, u32[]{:S(2)}, u32[]{:S(2)}) %collective-permute-start.16) | collective-permute-done | bytes 163872 | tf_op jit(solution)/shard_map/ppermute | solution.py:34
  115.5 4.6 %collective-permute-start.18 = (bf16[2,320,1,256]{3,1,2,0:T(8,128)(2,1)S(1)}, bf16[2,320,1,256]{3,1,2,0:T(8,128)(2,1)S(1)}, u32[]{:S(2)}, u32[]{:S(2)}) collective-permute-start(bf16[2,320,1,256]{3,1,2,0:T(8,128)(2,1)S(1)} %maximum_select_fusion), channel_id=1, source_target_pairs={{0,240},{16,0},{32,16},{48,32},{64,48},{80,64},{96,80},{112,96},{1... | collective-permute-start | bytes 983048 | tf_op jit(solution)/shard_map/ppermute | solution.py:48
  120.1 2.7 %collective-permute-done.17 = bf16[2,320,1,256]{3,1,2,0:T(8,128)(2,1)S(1)} collective-permute-done((bf16[2,320,1,256]{3,1,2,0:T(8,128)(2,1)S(1)}, bf16[2,320,1,256]{3,1,2,0:T(8,128)(2,1)S(1)}, u32[]{:S(2)}, u32[]{:S(2)}) %collective-permute-start.17) | collective-permute-done | bytes 327712 | tf_op jit(solution)/shard_map/ppermute | solution.py:45
  124.8 4.6 %collective-permute-start.20 = (bf16[2,320,1,256]{3,1,2,0:T(8,128)(2,1)S(1)}, bf16[2,320,1,256]{3,1,2,0:T(8,128)(2,1)S(1)}, u32[]{:S(2)}, u32[]{:S(2)}) collective-permute-start(bf16[2,320,1,256]{3,1,2,0:T(8,128)(2,1)S(1)} %collective-permute-done.18), channel_id=1, source_target_pairs={{0,240},{16,0},{32,16},{48,32},{64,48},{80,64},{96,80},{112,96},{1... | collective-permute-start | bytes 983048 | tf_op jit(solution)/shard_map/ppermute | solution.py:48
  129.4 4.5 %collective-permute-done.19 = bf16[2,320,1,256]{3,1,2,0:T(8,128)(2,1)S(1)} collective-permute-done((bf16[2,320,1,256]{3,1,2,0:T(8,128)(2,1)S(1)}, bf16[2,320,1,256]{3,1,2,0:T(8,128)(2,1)S(1)}, u32[]{:S(2)}, u32[]{:S(2)}) %collective-permute-start.19) | collective-permute-done | bytes 327712 | tf_op jit(solution)/shard_map/ppermute | solution.py:45
  135.9 4.6 %collective-permute-start.22 = (bf16[2,320,1,256]{3,1,2,0:T(8,128)(2,1)S(1)}, bf16[2,320,1,256]{3,1,2,0:T(8,128)(2,1)S(1)}, u32[]{:S(2)}, u32[]{:S(2)}) collective-permute-start(bf16[2,320,1,256]{3,1,2,0:T(8,128)(2,1)S(1)} %collective-permute-done.20), channel_id=1, source_target_pairs={{0,240},{16,0},{32,16},{48,32},{64,48},{80,64},{96,80},{112,96},{1... | collective-permute-start | bytes 983048 | tf_op jit(solution)/shard_map/ppermute | solution.py:48
  140.5 3.6 %collective-permute-done.21 = bf16[2,320,1,256]{3,1,2,0:T(8,128)(2,1)S(1)} collective-permute-done((bf16[2,320,1,256]{3,1,2,0:T(8,128)(2,1)S(1)}, bf16[2,320,1,256]{3,1,2,0:T(8,128)(2,1)S(1)}, u32[]{:S(2)}, u32[]{:S(2)}) %collective-permute-start.21) | collective-permute-done | bytes 327712 | tf_op jit(solution)/shard_map/ppermute | solution.py:45
  146.1 4.6 %collective-permute-start.24 = (bf16[2,320,1,256]{3,1,2,0:T(8,128)(2,1)S(1)}, bf16[2,320,1,256]{3,1,2,0:T(8,128)(2,1)S(1)}, u32[]{:S(2)}, u32[]{:S(2)}) collective-permute-start(bf16[2,320,1,256]{3,1,2,0:T(8,128)(2,1)S(1)} %collective-permute-done.22), channel_id=1, source_target_pairs={{0,240},{16,0},{32,16},{48,32},{64,48},{80,64},{96,80},{112,96},{1... | collective-permute-start | bytes 983048 | tf_op jit(solution)/shard_map/ppermute | solution.py:48
  150.7 2.4 collective-permute-done.23
  155.5 4.7 %collective-permute-start.26 = (bf16[2,320,1,256]{3,1,2,0:T(8,128)(2,1)S(1)}, bf16[2,320,1,256]{3,1,2,0:T(8,128)(2,1)S(1)}, u32[]{:S(2)}, u32[]{:S(2)}) collective-permute-start(bf16[2,320,1,256]{3,1,2,0:T(8,128)(2,1)S(1)} %collective-permute-done.24), channel_id=1, source_target_pairs={{0,240},{16,0},{32,16},{48,32},{64,48},{80,64},{96,80},{112,96},{1... | collective-permute-start | bytes 983048 | tf_op jit(solution)/shard_map/ppermute | solution.py:48
  164.7 4.6 %collective-permute-start.28 = (bf16[2,320,1,256]{3,1,2,0:T(8,128)(2,1)S(1)}, bf16[2,320,1,256]{3,1,2,0:T(8,128)(2,1)S(1)}, u32[]{:S(2)}, u32[]{:S(2)}) collective-permute-start(bf16[2,320,1,256]{3,1,2,0:T(8,128)(2,1)S(1)} %collective-permute-done.26), channel_id=1, source_target_pairs={{0,240},{16,0},{32,16},{48,32},{64,48},{80,64},{96,80},{112,96},{1... | collective-permute-start | bytes 983048 | tf_op jit(solution)/shard_map/ppermute | solution.py:48
  173.7 4.6 %collective-permute-start.30 = (bf16[2,320,1,256]{3,1,2,0:T(8,128)(2,1)S(1)}, bf16[2,320,1,256]{3,1,2,0:T(8,128)(2,1)S(1)}, u32[]{:S(2)}, u32[]{:S(2)}) collective-permute-start(bf16[2,320,1,256]{3,1,2,0:T(8,128)(2,1)S(1)} %collective-permute-done.28), channel_id=1, source_target_pairs={{0,240},{16,0},{32,16},{48,32},{64,48},{80,64},{96,80},{112,96},{1... | collective-permute-start | bytes 983048 | tf_op jit(solution)/shard_map/ppermute | solution.py:48
  183.7 7.2 %collective-permute-done.31 = bf16[2,320,1,256]{3,1,2,0:T(8,128)(2,1)S(1)} collective-permute-done((bf16[2,320,1,256]{3,1,2,0:T(8,128)(2,1)S(1)}, bf16[2,320,1,256]{3,1,2,0:T(8,128)(2,1)S(1)}, u32[]{:S(2)}, u32[]{:S(2)}) %collective-permute-start.31) | collective-permute-done | bytes 327712 | tf_op jit(solution)/shard_map/ppermute | solution.py:45
  193.0 2.4 fusion.57
  201.0 20.7 %collective-permute-start.36 = (bf16[160,1536]{1,0:T(8,128)(2,1)S(1)}, bf16[160,1536]{1,0:T(8,128)(2,1)S(1)}, u32[]{:S(2)}, u32[]{:S(2)}) collective-permute-start(bf16[160,1536]{1,0:T(8,128)(2,1)S(1)} %dynamic-slice_convert_fusion), channel_id=1, source_target_pairs={{0,1},{1,0},{2,3},{3,2},{4,5},{5,4},{6,7},{7,6},{8,9},{9,8},{10,11... | collective-permute-start | bytes 1474568 | tf_op jit(solution)/shard_map/ppermute | solution.py:78
  224.3 3.1 %collective-permute-start.37 = (bf16[160,768]{1,0:T(8,128)(2,1)S(1)}, bf16[160,768]{1,0:T(8,128)(2,1)S(1)}, u32[]{:S(2)}, u32[]{:S(2)}) collective-permute-start(bf16[160,768]{1,0:T(8,128)(2,1)S(1)} %dynamic-slice_convert_fusion.2), channel_id=1, source_target_pairs={{0,2},{1,3},{2,0},{3,1},{4,6},{5,7},{6,4},{7,5},{8,10},{9,11},{10,... | collective-permute-start | bytes 737288 | tf_op jit(solution)/shard_map/ppermute | solution.py:78
  227.6 2.3 collective-permute-start.33
  229.9 3.3 %collective-permute-done.37 = bf16[160,768]{1,0:T(8,128)(2,1)S(1)} collective-permute-done((bf16[160,768]{1,0:T(8,128)(2,1)S(1)}, bf16[160,768]{1,0:T(8,128)(2,1)S(1)}, u32[]{:S(2)}, u32[]{:S(2)}) %collective-permute-start.37) | collective-permute-done | bytes 245792 | tf_op jit(solution)/shard_map/ppermute | solution.py:78
  233.3 4.8 %collective-permute-start.38 = (bf16[160,384]{1,0:T(8,128)(2,1)S(1)}, bf16[160,384]{1,0:T(8,128)(2,1)S(1)}, u32[]{:S(2)}, u32[]{:S(2)}) collective-permute-start(bf16[160,384]{1,0:T(8,128)(2,1)S(1)} %dynamic-slice_convert_fusion.4), channel_id=1, source_target_pairs={{0,4},{1,5},{2,6},{3,7},{4,0},{5,1},{6,2},{7,3},{8,12},{9,13},{10,... | collective-permute-start | bytes 368648 | tf_op jit(solution)/shard_map/ppermute | solution.py:78
  244.0 4.1 %collective-permute-start.35 = (bf16[160,192]{1,0:T(8,128)(2,1)S(1)}, bf16[160,192]{1,0:T(8,128)(2,1)S(1)}, u32[]{:S(2)}, u32[]{:S(2)}) collective-permute-start(bf16[160,192]{1,0:T(8,128)(2,1)S(1)} %dynamic-slice_convert_fusion.7), channel_id=1, source_target_pairs={{0,4},{1,5},{2,6},{3,7},{4,0},{5,1},{6,2},{7,3},{8,12},{9,13},{10,... | collective-permute-start | bytes 184328 | tf_op jit(solution)/shard_map/ppermute | solution.py:78
  248.2 2.4 collective-permute-done.35
  (258 shorter events, 91.7 us)
Async XLA Ops:
  2.5 21.1 %collective-permute-start = (bf16[112,512]{1,0:T(8,128)(2,1)S(1)}, bf16[112,512]{1,0:T(8,128)(2,1)S(1)}, u32[]{:S(2)}, u32[]{:S(2)}) collective-permute-start(bf16[112,512]{1,0:T(8,128)(2,1)S(1)} %get-tuple-element.70), channel_id=1, source_target_pairs={{0,256},{16,272},{32,288},{48,304},{64,320},{80,336},{96,352},{112... | collective-permute-start | bytes 344072 | tf_op jit(solution)/shard_map/ppermute | solution.py:34
  9.2 26.3 %collective-permute-start.40 = (bf16[320,192]{1,0:T(8,128)(2,1)S(1)}, bf16[320,192]{1,0:T(8,128)(2,1)S(1)}, u32[]{:S(2)}, u32[]{:S(2)}) collective-permute-start(bf16[320,192]{1,0:T(8,128)(2,1)S(1)} %constant_dynamic-slice_fusion), channel_id=1, source_target_pairs={{0,16},{16,32},{32,48},{48,64},{64,80},{80,96},{96,112},{112,128},... | collective-permute-start | bytes 368648 | tf_op jit(solution)/shard_map/ppermute | solution.py:19
  23.7 14.5 %collective-permute-start.1 = (bf16[2,112,512]{2,1,0:T(8,128)(2,1)S(1)}, bf16[2,112,512]{2,1,0:T(8,128)(2,1)S(1)}, u32[]{:S(2)}, u32[]{:S(2)}) collective-permute-start(bf16[2,112,512]{2,1,0:T(8,128)(2,1)S(1)} %maximum_select_fusion.2), channel_id=1, source_target_pairs={{0,16},{16,32},{32,48},{48,64},{64,80},{80,96},{96,112},{112,128},... | collective-permute-start | bytes 688136 | tf_op jit(solution)/shard_map/ppermute | solution.py:45
  27.2 12.9 %collective-permute-start.2 = (bf16[2,112,512]{2,1,0:T(8,128)(2,1)S(1)}, bf16[2,112,512]{2,1,0:T(8,128)(2,1)S(1)}, u32[]{:S(2)}, u32[]{:S(2)}) collective-permute-start(bf16[2,112,512]{2,1,0:T(8,128)(2,1)S(1)} %maximum_select_fusion.2), channel_id=1, source_target_pairs={{0,240},{16,0},{32,16},{48,32},{64,48},{80,64},{96,80},{112,96},{1... | collective-permute-start | bytes 688136 | tf_op jit(solution)/shard_map/ppermute | solution.py:48
  38.2 8.6 %collective-permute-start.3 = (bf16[2,112,512]{2,1,0:T(8,128)(2,1)S(1)}, bf16[2,112,512]{2,1,0:T(8,128)(2,1)S(1)}, u32[]{:S(2)}, u32[]{:S(2)}) collective-permute-start(bf16[2,112,512]{2,1,0:T(8,128)(2,1)S(1)} %collective-permute-done.1), channel_id=1, source_target_pairs={{0,16},{16,32},{32,48},{48,64},{64,80},{80,96},{96,112},{112,128},... | collective-permute-start | bytes 688136 | tf_op jit(solution)/shard_map/ppermute | solution.py:45
  40.1 8.6 %collective-permute-start.4 = (bf16[2,112,512]{2,1,0:T(8,128)(2,1)S(1)}, bf16[2,112,512]{2,1,0:T(8,128)(2,1)S(1)}, u32[]{:S(2)}, u32[]{:S(2)}) collective-permute-start(bf16[2,112,512]{2,1,0:T(8,128)(2,1)S(1)} %collective-permute-done.2), channel_id=1, source_target_pairs={{0,240},{16,0},{32,16},{48,32},{64,48},{80,64},{96,80},{112,96},{1... | collective-permute-start | bytes 688136 | tf_op jit(solution)/shard_map/ppermute | solution.py:48
  46.8 8.0 %collective-permute-start.5 = (bf16[2,112,512]{2,1,0:T(8,128)(2,1)S(1)}, bf16[2,112,512]{2,1,0:T(8,128)(2,1)S(1)}, u32[]{:S(2)}, u32[]{:S(2)}) collective-permute-start(bf16[2,112,512]{2,1,0:T(8,128)(2,1)S(1)} %collective-permute-done.3), channel_id=1, source_target_pairs={{0,16},{16,32},{32,48},{48,64},{64,80},{80,96},{96,112},{112,128},... | collective-permute-start | bytes 688136 | tf_op jit(solution)/shard_map/ppermute | solution.py:45
  48.7 8.0 %collective-permute-start.6 = (bf16[2,112,512]{2,1,0:T(8,128)(2,1)S(1)}, bf16[2,112,512]{2,1,0:T(8,128)(2,1)S(1)}, u32[]{:S(2)}, u32[]{:S(2)}) collective-permute-start(bf16[2,112,512]{2,1,0:T(8,128)(2,1)S(1)} %collective-permute-done.4), channel_id=1, source_target_pairs={{0,240},{16,0},{32,16},{48,32},{64,48},{80,64},{96,80},{112,96},{1... | collective-permute-start | bytes 688136 | tf_op jit(solution)/shard_map/ppermute | solution.py:48
  54.8 8.0 %collective-permute-start.7 = (bf16[2,112,512]{2,1,0:T(8,128)(2,1)S(1)}, bf16[2,112,512]{2,1,0:T(8,128)(2,1)S(1)}, u32[]{:S(2)}, u32[]{:S(2)}) collective-permute-start(bf16[2,112,512]{2,1,0:T(8,128)(2,1)S(1)} %collective-permute-done.5), channel_id=1, source_target_pairs={{0,16},{16,32},{32,48},{48,64},{64,80},{80,96},{96,112},{112,128},... | collective-permute-start | bytes 688136 | tf_op jit(solution)/shard_map/ppermute | solution.py:45
  62.7 8.0 %collective-permute-start.9 = (bf16[2,112,512]{2,1,0:T(8,128)(2,1)S(1)}, bf16[2,112,512]{2,1,0:T(8,128)(2,1)S(1)}, u32[]{:S(2)}, u32[]{:S(2)}) collective-permute-start(bf16[2,112,512]{2,1,0:T(8,128)(2,1)S(1)} %collective-permute-done.7), channel_id=1, source_target_pairs={{0,16},{16,32},{32,48},{48,64},{64,80},{80,96},{96,112},{112,128},... | collective-permute-start | bytes 688136 | tf_op jit(solution)/shard_map/ppermute | solution.py:45
  70.7 8.0 %collective-permute-start.11 = (bf16[2,112,512]{2,1,0:T(8,128)(2,1)S(1)}, bf16[2,112,512]{2,1,0:T(8,128)(2,1)S(1)}, u32[]{:S(2)}, u32[]{:S(2)}) collective-permute-start(bf16[2,112,512]{2,1,0:T(8,128)(2,1)S(1)} %collective-permute-done.9), channel_id=1, source_target_pairs={{0,16},{16,32},{32,48},{48,64},{64,80},{80,96},{96,112},{112,128},... | collective-permute-start | bytes 688136 | tf_op jit(solution)/shard_map/ppermute | solution.py:45
  78.7 8.8 %collective-permute-start.13 = (bf16[2,112,512]{2,1,0:T(8,128)(2,1)S(1)}, bf16[2,112,512]{2,1,0:T(8,128)(2,1)S(1)}, u32[]{:S(2)}, u32[]{:S(2)}) collective-permute-start(bf16[2,112,512]{2,1,0:T(8,128)(2,1)S(1)} %collective-permute-done.11), channel_id=1, source_target_pairs={{0,16},{16,32},{32,48},{48,64},{64,80},{80,96},{96,112},{112,128},... | collective-permute-start | bytes 688136 | tf_op jit(solution)/shard_map/ppermute | solution.py:45
  80.6 8.9 %collective-permute-start.14 = (bf16[2,112,512]{2,1,0:T(8,128)(2,1)S(1)}, bf16[2,112,512]{2,1,0:T(8,128)(2,1)S(1)}, u32[]{:S(2)}, u32[]{:S(2)}) collective-permute-start(bf16[2,112,512]{2,1,0:T(8,128)(2,1)S(1)} %collective-permute-done.12), channel_id=1, source_target_pairs={{0,240},{16,0},{32,16},{48,32},{64,48},{80,64},{96,80},{112,96},{1... | collective-permute-start | bytes 688136 | tf_op jit(solution)/shard_map/ppermute | solution.py:48
  87.5 9.9 %collective-permute-start.15 = (bf16[2,112,512]{2,1,0:T(8,128)(2,1)S(1)}, bf16[2,112,512]{2,1,0:T(8,128)(2,1)S(1)}, u32[]{:S(2)}, u32[]{:S(2)}) collective-permute-start(bf16[2,112,512]{2,1,0:T(8,128)(2,1)S(1)} %collective-permute-done.13), channel_id=1, source_target_pairs={{0,16},{16,32},{32,48},{48,64},{64,80},{80,96},{96,112},{112,128},... | collective-permute-start | bytes 688136 | tf_op jit(solution)/shard_map/ppermute | solution.py:45
  113.5 9.3 %collective-permute-start.17 = (bf16[2,320,1,256]{3,1,2,0:T(8,128)(2,1)S(1)}, bf16[2,320,1,256]{3,1,2,0:T(8,128)(2,1)S(1)}, u32[]{:S(2)}, u32[]{:S(2)}) collective-permute-start(bf16[2,320,1,256]{3,1,2,0:T(8,128)(2,1)S(1)} %maximum_select_fusion), channel_id=1, source_target_pairs={{0,16},{16,32},{32,48},{48,64},{64,80},{80,96},{96,112},{112,128},... | collective-permute-start | bytes 983048 | tf_op jit(solution)/shard_map/ppermute | solution.py:45
  115.5 9.3 %collective-permute-start.18 = (bf16[2,320,1,256]{3,1,2,0:T(8,128)(2,1)S(1)}, bf16[2,320,1,256]{3,1,2,0:T(8,128)(2,1)S(1)}, u32[]{:S(2)}, u32[]{:S(2)}) collective-permute-start(bf16[2,320,1,256]{3,1,2,0:T(8,128)(2,1)S(1)} %maximum_select_fusion), channel_id=1, source_target_pairs={{0,240},{16,0},{32,16},{48,32},{64,48},{80,64},{96,80},{112,96},{1... | collective-permute-start | bytes 983048 | tf_op jit(solution)/shard_map/ppermute | solution.py:48
  122.8 11.1 %collective-permute-start.19 = (bf16[2,320,1,256]{3,1,2,0:T(8,128)(2,1)S(1)}, bf16[2,320,1,256]{3,1,2,0:T(8,128)(2,1)S(1)}, u32[]{:S(2)}, u32[]{:S(2)}) collective-permute-start(bf16[2,320,1,256]{3,1,2,0:T(8,128)(2,1)S(1)} %collective-permute-done.17), channel_id=1, source_target_pairs={{0,16},{16,32},{32,48},{48,64},{64,80},{80,96},{96,112},{112,128},... | collective-permute-start | bytes 983048 | tf_op jit(solution)/shard_map/ppermute | solution.py:45
  124.8 11.1 %collective-permute-start.20 = (bf16[2,320,1,256]{3,1,2,0:T(8,128)(2,1)S(1)}, bf16[2,320,1,256]{3,1,2,0:T(8,128)(2,1)S(1)}, u32[]{:S(2)}, u32[]{:S(2)}) collective-permute-start(bf16[2,320,1,256]{3,1,2,0:T(8,128)(2,1)S(1)} %collective-permute-done.18), channel_id=1, source_target_pairs={{0,240},{16,0},{32,16},{48,32},{64,48},{80,64},{96,80},{112,96},{1... | collective-permute-start | bytes 983048 | tf_op jit(solution)/shard_map/ppermute | solution.py:48
  133.9 10.2 %collective-permute-start.21 = (bf16[2,320,1,256]{3,1,2,0:T(8,128)(2,1)S(1)}, bf16[2,320,1,256]{3,1,2,0:T(8,128)(2,1)S(1)}, u32[]{:S(2)}, u32[]{:S(2)}) collective-permute-start(bf16[2,320,1,256]{3,1,2,0:T(8,128)(2,1)S(1)} %collective-permute-done.19), channel_id=1, source_target_pairs={{0,16},{16,32},{32,48},{48,64},{64,80},{80,96},{96,112},{112,128},... | collective-permute-start | bytes 983048 | tf_op jit(solution)/shard_map/ppermute | solution.py:45
  135.9 10.2 %collective-permute-start.22 = (bf16[2,320,1,256]{3,1,2,0:T(8,128)(2,1)S(1)}, bf16[2,320,1,256]{3,1,2,0:T(8,128)(2,1)S(1)}, u32[]{:S(2)}, u32[]{:S(2)}) collective-permute-start(bf16[2,320,1,256]{3,1,2,0:T(8,128)(2,1)S(1)} %collective-permute-done.20), channel_id=1, source_target_pairs={{0,240},{16,0},{32,16},{48,32},{64,48},{80,64},{96,80},{112,96},{1... | collective-permute-start | bytes 983048 | tf_op jit(solution)/shard_map/ppermute | solution.py:48
  144.1 9.0 %collective-permute-start.23 = (bf16[2,320,1,256]{3,1,2,0:T(8,128)(2,1)S(1)}, bf16[2,320,1,256]{3,1,2,0:T(8,128)(2,1)S(1)}, u32[]{:S(2)}, u32[]{:S(2)}) collective-permute-start(bf16[2,320,1,256]{3,1,2,0:T(8,128)(2,1)S(1)} %collective-permute-done.21), channel_id=1, source_target_pairs={{0,16},{16,32},{32,48},{48,64},{64,80},{80,96},{96,112},{112,128},... | collective-permute-start | bytes 983048 | tf_op jit(solution)/shard_map/ppermute | solution.py:45
  146.1 9.4 %collective-permute-start.24 = (bf16[2,320,1,256]{3,1,2,0:T(8,128)(2,1)S(1)}, bf16[2,320,1,256]{3,1,2,0:T(8,128)(2,1)S(1)}, u32[]{:S(2)}, u32[]{:S(2)}) collective-permute-start(bf16[2,320,1,256]{3,1,2,0:T(8,128)(2,1)S(1)} %collective-permute-done.22), channel_id=1, source_target_pairs={{0,240},{16,0},{32,16},{48,32},{64,48},{80,64},{96,80},{112,96},{1... | collective-permute-start | bytes 983048 | tf_op jit(solution)/shard_map/ppermute | solution.py:48
  153.1 9.0 %collective-permute-start.25 = (bf16[2,320,1,256]{3,1,2,0:T(8,128)(2,1)S(1)}, bf16[2,320,1,256]{3,1,2,0:T(8,128)(2,1)S(1)}, u32[]{:S(2)}, u32[]{:S(2)}) collective-permute-start(bf16[2,320,1,256]{3,1,2,0:T(8,128)(2,1)S(1)} %collective-permute-done.23), channel_id=1, source_target_pairs={{0,16},{16,32},{32,48},{48,64},{64,80},{80,96},{96,112},{112,128},... | collective-permute-start | bytes 983048 | tf_op jit(solution)/shard_map/ppermute | solution.py:45
  155.5 9.2 %collective-permute-start.26 = (bf16[2,320,1,256]{3,1,2,0:T(8,128)(2,1)S(1)}, bf16[2,320,1,256]{3,1,2,0:T(8,128)(2,1)S(1)}, u32[]{:S(2)}, u32[]{:S(2)}) collective-permute-start(bf16[2,320,1,256]{3,1,2,0:T(8,128)(2,1)S(1)} %collective-permute-done.24), channel_id=1, source_target_pairs={{0,240},{16,0},{32,16},{48,32},{64,48},{80,64},{96,80},{112,96},{1... | collective-permute-start | bytes 983048 | tf_op jit(solution)/shard_map/ppermute | solution.py:48
  162.1 9.0 %collective-permute-start.27 = (bf16[2,320,1,256]{3,1,2,0:T(8,128)(2,1)S(1)}, bf16[2,320,1,256]{3,1,2,0:T(8,128)(2,1)S(1)}, u32[]{:S(2)}, u32[]{:S(2)}) collective-permute-start(bf16[2,320,1,256]{3,1,2,0:T(8,128)(2,1)S(1)} %collective-permute-done.25), channel_id=1, source_target_pairs={{0,16},{16,32},{32,48},{48,64},{64,80},{80,96},{96,112},{112,128},... | collective-permute-start | bytes 983048 | tf_op jit(solution)/shard_map/ppermute | solution.py:45
  164.7 9.0 %collective-permute-start.28 = (bf16[2,320,1,256]{3,1,2,0:T(8,128)(2,1)S(1)}, bf16[2,320,1,256]{3,1,2,0:T(8,128)(2,1)S(1)}, u32[]{:S(2)}, u32[]{:S(2)}) collective-permute-start(bf16[2,320,1,256]{3,1,2,0:T(8,128)(2,1)S(1)} %collective-permute-done.26), channel_id=1, source_target_pairs={{0,240},{16,0},{32,16},{48,32},{64,48},{80,64},{96,80},{112,96},{1... | collective-permute-start | bytes 983048 | tf_op jit(solution)/shard_map/ppermute | solution.py:48
  171.2 9.3 %collective-permute-start.29 = (bf16[2,320,1,256]{3,1,2,0:T(8,128)(2,1)S(1)}, bf16[2,320,1,256]{3,1,2,0:T(8,128)(2,1)S(1)}, u32[]{:S(2)}, u32[]{:S(2)}) collective-permute-start(bf16[2,320,1,256]{3,1,2,0:T(8,128)(2,1)S(1)} %collective-permute-done.27), channel_id=1, source_target_pairs={{0,16},{16,32},{32,48},{48,64},{64,80},{80,96},{96,112},{112,128},... | collective-permute-start | bytes 983048 | tf_op jit(solution)/shard_map/ppermute | solution.py:45
  173.7 9.3 %collective-permute-start.30 = (bf16[2,320,1,256]{3,1,2,0:T(8,128)(2,1)S(1)}, bf16[2,320,1,256]{3,1,2,0:T(8,128)(2,1)S(1)}, u32[]{:S(2)}, u32[]{:S(2)}) collective-permute-start(bf16[2,320,1,256]{3,1,2,0:T(8,128)(2,1)S(1)} %collective-permute-done.28), channel_id=1, source_target_pairs={{0,240},{16,0},{32,16},{48,32},{64,48},{80,64},{96,80},{112,96},{1... | collective-permute-start | bytes 983048 | tf_op jit(solution)/shard_map/ppermute | solution.py:48
  180.5 10.4 %collective-permute-start.31 = (bf16[2,320,1,256]{3,1,2,0:T(8,128)(2,1)S(1)}, bf16[2,320,1,256]{3,1,2,0:T(8,128)(2,1)S(1)}, u32[]{:S(2)}, u32[]{:S(2)}) collective-permute-start(bf16[2,320,1,256]{3,1,2,0:T(8,128)(2,1)S(1)} %collective-permute-done.29), channel_id=1, source_target_pairs={{0,16},{16,32},{32,48},{48,64},{64,80},{80,96},{96,112},{112,128},... | collective-permute-start | bytes 983048 | tf_op jit(solution)/shard_map/ppermute | solution.py:45
  201.0 23.2 %collective-permute-start.36 = (bf16[160,1536]{1,0:T(8,128)(2,1)S(1)}, bf16[160,1536]{1,0:T(8,128)(2,1)S(1)}, u32[]{:S(2)}, u32[]{:S(2)}) collective-permute-start(bf16[160,1536]{1,0:T(8,128)(2,1)S(1)} %dynamic-slice_convert_fusion), channel_id=1, source_target_pairs={{0,1},{1,0},{2,3},{3,2},{4,5},{5,4},{6,7},{7,6},{8,9},{9,8},{10,11... | collective-permute-start | bytes 1474568 | tf_op jit(solution)/shard_map/ppermute | solution.py:78
  224.3 8.9 %collective-permute-start.37 = (bf16[160,768]{1,0:T(8,128)(2,1)S(1)}, bf16[160,768]{1,0:T(8,128)(2,1)S(1)}, u32[]{:S(2)}, u32[]{:S(2)}) collective-permute-start(bf16[160,768]{1,0:T(8,128)(2,1)S(1)} %dynamic-slice_convert_fusion.2), channel_id=1, source_target_pairs={{0,2},{1,3},{2,0},{3,1},{4,6},{5,7},{6,4},{7,5},{8,10},{9,11},{10,... | collective-permute-start | bytes 737288 | tf_op jit(solution)/shard_map/ppermute | solution.py:78
  227.6 10.5 %collective-permute-start.33 = (bf16[160,768]{1,0:T(8,128)(2,1)S(1)}, bf16[160,768]{1,0:T(8,128)(2,1)S(1)}, u32[]{:S(2)}, u32[]{:S(2)}) collective-permute-start(bf16[160,768]{1,0:T(8,128)(2,1)S(1)} %dynamic-slice_convert_fusion.3), channel_id=1, source_target_pairs={{0,8},{1,9},{2,10},{3,11},{4,12},{5,13},{6,14},{7,15},{8,0},{9,1},... | collective-permute-start | bytes 737288 | tf_op jit(solution)/shard_map/ppermute | solution.py:78
  (36 other events, 489.7 us)

commit v4 on v3

--- a/solution.py
+++ b/solution.py
@@ -57,13 +57,6 @@
         gathered = lax.dynamic_update_index_in_dim(gathered, piece, source, 0)
     gathered = jnp.swapaxes(gathered, 0, 1)
     return gathered.reshape((2 * ring * block.shape[0],) + block.shape[1:])
-
-
-def block_order(size, order):
-    bits = len(order)
-    return [
-        sum(((j >> order[s]) & 1) << (bits - 1 - s) for s in range(bits)) for j in range(size)
-    ]
 
 
 def halving_scatter(partial, axis, order):
@@ -135,7 +128,7 @@
     shares_hi = local_shares.astype(jnp.bfloat16)
     shares_lo = (local_shares - shares_hi.astype(jnp.float32)).astype(jnp.bfloat16)
     share_count = 4 * rows_here
-    extra_rows = 16 * ((share_count + 16 * width - 1) // (16 * width))
+    extra_rows = 8 * ((share_count + 8 * width - 1) // (8 * width))
     share_block = jnp.zeros((extra_rows * width,), jnp.bfloat16)
     share_block = share_block.at[:share_count].set(
         jnp.concatenate([shares_hi, shares_lo], axis=1).reshape(share_count)
@@ -251,7 +244,7 @@
     shares_hi = local_shares.astype(jnp.bfloat16)
     shares_lo = (local_shares - shares_hi.astype(jnp.float32)).astype(jnp.bfloat16)
     share_count = 4 * rows_here
-    extra_rows = 16 * ((share_count + 16 * width - 1) // (16 * width))
+    extra_rows = 8 * ((share_count + 8 * width - 1) // (8 * width))
     share_block = jnp.zeros((extra_rows * width,), jnp.bfloat16)
     share_block = share_block.at[:share_count].set(
         jnp.concatenate([shares_hi, shares_lo], axis=1).reshape(share_count)
@@ -329,9 +322,11 @@
     orders = [[0, bits - 1] + middle, [0] + middle + [bits - 1]]
     head_parts = []
     for part, order in enumerate(orders):
-        positions = block_order(size, order)
-        by_block = o_piece.reshape((size, full_rows // size) + o_piece.shape[1:])
-        permuted = jnp.stack([by_block[positions.index(q)] for q in range(size)])
+        by_bit = o_piece.reshape((2,) * bits + (full_rows // size,) + o_piece.shape[1:])
+        permuted = jnp.transpose(
+            by_bit,
+            [bits - 1 - bit for bit in order] + list(range(bits, by_bit.ndim)),
+        )
         partial_out = jnp.einsum(
             "nhe,rhe->nr",
             attended[part * half_rows : (part + 1) * half_rows],

time: 256 us -> 249 us (0.973)
  other arithmetic: 17.8 us -> 11.8 us
  matrix products: 13.1 us -> 18.2 us
  waiting for transfers between devices: 55.6 us -> 51.5 us
    ppermute x16, waiting for transfers between devices: 43.2 us -> 38.6 us  [ring_pieces(): ahead = lax.ppermute(ahead, axis, forward)]
    select_n x9, other arithmetic: 4.42 us -> 0.27 us  [per_device(): jnp.concatenate([jnp.concatenate([source * tok_rows + token_ids, (ring +...]
    dot_general x9, matrix products: 5.25 us -> 8.1 us  [attend_piece(): jnp.einsum('nhe,mhe->nhm', queries, key_part, preferred_element_type=jnp....]
    dot_general x9, matrix products: 4.93 us -> 7.72 us  [attend_piece(): jnp.einsum('nhm,mhe->nhe', exponent.astype(jnp.bfloat16), value_part, pre...]
  transfers between devices with their start and end apart: 41 -> 41, of which waited for: 21 -> 20; matrix products, arithmetic and copies ran while one was open for 8% -> 10% of each run, Pallas kernels for 0% -> 0%
where the time goes in v4:
time: 249 us; the launch traced here: 245 us
  starting transfers between devices  151 us (61%)
  waiting for transfers between devices  51.5 us (21%)
  matrix products  18.2 us (7%)
  other arithmetic  11.8 us (5%)
  local copies, waits for them, and re-layouts  10.3 us (4%)
    ppermute x14, starting transfers between devices, ring_pieces(): behind = lax.ppermute(behind, axis, backward)  67.8 us
    ppermute x8, starting transfers between devices, halving_scatter(): lax.ppermute(send.astype(jnp.bfloat16), axis, [(i, i ^ 1 << bit) for i in...  39.6 us
    ppermute x16, waiting for transfers between devices, ring_pieces(): ahead = lax.ppermute(ahead, axis, forward)  38.6 us
    ppermute x16, starting transfers between devices, ring_pieces(): ahead = lax.ppermute(ahead, axis, forward)  32.4 us
    dot_general x9, matrix products, attend_piece(): jnp.einsum('nhe,mhe->nhm', queries, key_part, preferred_element_type=jnp....  8.1 us
    dot_general x9, matrix products, attend_piece(): jnp.einsum('nhm,mhe->nhe', exponent.astype(jnp.bfloat16), value_part, pre...  7.72 us
    ppermute x2, starting transfers between devices, ring_pieces(): lax.ppermute(block, axis, [(i, (i + ring) % size) for i in range(size)])  7.57 us
    ppermute x8, waiting for transfers between devices, halving_scatter(): lax.ppermute(send.astype(jnp.bfloat16), axis, [(i, i ^ 1 << bit) for i in...  7.39 us
  transfers between devices with their start and end apart: 41, of which 20 were waited for; matrix products, arithmetic and copies ran while one was open for 10% of the time, Pallas kernels for 0%

profile of v4, /device:TPU:1, one launch (start us, length us, event | category | flops | bytes accessed | tf_op | source)
XLA Modules:
  0.0 245.0 jit_solution(15281979723698282611)
XLA Ops:
  2.4 5.7 %collective-permute-start = (bf16[104,512]{1,0:T(8,128)(2,1)S(1)}, bf16[104,512]{1,0:T(8,128)(2,1)S(1)}, u32[]{:S(2)}, u32[]{:S(2)}) collective-permute-start(bf16[104,512]{1,0:T(8,128)(2,1)S(1)} %get-tuple-element.54), channel_id=1, source_target_pairs={{0,256},{16,272},{32,288},{48,304},{64,320},{80,336},{96,352},{112... | collective-permute-start | bytes 319496 | tf_op jit(solution)/shard_map/ppermute | solution.py:34
  9.2 3.6 %collective-permute-start.40 = (bf16[320,192]{1,0:T(8,128)(2,1)S(1)}, bf16[320,192]{1,0:T(8,128)(2,1)S(1)}, u32[]{:S(2)}, u32[]{:S(2)}) collective-permute-start(bf16[320,192]{1,0:T(8,128)(2,1)S(1)} %constant_dynamic-slice_fusion), channel_id=1, source_target_pairs={{0,16},{16,32},{32,48},{48,64},{64,80},{80,96},{96,112},{112,128},... | collective-permute-start | bytes 368648 | tf_op jit(solution)/shard_map/ppermute | solution.py:19
  16.8 3.5 %collective-permute-start.1 = (bf16[2,104,512]{2,1,0:T(8,128)(2,1)S(1)}, bf16[2,104,512]{2,1,0:T(8,128)(2,1)S(1)}, u32[]{:S(2)}, u32[]{:S(2)}) collective-permute-start(bf16[2,104,512]{2,1,0:T(8,128)(2,1)S(1)} %maximum_select_fusion.2), channel_id=1, source_target_pairs={{0,16},{16,32},{32,48},{48,64},{64,80},{80,96},{96,112},{112,128},... | collective-permute-start | bytes 638984 | tf_op jit(solution)/shard_map/ppermute | solution.py:45
  20.3 7.9 %collective-permute-start.2 = (bf16[2,104,512]{2,1,0:T(8,128)(2,1)S(1)}, bf16[2,104,512]{2,1,0:T(8,128)(2,1)S(1)}, u32[]{:S(2)}, u32[]{:S(2)}) collective-permute-start(bf16[2,104,512]{2,1,0:T(8,128)(2,1)S(1)} %maximum_select_fusion.2), channel_id=1, source_target_pairs={{0,240},{16,0},{32,16},{48,32},{64,48},{80,64},{96,80},{112,96},{1... | collective-permute-start | bytes 638984 | tf_op jit(solution)/shard_map/ppermute | solution.py:48
  28.5 2.4 collective-permute-done.1
  32.9 4.6 %collective-permute-start.4 = (bf16[2,104,512]{2,1,0:T(8,128)(2,1)S(1)}, bf16[2,104,512]{2,1,0:T(8,128)(2,1)S(1)}, u32[]{:S(2)}, u32[]{:S(2)}) collective-permute-start(bf16[2,104,512]{2,1,0:T(8,128)(2,1)S(1)} %collective-permute-done.2), channel_id=1, source_target_pairs={{0,240},{16,0},{32,16},{48,32},{64,48},{80,64},{96,80},{112,96},{1... | collective-permute-start | bytes 638984 | tf_op jit(solution)/shard_map/ppermute | solution.py:48
  41.2 4.6 %collective-permute-start.6 = (bf16[2,104,512]{2,1,0:T(8,128)(2,1)S(1)}, bf16[2,104,512]{2,1,0:T(8,128)(2,1)S(1)}, u32[]{:S(2)}, u32[]{:S(2)}) collective-permute-start(bf16[2,104,512]{2,1,0:T(8,128)(2,1)S(1)} %collective-permute-done.4), channel_id=1, source_target_pairs={{0,240},{16,0},{32,16},{48,32},{64,48},{80,64},{96,80},{112,96},{1... | collective-permute-start | bytes 638984 | tf_op jit(solution)/shard_map/ppermute | solution.py:48
  48.9 4.6 %collective-permute-start.8 = (bf16[2,104,512]{2,1,0:T(8,128)(2,1)S(1)}, bf16[2,104,512]{2,1,0:T(8,128)(2,1)S(1)}, u32[]{:S(2)}, u32[]{:S(2)}) collective-permute-start(bf16[2,104,512]{2,1,0:T(8,128)(2,1)S(1)} %collective-permute-done.6), channel_id=1, source_target_pairs={{0,240},{16,0},{32,16},{48,32},{64,48},{80,64},{96,80},{112,96},{1... | collective-permute-start | bytes 638984 | tf_op jit(solution)/shard_map/ppermute | solution.py:48
  56.7 4.6 %collective-permute-start.10 = (bf16[2,104,512]{2,1,0:T(8,128)(2,1)S(1)}, bf16[2,104,512]{2,1,0:T(8,128)(2,1)S(1)}, u32[]{:S(2)}, u32[]{:S(2)}) collective-permute-start(bf16[2,104,512]{2,1,0:T(8,128)(2,1)S(1)} %collective-permute-done.8), channel_id=1, source_target_pairs={{0,240},{16,0},{32,16},{48,32},{64,48},{80,64},{96,80},{112,96},{1... | collective-permute-start | bytes 638984 | tf_op jit(solution)/shard_map/ppermute | solution.py:48
  64.5 4.6 %collective-permute-start.12 = (bf16[2,104,512]{2,1,0:T(8,128)(2,1)S(1)}, bf16[2,104,512]{2,1,0:T(8,128)(2,1)S(1)}, u32[]{:S(2)}, u32[]{:S(2)}) collective-permute-start(bf16[2,104,512]{2,1,0:T(8,128)(2,1)S(1)} %collective-permute-done.10), channel_id=1, source_target_pairs={{0,240},{16,0},{32,16},{48,32},{64,48},{80,64},{96,80},{112,96},{1... | collective-permute-start | bytes 638984 | tf_op jit(solution)/shard_map/ppermute | solution.py:48
  72.3 4.6 %collective-permute-start.14 = (bf16[2,104,512]{2,1,0:T(8,128)(2,1)S(1)}, bf16[2,104,512]{2,1,0:T(8,128)(2,1)S(1)}, u32[]{:S(2)}, u32[]{:S(2)}) collective-permute-start(bf16[2,104,512]{2,1,0:T(8,128)(2,1)S(1)} %collective-permute-done.12), channel_id=1, source_target_pairs={{0,240},{16,0},{32,16},{48,32},{64,48},{80,64},{96,80},{112,96},{1... | collective-permute-start | bytes 638984 | tf_op jit(solution)/shard_map/ppermute | solution.py:48
  81.0 7.8 %collective-permute-done.15 = bf16[2,104,512]{2,1,0:T(8,128)(2,1)S(1)} collective-permute-done((bf16[2,104,512]{2,1,0:T(8,128)(2,1)S(1)}, bf16[2,104,512]{2,1,0:T(8,128)(2,1)S(1)}, u32[]{:S(2)}, u32[]{:S(2)}) %collective-permute-start.15) | collective-permute-done | bytes 213024 | tf_op jit(solution)/shard_map/ppermute | solution.py:45
  98.8 5.5 %collective-permute-done.16 = bf16[320,1,256]{2,0,1:T(8,128)(2,1)S(1)} collective-permute-done((bf16[320,1,256]{2,0,1:T(8,128)(2,1)S(1)}, bf16[320,1,256]{2,0,1:T(8,128)(2,1)S(1)}, u32[]{:S(2)}, u32[]{:S(2)}) %collective-permute-start.16) | collective-permute-done | bytes 163872 | tf_op jit(solution)/shard_map/ppermute | solution.py:34
  106.3 4.6 %collective-permute-start.18 = (bf16[2,320,1,256]{3,1,2,0:T(8,128)(2,1)S(1)}, bf16[2,320,1,256]{3,1,2,0:T(8,128)(2,1)}, u32[]{:S(2)}, u32[]{:S(2)}) collective-permute-start(bf16[2,320,1,256]{3,1,2,0:T(8,128)(2,1)S(1)} %maximum_select_fusion), channel_id=1, source_target_pairs={{0,240},{16,0},{32,16},{48,32},{64,48},{80,64},{96,80},{112,96},{1... | collective-permute-start | bytes 983048 | tf_op jit(solution)/shard_map/ppermute | solution.py:48
  110.9 2.7 %collective-permute-done.17 = bf16[2,320,1,256]{3,1,2,0:T(8,128)(2,1)S(1)} collective-permute-done((bf16[2,320,1,256]{3,1,2,0:T(8,128)(2,1)S(1)}, bf16[2,320,1,256]{3,1,2,0:T(8,128)(2,1)S(1)}, u32[]{:S(2)}, u32[]{:S(2)}) %collective-permute-start.17) | collective-permute-done | bytes 327712 | tf_op jit(solution)/shard_map/ppermute | solution.py:45
  115.6 4.6 %collective-permute-start.20 = (bf16[2,320,1,256]{3,1,2,0:T(8,128)(2,1)}, bf16[2,320,1,256]{3,1,2,0:T(8,128)(2,1)}, u32[]{:S(2)}, u32[]{:S(2)}) collective-permute-start(bf16[2,320,1,256]{3,1,2,0:T(8,128)(2,1)} %collective-permute-done.18), channel_id=1, source_target_pairs={{0,240},{16,0},{32,16},{48,32},{64,48},{80,64},{96,80},{112,96},{1... | collective-permute-start | bytes 983048 | tf_op jit(solution)/shard_map/ppermute | solution.py:48
  120.2 4.6 %collective-permute-done.19 = bf16[2,320,1,256]{3,1,2,0:T(8,128)(2,1)} collective-permute-done((bf16[2,320,1,256]{3,1,2,0:T(8,128)(2,1)S(1)}, bf16[2,320,1,256]{3,1,2,0:T(8,128)(2,1)}, u32[]{:S(2)}, u32[]{:S(2)}) %collective-permute-start.19) | collective-permute-done | bytes 327712 | tf_op jit(solution)/shard_map/ppermute | solution.py:45
  127.1 4.6 %collective-permute-start.22 = (bf16[2,320,1,256]{3,1,2,0:T(8,128)(2,1)}, bf16[2,320,1,256]{3,1,2,0:T(8,128)(2,1)S(1)}, u32[]{:S(2)}, u32[]{:S(2)}) collective-permute-start(bf16[2,320,1,256]{3,1,2,0:T(8,128)(2,1)} %collective-permute-done.20), channel_id=1, source_target_pairs={{0,240},{16,0},{32,16},{48,32},{64,48},{80,64},{96,80},{112,96},{1... | collective-permute-start | bytes 983048 | tf_op jit(solution)/shard_map/ppermute | solution.py:48
  131.8 3.8 %collective-permute-done.21 = bf16[2,320,1,256]{3,1,2,0:T(8,128)(2,1)} collective-permute-done((bf16[2,320,1,256]{3,1,2,0:T(8,128)(2,1)}, bf16[2,320,1,256]{3,1,2,0:T(8,128)(2,1)}, u32[]{:S(2)}, u32[]{:S(2)}) %collective-permute-start.21) | collective-permute-done | bytes 327712 | tf_op jit(solution)/shard_map/ppermute | solution.py:45
  137.6 4.7 %collective-permute-start.24 = (bf16[2,320,1,256]{3,1,2,0:T(8,128)(2,1)S(1)}, bf16[2,320,1,256]{3,1,2,0:T(8,128)(2,1)S(1)}, u32[]{:S(2)}, u32[]{:S(2)}) collective-permute-start(bf16[2,320,1,256]{3,1,2,0:T(8,128)(2,1)S(1)} %collective-permute-done.22), channel_id=1, source_target_pairs={{0,240},{16,0},{32,16},{48,32},{64,48},{80,64},{96,80},{112,96},{1... | collective-permute-start | bytes 983048 | tf_op jit(solution)/shard_map/ppermute | solution.py:48
  147.8 4.6 %collective-permute-start.26 = (bf16[2,320,1,256]{3,1,2,0:T(8,128)(2,1)S(1)}, bf16[2,320,1,256]{3,1,2,0:T(8,128)(2,1)S(1)}, u32[]{:S(2)}, u32[]{:S(2)}) collective-permute-start(bf16[2,320,1,256]{3,1,2,0:T(8,128)(2,1)S(1)} %collective-permute-done.24), channel_id=1, source_target_pairs={{0,240},{16,0},{32,16},{48,32},{64,48},{80,64},{96,80},{112,96},{1... | collective-permute-start | bytes 983048 | tf_op jit(solution)/shard_map/ppermute | solution.py:48
  158.1 4.6 %collective-permute-start.28 = (bf16[2,320,1,256]{3,1,2,0:T(8,128)(2,1)S(1)}, bf16[2,320,1,256]{3,1,2,0:T(8,128)(2,1)S(1)}, u32[]{:S(2)}, u32[]{:S(2)}) collective-permute-start(bf16[2,320,1,256]{3,1,2,0:T(8,128)(2,1)S(1)} %collective-permute-done.26), channel_id=1, source_target_pairs={{0,240},{16,0},{32,16},{48,32},{64,48},{80,64},{96,80},{112,96},{1... | collective-permute-start | bytes 983048 | tf_op jit(solution)/shard_map/ppermute | solution.py:48
  166.8 4.9 %collective-permute-start.30 = (bf16[2,320,1,256]{3,1,2,0:T(8,128)(2,1)S(1)}, bf16[2,320,1,256]{3,1,2,0:T(8,128)(2,1)S(1)}, u32[]{:S(2)}, u32[]{:S(2)}) collective-permute-start(bf16[2,320,1,256]{3,1,2,0:T(8,128)(2,1)S(1)} %collective-permute-done.28), channel_id=1, source_target_pairs={{0,240},{16,0},{32,16},{48,32},{64,48},{80,64},{96,80},{112,96},{1... | collective-permute-start | bytes 983048 | tf_op jit(solution)/shard_map/ppermute | solution.py:48
  176.5 6.1 %collective-permute-done.31 = bf16[2,320,1,256]{3,1,2,0:T(8,128)(2,1)S(1)} collective-permute-done((bf16[2,320,1,256]{3,1,2,0:T(8,128)(2,1)S(1)}, bf16[2,320,1,256]{3,1,2,0:T(8,128)(2,1)S(1)}, u32[]{:S(2)}, u32[]{:S(2)}) %collective-permute-start.31) | collective-permute-done | bytes 327712 | tf_op jit(solution)/shard_map/ppermute | solution.py:45
  184.8 2.4 fusion.57
  195.5 19.7 %collective-permute-start.36 = (bf16[160,1536]{1,0:T(8,128)(2,1)S(1)}, bf16[160,1536]{1,0:T(8,128)(2,1)S(1)}, u32[]{:S(2)}, u32[]{:S(2)}) collective-permute-start(bf16[160,1536]{1,0:T(8,128)(2,1)S(1)} %dynamic-slice_convert_fusion), channel_id=1, source_target_pairs={{0,1},{1,0},{2,3},{3,2},{4,5},{5,4},{6,7},{7,6},{8,9},{9,8},{10,11... | collective-permute-start | bytes 1474568 | tf_op jit(solution)/shard_map/ppermute | solution.py:71
  217.8 3.1 %collective-permute-start.37 = (bf16[160,768]{1,0:T(8,128)(2,1)S(1)}, bf16[160,768]{1,0:T(8,128)(2,1)S(1)}, u32[]{:S(2)}, u32[]{:S(2)}) collective-permute-start(bf16[160,768]{1,0:T(8,128)(2,1)S(1)} %dynamic-slice_convert_fusion.2), channel_id=1, source_target_pairs={{0,2},{1,3},{2,0},{3,1},{4,6},{5,7},{6,4},{7,5},{8,10},{9,11},{10,... | collective-permute-start | bytes 737288 | tf_op jit(solution)/shard_map/ppermute | solution.py:71
  223.1 3.6 %collective-permute-done.37 = bf16[160,768]{1,0:T(8,128)(2,1)S(1)} collective-permute-done((bf16[160,768]{1,0:T(8,128)(2,1)S(1)}, bf16[160,768]{1,0:T(8,128)(2,1)S(1)}, u32[]{:S(2)}, u32[]{:S(2)}) %collective-permute-start.37) | collective-permute-done | bytes 245792 | tf_op jit(solution)/shard_map/ppermute | solution.py:71
  226.8 4.7 %collective-permute-start.38 = (bf16[160,384]{1,0:T(8,128)(2,1)S(1)}, bf16[160,384]{1,0:T(8,128)(2,1)S(1)}, u32[]{:S(2)}, u32[]{:S(2)}) collective-permute-start(bf16[160,384]{1,0:T(8,128)(2,1)S(1)} %dynamic-slice_convert_fusion.4), channel_id=1, source_target_pairs={{0,4},{1,5},{2,6},{3,7},{4,0},{5,1},{6,2},{7,3},{8,12},{9,13},{10,... | collective-permute-start | bytes 368648 | tf_op jit(solution)/shard_map/ppermute | solution.py:71
  231.6 2.2 collective-permute-start.34
  237.3 4.0 %collective-permute-start.35 = (bf16[160,192]{1,0:T(8,128)(2,1)S(1)}, bf16[160,192]{1,0:T(8,128)(2,1)S(1)}, u32[]{:S(2)}, u32[]{:S(2)}) collective-permute-start(bf16[160,192]{1,0:T(8,128)(2,1)S(1)} %dynamic-slice_convert_fusion.7), channel_id=1, source_target_pairs={{0,4},{1,5},{2,6},{3,7},{4,0},{5,1},{6,2},{7,3},{8,12},{9,13},{10,... | collective-permute-start | bytes 184328 | tf_op jit(solution)/shard_map/ppermute | solution.py:71
  241.5 2.5 %collective-permute-done.35 = bf16[160,192]{1,0:T(8,128)(2,1)S(1)} collective-permute-done((bf16[160,192]{1,0:T(8,128)(2,1)S(1)}, bf16[160,192]{1,0:T(8,128)(2,1)S(1)}, u32[]{:S(2)}, u32[]{:S(2)}) %collective-permute-start.35) | collective-permute-done | bytes 61472 | tf_op jit(solution)/shard_map/ppermute | solution.py:71
  (203 shorter events, 86.9 us)
Async XLA Ops:
  2.4 14.3 %collective-permute-start = (bf16[104,512]{1,0:T(8,128)(2,1)S(1)}, bf16[104,512]{1,0:T(8,128)(2,1)S(1)}, u32[]{:S(2)}, u32[]{:S(2)}) collective-permute-start(bf16[104,512]{1,0:T(8,128)(2,1)S(1)} %get-tuple-element.54), channel_id=1, source_target_pairs={{0,256},{16,272},{32,288},{48,304},{64,320},{80,336},{96,352},{112... | collective-permute-start | bytes 319496 | tf_op jit(solution)/shard_map/ppermute | solution.py:34
  9.2 122.5 %collective-permute-start.40 = (bf16[320,192]{1,0:T(8,128)(2,1)S(1)}, bf16[320,192]{1,0:T(8,128)(2,1)S(1)}, u32[]{:S(2)}, u32[]{:S(2)}) collective-permute-start(bf16[320,192]{1,0:T(8,128)(2,1)S(1)} %constant_dynamic-slice_fusion), channel_id=1, source_target_pairs={{0,16},{16,32},{32,48},{48,64},{64,80},{80,96},{96,112},{112,128},... | collective-permute-start | bytes 368648 | tf_op jit(solution)/shard_map/ppermute | solution.py:19
  16.8 14.1 %collective-permute-start.1 = (bf16[2,104,512]{2,1,0:T(8,128)(2,1)S(1)}, bf16[2,104,512]{2,1,0:T(8,128)(2,1)S(1)}, u32[]{:S(2)}, u32[]{:S(2)}) collective-permute-start(bf16[2,104,512]{2,1,0:T(8,128)(2,1)S(1)} %maximum_select_fusion.2), channel_id=1, source_target_pairs={{0,16},{16,32},{32,48},{48,64},{64,80},{80,96},{96,112},{112,128},... | collective-permute-start | bytes 638984 | tf_op jit(solution)/shard_map/ppermute | solution.py:45
  20.3 12.5 %collective-permute-start.2 = (bf16[2,104,512]{2,1,0:T(8,128)(2,1)S(1)}, bf16[2,104,512]{2,1,0:T(8,128)(2,1)S(1)}, u32[]{:S(2)}, u32[]{:S(2)}) collective-permute-start(bf16[2,104,512]{2,1,0:T(8,128)(2,1)S(1)} %maximum_select_fusion.2), channel_id=1, source_target_pairs={{0,240},{16,0},{32,16},{48,32},{64,48},{80,64},{96,80},{112,96},{1... | collective-permute-start | bytes 638984 | tf_op jit(solution)/shard_map/ppermute | solution.py:48
  30.9 8.3 %collective-permute-start.3 = (bf16[2,104,512]{2,1,0:T(8,128)(2,1)S(1)}, bf16[2,104,512]{2,1,0:T(8,128)(2,1)S(1)}, u32[]{:S(2)}, u32[]{:S(2)}) collective-permute-start(bf16[2,104,512]{2,1,0:T(8,128)(2,1)S(1)} %collective-permute-done.1), channel_id=1, source_target_pairs={{0,16},{16,32},{32,48},{48,64},{64,80},{80,96},{96,112},{112,128},... | collective-permute-start | bytes 638984 | tf_op jit(solution)/shard_map/ppermute | solution.py:45
  32.9 8.3 %collective-permute-start.4 = (bf16[2,104,512]{2,1,0:T(8,128)(2,1)S(1)}, bf16[2,104,512]{2,1,0:T(8,128)(2,1)S(1)}, u32[]{:S(2)}, u32[]{:S(2)}) collective-permute-start(bf16[2,104,512]{2,1,0:T(8,128)(2,1)S(1)} %collective-permute-done.2), channel_id=1, source_target_pairs={{0,240},{16,0},{32,16},{48,32},{64,48},{80,64},{96,80},{112,96},{1... | collective-permute-start | bytes 638984 | tf_op jit(solution)/shard_map/ppermute | solution.py:48
  39.2 7.8 %collective-permute-start.5 = (bf16[2,104,512]{2,1,0:T(8,128)(2,1)S(1)}, bf16[2,104,512]{2,1,0:T(8,128)(2,1)S(1)}, u32[]{:S(2)}, u32[]{:S(2)}) collective-permute-start(bf16[2,104,512]{2,1,0:T(8,128)(2,1)S(1)} %collective-permute-done.3), channel_id=1, source_target_pairs={{0,16},{16,32},{32,48},{48,64},{64,80},{80,96},{96,112},{112,128},... | collective-permute-start | bytes 638984 | tf_op jit(solution)/shard_map/ppermute | solution.py:45
  41.2 7.8 %collective-permute-start.6 = (bf16[2,104,512]{2,1,0:T(8,128)(2,1)S(1)}, bf16[2,104,512]{2,1,0:T(8,128)(2,1)S(1)}, u32[]{:S(2)}, u32[]{:S(2)}) collective-permute-start(bf16[2,104,512]{2,1,0:T(8,128)(2,1)S(1)} %collective-permute-done.4), channel_id=1, source_target_pairs={{0,240},{16,0},{32,16},{48,32},{64,48},{80,64},{96,80},{112,96},{1... | collective-permute-start | bytes 638984 | tf_op jit(solution)/shard_map/ppermute | solution.py:48
  47.0 7.8 %collective-permute-start.7 = (bf16[2,104,512]{2,1,0:T(8,128)(2,1)S(1)}, bf16[2,104,512]{2,1,0:T(8,128)(2,1)S(1)}, u32[]{:S(2)}, u32[]{:S(2)}) collective-permute-start(bf16[2,104,512]{2,1,0:T(8,128)(2,1)S(1)} %collective-permute-done.5), channel_id=1, source_target_pairs={{0,16},{16,32},{32,48},{48,64},{64,80},{80,96},{96,112},{112,128},... | collective-permute-start | bytes 638984 | tf_op jit(solution)/shard_map/ppermute | solution.py:45
  54.8 7.8 %collective-permute-start.9 = (bf16[2,104,512]{2,1,0:T(8,128)(2,1)S(1)}, bf16[2,104,512]{2,1,0:T(8,128)(2,1)S(1)}, u32[]{:S(2)}, u32[]{:S(2)}) collective-permute-start(bf16[2,104,512]{2,1,0:T(8,128)(2,1)S(1)} %collective-permute-done.7), channel_id=1, source_target_pairs={{0,16},{16,32},{32,48},{48,64},{64,80},{80,96},{96,112},{112,128},... | collective-permute-start | bytes 638984 | tf_op jit(solution)/shard_map/ppermute | solution.py:45
  62.6 7.8 %collective-permute-start.11 = (bf16[2,104,512]{2,1,0:T(8,128)(2,1)S(1)}, bf16[2,104,512]{2,1,0:T(8,128)(2,1)S(1)}, u32[]{:S(2)}, u32[]{:S(2)}) collective-permute-start(bf16[2,104,512]{2,1,0:T(8,128)(2,1)S(1)} %collective-permute-done.9), channel_id=1, source_target_pairs={{0,16},{16,32},{32,48},{48,64},{64,80},{80,96},{96,112},{112,128},... | collective-permute-start | bytes 638984 | tf_op jit(solution)/shard_map/ppermute | solution.py:45
  70.4 8.7 %collective-permute-start.13 = (bf16[2,104,512]{2,1,0:T(8,128)(2,1)S(1)}, bf16[2,104,512]{2,1,0:T(8,128)(2,1)S(1)}, u32[]{:S(2)}, u32[]{:S(2)}) collective-permute-start(bf16[2,104,512]{2,1,0:T(8,128)(2,1)S(1)} %collective-permute-done.11), channel_id=1, source_target_pairs={{0,16},{16,32},{32,48},{48,64},{64,80},{80,96},{96,112},{112,128},... | collective-permute-start | bytes 638984 | tf_op jit(solution)/shard_map/ppermute | solution.py:45
  72.3 8.7 %collective-permute-start.14 = (bf16[2,104,512]{2,1,0:T(8,128)(2,1)S(1)}, bf16[2,104,512]{2,1,0:T(8,128)(2,1)S(1)}, u32[]{:S(2)}, u32[]{:S(2)}) collective-permute-start(bf16[2,104,512]{2,1,0:T(8,128)(2,1)S(1)} %collective-permute-done.12), channel_id=1, source_target_pairs={{0,240},{16,0},{32,16},{48,32},{64,48},{80,64},{96,80},{112,96},{1... | collective-permute-start | bytes 638984 | tf_op jit(solution)/shard_map/ppermute | solution.py:48
  79.0 9.8 %collective-permute-start.15 = (bf16[2,104,512]{2,1,0:T(8,128)(2,1)S(1)}, bf16[2,104,512]{2,1,0:T(8,128)(2,1)S(1)}, u32[]{:S(2)}, u32[]{:S(2)}) collective-permute-start(bf16[2,104,512]{2,1,0:T(8,128)(2,1)S(1)} %collective-permute-done.13), channel_id=1, source_target_pairs={{0,16},{16,32},{32,48},{48,64},{64,80},{80,96},{96,112},{112,128},... | collective-permute-start | bytes 638984 | tf_op jit(solution)/shard_map/ppermute | solution.py:45
  104.3 9.3 %collective-permute-start.17 = (bf16[2,320,1,256]{3,1,2,0:T(8,128)(2,1)S(1)}, bf16[2,320,1,256]{3,1,2,0:T(8,128)(2,1)S(1)}, u32[]{:S(2)}, u32[]{:S(2)}) collective-permute-start(bf16[2,320,1,256]{3,1,2,0:T(8,128)(2,1)S(1)} %maximum_select_fusion), channel_id=1, source_target_pairs={{0,16},{16,32},{32,48},{48,64},{64,80},{80,96},{96,112},{112,128},... | collective-permute-start | bytes 983048 | tf_op jit(solution)/shard_map/ppermute | solution.py:45
  106.3 9.3 %collective-permute-start.18 = (bf16[2,320,1,256]{3,1,2,0:T(8,128)(2,1)S(1)}, bf16[2,320,1,256]{3,1,2,0:T(8,128)(2,1)}, u32[]{:S(2)}, u32[]{:S(2)}) collective-permute-start(bf16[2,320,1,256]{3,1,2,0:T(8,128)(2,1)S(1)} %maximum_select_fusion), channel_id=1, source_target_pairs={{0,240},{16,0},{32,16},{48,32},{64,48},{80,64},{96,80},{112,96},{1... | collective-permute-start | bytes 983048 | tf_op jit(solution)/shard_map/ppermute | solution.py:48
  113.7 11.2 %collective-permute-start.19 = (bf16[2,320,1,256]{3,1,2,0:T(8,128)(2,1)S(1)}, bf16[2,320,1,256]{3,1,2,0:T(8,128)(2,1)}, u32[]{:S(2)}, u32[]{:S(2)}) collective-permute-start(bf16[2,320,1,256]{3,1,2,0:T(8,128)(2,1)S(1)} %collective-permute-done.17), channel_id=1, source_target_pairs={{0,16},{16,32},{32,48},{48,64},{64,80},{80,96},{96,112},{112,128},... | collective-permute-start | bytes 983048 | tf_op jit(solution)/shard_map/ppermute | solution.py:45
  115.6 11.5 %collective-permute-start.20 = (bf16[2,320,1,256]{3,1,2,0:T(8,128)(2,1)}, bf16[2,320,1,256]{3,1,2,0:T(8,128)(2,1)}, u32[]{:S(2)}, u32[]{:S(2)}) collective-permute-start(bf16[2,320,1,256]{3,1,2,0:T(8,128)(2,1)} %collective-permute-done.18), channel_id=1, source_target_pairs={{0,240},{16,0},{32,16},{48,32},{64,48},{80,64},{96,80},{112,96},{1... | collective-permute-start | bytes 983048 | tf_op jit(solution)/shard_map/ppermute | solution.py:48
  124.8 10.8 %collective-permute-start.21 = (bf16[2,320,1,256]{3,1,2,0:T(8,128)(2,1)}, bf16[2,320,1,256]{3,1,2,0:T(8,128)(2,1)}, u32[]{:S(2)}, u32[]{:S(2)}) collective-permute-start(bf16[2,320,1,256]{3,1,2,0:T(8,128)(2,1)} %collective-permute-done.19), channel_id=1, source_target_pairs={{0,16},{16,32},{32,48},{48,64},{64,80},{80,96},{96,112},{112,128},... | collective-permute-start | bytes 983048 | tf_op jit(solution)/shard_map/ppermute | solution.py:45
  127.1 10.5 %collective-permute-start.22 = (bf16[2,320,1,256]{3,1,2,0:T(8,128)(2,1)}, bf16[2,320,1,256]{3,1,2,0:T(8,128)(2,1)S(1)}, u32[]{:S(2)}, u32[]{:S(2)}) collective-permute-start(bf16[2,320,1,256]{3,1,2,0:T(8,128)(2,1)} %collective-permute-done.20), channel_id=1, source_target_pairs={{0,240},{16,0},{32,16},{48,32},{64,48},{80,64},{96,80},{112,96},{1... | collective-permute-start | bytes 983048 | tf_op jit(solution)/shard_map/ppermute | solution.py:48
  135.6 9.8 %collective-permute-start.23 = (bf16[2,320,1,256]{3,1,2,0:T(8,128)(2,1)}, bf16[2,320,1,256]{3,1,2,0:T(8,128)(2,1)S(1)}, u32[]{:S(2)}, u32[]{:S(2)}) collective-permute-start(bf16[2,320,1,256]{3,1,2,0:T(8,128)(2,1)} %collective-permute-done.21), channel_id=1, source_target_pairs={{0,16},{16,32},{32,48},{48,64},{64,80},{80,96},{96,112},{112,128},... | collective-permute-start | bytes 983048 | tf_op jit(solution)/shard_map/ppermute | solution.py:45
  137.6 10.2 %collective-permute-start.24 = (bf16[2,320,1,256]{3,1,2,0:T(8,128)(2,1)S(1)}, bf16[2,320,1,256]{3,1,2,0:T(8,128)(2,1)S(1)}, u32[]{:S(2)}, u32[]{:S(2)}) collective-permute-start(bf16[2,320,1,256]{3,1,2,0:T(8,128)(2,1)S(1)} %collective-permute-done.22), channel_id=1, source_target_pairs={{0,240},{16,0},{32,16},{48,32},{64,48},{80,64},{96,80},{112,96},{1... | collective-permute-start | bytes 983048 | tf_op jit(solution)/shard_map/ppermute | solution.py:48
  145.4 9.0 %collective-permute-start.25 = (bf16[2,320,1,256]{3,1,2,0:T(8,128)(2,1)S(1)}, bf16[2,320,1,256]{3,1,2,0:T(8,128)(2,1)S(1)}, u32[]{:S(2)}, u32[]{:S(2)}) collective-permute-start(bf16[2,320,1,256]{3,1,2,0:T(8,128)(2,1)S(1)} %collective-permute-done.23), channel_id=1, source_target_pairs={{0,16},{16,32},{32,48},{48,64},{64,80},{80,96},{96,112},{112,128},... | collective-permute-start | bytes 983048 | tf_op jit(solution)/shard_map/ppermute | solution.py:45
  147.8 10.4 %collective-permute-start.26 = (bf16[2,320,1,256]{3,1,2,0:T(8,128)(2,1)S(1)}, bf16[2,320,1,256]{3,1,2,0:T(8,128)(2,1)S(1)}, u32[]{:S(2)}, u32[]{:S(2)}) collective-permute-start(bf16[2,320,1,256]{3,1,2,0:T(8,128)(2,1)S(1)} %collective-permute-done.24), channel_id=1, source_target_pairs={{0,240},{16,0},{32,16},{48,32},{64,48},{80,64},{96,80},{112,96},{1... | collective-permute-start | bytes 983048 | tf_op jit(solution)/shard_map/ppermute | solution.py:48
  154.4 9.9 %collective-permute-start.27 = (bf16[2,320,1,256]{3,1,2,0:T(8,128)(2,1)S(1)}, bf16[2,320,1,256]{3,1,2,0:T(8,128)(2,1)S(1)}, u32[]{:S(2)}, u32[]{:S(2)}) collective-permute-start(bf16[2,320,1,256]{3,1,2,0:T(8,128)(2,1)S(1)} %collective-permute-done.25), channel_id=1, source_target_pairs={{0,16},{16,32},{32,48},{48,64},{64,80},{80,96},{96,112},{112,128},... | collective-permute-start | bytes 983048 | tf_op jit(solution)/shard_map/ppermute | solution.py:45
  158.1 8.7 %collective-permute-start.28 = (bf16[2,320,1,256]{3,1,2,0:T(8,128)(2,1)S(1)}, bf16[2,320,1,256]{3,1,2,0:T(8,128)(2,1)S(1)}, u32[]{:S(2)}, u32[]{:S(2)}) collective-permute-start(bf16[2,320,1,256]{3,1,2,0:T(8,128)(2,1)S(1)} %collective-permute-done.26), channel_id=1, source_target_pairs={{0,240},{16,0},{32,16},{48,32},{64,48},{80,64},{96,80},{112,96},{1... | collective-permute-start | bytes 983048 | tf_op jit(solution)/shard_map/ppermute | solution.py:48
  164.3 9.0 %collective-permute-start.29 = (bf16[2,320,1,256]{3,1,2,0:T(8,128)(2,1)S(1)}, bf16[2,320,1,256]{3,1,2,0:T(8,128)(2,1)S(1)}, u32[]{:S(2)}, u32[]{:S(2)}) collective-permute-start(bf16[2,320,1,256]{3,1,2,0:T(8,128)(2,1)S(1)} %collective-permute-done.27), channel_id=1, source_target_pairs={{0,16},{16,32},{32,48},{48,64},{64,80},{80,96},{96,112},{112,128},... | collective-permute-start | bytes 983048 | tf_op jit(solution)/shard_map/ppermute | solution.py:45
  166.8 9.0 %collective-permute-start.30 = (bf16[2,320,1,256]{3,1,2,0:T(8,128)(2,1)S(1)}, bf16[2,320,1,256]{3,1,2,0:T(8,128)(2,1)S(1)}, u32[]{:S(2)}, u32[]{:S(2)}) collective-permute-start(bf16[2,320,1,256]{3,1,2,0:T(8,128)(2,1)S(1)} %collective-permute-done.28), channel_id=1, source_target_pairs={{0,240},{16,0},{32,16},{48,32},{64,48},{80,64},{96,80},{112,96},{1... | collective-permute-start | bytes 983048 | tf_op jit(solution)/shard_map/ppermute | solution.py:48
  173.3 9.3 %collective-permute-start.31 = (bf16[2,320,1,256]{3,1,2,0:T(8,128)(2,1)S(1)}, bf16[2,320,1,256]{3,1,2,0:T(8,128)(2,1)S(1)}, u32[]{:S(2)}, u32[]{:S(2)}) collective-permute-start(bf16[2,320,1,256]{3,1,2,0:T(8,128)(2,1)S(1)} %collective-permute-done.29), channel_id=1, source_target_pairs={{0,16},{16,32},{32,48},{48,64},{64,80},{80,96},{96,112},{112,128},... | collective-permute-start | bytes 983048 | tf_op jit(solution)/shard_map/ppermute | solution.py:45
  195.5 22.1 %collective-permute-start.36 = (bf16[160,1536]{1,0:T(8,128)(2,1)S(1)}, bf16[160,1536]{1,0:T(8,128)(2,1)S(1)}, u32[]{:S(2)}, u32[]{:S(2)}) collective-permute-start(bf16[160,1536]{1,0:T(8,128)(2,1)S(1)} %dynamic-slice_convert_fusion), channel_id=1, source_target_pairs={{0,1},{1,0},{2,3},{3,2},{4,5},{5,4},{6,7},{7,6},{8,9},{9,8},{10,11... | collective-permute-start | bytes 1474568 | tf_op jit(solution)/shard_map/ppermute | solution.py:71
  217.8 8.9 %collective-permute-start.37 = (bf16[160,768]{1,0:T(8,128)(2,1)S(1)}, bf16[160,768]{1,0:T(8,128)(2,1)S(1)}, u32[]{:S(2)}, u32[]{:S(2)}) collective-permute-start(bf16[160,768]{1,0:T(8,128)(2,1)S(1)} %dynamic-slice_convert_fusion.2), channel_id=1, source_target_pairs={{0,2},{1,3},{2,0},{3,1},{4,6},{5,7},{6,4},{7,5},{8,10},{9,11},{10,... | collective-permute-start | bytes 737288 | tf_op jit(solution)/shard_map/ppermute | solution.py:71
  221.1 10.4 %collective-permute-start.33 = (bf16[160,768]{1,0:T(8,128)(2,1)S(1)}, bf16[160,768]{1,0:T(8,128)(2,1)S(1)}, u32[]{:S(2)}, u32[]{:S(2)}) collective-permute-start(bf16[160,768]{1,0:T(8,128)(2,1)S(1)} %dynamic-slice_convert_fusion.3), channel_id=1, source_target_pairs={{0,8},{1,9},{2,10},{3,11},{4,12},{5,13},{6,14},{7,15},{8,0},{9,1},... | collective-permute-start | bytes 737288 | tf_op jit(solution)/shard_map/ppermute | solution.py:71
  (19 other events, 137.8 us)

commit v5 on v4

--- a/solution.py
+++ b/solution.py
@@ -76,6 +76,289 @@
 
 
 def attend_piece(state_now, kv_piece, key_frame, queries, query_frame, query_first, head_dim):
+    run_max, run_sum, accumulated = state_now
+    key_part = kv_piece[:, :, :head_dim]
+    value_part = kv_piece[:, :, head_dim:]
+    scores = jnp.einsum(
+        "nhe,mhe->nhm", queries, key_part, preferred_element_type=jnp.float32
+    ) * head_dim ** (-0.5)
+    allowed = (key_frame[None, :] <= query_frame[:, None]) & (
+        key_frame[None, :] >= query_first[:, None]
+    )
+    masked = jnp.where(allowed[:, None, :], scores, NEG)
+    new_max = jnp.maximum(run_max, masked.max(-1))
+    exponent = jnp.where(allowed[:, None, :], jnp.exp(masked - new_max[..., None]), 0.0)
+    factor = jnp.exp(run_max - new_max)
+    run_sum = run_sum * factor + exponent.sum(-1)
+    accumulated = accumulated * factor[..., None] + jnp.einsum(
+        "nhm,mhe->nhe",
+        exponent.astype(jnp.bfloat16),
+        value_part,
+        preferred_element_type=jnp.float32,
+    )
+    return (new_max, run_sum, accumulated)
+
+
+def per_device(
+    latents, timestep, offsets, qkv_weight, mod_weight, gate_weight, out_weight, conv_weight
+):
+    tok_rows = latents.shape[0]
+    heads_here = qkv_weight.shape[1]
+    head_dim = out_weight.shape[2]
+    chan_here = gate_weight.shape[1]
+    frame_size = HH * WW
+    frames_here = tok_rows // frame_size
+    position = lax.axis_index("ctx")
+    column = lax.axis_index("fsdp")
+    time_act = time_features(timestep, gate_weight.shape[0])
+    gate_vec = jnp.dot(time_act, gate_weight, preferred_element_type=jnp.float32)
+    float_rows = latents.astype(jnp.float32)
+    centred = float_rows - float_rows.mean(-1, keepdims=True)
+    variance = (centred * centred).mean(-1, keepdims=True)
+    normed = centred * lax.rsqrt(variance + EPS)
+
+    rows_here = qkv_weight.shape[0]
+    qkv_width = qkv_weight.shape[2]
+    qkv_cols = heads_here * qkv_width
+    out_cols = heads_here * head_dim
+    width = qkv_cols + out_cols
+    local_shares = jnp.einsum(
+        "rjt,t->rj", mod_weight, time_act, preferred_element_type=jnp.float32
+    )
+    shares_hi = local_shares.astype(jnp.bfloat16)
+    shares_lo = (local_shares - shares_hi.astype(jnp.float32)).astype(jnp.bfloat16)
+    share_count = 4 * rows_here
+    extra_rows = 8 * ((share_count + 8 * width - 1) // (8 * width))
+    share_block = jnp.zeros((extra_rows * width,), jnp.bfloat16)
+    share_block = share_block.at[:share_count].set(
+        jnp.concatenate([shares_hi, shares_lo], axis=1).reshape(share_count)
+    )
+    bundle = jnp.concatenate(
+        [
+            jnp.concatenate(
+                [
+                    qkv_weight.reshape(rows_here, qkv_cols),
+                    out_weight.reshape(rows_here, out_cols),
+                ],
+                axis=1,
+            ),
+            share_block.reshape(extra_rows, width),
+        ],
+        axis=0,
+    )
+    gathered = ring_gather(bundle, "ctx")
+    blocks = gathered.shape[0] // bundle.shape[0]
+    gathered = gathered.reshape(blocks, rows_here + extra_rows, width)
+    full_rows = blocks * rows_here
+    w_piece = gathered[:, :rows_here, :qkv_cols].reshape(full_rows, heads_here, qkv_width)
+    o_piece = gathered[:, :rows_here, qkv_cols:].reshape(full_rows, heads_here, head_dim)
+    share_bits = (
+        gathered[:, rows_here:, :]
+        .reshape(blocks, extra_rows * width)[:, :share_count]
+        .reshape(full_rows, 4)
+        .astype(jnp.float32)
+    )
+    shares = share_bits[:, :2] + share_bits[:, 2:]
+
+    modulated = (normed * (1.0 + shares[:, 1]) + shares[:, 0]).astype(jnp.bfloat16)
+    projected_qkv = jnp.einsum(
+        "nr,rhc->nhc", modulated, w_piece, preferred_element_type=jnp.float32
+    ).astype(jnp.bfloat16)
+    queries = projected_qkv[:, :, :head_dim]
+    packed = projected_qkv[:, :, head_dim:]
+    query_frame = position * frames_here + jnp.arange(tok_rows, dtype=jnp.int32) // frame_size
+    local_first = lax.dynamic_slice_in_dim(offsets, position * frames_here, frames_here, 0)
+    query_first = jnp.repeat(local_first, frame_size)
+    state = (
+        jnp.full((tok_rows, heads_here), NEG, jnp.float32),
+        jnp.zeros((tok_rows, heads_here), jnp.float32),
+        jnp.zeros((tok_rows, heads_here, head_dim), jnp.float32),
+    )
+    size = lax.axis_size("ctx")
+    ring = size // 2
+    partner = lax.ppermute(packed, "ctx", [(i, (i + ring) % size) for i in range(size)])
+    pair = jnp.where(
+        position // ring == 0, jnp.stack([packed, partner]), jnp.stack([partner, packed])
+    )
+    ring_pos = position % ring
+    forward = [(y * ring + a, y * ring + (a + 1) % ring) for y in range(2) for a in range(ring)]
+    backward = [(y * ring + a, y * ring + (a - 1) % ring) for y in range(2) for a in range(ring)]
+    token_ids = jnp.arange(tok_rows, dtype=jnp.int32)
+
+    def fold(state_in, piece, source):
+        key_frame = (
+            jnp.concatenate(
+                [source * tok_rows + token_ids, (ring + source) * tok_rows + token_ids]
+            )
+            // frame_size
+        )
+        return attend_piece(
+            state_in,
+            piece.reshape((2 * tok_rows,) + piece.shape[2:]),
+            key_frame,
+            queries,
+            query_frame,
+            query_first,
+            head_dim,
+        )
+
+    states = [fold(state, pair, ring_pos)]
+    ahead = pair
+    behind = pair
+    for step in range(1, ring // 2 + 1):
+        if step > 1:
+            ahead, behind, _ = lax.optimization_barrier((ahead, behind, states[step - 2]))
+        ahead = lax.ppermute(ahead, "ctx", forward)
+        has_behind = step < ring - ring // 2
+        if has_behind:
+            behind = lax.ppermute(behind, "ctx", backward)
+        folded = fold(states[-1], ahead, (ring_pos - step) % ring)
+        if has_behind:
+            folded = fold(folded, behind, (ring_pos + step) % ring)
+        states.append(folded)
+    state = states[-1]
+    run_max, run_sum, accumulated = state_now
+    key_part = kv_piece[:, :, :head_dim]
+    value_part = kv_piece[:, :, head_dim:]
+    scores = jnp.einsum(
+        "nhe,mhe->nhm", queries, key_part, preferred_element_type=jnp.float32
+    ) * head_dim ** (-0.5)
+    allowed = (key_frame[None, :] <= query_frame[:, None]) & (
+        key_frame[None, :] >= query_first[:, None]
+    )
+    masked = jnp.where(allowed[:, None, :], scores, NEG)
+    new_max = jnp.maximum(run_max, masked.max(-1))
+    exponent = jnp.where(allowed[:, None, :], jnp.exp(masked - new_max[..., None]), 0.0)
+    factor = jnp.exp(run_max - new_max)
+    run_sum = run_sum * factor + exponent.sum(-1)
+    accumulated = accumulated * factor[..., None] + jnp.einsum(
+        "nhm,mhe->nhe",
+        exponent.astype(jnp.bfloat16),
+        value_part,
+        preferred_element_type=jnp.float32,
+    )
+    return (new_max, run_sum, accumulated)
+
+
+def per_device(
+    latents, timestep, offsets, qkv_weight, mod_weight, gate_weight, out_weight, conv_weight
+):
+    tok_rows = latents.shape[0]
+    heads_here = qkv_weight.shape[1]
+    head_dim = out_weight.shape[2]
+    chan_here = gate_weight.shape[1]
+    frame_size = HH * WW
+    frames_here = tok_rows // frame_size
+    position = lax.axis_index("ctx")
+    column = lax.axis_index("fsdp")
+    time_act = time_features(timestep, gate_weight.shape[0])
+    gate_vec = jnp.dot(time_act, gate_weight, preferred_element_type=jnp.float32)
+    float_rows = latents.astype(jnp.float32)
+    centred = float_rows - float_rows.mean(-1, keepdims=True)
+    variance = (centred * centred).mean(-1, keepdims=True)
+    normed = centred * lax.rsqrt(variance + EPS)
+
+    rows_here = qkv_weight.shape[0]
+    qkv_width = qkv_weight.shape[2]
+    qkv_cols = heads_here * qkv_width
+    out_cols = heads_here * head_dim
+    width = qkv_cols + out_cols
+    local_shares = jnp.einsum(
+        "rjt,t->rj", mod_weight, time_act, preferred_element_type=jnp.float32
+    )
+    shares_hi = local_shares.astype(jnp.bfloat16)
+    shares_lo = (local_shares - shares_hi.astype(jnp.float32)).astype(jnp.bfloat16)
+    share_count = 4 * rows_here
+    extra_rows = 8 * ((share_count + 8 * width - 1) // (8 * width))
+    share_block = jnp.zeros((extra_rows * width,), jnp.bfloat16)
+    share_block = share_block.at[:share_count].set(
+        jnp.concatenate([shares_hi, shares_lo], axis=1).reshape(share_count)
+    )
+    bundle = jnp.concatenate(
+        [
+            jnp.concatenate(
+                [
+                    qkv_weight.reshape(rows_here, qkv_cols),
+                    out_weight.reshape(rows_here, out_cols),
+                ],
+                axis=1,
+            ),
+            share_block.reshape(extra_rows, width),
+        ],
+        axis=0,
+    )
+    gathered = ring_gather(bundle, "ctx")
+    blocks = gathered.shape[0] // bundle.shape[0]
+    gathered = gathered.reshape(blocks, rows_here + extra_rows, width)
+    full_rows = blocks * rows_here
+    w_piece = gathered[:, :rows_here, :qkv_cols].reshape(full_rows, heads_here, qkv_width)
+    o_piece = gathered[:, :rows_here, qkv_cols:].reshape(full_rows, heads_here, head_dim)
+    share_bits = (
+        gathered[:, rows_here:, :]
+        .reshape(blocks, extra_rows * width)[:, :share_count]
+        .reshape(full_rows, 4)
+        .astype(jnp.float32)
+    )
+    shares = share_bits[:, :2] + share_bits[:, 2:]
+
+    modulated = (normed * (1.0 + shares[:, 1]) + shares[:, 0]).astype(jnp.bfloat16)
+    projected_qkv = jnp.einsum(
+        "nr,rhc->nhc", modulated, w_piece, preferred_element_type=jnp.float32
+    ).astype(jnp.bfloat16)
+    queries = projected_qkv[:, :, :head_dim]
+    packed = projected_qkv[:, :, head_dim:]
+    query_frame = position * frames_here + jnp.arange(tok_rows, dtype=jnp.int32) // frame_size
+    local_first = lax.dynamic_slice_in_dim(offsets, position * frames_here, frames_here, 0)
+    query_first = jnp.repeat(local_first, frame_size)
+    state = (
+        jnp.full((tok_rows, heads_here), NEG, jnp.float32),
+        jnp.zeros((tok_rows, heads_here), jnp.float32),
+        jnp.zeros((tok_rows, heads_here, head_dim), jnp.float32),
+    )
+    size = lax.axis_size("ctx")
+    ring = size // 2
+    partner = lax.ppermute(packed, "ctx", [(i, (i + ring) % size) for i in range(size)])
+    pair = jnp.where(
+        position // ring == 0, jnp.stack([packed, partner]), jnp.stack([partner, packed])
+    )
+    ring_pos = position % ring
+    forward = [(y * ring + a, y * ring + (a + 1) % ring) for y in range(2) for a in range(ring)]
+    backward = [(y * ring + a, y * ring + (a - 1) % ring) for y in range(2) for a in range(ring)]
+    token_ids = jnp.arange(tok_rows, dtype=jnp.int32)
+
+    def fold(state_in, piece, source):
+        key_frame = (
+            jnp.concatenate(
+                [source * tok_rows + token_ids, (ring + source) * tok_rows + token_ids]
+            )
+            // frame_size
+        )
+        return attend_piece(
+            state_in,
+            piece.reshape((2 * tok_rows,) + piece.shape[2:]),
+            key_frame,
+            queries,
+            query_frame,
+            query_first,
+            head_dim,
+        )
+
+    ahead = pair
+    behind = pair
+    lagging = state
+    state = fold(state, pair, ring_pos)
+    for step in range(1, ring // 2 + 1):
+        if step > 1:
+            ahead, behind, lagging = lax.optimization_barrier((ahead, behind, lagging))
+            state = lagging if step == 2 else state
+        ahead = lax.ppermute(ahead, "ctx", forward)
+        has_behind = step < ring - ring // 2
+        if has_behind:
+            behind = lax.ppermute(behind, "ctx", backward)
+        lagging = state
+        state = fold(state, ahead, (ring_pos - step) % ring)
+        if has_behind:
+            state = fold(state, behind, (ring_pos + step) % ring)
     run_max, run_sum, accumulated = state_now
     key_part = kv_piece[:, :, :head_dim]
     value_part = kv_piece[:, :, head_dim:]

time: 249 us -> 249 us (level)
  no operation moved by 1% of the time
where the time goes in v5:
time: 249 us; the launch traced here: 245 us
  starting transfers between devices  151 us (61%)
  waiting for transfers between devices  51.5 us (21%)
  matrix products  18.2 us (7%)
  other arithmetic  11.8 us (5%)
  local copies, waits for them, and re-layouts  10.3 us (4%)
    ppermute x14, starting transfers between devices, ring_pieces(): behind = lax.ppermute(behind, axis, backward)  67.8 us
    ppermute x8, starting transfers between devices, halving_scatter(): lax.ppermute(send.astype(jnp.bfloat16), axis, [(i, i ^ 1 << bit) for i in...  39.6 us
    ppermute x16, waiting for transfers between devices, ring_pieces(): ahead = lax.ppermute(ahead, axis, forward)  38.6 us
    ppermute x16, starting transfers between devices, ring_pieces(): ahead = lax.ppermute(ahead, axis, forward)  32.4 us
    dot_general x9, matrix products, attend_piece(): jnp.einsum('nhe,mhe->nhm', queries, key_part, preferred_element_type=jnp....  8.1 us
    dot_general x9, matrix products, attend_piece(): jnp.einsum('nhm,mhe->nhe', exponent.astype(jnp.bfloat16), value_part, pre...  7.72 us
    ppermute x2, starting transfers between devices, ring_pieces(): lax.ppermute(block, axis, [(i, (i + ring) % size) for i in range(size)])  7.57 us
    ppermute x8, waiting for transfers between devices, halving_scatter(): lax.ppermute(send.astype(jnp.bfloat16), axis, [(i, i ^ 1 << bit) for i in...  7.39 us
  transfers between devices with their start and end apart: 41, of which 20 were waited for; matrix products, arithmetic and copies ran while one was open for 10% of the time, Pallas kernels for 0%

profile of v5, /device:TPU:1, one launch (start us, length us, event | category | flops | bytes accessed | tf_op | source)
XLA Modules:
  0.0 245.0 jit_solution(15281979723698282611)
XLA Ops:
  2.4 5.7 %collective-permute-start = (bf16[104,512]{1,0:T(8,128)(2,1)S(1)}, bf16[104,512]{1,0:T(8,128)(2,1)S(1)}, u32[]{:S(2)}, u32[]{:S(2)}) collective-permute-start(bf16[104,512]{1,0:T(8,128)(2,1)S(1)} %get-tuple-element.54), channel_id=1, source_target_pairs={{0,256},{16,272},{32,288},{48,304},{64,320},{80,336},{96,352},{112... | collective-permute-start | bytes 319496 | tf_op jit(solution)/shard_map/ppermute | solution.py:34
  9.2 3.6 %collective-permute-start.40 = (bf16[320,192]{1,0:T(8,128)(2,1)S(1)}, bf16[320,192]{1,0:T(8,128)(2,1)S(1)}, u32[]{:S(2)}, u32[]{:S(2)}) collective-permute-start(bf16[320,192]{1,0:T(8,128)(2,1)S(1)} %constant_dynamic-slice_fusion), channel_id=1, source_target_pairs={{0,16},{16,32},{32,48},{48,64},{64,80},{80,96},{96,112},{112,128},... | collective-permute-start | bytes 368648 | tf_op jit(solution)/shard_map/ppermute | solution.py:19
  16.8 3.5 %collective-permute-start.1 = (bf16[2,104,512]{2,1,0:T(8,128)(2,1)S(1)}, bf16[2,104,512]{2,1,0:T(8,128)(2,1)S(1)}, u32[]{:S(2)}, u32[]{:S(2)}) collective-permute-start(bf16[2,104,512]{2,1,0:T(8,128)(2,1)S(1)} %maximum_select_fusion.2), channel_id=1, source_target_pairs={{0,16},{16,32},{32,48},{48,64},{64,80},{80,96},{96,112},{112,128},... | collective-permute-start | bytes 638984 | tf_op jit(solution)/shard_map/ppermute | solution.py:45
  20.3 7.9 %collective-permute-start.2 = (bf16[2,104,512]{2,1,0:T(8,128)(2,1)S(1)}, bf16[2,104,512]{2,1,0:T(8,128)(2,1)S(1)}, u32[]{:S(2)}, u32[]{:S(2)}) collective-permute-start(bf16[2,104,512]{2,1,0:T(8,128)(2,1)S(1)} %maximum_select_fusion.2), channel_id=1, source_target_pairs={{0,240},{16,0},{32,16},{48,32},{64,48},{80,64},{96,80},{112,96},{1... | collective-permute-start | bytes 638984 | tf_op jit(solution)/shard_map/ppermute | solution.py:48
  28.5 2.4 collective-permute-done.1
  32.9 4.6 %collective-permute-start.4 = (bf16[2,104,512]{2,1,0:T(8,128)(2,1)S(1)}, bf16[2,104,512]{2,1,0:T(8,128)(2,1)S(1)}, u32[]{:S(2)}, u32[]{:S(2)}) collective-permute-start(bf16[2,104,512]{2,1,0:T(8,128)(2,1)S(1)} %collective-permute-done.2), channel_id=1, source_target_pairs={{0,240},{16,0},{32,16},{48,32},{64,48},{80,64},{96,80},{112,96},{1... | collective-permute-start | bytes 638984 | tf_op jit(solution)/shard_map/ppermute | solution.py:48
  41.2 4.6 %collective-permute-start.6 = (bf16[2,104,512]{2,1,0:T(8,128)(2,1)S(1)}, bf16[2,104,512]{2,1,0:T(8,128)(2,1)S(1)}, u32[]{:S(2)}, u32[]{:S(2)}) collective-permute-start(bf16[2,104,512]{2,1,0:T(8,128)(2,1)S(1)} %collective-permute-done.4), channel_id=1, source_target_pairs={{0,240},{16,0},{32,16},{48,32},{64,48},{80,64},{96,80},{112,96},{1... | collective-permute-start | bytes 638984 | tf_op jit(solution)/shard_map/ppermute | solution.py:48
  48.9 4.6 %collective-permute-start.8 = (bf16[2,104,512]{2,1,0:T(8,128)(2,1)S(1)}, bf16[2,104,512]{2,1,0:T(8,128)(2,1)S(1)}, u32[]{:S(2)}, u32[]{:S(2)}) collective-permute-start(bf16[2,104,512]{2,1,0:T(8,128)(2,1)S(1)} %collective-permute-done.6), channel_id=1, source_target_pairs={{0,240},{16,0},{32,16},{48,32},{64,48},{80,64},{96,80},{112,96},{1... | collective-permute-start | bytes 638984 | tf_op jit(solution)/shard_map/ppermute | solution.py:48
  56.7 4.6 %collective-permute-start.10 = (bf16[2,104,512]{2,1,0:T(8,128)(2,1)S(1)}, bf16[2,104,512]{2,1,0:T(8,128)(2,1)S(1)}, u32[]{:S(2)}, u32[]{:S(2)}) collective-permute-start(bf16[2,104,512]{2,1,0:T(8,128)(2,1)S(1)} %collective-permute-done.8), channel_id=1, source_target_pairs={{0,240},{16,0},{32,16},{48,32},{64,48},{80,64},{96,80},{112,96},{1... | collective-permute-start | bytes 638984 | tf_op jit(solution)/shard_map/ppermute | solution.py:48
  64.5 4.6 %collective-permute-start.12 = (bf16[2,104,512]{2,1,0:T(8,128)(2,1)S(1)}, bf16[2,104,512]{2,1,0:T(8,128)(2,1)S(1)}, u32[]{:S(2)}, u32[]{:S(2)}) collective-permute-start(bf16[2,104,512]{2,1,0:T(8,128)(2,1)S(1)} %collective-permute-done.10), channel_id=1, source_target_pairs={{0,240},{16,0},{32,16},{48,32},{64,48},{80,64},{96,80},{112,96},{1... | collective-permute-start | bytes 638984 | tf_op jit(solution)/shard_map/ppermute | solution.py:48
  72.3 4.6 %collective-permute-start.14 = (bf16[2,104,512]{2,1,0:T(8,128)(2,1)S(1)}, bf16[2,104,512]{2,1,0:T(8,128)(2,1)S(1)}, u32[]{:S(2)}, u32[]{:S(2)}) collective-permute-start(bf16[2,104,512]{2,1,0:T(8,128)(2,1)S(1)} %collective-permute-done.12), channel_id=1, source_target_pairs={{0,240},{16,0},{32,16},{48,32},{64,48},{80,64},{96,80},{112,96},{1... | collective-permute-start | bytes 638984 | tf_op jit(solution)/shard_map/ppermute | solution.py:48
  81.0 7.8 %collective-permute-done.15 = bf16[2,104,512]{2,1,0:T(8,128)(2,1)S(1)} collective-permute-done((bf16[2,104,512]{2,1,0:T(8,128)(2,1)S(1)}, bf16[2,104,512]{2,1,0:T(8,128)(2,1)S(1)}, u32[]{:S(2)}, u32[]{:S(2)}) %collective-permute-start.15) | collective-permute-done | bytes 213024 | tf_op jit(solution)/shard_map/ppermute | solution.py:45
  98.8 5.5 %collective-permute-done.16 = bf16[320,1,256]{2,0,1:T(8,128)(2,1)S(1)} collective-permute-done((bf16[320,1,256]{2,0,1:T(8,128)(2,1)S(1)}, bf16[320,1,256]{2,0,1:T(8,128)(2,1)S(1)}, u32[]{:S(2)}, u32[]{:S(2)}) %collective-permute-start.16) | collective-permute-done | bytes 163872 | tf_op jit(solution)/shard_map/ppermute | solution.py:34
  106.3 4.6 %collective-permute-start.18 = (bf16[2,320,1,256]{3,1,2,0:T(8,128)(2,1)S(1)}, bf16[2,320,1,256]{3,1,2,0:T(8,128)(2,1)}, u32[]{:S(2)}, u32[]{:S(2)}) collective-permute-start(bf16[2,320,1,256]{3,1,2,0:T(8,128)(2,1)S(1)} %maximum_select_fusion), channel_id=1, source_target_pairs={{0,240},{16,0},{32,16},{48,32},{64,48},{80,64},{96,80},{112,96},{1... | collective-permute-start | bytes 983048 | tf_op jit(solution)/shard_map/ppermute | solution.py:48
  110.9 2.7 %collective-permute-done.17 = bf16[2,320,1,256]{3,1,2,0:T(8,128)(2,1)S(1)} collective-permute-done((bf16[2,320,1,256]{3,1,2,0:T(8,128)(2,1)S(1)}, bf16[2,320,1,256]{3,1,2,0:T(8,128)(2,1)S(1)}, u32[]{:S(2)}, u32[]{:S(2)}) %collective-permute-start.17) | collective-permute-done | bytes 327712 | tf_op jit(solution)/shard_map/ppermute | solution.py:45
  115.6 4.6 %collective-permute-start.20 = (bf16[2,320,1,256]{3,1,2,0:T(8,128)(2,1)}, bf16[2,320,1,256]{3,1,2,0:T(8,128)(2,1)}, u32[]{:S(2)}, u32[]{:S(2)}) collective-permute-start(bf16[2,320,1,256]{3,1,2,0:T(8,128)(2,1)} %collective-permute-done.18), channel_id=1, source_target_pairs={{0,240},{16,0},{32,16},{48,32},{64,48},{80,64},{96,80},{112,96},{1... | collective-permute-start | bytes 983048 | tf_op jit(solution)/shard_map/ppermute | solution.py:48
  120.2 4.6 %collective-permute-done.19 = bf16[2,320,1,256]{3,1,2,0:T(8,128)(2,1)} collective-permute-done((bf16[2,320,1,256]{3,1,2,0:T(8,128)(2,1)S(1)}, bf16[2,320,1,256]{3,1,2,0:T(8,128)(2,1)}, u32[]{:S(2)}, u32[]{:S(2)}) %collective-permute-start.19) | collective-permute-done | bytes 327712 | tf_op jit(solution)/shard_map/ppermute | solution.py:45
  127.1 4.6 %collective-permute-start.22 = (bf16[2,320,1,256]{3,1,2,0:T(8,128)(2,1)}, bf16[2,320,1,256]{3,1,2,0:T(8,128)(2,1)S(1)}, u32[]{:S(2)}, u32[]{:S(2)}) collective-permute-start(bf16[2,320,1,256]{3,1,2,0:T(8,128)(2,1)} %collective-permute-done.20), channel_id=1, source_target_pairs={{0,240},{16,0},{32,16},{48,32},{64,48},{80,64},{96,80},{112,96},{1... | collective-permute-start | bytes 983048 | tf_op jit(solution)/shard_map/ppermute | solution.py:48
  131.8 3.8 %collective-permute-done.21 = bf16[2,320,1,256]{3,1,2,0:T(8,128)(2,1)} collective-permute-done((bf16[2,320,1,256]{3,1,2,0:T(8,128)(2,1)}, bf16[2,320,1,256]{3,1,2,0:T(8,128)(2,1)}, u32[]{:S(2)}, u32[]{:S(2)}) %collective-permute-start.21) | collective-permute-done | bytes 327712 | tf_op jit(solution)/shard_map/ppermute | solution.py:45
  137.6 4.7 %collective-permute-start.24 = (bf16[2,320,1,256]{3,1,2,0:T(8,128)(2,1)S(1)}, bf16[2,320,1,256]{3,1,2,0:T(8,128)(2,1)S(1)}, u32[]{:S(2)}, u32[]{:S(2)}) collective-permute-start(bf16[2,320,1,256]{3,1,2,0:T(8,128)(2,1)S(1)} %collective-permute-done.22), channel_id=1, source_target_pairs={{0,240},{16,0},{32,16},{48,32},{64,48},{80,64},{96,80},{112,96},{1... | collective-permute-start | bytes 983048 | tf_op jit(solution)/shard_map/ppermute | solution.py:48
  147.8 4.6 %collective-permute-start.26 = (bf16[2,320,1,256]{3,1,2,0:T(8,128)(2,1)S(1)}, bf16[2,320,1,256]{3,1,2,0:T(8,128)(2,1)S(1)}, u32[]{:S(2)}, u32[]{:S(2)}) collective-permute-start(bf16[2,320,1,256]{3,1,2,0:T(8,128)(2,1)S(1)} %collective-permute-done.24), channel_id=1, source_target_pairs={{0,240},{16,0},{32,16},{48,32},{64,48},{80,64},{96,80},{112,96},{1... | collective-permute-start | bytes 983048 | tf_op jit(solution)/shard_map/ppermute | solution.py:48
  158.1 4.6 %collective-permute-start.28 = (bf16[2,320,1,256]{3,1,2,0:T(8,128)(2,1)S(1)}, bf16[2,320,1,256]{3,1,2,0:T(8,128)(2,1)S(1)}, u32[]{:S(2)}, u32[]{:S(2)}) collective-permute-start(bf16[2,320,1,256]{3,1,2,0:T(8,128)(2,1)S(1)} %collective-permute-done.26), channel_id=1, source_target_pairs={{0,240},{16,0},{32,16},{48,32},{64,48},{80,64},{96,80},{112,96},{1... | collective-permute-start | bytes 983048 | tf_op jit(solution)/shard_map/ppermute | solution.py:48
  166.8 4.9 %collective-permute-start.30 = (bf16[2,320,1,256]{3,1,2,0:T(8,128)(2,1)S(1)}, bf16[2,320,1,256]{3,1,2,0:T(8,128)(2,1)S(1)}, u32[]{:S(2)}, u32[]{:S(2)}) collective-permute-start(bf16[2,320,1,256]{3,1,2,0:T(8,128)(2,1)S(1)} %collective-permute-done.28), channel_id=1, source_target_pairs={{0,240},{16,0},{32,16},{48,32},{64,48},{80,64},{96,80},{112,96},{1... | collective-permute-start | bytes 983048 | tf_op jit(solution)/shard_map/ppermute | solution.py:48
  176.5 6.1 %collective-permute-done.31 = bf16[2,320,1,256]{3,1,2,0:T(8,128)(2,1)S(1)} collective-permute-done((bf16[2,320,1,256]{3,1,2,0:T(8,128)(2,1)S(1)}, bf16[2,320,1,256]{3,1,2,0:T(8,128)(2,1)S(1)}, u32[]{:S(2)}, u32[]{:S(2)}) %collective-permute-start.31) | collective-permute-done | bytes 327712 | tf_op jit(solution)/shard_map/ppermute | solution.py:45
  184.8 2.4 fusion.57
  195.5 19.7 %collective-permute-start.36 = (bf16[160,1536]{1,0:T(8,128)(2,1)S(1)}, bf16[160,1536]{1,0:T(8,128)(2,1)S(1)}, u32[]{:S(2)}, u32[]{:S(2)}) collective-permute-start(bf16[160,1536]{1,0:T(8,128)(2,1)S(1)} %dynamic-slice_convert_fusion), channel_id=1, source_target_pairs={{0,1},{1,0},{2,3},{3,2},{4,5},{5,4},{6,7},{7,6},{8,9},{9,8},{10,11... | collective-permute-start | bytes 1474568 | tf_op jit(solution)/shard_map/ppermute | solution.py:71
  217.8 3.1 %collective-permute-start.37 = (bf16[160,768]{1,0:T(8,128)(2,1)S(1)}, bf16[160,768]{1,0:T(8,128)(2,1)S(1)}, u32[]{:S(2)}, u32[]{:S(2)}) collective-permute-start(bf16[160,768]{1,0:T(8,128)(2,1)S(1)} %dynamic-slice_convert_fusion.2), channel_id=1, source_target_pairs={{0,2},{1,3},{2,0},{3,1},{4,6},{5,7},{6,4},{7,5},{8,10},{9,11},{10,... | collective-permute-start | bytes 737288 | tf_op jit(solution)/shard_map/ppermute | solution.py:71
  223.1 3.6 %collective-permute-done.37 = bf16[160,768]{1,0:T(8,128)(2,1)S(1)} collective-permute-done((bf16[160,768]{1,0:T(8,128)(2,1)S(1)}, bf16[160,768]{1,0:T(8,128)(2,1)S(1)}, u32[]{:S(2)}, u32[]{:S(2)}) %collective-permute-start.37) | collective-permute-done | bytes 245792 | tf_op jit(solution)/shard_map/ppermute | solution.py:71
  226.8 4.7 %collective-permute-start.38 = (bf16[160,384]{1,0:T(8,128)(2,1)S(1)}, bf16[160,384]{1,0:T(8,128)(2,1)S(1)}, u32[]{:S(2)}, u32[]{:S(2)}) collective-permute-start(bf16[160,384]{1,0:T(8,128)(2,1)S(1)} %dynamic-slice_convert_fusion.4), channel_id=1, source_target_pairs={{0,4},{1,5},{2,6},{3,7},{4,0},{5,1},{6,2},{7,3},{8,12},{9,13},{10,... | collective-permute-start | bytes 368648 | tf_op jit(solution)/shard_map/ppermute | solution.py:71
  231.6 2.2 collective-permute-start.34
  237.3 4.0 %collective-permute-start.35 = (bf16[160,192]{1,0:T(8,128)(2,1)S(1)}, bf16[160,192]{1,0:T(8,128)(2,1)S(1)}, u32[]{:S(2)}, u32[]{:S(2)}) collective-permute-start(bf16[160,192]{1,0:T(8,128)(2,1)S(1)} %dynamic-slice_convert_fusion.7), channel_id=1, source_target_pairs={{0,4},{1,5},{2,6},{3,7},{4,0},{5,1},{6,2},{7,3},{8,12},{9,13},{10,... | collective-permute-start | bytes 184328 | tf_op jit(solution)/shard_map/ppermute | solution.py:71
  241.5 2.5 %collective-permute-done.35 = bf16[160,192]{1,0:T(8,128)(2,1)S(1)} collective-permute-done((bf16[160,192]{1,0:T(8,128)(2,1)S(1)}, bf16[160,192]{1,0:T(8,128)(2,1)S(1)}, u32[]{:S(2)}, u32[]{:S(2)}) %collective-permute-start.35) | collective-permute-done | bytes 61472 | tf_op jit(solution)/shard_map/ppermute | solution.py:71
  (203 shorter events, 86.9 us)
Async XLA Ops:
  2.4 14.3 %collective-permute-start = (bf16[104,512]{1,0:T(8,128)(2,1)S(1)}, bf16[104,512]{1,0:T(8,128)(2,1)S(1)}, u32[]{:S(2)}, u32[]{:S(2)}) collective-permute-start(bf16[104,512]{1,0:T(8,128)(2,1)S(1)} %get-tuple-element.54), channel_id=1, source_target_pairs={{0,256},{16,272},{32,288},{48,304},{64,320},{80,336},{96,352},{112... | collective-permute-start | bytes 319496 | tf_op jit(solution)/shard_map/ppermute | solution.py:34
  9.2 122.5 %collective-permute-start.40 = (bf16[320,192]{1,0:T(8,128)(2,1)S(1)}, bf16[320,192]{1,0:T(8,128)(2,1)S(1)}, u32[]{:S(2)}, u32[]{:S(2)}) collective-permute-start(bf16[320,192]{1,0:T(8,128)(2,1)S(1)} %constant_dynamic-slice_fusion), channel_id=1, source_target_pairs={{0,16},{16,32},{32,48},{48,64},{64,80},{80,96},{96,112},{112,128},... | collective-permute-start | bytes 368648 | tf_op jit(solution)/shard_map/ppermute | solution.py:19
  16.8 14.1 %collective-permute-start.1 = (bf16[2,104,512]{2,1,0:T(8,128)(2,1)S(1)}, bf16[2,104,512]{2,1,0:T(8,128)(2,1)S(1)}, u32[]{:S(2)}, u32[]{:S(2)}) collective-permute-start(bf16[2,104,512]{2,1,0:T(8,128)(2,1)S(1)} %maximum_select_fusion.2), channel_id=1, source_target_pairs={{0,16},{16,32},{32,48},{48,64},{64,80},{80,96},{96,112},{112,128},... | collective-permute-start | bytes 638984 | tf_op jit(solution)/shard_map/ppermute | solution.py:45
  20.3 12.5 %collective-permute-start.2 = (bf16[2,104,512]{2,1,0:T(8,128)(2,1)S(1)}, bf16[2,104,512]{2,1,0:T(8,128)(2,1)S(1)}, u32[]{:S(2)}, u32[]{:S(2)}) collective-permute-start(bf16[2,104,512]{2,1,0:T(8,128)(2,1)S(1)} %maximum_select_fusion.2), channel_id=1, source_target_pairs={{0,240},{16,0},{32,16},{48,32},{64,48},{80,64},{96,80},{112,96},{1... | collective-permute-start | bytes 638984 | tf_op jit(solution)/shard_map/ppermute | solution.py:48
  30.9 8.3 %collective-permute-start.3 = (bf16[2,104,512]{2,1,0:T(8,128)(2,1)S(1)}, bf16[2,104,512]{2,1,0:T(8,128)(2,1)S(1)}, u32[]{:S(2)}, u32[]{:S(2)}) collective-permute-start(bf16[2,104,512]{2,1,0:T(8,128)(2,1)S(1)} %collective-permute-done.1), channel_id=1, source_target_pairs={{0,16},{16,32},{32,48},{48,64},{64,80},{80,96},{96,112},{112,128},... | collective-permute-start | bytes 638984 | tf_op jit(solution)/shard_map/ppermute | solution.py:45
  32.9 8.3 %collective-permute-start.4 = (bf16[2,104,512]{2,1,0:T(8,128)(2,1)S(1)}, bf16[2,104,512]{2,1,0:T(8,128)(2,1)S(1)}, u32[]{:S(2)}, u32[]{:S(2)}) collective-permute-start(bf16[2,104,512]{2,1,0:T(8,128)(2,1)S(1)} %collective-permute-done.2), channel_id=1, source_target_pairs={{0,240},{16,0},{32,16},{48,32},{64,48},{80,64},{96,80},{112,96},{1... | collective-permute-start | bytes 638984 | tf_op jit(solution)/shard_map/ppermute | solution.py:48
  39.2 7.8 %collective-permute-start.5 = (bf16[2,104,512]{2,1,0:T(8,128)(2,1)S(1)}, bf16[2,104,512]{2,1,0:T(8,128)(2,1)S(1)}, u32[]{:S(2)}, u32[]{:S(2)}) collective-permute-start(bf16[2,104,512]{2,1,0:T(8,128)(2,1)S(1)} %collective-permute-done.3), channel_id=1, source_target_pairs={{0,16},{16,32},{32,48},{48,64},{64,80},{80,96},{96,112},{112,128},... | collective-permute-start | bytes 638984 | tf_op jit(solution)/shard_map/ppermute | solution.py:45
  41.2 7.8 %collective-permute-start.6 = (bf16[2,104,512]{2,1,0:T(8,128)(2,1)S(1)}, bf16[2,104,512]{2,1,0:T(8,128)(2,1)S(1)}, u32[]{:S(2)}, u32[]{:S(2)}) collective-permute-start(bf16[2,104,512]{2,1,0:T(8,128)(2,1)S(1)} %collective-permute-done.4), channel_id=1, source_target_pairs={{0,240},{16,0},{32,16},{48,32},{64,48},{80,64},{96,80},{112,96},{1... | collective-permute-start | bytes 638984 | tf_op jit(solution)/shard_map/ppermute | solution.py:48
  47.0 7.8 %collective-permute-start.7 = (bf16[2,104,512]{2,1,0:T(8,128)(2,1)S(1)}, bf16[2,104,512]{2,1,0:T(8,128)(2,1)S(1)}, u32[]{:S(2)}, u32[]{:S(2)}) collective-permute-start(bf16[2,104,512]{2,1,0:T(8,128)(2,1)S(1)} %collective-permute-done.5), channel_id=1, source_target_pairs={{0,16},{16,32},{32,48},{48,64},{64,80},{80,96},{96,112},{112,128},... | collective-permute-start | bytes 638984 | tf_op jit(solution)/shard_map/ppermute | solution.py:45
  54.8 7.8 %collective-permute-start.9 = (bf16[2,104,512]{2,1,0:T(8,128)(2,1)S(1)}, bf16[2,104,512]{2,1,0:T(8,128)(2,1)S(1)}, u32[]{:S(2)}, u32[]{:S(2)}) collective-permute-start(bf16[2,104,512]{2,1,0:T(8,128)(2,1)S(1)} %collective-permute-done.7), channel_id=1, source_target_pairs={{0,16},{16,32},{32,48},{48,64},{64,80},{80,96},{96,112},{112,128},... | collective-permute-start | bytes 638984 | tf_op jit(solution)/shard_map/ppermute | solution.py:45
  62.6 7.8 %collective-permute-start.11 = (bf16[2,104,512]{2,1,0:T(8,128)(2,1)S(1)}, bf16[2,104,512]{2,1,0:T(8,128)(2,1)S(1)}, u32[]{:S(2)}, u32[]{:S(2)}) collective-permute-start(bf16[2,104,512]{2,1,0:T(8,128)(2,1)S(1)} %collective-permute-done.9), channel_id=1, source_target_pairs={{0,16},{16,32},{32,48},{48,64},{64,80},{80,96},{96,112},{112,128},... | collective-permute-start | bytes 638984 | tf_op jit(solution)/shard_map/ppermute | solution.py:45
  70.4 8.7 %collective-permute-start.13 = (bf16[2,104,512]{2,1,0:T(8,128)(2,1)S(1)}, bf16[2,104,512]{2,1,0:T(8,128)(2,1)S(1)}, u32[]{:S(2)}, u32[]{:S(2)}) collective-permute-start(bf16[2,104,512]{2,1,0:T(8,128)(2,1)S(1)} %collective-permute-done.11), channel_id=1, source_target_pairs={{0,16},{16,32},{32,48},{48,64},{64,80},{80,96},{96,112},{112,128},... | collective-permute-start | bytes 638984 | tf_op jit(solution)/shard_map/ppermute | solution.py:45
  72.3 8.7 %collective-permute-start.14 = (bf16[2,104,512]{2,1,0:T(8,128)(2,1)S(1)}, bf16[2,104,512]{2,1,0:T(8,128)(2,1)S(1)}, u32[]{:S(2)}, u32[]{:S(2)}) collective-permute-start(bf16[2,104,512]{2,1,0:T(8,128)(2,1)S(1)} %collective-permute-done.12), channel_id=1, source_target_pairs={{0,240},{16,0},{32,16},{48,32},{64,48},{80,64},{96,80},{112,96},{1... | collective-permute-start | bytes 638984 | tf_op jit(solution)/shard_map/ppermute | solution.py:48
  79.0 9.8 %collective-permute-start.15 = (bf16[2,104,512]{2,1,0:T(8,128)(2,1)S(1)}, bf16[2,104,512]{2,1,0:T(8,128)(2,1)S(1)}, u32[]{:S(2)}, u32[]{:S(2)}) collective-permute-start(bf16[2,104,512]{2,1,0:T(8,128)(2,1)S(1)} %collective-permute-done.13), channel_id=1, source_target_pairs={{0,16},{16,32},{32,48},{48,64},{64,80},{80,96},{96,112},{112,128},... | collective-permute-start | bytes 638984 | tf_op jit(solution)/shard_map/ppermute | solution.py:45
  104.3 9.3 %collective-permute-start.17 = (bf16[2,320,1,256]{3,1,2,0:T(8,128)(2,1)S(1)}, bf16[2,320,1,256]{3,1,2,0:T(8,128)(2,1)S(1)}, u32[]{:S(2)}, u32[]{:S(2)}) collective-permute-start(bf16[2,320,1,256]{3,1,2,0:T(8,128)(2,1)S(1)} %maximum_select_fusion), channel_id=1, source_target_pairs={{0,16},{16,32},{32,48},{48,64},{64,80},{80,96},{96,112},{112,128},... | collective-permute-start | bytes 983048 | tf_op jit(solution)/shard_map/ppermute | solution.py:45
  106.3 9.3 %collective-permute-start.18 = (bf16[2,320,1,256]{3,1,2,0:T(8,128)(2,1)S(1)}, bf16[2,320,1,256]{3,1,2,0:T(8,128)(2,1)}, u32[]{:S(2)}, u32[]{:S(2)}) collective-permute-start(bf16[2,320,1,256]{3,1,2,0:T(8,128)(2,1)S(1)} %maximum_select_fusion), channel_id=1, source_target_pairs={{0,240},{16,0},{32,16},{48,32},{64,48},{80,64},{96,80},{112,96},{1... | collective-permute-start | bytes 983048 | tf_op jit(solution)/shard_map/ppermute | solution.py:48
  113.7 11.2 %collective-permute-start.19 = (bf16[2,320,1,256]{3,1,2,0:T(8,128)(2,1)S(1)}, bf16[2,320,1,256]{3,1,2,0:T(8,128)(2,1)}, u32[]{:S(2)}, u32[]{:S(2)}) collective-permute-start(bf16[2,320,1,256]{3,1,2,0:T(8,128)(2,1)S(1)} %collective-permute-done.17), channel_id=1, source_target_pairs={{0,16},{16,32},{32,48},{48,64},{64,80},{80,96},{96,112},{112,128},... | collective-permute-start | bytes 983048 | tf_op jit(solution)/shard_map/ppermute | solution.py:45
  115.6 11.5 %collective-permute-start.20 = (bf16[2,320,1,256]{3,1,2,0:T(8,128)(2,1)}, bf16[2,320,1,256]{3,1,2,0:T(8,128)(2,1)}, u32[]{:S(2)}, u32[]{:S(2)}) collective-permute-start(bf16[2,320,1,256]{3,1,2,0:T(8,128)(2,1)} %collective-permute-done.18), channel_id=1, source_target_pairs={{0,240},{16,0},{32,16},{48,32},{64,48},{80,64},{96,80},{112,96},{1... | collective-permute-start | bytes 983048 | tf_op jit(solution)/shard_map/ppermute | solution.py:48
  124.8 10.8 %collective-permute-start.21 = (bf16[2,320,1,256]{3,1,2,0:T(8,128)(2,1)}, bf16[2,320,1,256]{3,1,2,0:T(8,128)(2,1)}, u32[]{:S(2)}, u32[]{:S(2)}) collective-permute-start(bf16[2,320,1,256]{3,1,2,0:T(8,128)(2,1)} %collective-permute-done.19), channel_id=1, source_target_pairs={{0,16},{16,32},{32,48},{48,64},{64,80},{80,96},{96,112},{112,128},... | collective-permute-start | bytes 983048 | tf_op jit(solution)/shard_map/ppermute | solution.py:45
  127.1 10.5 %collective-permute-start.22 = (bf16[2,320,1,256]{3,1,2,0:T(8,128)(2,1)}, bf16[2,320,1,256]{3,1,2,0:T(8,128)(2,1)S(1)}, u32[]{:S(2)}, u32[]{:S(2)}) collective-permute-start(bf16[2,320,1,256]{3,1,2,0:T(8,128)(2,1)} %collective-permute-done.20), channel_id=1, source_target_pairs={{0,240},{16,0},{32,16},{48,32},{64,48},{80,64},{96,80},{112,96},{1... | collective-permute-start | bytes 983048 | tf_op jit(solution)/shard_map/ppermute | solution.py:48
  135.6 9.8 %collective-permute-start.23 = (bf16[2,320,1,256]{3,1,2,0:T(8,128)(2,1)}, bf16[2,320,1,256]{3,1,2,0:T(8,128)(2,1)S(1)}, u32[]{:S(2)}, u32[]{:S(2)}) collective-permute-start(bf16[2,320,1,256]{3,1,2,0:T(8,128)(2,1)} %collective-permute-done.21), channel_id=1, source_target_pairs={{0,16},{16,32},{32,48},{48,64},{64,80},{80,96},{96,112},{112,128},... | collective-permute-start | bytes 983048 | tf_op jit(solution)/shard_map/ppermute | solution.py:45
  137.6 10.2 %collective-permute-start.24 = (bf16[2,320,1,256]{3,1,2,0:T(8,128)(2,1)S(1)}, bf16[2,320,1,256]{3,1,2,0:T(8,128)(2,1)S(1)}, u32[]{:S(2)}, u32[]{:S(2)}) collective-permute-start(bf16[2,320,1,256]{3,1,2,0:T(8,128)(2,1)S(1)} %collective-permute-done.22), channel_id=1, source_target_pairs={{0,240},{16,0},{32,16},{48,32},{64,48},{80,64},{96,80},{112,96},{1... | collective-permute-start | bytes 983048 | tf_op jit(solution)/shard_map/ppermute | solution.py:48
  145.4 9.0 %collective-permute-start.25 = (bf16[2,320,1,256]{3,1,2,0:T(8,128)(2,1)S(1)}, bf16[2,320,1,256]{3,1,2,0:T(8,128)(2,1)S(1)}, u32[]{:S(2)}, u32[]{:S(2)}) collective-permute-start(bf16[2,320,1,256]{3,1,2,0:T(8,128)(2,1)S(1)} %collective-permute-done.23), channel_id=1, source_target_pairs={{0,16},{16,32},{32,48},{48,64},{64,80},{80,96},{96,112},{112,128},... | collective-permute-start | bytes 983048 | tf_op jit(solution)/shard_map/ppermute | solution.py:45
  147.8 10.4 %collective-permute-start.26 = (bf16[2,320,1,256]{3,1,2,0:T(8,128)(2,1)S(1)}, bf16[2,320,1,256]{3,1,2,0:T(8,128)(2,1)S(1)}, u32[]{:S(2)}, u32[]{:S(2)}) collective-permute-start(bf16[2,320,1,256]{3,1,2,0:T(8,128)(2,1)S(1)} %collective-permute-done.24), channel_id=1, source_target_pairs={{0,240},{16,0},{32,16},{48,32},{64,48},{80,64},{96,80},{112,96},{1... | collective-permute-start | bytes 983048 | tf_op jit(solution)/shard_map/ppermute | solution.py:48
  154.4 9.9 %collective-permute-start.27 = (bf16[2,320,1,256]{3,1,2,0:T(8,128)(2,1)S(1)}, bf16[2,320,1,256]{3,1,2,0:T(8,128)(2,1)S(1)}, u32[]{:S(2)}, u32[]{:S(2)}) collective-permute-start(bf16[2,320,1,256]{3,1,2,0:T(8,128)(2,1)S(1)} %collective-permute-done.25), channel_id=1, source_target_pairs={{0,16},{16,32},{32,48},{48,64},{64,80},{80,96},{96,112},{112,128},... | collective-permute-start | bytes 983048 | tf_op jit(solution)/shard_map/ppermute | solution.py:45
  158.1 8.7 %collective-permute-start.28 = (bf16[2,320,1,256]{3,1,2,0:T(8,128)(2,1)S(1)}, bf16[2,320,1,256]{3,1,2,0:T(8,128)(2,1)S(1)}, u32[]{:S(2)}, u32[]{:S(2)}) collective-permute-start(bf16[2,320,1,256]{3,1,2,0:T(8,128)(2,1)S(1)} %collective-permute-done.26), channel_id=1, source_target_pairs={{0,240},{16,0},{32,16},{48,32},{64,48},{80,64},{96,80},{112,96},{1... | collective-permute-start | bytes 983048 | tf_op jit(solution)/shard_map/ppermute | solution.py:48
  164.3 9.0 %collective-permute-start.29 = (bf16[2,320,1,256]{3,1,2,0:T(8,128)(2,1)S(1)}, bf16[2,320,1,256]{3,1,2,0:T(8,128)(2,1)S(1)}, u32[]{:S(2)}, u32[]{:S(2)}) collective-permute-start(bf16[2,320,1,256]{3,1,2,0:T(8,128)(2,1)S(1)} %collective-permute-done.27), channel_id=1, source_target_pairs={{0,16},{16,32},{32,48},{48,64},{64,80},{80,96},{96,112},{112,128},... | collective-permute-start | bytes 983048 | tf_op jit(solution)/shard_map/ppermute | solution.py:45
  166.8 9.0 %collective-permute-start.30 = (bf16[2,320,1,256]{3,1,2,0:T(8,128)(2,1)S(1)}, bf16[2,320,1,256]{3,1,2,0:T(8,128)(2,1)S(1)}, u32[]{:S(2)}, u32[]{:S(2)}) collective-permute-start(bf16[2,320,1,256]{3,1,2,0:T(8,128)(2,1)S(1)} %collective-permute-done.28), channel_id=1, source_target_pairs={{0,240},{16,0},{32,16},{48,32},{64,48},{80,64},{96,80},{112,96},{1... | collective-permute-start | bytes 983048 | tf_op jit(solution)/shard_map/ppermute | solution.py:48
  173.3 9.3 %collective-permute-start.31 = (bf16[2,320,1,256]{3,1,2,0:T(8,128)(2,1)S(1)}, bf16[2,320,1,256]{3,1,2,0:T(8,128)(2,1)S(1)}, u32[]{:S(2)}, u32[]{:S(2)}) collective-permute-start(bf16[2,320,1,256]{3,1,2,0:T(8,128)(2,1)S(1)} %collective-permute-done.29), channel_id=1, source_target_pairs={{0,16},{16,32},{32,48},{48,64},{64,80},{80,96},{96,112},{112,128},... | collective-permute-start | bytes 983048 | tf_op jit(solution)/shard_map/ppermute | solution.py:45
  195.5 22.1 %collective-permute-start.36 = (bf16[160,1536]{1,0:T(8,128)(2,1)S(1)}, bf16[160,1536]{1,0:T(8,128)(2,1)S(1)}, u32[]{:S(2)}, u32[]{:S(2)}) collective-permute-start(bf16[160,1536]{1,0:T(8,128)(2,1)S(1)} %dynamic-slice_convert_fusion), channel_id=1, source_target_pairs={{0,1},{1,0},{2,3},{3,2},{4,5},{5,4},{6,7},{7,6},{8,9},{9,8},{10,11... | collective-permute-start | bytes 1474568 | tf_op jit(solution)/shard_map/ppermute | solution.py:71
  217.8 8.9 %collective-permute-start.37 = (bf16[160,768]{1,0:T(8,128)(2,1)S(1)}, bf16[160,768]{1,0:T(8,128)(2,1)S(1)}, u32[]{:S(2)}, u32[]{:S(2)}) collective-permute-start(bf16[160,768]{1,0:T(8,128)(2,1)S(1)} %dynamic-slice_convert_fusion.2), channel_id=1, source_target_pairs={{0,2},{1,3},{2,0},{3,1},{4,6},{5,7},{6,4},{7,5},{8,10},{9,11},{10,... | collective-permute-start | bytes 737288 | tf_op jit(solution)/shard_map/ppermute | solution.py:71
  221.1 10.4 %collective-permute-start.33 = (bf16[160,768]{1,0:T(8,128)(2,1)S(1)}, bf16[160,768]{1,0:T(8,128)(2,1)S(1)}, u32[]{:S(2)}, u32[]{:S(2)}) collective-permute-start(bf16[160,768]{1,0:T(8,128)(2,1)S(1)} %dynamic-slice_convert_fusion.3), channel_id=1, source_target_pairs={{0,8},{1,9},{2,10},{3,11},{4,12},{5,13},{6,14},{7,15},{8,0},{9,1},... | collective-permute-start | bytes 737288 | tf_op jit(solution)/shard_map/ppermute | solution.py:71
  (19 other events, 137.8 us)

commit v6 on v2

--- a/solution.py
+++ b/solution.py
@@ -59,28 +59,20 @@
     return gathered.reshape((2 * ring * block.shape[0],) + block.shape[1:])
 
 
-def halving_scatter(partial, axis):
+def halving_scatter(partial, axis, order):
     size = lax.axis_size(axis)
-    bits = size.bit_length() - 1
     position = lax.axis_index(axis)
-    rows, cols = partial.shape
-    width = cols // size
-    state = partial.reshape((rows,) + (2,) * bits + (width,))
-    axis_bits = [bits - 1 - a for a in range(bits)]
-    order = [0] + ([bits - 1] if bits > 1 else []) + list(range(1, bits - 1))
+    state = partial
     for bit in order:
-        dim = 1 + axis_bits.index(bit)
+        half = state.shape[1] // 2
         mine = (position >> bit) & 1
-        low = lax.index_in_dim(state, 0, dim, keepdims=False)
-        high = lax.index_in_dim(state, 1, dim, keepdims=False)
-        keep = jnp.where(mine == 0, low, high)
-        send = jnp.where(mine == 0, high, low)
+        keep = lax.dynamic_slice_in_dim(state, mine * half, half, 1)
+        send = lax.dynamic_slice_in_dim(state, (1 - mine) * half, half, 1)
         got = lax.ppermute(
             send.astype(jnp.bfloat16), axis, [(i, i ^ (1 << bit)) for i in range(size)]
         )
         state = keep + got.astype(jnp.float32)
-        axis_bits.remove(bit)
-    return state.reshape(rows, width)
+    return state
 
 
 def attend_piece(state_now, kv_piece, key_frame, queries, query_frame, query_first, head_dim):
@@ -136,7 +128,7 @@
     shares_hi = local_shares.astype(jnp.bfloat16)
     shares_lo = (local_shares - shares_hi.astype(jnp.float32)).astype(jnp.bfloat16)
     share_count = 4 * rows_here
-    extra_rows = 16 * ((share_count + 16 * width - 1) // (16 * width))
+    extra_rows = 8 * ((share_count + 8 * width - 1) // (8 * width))
     share_block = jnp.zeros((extra_rows * width,), jnp.bfloat16)
     share_block = share_block.at[:share_count].set(
         jnp.concatenate([shares_hi, shares_lo], axis=1).reshape(share_count)
@@ -182,17 +174,26 @@
         jnp.zeros((tok_rows, heads_here), jnp.float32),
         jnp.zeros((tok_rows, heads_here, head_dim), jnp.float32),
     )
-    kv_pieces, ring = ring_pieces(packed, "ctx")
+    size = lax.axis_size("ctx")
+    ring = size // 2
+    partner = lax.ppermute(packed, "ctx", [(i, (i + ring) % size) for i in range(size)])
+    pair = jnp.where(
+        position // ring == 0, jnp.stack([packed, partner]), jnp.stack([partner, packed])
+    )
+    ring_pos = position % ring
+    forward = [(y * ring + a, y * ring + (a + 1) % ring) for y in range(2) for a in range(ring)]
+    backward = [(y * ring + a, y * ring + (a - 1) % ring) for y in range(2) for a in range(ring)]
     token_ids = jnp.arange(tok_rows, dtype=jnp.int32)
-    for piece, source in kv_pieces:
+
+    def fold(state_in, piece, source):
         key_frame = (
             jnp.concatenate(
                 [source * tok_rows + token_ids, (ring + source) * tok_rows + token_ids]
             )
             // frame_size
         )
-        state = attend_piece(
-            state,
+        return attend_piece(
+            state_in,
             piece.reshape((2 * tok_rows,) + piece.shape[2:]),
             key_frame,
             queries,
@@ -200,15 +201,44 @@
             query_first,
             head_dim,
         )
+
+    ahead = pair
+    behind = pair
+    waiting = [(pair, ring_pos)]
+    for step in range(1, ring // 2 + 1):
+        ahead, behind, state = lax.optimization_barrier((ahead, behind, state))
+        ahead = lax.ppermute(ahead, "ctx", forward)
+        arrived = [(ahead, (ring_pos - step) % ring)]
+        if step < ring - ring // 2:
+            behind = lax.ppermute(behind, "ctx", backward)
+            arrived.append((behind, (ring_pos + step) % ring))
+        for piece, source in waiting:
+            state = fold(state, piece, source)
+        waiting = arrived
+    for piece, source in waiting:
+        state = fold(state, piece, source)
     run_max, run_sum, accumulated = state
     attended = (accumulated / run_sum[..., None]).astype(jnp.bfloat16)
-    partial_out = jnp.einsum(
-        "nhe,rhe->nr",
-        attended,
-        o_piece,
-        preferred_element_type=jnp.float32,
-    )
-    head_total = halving_scatter(partial_out, "fsdp")
+    size = lax.axis_size("fsdp")
+    bits = size.bit_length() - 1
+    middle = list(range(1, bits - 1))
+    half_rows = tok_rows // 2
+    orders = [[0, bits - 1] + middle, [0] + middle + [bits - 1]]
+    head_parts = []
+    for part, order in enumerate(orders):
+        by_bit = o_piece.reshape((2,) * bits + (full_rows // size,) + o_piece.shape[1:])
+        permuted = jnp.transpose(
+            by_bit,
+            [bits - 1 - bit for bit in order] + list(range(bits, by_bit.ndim)),
+        )
+        partial_out = jnp.einsum(
+            "nhe,rhe->nr",
+            attended[part * half_rows : (part + 1) * half_rows],
+            permuted.reshape(o_piece.shape),
+            preferred_element_type=jnp.float32,
+        )
+        head_parts.append(halving_scatter(partial_out, "fsdp", order))
+    head_total = jnp.concatenate(head_parts, axis=0)
     own_chan = lax.dynamic_slice_in_dim(latents, column * chan_here, chan_here, 1)
     before = passed_along(own_chan, "ctx", 1)
     stacked = (

time: 275 us -> 261 us (0.949); the launches traced: 274 us -> 257 us
  other arithmetic: 29.1 us -> 14 us
  starting transfers between devices: 144 us -> 156 us
  waiting for transfers between devices: 68.9 us -> 59.1 us
    ppermute x0 -> x16, starting transfers between devices: none -> 53.8 us  [the longest x7 31.6 us: per_device(): behind = lax.ppermute(behind, 'ctx', backward)]
    ppermute x0 -> x16, waiting for transfers between devices: none -> 33.5 us  [the longest x8 17.4 us: per_device(): ahead = lax.ppermute(ahead, 'ctx', forward)]
    ppermute x14 -> x7, starting transfers between devices: 68.2 us -> 35.3 us  [ring_pieces(): behind = lax.ppermute(behind, axis, backward)]
    ppermute x16 -> x8, starting transfers between devices: 33.9 us -> 16.9 us  [ring_pieces(): ahead = lax.ppermute(ahead, axis, forward)]
    ppermute x4 -> x8, waiting for transfers between devices: 22 us -> 6.84 us  [halving_scatter(): lax.ppermute(send.astype(jnp.bfloat16), axis, [(i, i ^ 1 << bit) for i in...]
    ppermute x16 -> x8, waiting for transfers between devices: 33.7 us -> 18.7 us  [ring_pieces(): ahead = lax.ppermute(ahead, axis, forward)]
    ppermute x4 -> x8, starting transfers between devices: 30.5 us -> 41.2 us  [halving_scatter(): lax.ppermute(send.astype(jnp.bfloat16), axis, [(i, i ^ 1 << bit) for i in...]
    ppermute x14 -> x7, waiting for transfers between devices: 10.1 us -> 0.02 us  [ring_pieces(): behind = lax.ppermute(behind, axis, backward)]
  transfers between devices with their start and end apart: 37 -> 41, of which waited for: 19 -> 27; matrix products, arithmetic and copies ran while one was open for 10% -> 10% of each run, Pallas kernels for 0% -> 0%
where the time goes in v6:
time: 261 us; the launch traced here: 257 us
  starting transfers between devices  156 us (60%)
  waiting for transfers between devices  59.1 us (23%)
  matrix products  15.6 us (6%)
  other arithmetic  14 us (5%)
  local copies, waits for them, and re-layouts  9.32 us (4%)
    ppermute x8, starting transfers between devices, halving_scatter(): lax.ppermute(send.astype(jnp.bfloat16), axis, [(i, i ^ 1 << bit) for i in...  41.2 us
    ppermute x7, starting transfers between devices, ring_pieces(): behind = lax.ppermute(behind, axis, backward)  35.3 us
    ppermute x7, starting transfers between devices, per_device(): behind = lax.ppermute(behind, 'ctx', backward)  31.6 us
    ppermute x8, starting transfers between devices, per_device(): ahead = lax.ppermute(ahead, 'ctx', forward)  20.2 us
    ppermute x8, waiting for transfers between devices, ring_pieces(): ahead = lax.ppermute(ahead, axis, forward)  18.7 us
    ppermute x8, waiting for transfers between devices, per_device(): ahead = lax.ppermute(ahead, 'ctx', forward)  17.4 us
    ppermute x8, starting transfers between devices, ring_pieces(): ahead = lax.ppermute(ahead, axis, forward)  16.9 us
    ppermute x7, waiting for transfers between devices, per_device(): behind = lax.ppermute(behind, 'ctx', backward)  12.6 us
  transfers between devices with their start and end apart: 41, of which 27 were waited for; matrix products, arithmetic and copies ran while one was open for 10% of the time, Pallas kernels for 0%

profile of v6, /device:TPU:1, one launch (start us, length us, event | category | flops | bytes accessed | tf_op | source)
XLA Modules:
  0.0 257.0 jit_solution(16452437067084329838)
XLA Ops:
  2.3 5.7 %collective-permute-start = (bf16[104,512]{1,0:T(8,128)(2,1)S(1)}, bf16[104,512]{1,0:T(8,128)(2,1)S(1)}, u32[]{:S(2)}, u32[]{:S(2)}) collective-permute-start(bf16[104,512]{1,0:T(8,128)(2,1)S(1)} %get-tuple-element.169), channel_id=1, source_target_pairs={{0,256},{16,272},{32,288},{48,304},{64,320},{80,336},{96,352},{112... | collective-permute-start | bytes 319496 | tf_op jit(solution)/shard_map/ppermute | solution.py:34
  9.1 3.6 %collective-permute-start.40 = (bf16[320,192]{1,0:T(8,128)(2,1)S(1)}, bf16[320,192]{1,0:T(8,128)(2,1)S(1)}, u32[]{:S(2)}, u32[]{:S(2)}) collective-permute-start(bf16[320,192]{1,0:T(8,128)(2,1)S(1)} %constant_dynamic-slice_fusion), channel_id=1, source_target_pairs={{0,16},{16,32},{32,48},{48,64},{64,80},{80,96},{96,112},{112,128},... | collective-permute-start | bytes 368648 | tf_op jit(solution)/shard_map/ppermute | solution.py:19
  17.7 3.5 %collective-permute-start.1 = (bf16[2,104,512]{2,1,0:T(8,128)(2,1)S(1)}, bf16[2,104,512]{2,1,0:T(8,128)(2,1)S(1)}, u32[]{:S(2)}, u32[]{:S(2)}) collective-permute-start(bf16[2,104,512]{2,1,0:T(8,128)(2,1)S(1)} %maximum_select_fusion.2), channel_id=1, source_target_pairs={{0,16},{16,32},{32,48},{48,64},{64,80},{80,96},{96,112},{112,128},... | collective-permute-start | bytes 638984 | tf_op jit(solution)/shard_map/ppermute | solution.py:45
  21.3 7.9 %collective-permute-start.2 = (bf16[2,104,512]{2,1,0:T(8,128)(2,1)S(1)}, bf16[2,104,512]{2,1,0:T(8,128)(2,1)S(1)}, u32[]{:S(2)}, u32[]{:S(2)}) collective-permute-start(bf16[2,104,512]{2,1,0:T(8,128)(2,1)S(1)} %maximum_select_fusion.2), channel_id=1, source_target_pairs={{0,240},{16,0},{32,16},{48,32},{64,48},{80,64},{96,80},{112,96},{1... | collective-permute-start | bytes 638984 | tf_op jit(solution)/shard_map/ppermute | solution.py:48
  33.8 4.6 %collective-permute-start.4 = (bf16[2,104,512]{2,1,0:T(8,128)(2,1)S(1)}, bf16[2,104,512]{2,1,0:T(8,128)(2,1)S(1)}, u32[]{:S(2)}, u32[]{:S(2)}) collective-permute-start(bf16[2,104,512]{2,1,0:T(8,128)(2,1)S(1)} %collective-permute-done.2), channel_id=1, source_target_pairs={{0,240},{16,0},{32,16},{48,32},{64,48},{80,64},{96,80},{112,96},{1... | collective-permute-start | bytes 638984 | tf_op jit(solution)/shard_map/ppermute | solution.py:48
  42.1 4.6 %collective-permute-start.6 = (bf16[2,104,512]{2,1,0:T(8,128)(2,1)S(1)}, bf16[2,104,512]{2,1,0:T(8,128)(2,1)S(1)}, u32[]{:S(2)}, u32[]{:S(2)}) collective-permute-start(bf16[2,104,512]{2,1,0:T(8,128)(2,1)S(1)} %collective-permute-done.4), channel_id=1, source_target_pairs={{0,240},{16,0},{32,16},{48,32},{64,48},{80,64},{96,80},{112,96},{1... | collective-permute-start | bytes 638984 | tf_op jit(solution)/shard_map/ppermute | solution.py:48
  49.9 4.6 %collective-permute-start.8 = (bf16[2,104,512]{2,1,0:T(8,128)(2,1)S(1)}, bf16[2,104,512]{2,1,0:T(8,128)(2,1)S(1)}, u32[]{:S(2)}, u32[]{:S(2)}) collective-permute-start(bf16[2,104,512]{2,1,0:T(8,128)(2,1)S(1)} %collective-permute-done.6), channel_id=1, source_target_pairs={{0,240},{16,0},{32,16},{48,32},{64,48},{80,64},{96,80},{112,96},{1... | collective-permute-start | bytes 638984 | tf_op jit(solution)/shard_map/ppermute | solution.py:48
  57.7 4.6 %collective-permute-start.10 = (bf16[2,104,512]{2,1,0:T(8,128)(2,1)S(1)}, bf16[2,104,512]{2,1,0:T(8,128)(2,1)S(1)}, u32[]{:S(2)}, u32[]{:S(2)}) collective-permute-start(bf16[2,104,512]{2,1,0:T(8,128)(2,1)S(1)} %collective-permute-done.8), channel_id=1, source_target_pairs={{0,240},{16,0},{32,16},{48,32},{64,48},{80,64},{96,80},{112,96},{1... | collective-permute-start | bytes 638984 | tf_op jit(solution)/shard_map/ppermute | solution.py:48
  65.5 4.6 %collective-permute-start.12 = (bf16[2,104,512]{2,1,0:T(8,128)(2,1)S(1)}, bf16[2,104,512]{2,1,0:T(8,128)(2,1)S(1)}, u32[]{:S(2)}, u32[]{:S(2)}) collective-permute-start(bf16[2,104,512]{2,1,0:T(8,128)(2,1)S(1)} %collective-permute-done.10), channel_id=1, source_target_pairs={{0,240},{16,0},{32,16},{48,32},{64,48},{80,64},{96,80},{112,96},{1... | collective-permute-start | bytes 638984 | tf_op jit(solution)/shard_map/ppermute | solution.py:48
  73.2 4.6 %collective-permute-start.14 = (bf16[2,104,512]{2,1,0:T(8,128)(2,1)S(1)}, bf16[2,104,512]{2,1,0:T(8,128)(2,1)S(1)}, u32[]{:S(2)}, u32[]{:S(2)}) collective-permute-start(bf16[2,104,512]{2,1,0:T(8,128)(2,1)S(1)} %collective-permute-done.12), channel_id=1, source_target_pairs={{0,240},{16,0},{32,16},{48,32},{64,48},{80,64},{96,80},{112,96},{1... | collective-permute-start | bytes 638984 | tf_op jit(solution)/shard_map/ppermute | solution.py:48
  82.0 7.8 %collective-permute-done.15 = bf16[2,104,512]{2,1,0:T(8,128)(2,1)S(1)} collective-permute-done((bf16[2,104,512]{2,1,0:T(8,128)(2,1)S(1)}, bf16[2,104,512]{2,1,0:T(8,128)(2,1)S(1)}, u32[]{:S(2)}, u32[]{:S(2)}) %collective-permute-start.15) | collective-permute-done | bytes 213024 | tf_op jit(solution)/shard_map/ppermute | solution.py:45
  101.5 3.5 %collective-permute-done.16 = bf16[320,1,256]{2,0,1:T(8,128)(2,1)S(1)} collective-permute-done((bf16[320,1,256]{2,0,1:T(8,128)(2,1)S(1)}, bf16[320,1,256]{2,0,1:T(8,128)(2,1)S(1)}, u32[]{:S(2)}, u32[]{:S(2)}) %collective-permute-start.16) | collective-permute-done | bytes 163872 | tf_op jit(solution)/shard_map/ppermute | solution.py:179
  107.0 4.6 %collective-permute-start.18 = (bf16[2,320,1,256]{3,1,2,0:T(8,128)(2,1)S(1)}, bf16[2,320,1,256]{3,1,2,0:T(8,128)(2,1)S(1)}, u32[]{:S(2)}, u32[]{:S(2)}) collective-permute-start(bf16[2,320,1,256]{3,1,2,0:T(8,128)(2,1)S(1)} %maximum_select_fusion), channel_id=1, source_target_pairs={{0,240},{16,0},{32,16},{48,32},{64,48},{80,64},{96,80},{112,96},{1... | collective-permute-start | bytes 983048 | tf_op jit(solution)/shard_map/ppermute | solution.py:213
  117.5 5.2 %collective-permute-start.20 = (bf16[2,320,1,256]{3,1,2,0:T(8,128)(2,1)S(1)}, bf16[2,320,1,256]{3,1,2,0:T(8,128)(2,1)S(1)}, u32[]{:S(2)}, u32[]{:S(2)}) collective-permute-start(bf16[2,320,1,256]{3,1,2,0:T(8,128)(2,1)S(1)} %collective-permute-done.18), channel_id=1, source_target_pairs={{0,240},{16,0},{32,16},{48,32},{64,48},{80,64},{96,80},{112,96},{1... | collective-permute-start | bytes 983048 | tf_op jit(solution)/shard_map/ppermute | solution.py:213
  125.0 3.7 %collective-permute-done.19 = bf16[2,320,1,256]{3,1,2,0:T(8,128)(2,1)S(1)} collective-permute-done((bf16[2,320,1,256]{3,1,2,0:T(8,128)(2,1)S(1)}, bf16[2,320,1,256]{3,1,2,0:T(8,128)(2,1)S(1)}, u32[]{:S(2)}, u32[]{:S(2)}) %collective-permute-start.19) | collective-permute-done | bytes 327712 | tf_op jit(solution)/shard_map/ppermute | solution.py:210
  131.7 5.3 %collective-permute-start.22 = (bf16[2,320,1,256]{3,1,2,0:T(8,128)(2,1)S(1)}, bf16[2,320,1,256]{3,1,2,0:T(8,128)(2,1)S(1)}, u32[]{:S(2)}, u32[]{:S(2)}) collective-permute-start(bf16[2,320,1,256]{3,1,2,0:T(8,128)(2,1)S(1)} %collective-permute-done.20), channel_id=1, source_target_pairs={{0,240},{16,0},{32,16},{48,32},{64,48},{80,64},{96,80},{112,96},{1... | collective-permute-start | bytes 983048 | tf_op jit(solution)/shard_map/ppermute | solution.py:213
  139.3 3.2 %collective-permute-done.21 = bf16[2,320,1,256]{3,1,2,0:T(8,128)(2,1)S(1)} collective-permute-done((bf16[2,320,1,256]{3,1,2,0:T(8,128)(2,1)S(1)}, bf16[2,320,1,256]{3,1,2,0:T(8,128)(2,1)S(1)}, u32[]{:S(2)}, u32[]{:S(2)}) %collective-permute-start.21) | collective-permute-done | bytes 327712 | tf_op jit(solution)/shard_map/ppermute | solution.py:210
  145.6 5.1 %collective-permute-start.24 = (bf16[2,320,1,256]{3,1,2,0:T(8,128)(2,1)S(1)}, bf16[2,320,1,256]{3,1,2,0:T(8,128)(2,1)S(1)}, u32[]{:S(2)}, u32[]{:S(2)}) collective-permute-start(bf16[2,320,1,256]{3,1,2,0:T(8,128)(2,1)S(1)} %collective-permute-done.22), channel_id=1, source_target_pairs={{0,240},{16,0},{32,16},{48,32},{64,48},{80,64},{96,80},{112,96},{1... | collective-permute-start | bytes 983048 | tf_op jit(solution)/shard_map/ppermute | solution.py:213
  158.0 5.3 %collective-permute-start.26 = (bf16[2,320,1,256]{3,1,2,0:T(8,128)(2,1)S(1)}, bf16[2,320,1,256]{3,1,2,0:T(8,128)(2,1)S(1)}, u32[]{:S(2)}, u32[]{:S(2)}) collective-permute-start(bf16[2,320,1,256]{3,1,2,0:T(8,128)(2,1)S(1)} %collective-permute-done.24), channel_id=1, source_target_pairs={{0,240},{16,0},{32,16},{48,32},{64,48},{80,64},{96,80},{112,96},{1... | collective-permute-start | bytes 983048 | tf_op jit(solution)/shard_map/ppermute | solution.py:213
  167.0 4.3 %collective-permute-done.26 = bf16[2,320,1,256]{3,1,2,0:T(8,128)(2,1)S(1)} collective-permute-done((bf16[2,320,1,256]{3,1,2,0:T(8,128)(2,1)S(1)}, bf16[2,320,1,256]{3,1,2,0:T(8,128)(2,1)S(1)}, u32[]{:S(2)}, u32[]{:S(2)}) %collective-permute-start.26) | collective-permute-done | bytes 327712 | tf_op jit(solution)/shard_map/ppermute | solution.py:213
  171.3 3.9 %collective-permute-start.27 = (bf16[2,320,1,256]{3,1,2,0:T(8,128)(2,1)S(1)}, bf16[2,320,1,256]{3,1,2,0:T(8,128)(2,1)S(1)}, u32[]{:S(2)}, u32[]{:S(2)}) collective-permute-start(bf16[2,320,1,256]{3,1,2,0:T(8,128)(2,1)S(1)} %collective-permute-done.25), channel_id=1, source_target_pairs={{0,16},{16,32},{32,48},{48,64},{64,80},{80,96},{96,112},{112,128},... | collective-permute-start | bytes 983048 | tf_op jit(solution)/shard_map/ppermute | solution.py:210
  175.3 2.6 collective-permute-start.28
  183.4 3.1 %collective-permute-start.29 = (bf16[2,320,1,256]{3,1,2,0:T(8,128)(2,1)S(1)}, bf16[2,320,1,256]{3,1,2,0:T(8,128)(2,1)S(1)}, u32[]{:S(2)}, u32[]{:S(2)}) collective-permute-start(bf16[2,320,1,256]{3,1,2,0:T(8,128)(2,1)S(1)} %collective-permute-done.27), channel_id=1, source_target_pairs={{0,16},{16,32},{32,48},{48,64},{64,80},{80,96},{96,112},{112,128},... | collective-permute-start | bytes 983048 | tf_op jit(solution)/shard_map/ppermute | solution.py:210
  186.5 3.6 %collective-permute-start.30 = (bf16[2,320,1,256]{3,1,2,0:T(8,128)(2,1)S(1)}, bf16[2,320,1,256]{3,1,2,0:T(8,128)(2,1)S(1)}, u32[]{:S(2)}, u32[]{:S(2)}) collective-permute-start(bf16[2,320,1,256]{3,1,2,0:T(8,128)(2,1)S(1)} %collective-permute-done.28), channel_id=1, source_target_pairs={{0,240},{16,0},{32,16},{48,32},{64,48},{80,64},{96,80},{112,96},{1... | collective-permute-start | bytes 983048 | tf_op jit(solution)/shard_map/ppermute | solution.py:213
  194.7 3.4 %collective-permute-start.31 = (bf16[2,320,1,256]{3,1,2,0:T(8,128)(2,1)S(1)}, bf16[2,320,1,256]{3,1,2,0:T(8,128)(2,1)S(1)}, u32[]{:S(2)}, u32[]{:S(2)}) collective-permute-start(bf16[2,320,1,256]{3,1,2,0:T(8,128)(2,1)S(1)} %collective-permute-done.29), channel_id=1, source_target_pairs={{0,16},{16,32},{32,48},{48,64},{64,80},{80,96},{96,112},{112,128},... | collective-permute-start | bytes 983048 | tf_op jit(solution)/shard_map/ppermute | solution.py:210
  199.4 4.3 %collective-permute-done.31 = bf16[2,320,1,256]{3,1,2,0:T(8,128)(2,1)S(1)} collective-permute-done((bf16[2,320,1,256]{3,1,2,0:T(8,128)(2,1)S(1)}, bf16[2,320,1,256]{3,1,2,0:T(8,128)(2,1)S(1)}, u32[]{:S(2)}, u32[]{:S(2)}) %collective-permute-start.31) | collective-permute-done | bytes 327712 | tf_op jit(solution)/shard_map/ppermute | solution.py:210
  206.4 20.7 %collective-permute-start.36 = (bf16[160,1536]{1,0:T(8,128)(2,1)S(1)}, bf16[160,1536]{1,0:T(8,128)(2,1)S(1)}, u32[]{:S(2)}, u32[]{:S(2)}) collective-permute-start(bf16[160,1536]{1,0:T(8,128)(2,1)S(1)} %dynamic-slice_convert_fusion), channel_id=1, source_target_pairs={{0,1},{1,0},{2,3},{3,2},{4,5},{5,4},{6,7},{7,6},{8,9},{9,8},{10,11... | collective-permute-start | bytes 1474568 | tf_op jit(solution)/shard_map/ppermute | solution.py:71
  229.7 3.1 %collective-permute-start.37 = (bf16[160,768]{1,0:T(8,128)(2,1)S(1)}, bf16[160,768]{1,0:T(8,128)(2,1)S(1)}, u32[]{:S(2)}, u32[]{:S(2)}) collective-permute-start(bf16[160,768]{1,0:T(8,128)(2,1)S(1)} %dynamic-slice_convert_fusion.2), channel_id=1, source_target_pairs={{0,2},{1,3},{2,0},{3,1},{4,6},{5,7},{6,4},{7,5},{8,10},{9,11},{10,... | collective-permute-start | bytes 737288 | tf_op jit(solution)/shard_map/ppermute | solution.py:71
  235.3 3.3 %collective-permute-done.37 = bf16[160,768]{1,0:T(8,128)(2,1)S(1)} collective-permute-done((bf16[160,768]{1,0:T(8,128)(2,1)S(1)}, bf16[160,768]{1,0:T(8,128)(2,1)S(1)}, u32[]{:S(2)}, u32[]{:S(2)}) %collective-permute-start.37) | collective-permute-done | bytes 245792 | tf_op jit(solution)/shard_map/ppermute | solution.py:71
  238.7 4.7 %collective-permute-start.38 = (bf16[160,384]{1,0:T(8,128)(2,1)S(1)}, bf16[160,384]{1,0:T(8,128)(2,1)S(1)}, u32[]{:S(2)}, u32[]{:S(2)}) collective-permute-start(bf16[160,384]{1,0:T(8,128)(2,1)S(1)} %dynamic-slice_convert_fusion.4), channel_id=1, source_target_pairs={{0,4},{1,5},{2,6},{3,7},{4,0},{5,1},{6,2},{7,3},{8,12},{9,13},{10,... | collective-permute-start | bytes 368648 | tf_op jit(solution)/shard_map/ppermute | solution.py:71
  249.3 4.0 %collective-permute-start.35 = (bf16[160,192]{1,0:T(8,128)(2,1)S(1)}, bf16[160,192]{1,0:T(8,128)(2,1)S(1)}, u32[]{:S(2)}, u32[]{:S(2)}) collective-permute-start(bf16[160,192]{1,0:T(8,128)(2,1)S(1)} %dynamic-slice_convert_fusion.7), channel_id=1, source_target_pairs={{0,4},{1,5},{2,6},{3,7},{4,0},{5,1},{6,2},{7,3},{8,12},{9,13},{10,... | collective-permute-start | bytes 184328 | tf_op jit(solution)/shard_map/ppermute | solution.py:71
  253.4 2.6 collective-permute-done.35
  (237 shorter events, 99.2 us)
Async XLA Ops:
  2.3 15.4 %collective-permute-start = (bf16[104,512]{1,0:T(8,128)(2,1)S(1)}, bf16[104,512]{1,0:T(8,128)(2,1)S(1)}, u32[]{:S(2)}, u32[]{:S(2)}) collective-permute-start(bf16[104,512]{1,0:T(8,128)(2,1)S(1)} %get-tuple-element.169), channel_id=1, source_target_pairs={{0,256},{16,272},{32,288},{48,304},{64,320},{80,336},{96,352},{112... | collective-permute-start | bytes 319496 | tf_op jit(solution)/shard_map/ppermute | solution.py:34
  9.1 20.4 %collective-permute-start.40 = (bf16[320,192]{1,0:T(8,128)(2,1)S(1)}, bf16[320,192]{1,0:T(8,128)(2,1)S(1)}, u32[]{:S(2)}, u32[]{:S(2)}) collective-permute-start(bf16[320,192]{1,0:T(8,128)(2,1)S(1)} %constant_dynamic-slice_fusion), channel_id=1, source_target_pairs={{0,16},{16,32},{32,48},{48,64},{64,80},{80,96},{96,112},{112,128},... | collective-permute-start | bytes 368648 | tf_op jit(solution)/shard_map/ppermute | solution.py:19
  17.7 14.1 %collective-permute-start.1 = (bf16[2,104,512]{2,1,0:T(8,128)(2,1)S(1)}, bf16[2,104,512]{2,1,0:T(8,128)(2,1)S(1)}, u32[]{:S(2)}, u32[]{:S(2)}) collective-permute-start(bf16[2,104,512]{2,1,0:T(8,128)(2,1)S(1)} %maximum_select_fusion.2), channel_id=1, source_target_pairs={{0,16},{16,32},{32,48},{48,64},{64,80},{80,96},{96,112},{112,128},... | collective-permute-start | bytes 638984 | tf_op jit(solution)/shard_map/ppermute | solution.py:45
  21.3 12.5 %collective-permute-start.2 = (bf16[2,104,512]{2,1,0:T(8,128)(2,1)S(1)}, bf16[2,104,512]{2,1,0:T(8,128)(2,1)S(1)}, u32[]{:S(2)}, u32[]{:S(2)}) collective-permute-start(bf16[2,104,512]{2,1,0:T(8,128)(2,1)S(1)} %maximum_select_fusion.2), channel_id=1, source_target_pairs={{0,240},{16,0},{32,16},{48,32},{64,48},{80,64},{96,80},{112,96},{1... | collective-permute-start | bytes 638984 | tf_op jit(solution)/shard_map/ppermute | solution.py:48
  31.9 8.3 %collective-permute-start.3 = (bf16[2,104,512]{2,1,0:T(8,128)(2,1)S(1)}, bf16[2,104,512]{2,1,0:T(8,128)(2,1)S(1)}, u32[]{:S(2)}, u32[]{:S(2)}) collective-permute-start(bf16[2,104,512]{2,1,0:T(8,128)(2,1)S(1)} %collective-permute-done.1), channel_id=1, source_target_pairs={{0,16},{16,32},{32,48},{48,64},{64,80},{80,96},{96,112},{112,128},... | collective-permute-start | bytes 638984 | tf_op jit(solution)/shard_map/ppermute | solution.py:45
  33.8 8.3 %collective-permute-start.4 = (bf16[2,104,512]{2,1,0:T(8,128)(2,1)S(1)}, bf16[2,104,512]{2,1,0:T(8,128)(2,1)S(1)}, u32[]{:S(2)}, u32[]{:S(2)}) collective-permute-start(bf16[2,104,512]{2,1,0:T(8,128)(2,1)S(1)} %collective-permute-done.2), channel_id=1, source_target_pairs={{0,240},{16,0},{32,16},{48,32},{64,48},{80,64},{96,80},{112,96},{1... | collective-permute-start | bytes 638984 | tf_op jit(solution)/shard_map/ppermute | solution.py:48
  40.2 7.8 %collective-permute-start.5 = (bf16[2,104,512]{2,1,0:T(8,128)(2,1)S(1)}, bf16[2,104,512]{2,1,0:T(8,128)(2,1)S(1)}, u32[]{:S(2)}, u32[]{:S(2)}) collective-permute-start(bf16[2,104,512]{2,1,0:T(8,128)(2,1)S(1)} %collective-permute-done.3), channel_id=1, source_target_pairs={{0,16},{16,32},{32,48},{48,64},{64,80},{80,96},{96,112},{112,128},... | collective-permute-start | bytes 638984 | tf_op jit(solution)/shard_map/ppermute | solution.py:45
  42.1 7.8 %collective-permute-start.6 = (bf16[2,104,512]{2,1,0:T(8,128)(2,1)S(1)}, bf16[2,104,512]{2,1,0:T(8,128)(2,1)S(1)}, u32[]{:S(2)}, u32[]{:S(2)}) collective-permute-start(bf16[2,104,512]{2,1,0:T(8,128)(2,1)S(1)} %collective-permute-done.4), channel_id=1, source_target_pairs={{0,240},{16,0},{32,16},{48,32},{64,48},{80,64},{96,80},{112,96},{1... | collective-permute-start | bytes 638984 | tf_op jit(solution)/shard_map/ppermute | solution.py:48
  48.0 7.8 %collective-permute-start.7 = (bf16[2,104,512]{2,1,0:T(8,128)(2,1)S(1)}, bf16[2,104,512]{2,1,0:T(8,128)(2,1)S(1)}, u32[]{:S(2)}, u32[]{:S(2)}) collective-permute-start(bf16[2,104,512]{2,1,0:T(8,128)(2,1)S(1)} %collective-permute-done.5), channel_id=1, source_target_pairs={{0,16},{16,32},{32,48},{48,64},{64,80},{80,96},{96,112},{112,128},... | collective-permute-start | bytes 638984 | tf_op jit(solution)/shard_map/ppermute | solution.py:45
  55.7 7.8 %collective-permute-start.9 = (bf16[2,104,512]{2,1,0:T(8,128)(2,1)S(1)}, bf16[2,104,512]{2,1,0:T(8,128)(2,1)S(1)}, u32[]{:S(2)}, u32[]{:S(2)}) collective-permute-start(bf16[2,104,512]{2,1,0:T(8,128)(2,1)S(1)} %collective-permute-done.7), channel_id=1, source_target_pairs={{0,16},{16,32},{32,48},{48,64},{64,80},{80,96},{96,112},{112,128},... | collective-permute-start | bytes 638984 | tf_op jit(solution)/shard_map/ppermute | solution.py:45
  63.5 7.8 %collective-permute-start.11 = (bf16[2,104,512]{2,1,0:T(8,128)(2,1)S(1)}, bf16[2,104,512]{2,1,0:T(8,128)(2,1)S(1)}, u32[]{:S(2)}, u32[]{:S(2)}) collective-permute-start(bf16[2,104,512]{2,1,0:T(8,128)(2,1)S(1)} %collective-permute-done.9), channel_id=1, source_target_pairs={{0,16},{16,32},{32,48},{48,64},{64,80},{80,96},{96,112},{112,128},... | collective-permute-start | bytes 638984 | tf_op jit(solution)/shard_map/ppermute | solution.py:45
  71.3 8.7 %collective-permute-start.13 = (bf16[2,104,512]{2,1,0:T(8,128)(2,1)S(1)}, bf16[2,104,512]{2,1,0:T(8,128)(2,1)S(1)}, u32[]{:S(2)}, u32[]{:S(2)}) collective-permute-start(bf16[2,104,512]{2,1,0:T(8,128)(2,1)S(1)} %collective-permute-done.11), channel_id=1, source_target_pairs={{0,16},{16,32},{32,48},{48,64},{64,80},{80,96},{96,112},{112,128},... | collective-permute-start | bytes 638984 | tf_op jit(solution)/shard_map/ppermute | solution.py:45
  73.2 8.7 %collective-permute-start.14 = (bf16[2,104,512]{2,1,0:T(8,128)(2,1)S(1)}, bf16[2,104,512]{2,1,0:T(8,128)(2,1)S(1)}, u32[]{:S(2)}, u32[]{:S(2)}) collective-permute-start(bf16[2,104,512]{2,1,0:T(8,128)(2,1)S(1)} %collective-permute-done.12), channel_id=1, source_target_pairs={{0,240},{16,0},{32,16},{48,32},{64,48},{80,64},{96,80},{112,96},{1... | collective-permute-start | bytes 638984 | tf_op jit(solution)/shard_map/ppermute | solution.py:48
  80.0 9.8 %collective-permute-start.15 = (bf16[2,104,512]{2,1,0:T(8,128)(2,1)S(1)}, bf16[2,104,512]{2,1,0:T(8,128)(2,1)S(1)}, u32[]{:S(2)}, u32[]{:S(2)}) collective-permute-start(bf16[2,104,512]{2,1,0:T(8,128)(2,1)S(1)} %collective-permute-done.13), channel_id=1, source_target_pairs={{0,16},{16,32},{32,48},{48,64},{64,80},{80,96},{96,112},{112,128},... | collective-permute-start | bytes 638984 | tf_op jit(solution)/shard_map/ppermute | solution.py:45
  105.0 9.3 %collective-permute-start.17 = (bf16[2,320,1,256]{3,1,2,0:T(8,128)(2,1)S(1)}, bf16[2,320,1,256]{3,1,2,0:T(8,128)(2,1)S(1)}, u32[]{:S(2)}, u32[]{:S(2)}) collective-permute-start(bf16[2,320,1,256]{3,1,2,0:T(8,128)(2,1)S(1)} %maximum_select_fusion), channel_id=1, source_target_pairs={{0,16},{16,32},{32,48},{48,64},{64,80},{80,96},{96,112},{112,128},... | collective-permute-start | bytes 983048 | tf_op jit(solution)/shard_map/ppermute | solution.py:210
  107.0 8.6 %collective-permute-start.18 = (bf16[2,320,1,256]{3,1,2,0:T(8,128)(2,1)S(1)}, bf16[2,320,1,256]{3,1,2,0:T(8,128)(2,1)S(1)}, u32[]{:S(2)}, u32[]{:S(2)}) collective-permute-start(bf16[2,320,1,256]{3,1,2,0:T(8,128)(2,1)S(1)} %maximum_select_fusion), channel_id=1, source_target_pairs={{0,240},{16,0},{32,16},{48,32},{64,48},{80,64},{96,80},{112,96},{1... | collective-permute-start | bytes 983048 | tf_op jit(solution)/shard_map/ppermute | solution.py:213
  115.5 13.2 %collective-permute-start.19 = (bf16[2,320,1,256]{3,1,2,0:T(8,128)(2,1)S(1)}, bf16[2,320,1,256]{3,1,2,0:T(8,128)(2,1)S(1)}, u32[]{:S(2)}, u32[]{:S(2)}) collective-permute-start(bf16[2,320,1,256]{3,1,2,0:T(8,128)(2,1)S(1)} %collective-permute-done.17), channel_id=1, source_target_pairs={{0,16},{16,32},{32,48},{48,64},{64,80},{80,96},{96,112},{112,128},... | collective-permute-start | bytes 983048 | tf_op jit(solution)/shard_map/ppermute | solution.py:210
  117.5 12.3 %collective-permute-start.20 = (bf16[2,320,1,256]{3,1,2,0:T(8,128)(2,1)S(1)}, bf16[2,320,1,256]{3,1,2,0:T(8,128)(2,1)S(1)}, u32[]{:S(2)}, u32[]{:S(2)}) collective-permute-start(bf16[2,320,1,256]{3,1,2,0:T(8,128)(2,1)S(1)} %collective-permute-done.18), channel_id=1, source_target_pairs={{0,240},{16,0},{32,16},{48,32},{64,48},{80,64},{96,80},{112,96},{1... | collective-permute-start | bytes 983048 | tf_op jit(solution)/shard_map/ppermute | solution.py:213
  129.7 12.8 %collective-permute-start.21 = (bf16[2,320,1,256]{3,1,2,0:T(8,128)(2,1)S(1)}, bf16[2,320,1,256]{3,1,2,0:T(8,128)(2,1)S(1)}, u32[]{:S(2)}, u32[]{:S(2)}) collective-permute-start(bf16[2,320,1,256]{3,1,2,0:T(8,128)(2,1)S(1)} %collective-permute-done.19), channel_id=1, source_target_pairs={{0,16},{16,32},{32,48},{48,64},{64,80},{80,96},{96,112},{112,128},... | collective-permute-start | bytes 983048 | tf_op jit(solution)/shard_map/ppermute | solution.py:210
  131.7 11.7 %collective-permute-start.22 = (bf16[2,320,1,256]{3,1,2,0:T(8,128)(2,1)S(1)}, bf16[2,320,1,256]{3,1,2,0:T(8,128)(2,1)S(1)}, u32[]{:S(2)}, u32[]{:S(2)}) collective-permute-start(bf16[2,320,1,256]{3,1,2,0:T(8,128)(2,1)S(1)} %collective-permute-done.20), channel_id=1, source_target_pairs={{0,240},{16,0},{32,16},{48,32},{64,48},{80,64},{96,80},{112,96},{1... | collective-permute-start | bytes 983048 | tf_op jit(solution)/shard_map/ppermute | solution.py:213
  143.4 11.8 %collective-permute-start.23 = (bf16[2,320,1,256]{3,1,2,0:T(8,128)(2,1)S(1)}, bf16[2,320,1,256]{3,1,2,0:T(8,128)(2,1)S(1)}, u32[]{:S(2)}, u32[]{:S(2)}) collective-permute-start(bf16[2,320,1,256]{3,1,2,0:T(8,128)(2,1)S(1)} %collective-permute-done.21), channel_id=1, source_target_pairs={{0,16},{16,32},{32,48},{48,64},{64,80},{80,96},{96,112},{112,128},... | collective-permute-start | bytes 983048 | tf_op jit(solution)/shard_map/ppermute | solution.py:210
  145.6 10.5 %collective-permute-start.24 = (bf16[2,320,1,256]{3,1,2,0:T(8,128)(2,1)S(1)}, bf16[2,320,1,256]{3,1,2,0:T(8,128)(2,1)S(1)}, u32[]{:S(2)}, u32[]{:S(2)}) collective-permute-start(bf16[2,320,1,256]{3,1,2,0:T(8,128)(2,1)S(1)} %collective-permute-done.22), channel_id=1, source_target_pairs={{0,240},{16,0},{32,16},{48,32},{64,48},{80,64},{96,80},{112,96},{1... | collective-permute-start | bytes 983048 | tf_op jit(solution)/shard_map/ppermute | solution.py:213
  156.1 10.9 %collective-permute-start.25 = (bf16[2,320,1,256]{3,1,2,0:T(8,128)(2,1)S(1)}, bf16[2,320,1,256]{3,1,2,0:T(8,128)(2,1)S(1)}, u32[]{:S(2)}, u32[]{:S(2)}) collective-permute-start(bf16[2,320,1,256]{3,1,2,0:T(8,128)(2,1)S(1)} %collective-permute-done.23), channel_id=1, source_target_pairs={{0,16},{16,32},{32,48},{48,64},{64,80},{80,96},{96,112},{112,128},... | collective-permute-start | bytes 983048 | tf_op jit(solution)/shard_map/ppermute | solution.py:210
  158.0 13.3 %collective-permute-start.26 = (bf16[2,320,1,256]{3,1,2,0:T(8,128)(2,1)S(1)}, bf16[2,320,1,256]{3,1,2,0:T(8,128)(2,1)S(1)}, u32[]{:S(2)}, u32[]{:S(2)}) collective-permute-start(bf16[2,320,1,256]{3,1,2,0:T(8,128)(2,1)S(1)} %collective-permute-done.24), channel_id=1, source_target_pairs={{0,240},{16,0},{32,16},{48,32},{64,48},{80,64},{96,80},{112,96},{1... | collective-permute-start | bytes 983048 | tf_op jit(solution)/shard_map/ppermute | solution.py:213
  171.3 9.9 %collective-permute-start.27 = (bf16[2,320,1,256]{3,1,2,0:T(8,128)(2,1)S(1)}, bf16[2,320,1,256]{3,1,2,0:T(8,128)(2,1)S(1)}, u32[]{:S(2)}, u32[]{:S(2)}) collective-permute-start(bf16[2,320,1,256]{3,1,2,0:T(8,128)(2,1)S(1)} %collective-permute-done.25), channel_id=1, source_target_pairs={{0,16},{16,32},{32,48},{48,64},{64,80},{80,96},{96,112},{112,128},... | collective-permute-start | bytes 983048 | tf_op jit(solution)/shard_map/ppermute | solution.py:210
  175.3 8.1 %collective-permute-start.28 = (bf16[2,320,1,256]{3,1,2,0:T(8,128)(2,1)S(1)}, bf16[2,320,1,256]{3,1,2,0:T(8,128)(2,1)S(1)}, u32[]{:S(2)}, u32[]{:S(2)}) collective-permute-start(bf16[2,320,1,256]{3,1,2,0:T(8,128)(2,1)S(1)} %collective-permute-done.26), channel_id=1, source_target_pairs={{0,240},{16,0},{32,16},{48,32},{64,48},{80,64},{96,80},{112,96},{1... | collective-permute-start | bytes 983048 | tf_op jit(solution)/shard_map/ppermute | solution.py:213
  183.4 9.1 %collective-permute-start.29 = (bf16[2,320,1,256]{3,1,2,0:T(8,128)(2,1)S(1)}, bf16[2,320,1,256]{3,1,2,0:T(8,128)(2,1)S(1)}, u32[]{:S(2)}, u32[]{:S(2)}) collective-permute-start(bf16[2,320,1,256]{3,1,2,0:T(8,128)(2,1)S(1)} %collective-permute-done.27), channel_id=1, source_target_pairs={{0,16},{16,32},{32,48},{48,64},{64,80},{80,96},{96,112},{112,128},... | collective-permute-start | bytes 983048 | tf_op jit(solution)/shard_map/ppermute | solution.py:210
  186.5 8.1 %collective-permute-start.30 = (bf16[2,320,1,256]{3,1,2,0:T(8,128)(2,1)S(1)}, bf16[2,320,1,256]{3,1,2,0:T(8,128)(2,1)S(1)}, u32[]{:S(2)}, u32[]{:S(2)}) collective-permute-start(bf16[2,320,1,256]{3,1,2,0:T(8,128)(2,1)S(1)} %collective-permute-done.28), channel_id=1, source_target_pairs={{0,240},{16,0},{32,16},{48,32},{64,48},{80,64},{96,80},{112,96},{1... | collective-permute-start | bytes 983048 | tf_op jit(solution)/shard_map/ppermute | solution.py:213
  194.7 9.0 %collective-permute-start.31 = (bf16[2,320,1,256]{3,1,2,0:T(8,128)(2,1)S(1)}, bf16[2,320,1,256]{3,1,2,0:T(8,128)(2,1)S(1)}, u32[]{:S(2)}, u32[]{:S(2)}) collective-permute-start(bf16[2,320,1,256]{3,1,2,0:T(8,128)(2,1)S(1)} %collective-permute-done.29), channel_id=1, source_target_pairs={{0,16},{16,32},{32,48},{48,64},{64,80},{80,96},{96,112},{112,128},... | collective-permute-start | bytes 983048 | tf_op jit(solution)/shard_map/ppermute | solution.py:210
  206.4 23.1 %collective-permute-start.36 = (bf16[160,1536]{1,0:T(8,128)(2,1)S(1)}, bf16[160,1536]{1,0:T(8,128)(2,1)S(1)}, u32[]{:S(2)}, u32[]{:S(2)}) collective-permute-start(bf16[160,1536]{1,0:T(8,128)(2,1)S(1)} %dynamic-slice_convert_fusion), channel_id=1, source_target_pairs={{0,1},{1,0},{2,3},{3,2},{4,5},{5,4},{6,7},{7,6},{8,9},{9,8},{10,11... | collective-permute-start | bytes 1474568 | tf_op jit(solution)/shard_map/ppermute | solution.py:71
  229.7 8.9 %collective-permute-start.37 = (bf16[160,768]{1,0:T(8,128)(2,1)S(1)}, bf16[160,768]{1,0:T(8,128)(2,1)S(1)}, u32[]{:S(2)}, u32[]{:S(2)}) collective-permute-start(bf16[160,768]{1,0:T(8,128)(2,1)S(1)} %dynamic-slice_convert_fusion.2), channel_id=1, source_target_pairs={{0,2},{1,3},{2,0},{3,1},{4,6},{5,7},{6,4},{7,5},{8,10},{9,11},{10,... | collective-permute-start | bytes 737288 | tf_op jit(solution)/shard_map/ppermute | solution.py:71
  233.0 10.4 %collective-permute-start.33 = (bf16[160,768]{1,0:T(8,128)(2,1)S(1)}, bf16[160,768]{1,0:T(8,128)(2,1)S(1)}, u32[]{:S(2)}, u32[]{:S(2)}) collective-permute-start(bf16[160,768]{1,0:T(8,128)(2,1)S(1)} %dynamic-slice_convert_fusion.3), channel_id=1, source_target_pairs={{0,8},{1,9},{2,10},{3,11},{4,12},{5,13},{6,14},{7,15},{8,0},{9,1},... | collective-permute-start | bytes 737288 | tf_op jit(solution)/shard_map/ppermute | solution.py:71
  (17 other events, 133.5 us)

commit v7 on v6

--- a/solution.py
+++ b/solution.py
@@ -206,7 +206,7 @@
     behind = pair
     waiting = [(pair, ring_pos)]
     for step in range(1, ring // 2 + 1):
-        ahead, behind, state = lax.optimization_barrier((ahead, behind, state))
+        ahead, state = lax.optimization_barrier((ahead, state))
         ahead = lax.ppermute(ahead, "ctx", forward)
         arrived = [(ahead, (ring_pos - step) % ring)]
         if step < ring - ring // 2:

time: 261 us -> 247 us (0.946)
  waiting for transfers between devices: 59.1 us -> 45.9 us
    ppermute x7, waiting for transfers between devices: 12.6 us -> 4.62 us  [per_device(): behind = lax.ppermute(behind, 'ctx', backward)]
    ppermute x8, waiting for transfers between devices: 17.4 us -> 12.3 us  [per_device(): ahead = lax.ppermute(ahead, 'ctx', forward)]
    ppermute x8, starting transfers between devices: 20.2 us -> 17.4 us  [per_device(): ahead = lax.ppermute(ahead, 'ctx', forward)]
  transfers between devices with their start and end apart: 41 -> 41, of which waited for: 27 -> 22; matrix products, arithmetic and copies ran while one was open for 10% -> 11% of each run, Pallas kernels for 0% -> 0%
where the time goes in v7:
time: 247 us; the launch traced here: 242 us
  starting transfers between devices  155 us (63%)
  waiting for transfers between devices  45.9 us (19%)
  matrix products  15.6 us (6%)
  other arithmetic  14.1 us (6%)
  local copies, waits for them, and re-layouts  9.32 us (4%)
  between operations  2.62 us (1%)
    ppermute x8, starting transfers between devices, halving_scatter(): lax.ppermute(send.astype(jnp.bfloat16), axis, [(i, i ^ 1 << bit) for i in...  42.9 us
    ppermute x7, starting transfers between devices, ring_pieces(): behind = lax.ppermute(behind, axis, backward)  35.3 us
    ppermute x7, starting transfers between devices, per_device(): behind = lax.ppermute(behind, 'ctx', backward)  31.4 us
    ppermute x8, waiting for transfers between devices, ring_pieces(): ahead = lax.ppermute(ahead, axis, forward)  18.7 us
    ppermute x8, starting transfers between devices, per_device(): ahead = lax.ppermute(ahead, 'ctx', forward)  17.4 us
    ppermute x8, starting transfers between devices, ring_pieces(): ahead = lax.ppermute(ahead, axis, forward)  16.9 us
    ppermute x8, waiting for transfers between devices, per_device(): ahead = lax.ppermute(ahead, 'ctx', forward)  12.3 us
    dot_general x16, matrix products, attend_piece(): jnp.einsum('nhe,mhe->nhm', queries, key_part, preferred_element_type=jnp....  7.02 us
  transfers between devices with their start and end apart: 41, of which 22 were waited for; matrix products, arithmetic and copies ran while one was open for 11% of the time, Pallas kernels for 0%

profile of v7, /device:TPU:1, one launch (start us, length us, event | category | flops | bytes accessed | tf_op | source)
XLA Modules:
  0.0 242.4 jit_solution(1559510584316818000)
XLA Ops:
  2.3 5.7 %collective-permute-start = (bf16[104,512]{1,0:T(8,128)(2,1)S(1)}, bf16[104,512]{1,0:T(8,128)(2,1)S(1)}, u32[]{:S(2)}, u32[]{:S(2)}) collective-permute-start(bf16[104,512]{1,0:T(8,128)(2,1)S(1)} %get-tuple-element.155), channel_id=1, source_target_pairs={{0,256},{16,272},{32,288},{48,304},{64,320},{80,336},{96,352},{112... | collective-permute-start | bytes 319496 | tf_op jit(solution)/shard_map/ppermute | solution.py:34
  9.1 3.6 %collective-permute-start.40 = (bf16[320,192]{1,0:T(8,128)(2,1)S(1)}, bf16[320,192]{1,0:T(8,128)(2,1)S(1)}, u32[]{:S(2)}, u32[]{:S(2)}) collective-permute-start(bf16[320,192]{1,0:T(8,128)(2,1)S(1)} %constant_dynamic-slice_fusion), channel_id=1, source_target_pairs={{0,16},{16,32},{32,48},{48,64},{64,80},{80,96},{96,112},{112,128},... | collective-permute-start | bytes 368648 | tf_op jit(solution)/shard_map/ppermute | solution.py:19
  17.8 3.5 %collective-permute-start.1 = (bf16[2,104,512]{2,1,0:T(8,128)(2,1)S(1)}, bf16[2,104,512]{2,1,0:T(8,128)(2,1)S(1)}, u32[]{:S(2)}, u32[]{:S(2)}) collective-permute-start(bf16[2,104,512]{2,1,0:T(8,128)(2,1)S(1)} %maximum_select_fusion.2), channel_id=1, source_target_pairs={{0,16},{16,32},{32,48},{48,64},{64,80},{80,96},{96,112},{112,128},... | collective-permute-start | bytes 638984 | tf_op jit(solution)/shard_map/ppermute | solution.py:45
  21.3 7.9 %collective-permute-start.2 = (bf16[2,104,512]{2,1,0:T(8,128)(2,1)S(1)}, bf16[2,104,512]{2,1,0:T(8,128)(2,1)S(1)}, u32[]{:S(2)}, u32[]{:S(2)}) collective-permute-start(bf16[2,104,512]{2,1,0:T(8,128)(2,1)S(1)} %maximum_select_fusion.2), channel_id=1, source_target_pairs={{0,240},{16,0},{32,16},{48,32},{64,48},{80,64},{96,80},{112,96},{1... | collective-permute-start | bytes 638984 | tf_op jit(solution)/shard_map/ppermute | solution.py:48
  29.7 2.3 collective-permute-done.1
  33.9 4.6 %collective-permute-start.4 = (bf16[2,104,512]{2,1,0:T(8,128)(2,1)S(1)}, bf16[2,104,512]{2,1,0:T(8,128)(2,1)S(1)}, u32[]{:S(2)}, u32[]{:S(2)}) collective-permute-start(bf16[2,104,512]{2,1,0:T(8,128)(2,1)S(1)} %collective-permute-done.2), channel_id=1, source_target_pairs={{0,240},{16,0},{32,16},{48,32},{64,48},{80,64},{96,80},{112,96},{1... | collective-permute-start | bytes 638984 | tf_op jit(solution)/shard_map/ppermute | solution.py:48
  42.2 4.6 %collective-permute-start.6 = (bf16[2,104,512]{2,1,0:T(8,128)(2,1)S(1)}, bf16[2,104,512]{2,1,0:T(8,128)(2,1)S(1)}, u32[]{:S(2)}, u32[]{:S(2)}) collective-permute-start(bf16[2,104,512]{2,1,0:T(8,128)(2,1)S(1)} %collective-permute-done.4), channel_id=1, source_target_pairs={{0,240},{16,0},{32,16},{48,32},{64,48},{80,64},{96,80},{112,96},{1... | collective-permute-start | bytes 638984 | tf_op jit(solution)/shard_map/ppermute | solution.py:48
  49.9 4.6 %collective-permute-start.8 = (bf16[2,104,512]{2,1,0:T(8,128)(2,1)S(1)}, bf16[2,104,512]{2,1,0:T(8,128)(2,1)S(1)}, u32[]{:S(2)}, u32[]{:S(2)}) collective-permute-start(bf16[2,104,512]{2,1,0:T(8,128)(2,1)S(1)} %collective-permute-done.6), channel_id=1, source_target_pairs={{0,240},{16,0},{32,16},{48,32},{64,48},{80,64},{96,80},{112,96},{1... | collective-permute-start | bytes 638984 | tf_op jit(solution)/shard_map/ppermute | solution.py:48
  57.7 4.6 %collective-permute-start.10 = (bf16[2,104,512]{2,1,0:T(8,128)(2,1)S(1)}, bf16[2,104,512]{2,1,0:T(8,128)(2,1)S(1)}, u32[]{:S(2)}, u32[]{:S(2)}) collective-permute-start(bf16[2,104,512]{2,1,0:T(8,128)(2,1)S(1)} %collective-permute-done.8), channel_id=1, source_target_pairs={{0,240},{16,0},{32,16},{48,32},{64,48},{80,64},{96,80},{112,96},{1... | collective-permute-start | bytes 638984 | tf_op jit(solution)/shard_map/ppermute | solution.py:48
  65.5 4.6 %collective-permute-start.12 = (bf16[2,104,512]{2,1,0:T(8,128)(2,1)S(1)}, bf16[2,104,512]{2,1,0:T(8,128)(2,1)S(1)}, u32[]{:S(2)}, u32[]{:S(2)}) collective-permute-start(bf16[2,104,512]{2,1,0:T(8,128)(2,1)S(1)} %collective-permute-done.10), channel_id=1, source_target_pairs={{0,240},{16,0},{32,16},{48,32},{64,48},{80,64},{96,80},{112,96},{1... | collective-permute-start | bytes 638984 | tf_op jit(solution)/shard_map/ppermute | solution.py:48
  73.3 4.6 %collective-permute-start.14 = (bf16[2,104,512]{2,1,0:T(8,128)(2,1)S(1)}, bf16[2,104,512]{2,1,0:T(8,128)(2,1)S(1)}, u32[]{:S(2)}, u32[]{:S(2)}) collective-permute-start(bf16[2,104,512]{2,1,0:T(8,128)(2,1)S(1)} %collective-permute-done.12), channel_id=1, source_target_pairs={{0,240},{16,0},{32,16},{48,32},{64,48},{80,64},{96,80},{112,96},{1... | collective-permute-start | bytes 638984 | tf_op jit(solution)/shard_map/ppermute | solution.py:48
  82.0 7.8 %collective-permute-done.15 = bf16[2,104,512]{2,1,0:T(8,128)(2,1)S(1)} collective-permute-done((bf16[2,104,512]{2,1,0:T(8,128)(2,1)S(1)}, bf16[2,104,512]{2,1,0:T(8,128)(2,1)S(1)}, u32[]{:S(2)}, u32[]{:S(2)}) %collective-permute-start.15) | collective-permute-done | bytes 213024 | tf_op jit(solution)/shard_map/ppermute | solution.py:45
  101.6 3.5 %collective-permute-done.16 = bf16[320,1,256]{2,0,1:T(8,128)(2,1)S(1)} collective-permute-done((bf16[320,1,256]{2,0,1:T(8,128)(2,1)S(1)}, bf16[320,1,256]{2,0,1:T(8,128)(2,1)S(1)}, u32[]{:S(2)}, u32[]{:S(2)}) %collective-permute-start.16) | collective-permute-done | bytes 163872 | tf_op jit(solution)/shard_map/ppermute | solution.py:179
  107.0 3.4 %collective-permute-start.17 = (bf16[2,320,1,256]{3,1,2,0:T(8,128)(2,1)S(1)}, bf16[2,320,1,256]{3,1,2,0:T(8,128)(2,1)S(1)}, u32[]{:S(2)}, u32[]{:S(2)}) collective-permute-start(bf16[2,320,1,256]{3,1,2,0:T(8,128)(2,1)S(1)} %maximum_select_fusion), channel_id=1, source_target_pairs={{0,16},{16,32},{32,48},{48,64},{64,80},{80,96},{96,112},{112,128},... | collective-permute-start | bytes 983048 | tf_op jit(solution)/shard_map/ppermute | solution.py:210
  111.7 4.4 %collective-permute-done.17 = bf16[2,320,1,256]{3,1,2,0:T(8,128)(2,1)S(1)} collective-permute-done((bf16[2,320,1,256]{3,1,2,0:T(8,128)(2,1)S(1)}, bf16[2,320,1,256]{3,1,2,0:T(8,128)(2,1)S(1)}, u32[]{:S(2)}, u32[]{:S(2)}) %collective-permute-start.17) | collective-permute-done | bytes 327712 | tf_op jit(solution)/shard_map/ppermute | solution.py:210
  116.1 2.3 collective-permute-start.18
  120.0 4.3 %collective-permute-start.21 = (bf16[2,320,1,256]{3,1,2,0:T(8,128)(2,1)S(1)}, bf16[2,320,1,256]{3,1,2,0:T(8,128)(2,1)S(1)}, u32[]{:S(2)}, u32[]{:S(2)}) collective-permute-start(bf16[2,320,1,256]{3,1,2,0:T(8,128)(2,1)S(1)} %collective-permute-done.19), channel_id=1, source_target_pairs={{0,240},{16,0},{32,16},{48,32},{64,48},{80,64},{96,80},{112,96},{1... | collective-permute-start | bytes 983048 | tf_op jit(solution)/shard_map/ppermute | solution.py:213
  130.4 4.6 %collective-permute-start.23 = (bf16[2,320,1,256]{3,1,2,0:T(8,128)(2,1)S(1)}, bf16[2,320,1,256]{3,1,2,0:T(8,128)(2,1)S(1)}, u32[]{:S(2)}, u32[]{:S(2)}) collective-permute-start(bf16[2,320,1,256]{3,1,2,0:T(8,128)(2,1)S(1)} %collective-permute-done.21), channel_id=1, source_target_pairs={{0,240},{16,0},{32,16},{48,32},{64,48},{80,64},{96,80},{112,96},{1... | collective-permute-start | bytes 983048 | tf_op jit(solution)/shard_map/ppermute | solution.py:213
  140.5 5.5 %collective-permute-start.25 = (bf16[2,320,1,256]{3,1,2,0:T(8,128)(2,1)S(1)}, bf16[2,320,1,256]{3,1,2,0:T(8,128)(2,1)S(1)}, u32[]{:S(2)}, u32[]{:S(2)}) collective-permute-start(bf16[2,320,1,256]{3,1,2,0:T(8,128)(2,1)S(1)} %collective-permute-done.23), channel_id=1, source_target_pairs={{0,240},{16,0},{32,16},{48,32},{64,48},{80,64},{96,80},{112,96},{1... | collective-permute-start | bytes 983048 | tf_op jit(solution)/shard_map/ppermute | solution.py:213
  151.5 5.0 %collective-permute-start.27 = (bf16[2,320,1,256]{3,1,2,0:T(8,128)(2,1)S(1)}, bf16[2,320,1,256]{3,1,2,0:T(8,128)(2,1)S(1)}, u32[]{:S(2)}, u32[]{:S(2)}) collective-permute-start(bf16[2,320,1,256]{3,1,2,0:T(8,128)(2,1)S(1)} %collective-permute-done.25), channel_id=1, source_target_pairs={{0,240},{16,0},{32,16},{48,32},{64,48},{80,64},{96,80},{112,96},{1... | collective-permute-start | bytes 983048 | tf_op jit(solution)/shard_map/ppermute | solution.py:213
  162.1 5.0 %collective-permute-start.29 = (bf16[2,320,1,256]{3,1,2,0:T(8,128)(2,1)S(1)}, bf16[2,320,1,256]{3,1,2,0:T(8,128)(2,1)S(1)}, u32[]{:S(2)}, u32[]{:S(2)}) collective-permute-start(bf16[2,320,1,256]{3,1,2,0:T(8,128)(2,1)S(1)} %collective-permute-done.27), channel_id=1, source_target_pairs={{0,240},{16,0},{32,16},{48,32},{64,48},{80,64},{96,80},{112,96},{1... | collective-permute-start | bytes 983048 | tf_op jit(solution)/shard_map/ppermute | solution.py:213
  173.1 5.0 %collective-permute-start.30 = (bf16[2,320,1,256]{3,1,2,0:T(8,128)(2,1)S(1)}, bf16[2,320,1,256]{3,1,2,0:T(8,128)(2,1)S(1)}, u32[]{:S(2)}, u32[]{:S(2)}) collective-permute-start(bf16[2,320,1,256]{3,1,2,0:T(8,128)(2,1)S(1)} %collective-permute-done.29), channel_id=1, source_target_pairs={{0,240},{16,0},{32,16},{48,32},{64,48},{80,64},{96,80},{112,96},{1... | collective-permute-start | bytes 983048 | tf_op jit(solution)/shard_map/ppermute | solution.py:213
  182.6 5.0 %collective-permute-done.31 = bf16[2,320,1,256]{3,1,2,0:T(8,128)(2,1)S(1)} collective-permute-done((bf16[2,320,1,256]{3,1,2,0:T(8,128)(2,1)S(1)}, bf16[2,320,1,256]{3,1,2,0:T(8,128)(2,1)S(1)}, u32[]{:S(2)}, u32[]{:S(2)}) %collective-permute-start.31) | collective-permute-done | bytes 327712 | tf_op jit(solution)/shard_map/ppermute | solution.py:210
  190.3 22.3 %collective-permute-start.36 = (bf16[160,1536]{1,0:T(8,128)(2,1)S(1)}, bf16[160,1536]{1,0:T(8,128)(2,1)S(1)}, u32[]{:S(2)}, u32[]{:S(2)}) collective-permute-start(bf16[160,1536]{1,0:T(8,128)(2,1)S(1)} %dynamic-slice_convert_fusion), channel_id=1, source_target_pairs={{0,1},{1,0},{2,3},{3,2},{4,5},{5,4},{6,7},{7,6},{8,9},{9,8},{10,11... | collective-permute-start | bytes 1474568 | tf_op jit(solution)/shard_map/ppermute | solution.py:71
  215.2 3.1 %collective-permute-start.37 = (bf16[160,768]{1,0:T(8,128)(2,1)S(1)}, bf16[160,768]{1,0:T(8,128)(2,1)S(1)}, u32[]{:S(2)}, u32[]{:S(2)}) collective-permute-start(bf16[160,768]{1,0:T(8,128)(2,1)S(1)} %dynamic-slice_convert_fusion.2), channel_id=1, source_target_pairs={{0,2},{1,3},{2,0},{3,1},{4,6},{5,7},{6,4},{7,5},{8,10},{9,11},{10,... | collective-permute-start | bytes 737288 | tf_op jit(solution)/shard_map/ppermute | solution.py:71
  218.5 2.3 collective-permute-start.33
  220.8 3.3 %collective-permute-done.37 = bf16[160,768]{1,0:T(8,128)(2,1)S(1)} collective-permute-done((bf16[160,768]{1,0:T(8,128)(2,1)S(1)}, bf16[160,768]{1,0:T(8,128)(2,1)S(1)}, u32[]{:S(2)}, u32[]{:S(2)}) %collective-permute-start.37) | collective-permute-done | bytes 245792 | tf_op jit(solution)/shard_map/ppermute | solution.py:71
  224.2 4.6 %collective-permute-start.38 = (bf16[160,384]{1,0:T(8,128)(2,1)S(1)}, bf16[160,384]{1,0:T(8,128)(2,1)S(1)}, u32[]{:S(2)}, u32[]{:S(2)}) collective-permute-start(bf16[160,384]{1,0:T(8,128)(2,1)S(1)} %dynamic-slice_convert_fusion.4), channel_id=1, source_target_pairs={{0,4},{1,5},{2,6},{3,7},{4,0},{5,1},{6,2},{7,3},{8,12},{9,13},{10,... | collective-permute-start | bytes 368648 | tf_op jit(solution)/shard_map/ppermute | solution.py:71
  228.9 2.2 collective-permute-start.34
  231.5 2.3 collective-permute-start.39
  234.7 4.0 %collective-permute-start.35 = (bf16[160,192]{1,0:T(8,128)(2,1)S(1)}, bf16[160,192]{1,0:T(8,128)(2,1)S(1)}, u32[]{:S(2)}, u32[]{:S(2)}) collective-permute-start(bf16[160,192]{1,0:T(8,128)(2,1)S(1)} %dynamic-slice_convert_fusion.7), channel_id=1, source_target_pairs={{0,4},{1,5},{2,6},{3,7},{4,0},{5,1},{6,2},{7,3},{8,12},{9,13},{10,... | collective-permute-start | bytes 184328 | tf_op jit(solution)/shard_map/ppermute | solution.py:71
  238.9 2.5 %collective-permute-done.35 = bf16[160,192]{1,0:T(8,128)(2,1)S(1)} collective-permute-done((bf16[160,192]{1,0:T(8,128)(2,1)S(1)}, bf16[160,192]{1,0:T(8,128)(2,1)S(1)}, u32[]{:S(2)}, u32[]{:S(2)}) %collective-permute-start.35) | collective-permute-done | bytes 61472 | tf_op jit(solution)/shard_map/ppermute | solution.py:71
  (236 shorter events, 87.0 us)
Async XLA Ops:
  2.3 15.4 %collective-permute-start = (bf16[104,512]{1,0:T(8,128)(2,1)S(1)}, bf16[104,512]{1,0:T(8,128)(2,1)S(1)}, u32[]{:S(2)}, u32[]{:S(2)}) collective-permute-start(bf16[104,512]{1,0:T(8,128)(2,1)S(1)} %get-tuple-element.155), channel_id=1, source_target_pairs={{0,256},{16,272},{32,288},{48,304},{64,320},{80,336},{96,352},{112... | collective-permute-start | bytes 319496 | tf_op jit(solution)/shard_map/ppermute | solution.py:34
  9.1 20.4 %collective-permute-start.40 = (bf16[320,192]{1,0:T(8,128)(2,1)S(1)}, bf16[320,192]{1,0:T(8,128)(2,1)S(1)}, u32[]{:S(2)}, u32[]{:S(2)}) collective-permute-start(bf16[320,192]{1,0:T(8,128)(2,1)S(1)} %constant_dynamic-slice_fusion), channel_id=1, source_target_pairs={{0,16},{16,32},{32,48},{48,64},{64,80},{80,96},{96,112},{112,128},... | collective-permute-start | bytes 368648 | tf_op jit(solution)/shard_map/ppermute | solution.py:19
  17.8 14.1 %collective-permute-start.1 = (bf16[2,104,512]{2,1,0:T(8,128)(2,1)S(1)}, bf16[2,104,512]{2,1,0:T(8,128)(2,1)S(1)}, u32[]{:S(2)}, u32[]{:S(2)}) collective-permute-start(bf16[2,104,512]{2,1,0:T(8,128)(2,1)S(1)} %maximum_select_fusion.2), channel_id=1, source_target_pairs={{0,16},{16,32},{32,48},{48,64},{64,80},{80,96},{96,112},{112,128},... | collective-permute-start | bytes 638984 | tf_op jit(solution)/shard_map/ppermute | solution.py:45
  21.3 12.5 %collective-permute-start.2 = (bf16[2,104,512]{2,1,0:T(8,128)(2,1)S(1)}, bf16[2,104,512]{2,1,0:T(8,128)(2,1)S(1)}, u32[]{:S(2)}, u32[]{:S(2)}) collective-permute-start(bf16[2,104,512]{2,1,0:T(8,128)(2,1)S(1)} %maximum_select_fusion.2), channel_id=1, source_target_pairs={{0,240},{16,0},{32,16},{48,32},{64,48},{80,64},{96,80},{112,96},{1... | collective-permute-start | bytes 638984 | tf_op jit(solution)/shard_map/ppermute | solution.py:48
  31.9 8.3 %collective-permute-start.3 = (bf16[2,104,512]{2,1,0:T(8,128)(2,1)S(1)}, bf16[2,104,512]{2,1,0:T(8,128)(2,1)S(1)}, u32[]{:S(2)}, u32[]{:S(2)}) collective-permute-start(bf16[2,104,512]{2,1,0:T(8,128)(2,1)S(1)} %collective-permute-done.1), channel_id=1, source_target_pairs={{0,16},{16,32},{32,48},{48,64},{64,80},{80,96},{96,112},{112,128},... | collective-permute-start | bytes 638984 | tf_op jit(solution)/shard_map/ppermute | solution.py:45
  33.9 8.3 %collective-permute-start.4 = (bf16[2,104,512]{2,1,0:T(8,128)(2,1)S(1)}, bf16[2,104,512]{2,1,0:T(8,128)(2,1)S(1)}, u32[]{:S(2)}, u32[]{:S(2)}) collective-permute-start(bf16[2,104,512]{2,1,0:T(8,128)(2,1)S(1)} %collective-permute-done.2), channel_id=1, source_target_pairs={{0,240},{16,0},{32,16},{48,32},{64,48},{80,64},{96,80},{112,96},{1... | collective-permute-start | bytes 638984 | tf_op jit(solution)/shard_map/ppermute | solution.py:48
  40.2 7.8 %collective-permute-start.5 = (bf16[2,104,512]{2,1,0:T(8,128)(2,1)S(1)}, bf16[2,104,512]{2,1,0:T(8,128)(2,1)S(1)}, u32[]{:S(2)}, u32[]{:S(2)}) collective-permute-start(bf16[2,104,512]{2,1,0:T(8,128)(2,1)S(1)} %collective-permute-done.3), channel_id=1, source_target_pairs={{0,16},{16,32},{32,48},{48,64},{64,80},{80,96},{96,112},{112,128},... | collective-permute-start | bytes 638984 | tf_op jit(solution)/shard_map/ppermute | solution.py:45
  42.2 7.8 %collective-permute-start.6 = (bf16[2,104,512]{2,1,0:T(8,128)(2,1)S(1)}, bf16[2,104,512]{2,1,0:T(8,128)(2,1)S(1)}, u32[]{:S(2)}, u32[]{:S(2)}) collective-permute-start(bf16[2,104,512]{2,1,0:T(8,128)(2,1)S(1)} %collective-permute-done.4), channel_id=1, source_target_pairs={{0,240},{16,0},{32,16},{48,32},{64,48},{80,64},{96,80},{112,96},{1... | collective-permute-start | bytes 638984 | tf_op jit(solution)/shard_map/ppermute | solution.py:48
  48.0 7.8 %collective-permute-start.7 = (bf16[2,104,512]{2,1,0:T(8,128)(2,1)S(1)}, bf16[2,104,512]{2,1,0:T(8,128)(2,1)S(1)}, u32[]{:S(2)}, u32[]{:S(2)}) collective-permute-start(bf16[2,104,512]{2,1,0:T(8,128)(2,1)S(1)} %collective-permute-done.5), channel_id=1, source_target_pairs={{0,16},{16,32},{32,48},{48,64},{64,80},{80,96},{96,112},{112,128},... | collective-permute-start | bytes 638984 | tf_op jit(solution)/shard_map/ppermute | solution.py:45
  55.8 7.8 %collective-permute-start.9 = (bf16[2,104,512]{2,1,0:T(8,128)(2,1)S(1)}, bf16[2,104,512]{2,1,0:T(8,128)(2,1)S(1)}, u32[]{:S(2)}, u32[]{:S(2)}) collective-permute-start(bf16[2,104,512]{2,1,0:T(8,128)(2,1)S(1)} %collective-permute-done.7), channel_id=1, source_target_pairs={{0,16},{16,32},{32,48},{48,64},{64,80},{80,96},{96,112},{112,128},... | collective-permute-start | bytes 638984 | tf_op jit(solution)/shard_map/ppermute | solution.py:45
  63.6 7.8 %collective-permute-start.11 = (bf16[2,104,512]{2,1,0:T(8,128)(2,1)S(1)}, bf16[2,104,512]{2,1,0:T(8,128)(2,1)S(1)}, u32[]{:S(2)}, u32[]{:S(2)}) collective-permute-start(bf16[2,104,512]{2,1,0:T(8,128)(2,1)S(1)} %collective-permute-done.9), channel_id=1, source_target_pairs={{0,16},{16,32},{32,48},{48,64},{64,80},{80,96},{96,112},{112,128},... | collective-permute-start | bytes 638984 | tf_op jit(solution)/shard_map/ppermute | solution.py:45
  71.4 8.7 %collective-permute-start.13 = (bf16[2,104,512]{2,1,0:T(8,128)(2,1)S(1)}, bf16[2,104,512]{2,1,0:T(8,128)(2,1)S(1)}, u32[]{:S(2)}, u32[]{:S(2)}) collective-permute-start(bf16[2,104,512]{2,1,0:T(8,128)(2,1)S(1)} %collective-permute-done.11), channel_id=1, source_target_pairs={{0,16},{16,32},{32,48},{48,64},{64,80},{80,96},{96,112},{112,128},... | collective-permute-start | bytes 638984 | tf_op jit(solution)/shard_map/ppermute | solution.py:45
  73.3 8.7 %collective-permute-start.14 = (bf16[2,104,512]{2,1,0:T(8,128)(2,1)S(1)}, bf16[2,104,512]{2,1,0:T(8,128)(2,1)S(1)}, u32[]{:S(2)}, u32[]{:S(2)}) collective-permute-start(bf16[2,104,512]{2,1,0:T(8,128)(2,1)S(1)} %collective-permute-done.12), channel_id=1, source_target_pairs={{0,240},{16,0},{32,16},{48,32},{64,48},{80,64},{96,80},{112,96},{1... | collective-permute-start | bytes 638984 | tf_op jit(solution)/shard_map/ppermute | solution.py:48
  80.0 9.8 %collective-permute-start.15 = (bf16[2,104,512]{2,1,0:T(8,128)(2,1)S(1)}, bf16[2,104,512]{2,1,0:T(8,128)(2,1)S(1)}, u32[]{:S(2)}, u32[]{:S(2)}) collective-permute-start(bf16[2,104,512]{2,1,0:T(8,128)(2,1)S(1)} %collective-permute-done.13), channel_id=1, source_target_pairs={{0,16},{16,32},{32,48},{48,64},{64,80},{80,96},{96,112},{112,128},... | collective-permute-start | bytes 638984 | tf_op jit(solution)/shard_map/ppermute | solution.py:45
  105.1 13.3 %collective-permute-start.19 = (bf16[2,320,1,256]{3,1,2,0:T(8,128)(2,1)S(1)}, bf16[2,320,1,256]{3,1,2,0:T(8,128)(2,1)S(1)}, u32[]{:S(2)}, u32[]{:S(2)}) collective-permute-start(bf16[2,320,1,256]{3,1,2,0:T(8,128)(2,1)S(1)} %maximum_select_fusion), channel_id=1, source_target_pairs={{0,240},{16,0},{32,16},{48,32},{64,48},{80,64},{96,80},{112,96},{1... | collective-permute-start | bytes 983048 | tf_op jit(solution)/shard_map/ppermute | solution.py:213
  107.0 9.0 %collective-permute-start.17 = (bf16[2,320,1,256]{3,1,2,0:T(8,128)(2,1)S(1)}, bf16[2,320,1,256]{3,1,2,0:T(8,128)(2,1)S(1)}, u32[]{:S(2)}, u32[]{:S(2)}) collective-permute-start(bf16[2,320,1,256]{3,1,2,0:T(8,128)(2,1)S(1)} %maximum_select_fusion), channel_id=1, source_target_pairs={{0,16},{16,32},{32,48},{48,64},{64,80},{80,96},{96,112},{112,128},... | collective-permute-start | bytes 983048 | tf_op jit(solution)/shard_map/ppermute | solution.py:210
  116.1 10.9 %collective-permute-start.18 = (bf16[2,320,1,256]{3,1,2,0:T(8,128)(2,1)S(1)}, bf16[2,320,1,256]{3,1,2,0:T(8,128)(2,1)S(1)}, u32[]{:S(2)}, u32[]{:S(2)}) collective-permute-start(bf16[2,320,1,256]{3,1,2,0:T(8,128)(2,1)S(1)} %collective-permute-done.17), channel_id=1, source_target_pairs={{0,16},{16,32},{32,48},{48,64},{64,80},{80,96},{96,112},{112,128},... | collective-permute-start | bytes 983048 | tf_op jit(solution)/shard_map/ppermute | solution.py:210
  120.0 8.9 %collective-permute-start.21 = (bf16[2,320,1,256]{3,1,2,0:T(8,128)(2,1)S(1)}, bf16[2,320,1,256]{3,1,2,0:T(8,128)(2,1)S(1)}, u32[]{:S(2)}, u32[]{:S(2)}) collective-permute-start(bf16[2,320,1,256]{3,1,2,0:T(8,128)(2,1)S(1)} %collective-permute-done.19), channel_id=1, source_target_pairs={{0,240},{16,0},{32,16},{48,32},{64,48},{80,64},{96,80},{112,96},{1... | collective-permute-start | bytes 983048 | tf_op jit(solution)/shard_map/ppermute | solution.py:213
  126.9 9.9 %collective-permute-start.20 = (bf16[2,320,1,256]{3,1,2,0:T(8,128)(2,1)S(1)}, bf16[2,320,1,256]{3,1,2,0:T(8,128)(2,1)S(1)}, u32[]{:S(2)}, u32[]{:S(2)}) collective-permute-start(bf16[2,320,1,256]{3,1,2,0:T(8,128)(2,1)S(1)} %collective-permute-done.18), channel_id=1, source_target_pairs={{0,16},{16,32},{32,48},{48,64},{64,80},{80,96},{96,112},{112,128},... | collective-permute-start | bytes 983048 | tf_op jit(solution)/shard_map/ppermute | solution.py:210
  130.4 8.6 %collective-permute-start.23 = (bf16[2,320,1,256]{3,1,2,0:T(8,128)(2,1)S(1)}, bf16[2,320,1,256]{3,1,2,0:T(8,128)(2,1)S(1)}, u32[]{:S(2)}, u32[]{:S(2)}) collective-permute-start(bf16[2,320,1,256]{3,1,2,0:T(8,128)(2,1)S(1)} %collective-permute-done.21), channel_id=1, source_target_pairs={{0,240},{16,0},{32,16},{48,32},{64,48},{80,64},{96,80},{112,96},{1... | collective-permute-start | bytes 983048 | tf_op jit(solution)/shard_map/ppermute | solution.py:213
  136.9 9.9 %collective-permute-start.22 = (bf16[2,320,1,256]{3,1,2,0:T(8,128)(2,1)S(1)}, bf16[2,320,1,256]{3,1,2,0:T(8,128)(2,1)S(1)}, u32[]{:S(2)}, u32[]{:S(2)}) collective-permute-start(bf16[2,320,1,256]{3,1,2,0:T(8,128)(2,1)S(1)} %collective-permute-done.20), channel_id=1, source_target_pairs={{0,16},{16,32},{32,48},{48,64},{64,80},{80,96},{96,112},{112,128},... | collective-permute-start | bytes 983048 | tf_op jit(solution)/shard_map/ppermute | solution.py:210
  140.5 9.5 %collective-permute-start.25 = (bf16[2,320,1,256]{3,1,2,0:T(8,128)(2,1)S(1)}, bf16[2,320,1,256]{3,1,2,0:T(8,128)(2,1)S(1)}, u32[]{:S(2)}, u32[]{:S(2)}) collective-permute-start(bf16[2,320,1,256]{3,1,2,0:T(8,128)(2,1)S(1)} %collective-permute-done.23), channel_id=1, source_target_pairs={{0,240},{16,0},{32,16},{48,32},{64,48},{80,64},{96,80},{112,96},{1... | collective-permute-start | bytes 983048 | tf_op jit(solution)/shard_map/ppermute | solution.py:213
  146.8 10.6 %collective-permute-start.24 = (bf16[2,320,1,256]{3,1,2,0:T(8,128)(2,1)S(1)}, bf16[2,320,1,256]{3,1,2,0:T(8,128)(2,1)S(1)}, u32[]{:S(2)}, u32[]{:S(2)}) collective-permute-start(bf16[2,320,1,256]{3,1,2,0:T(8,128)(2,1)S(1)} %collective-permute-done.22), channel_id=1, source_target_pairs={{0,16},{16,32},{32,48},{48,64},{64,80},{80,96},{96,112},{112,128},... | collective-permute-start | bytes 983048 | tf_op jit(solution)/shard_map/ppermute | solution.py:210
  151.5 9.1 %collective-permute-start.27 = (bf16[2,320,1,256]{3,1,2,0:T(8,128)(2,1)S(1)}, bf16[2,320,1,256]{3,1,2,0:T(8,128)(2,1)S(1)}, u32[]{:S(2)}, u32[]{:S(2)}) collective-permute-start(bf16[2,320,1,256]{3,1,2,0:T(8,128)(2,1)S(1)} %collective-permute-done.25), channel_id=1, source_target_pairs={{0,240},{16,0},{32,16},{48,32},{64,48},{80,64},{96,80},{112,96},{1... | collective-permute-start | bytes 983048 | tf_op jit(solution)/shard_map/ppermute | solution.py:213
  157.4 10.6 %collective-permute-start.26 = (bf16[2,320,1,256]{3,1,2,0:T(8,128)(2,1)S(1)}, bf16[2,320,1,256]{3,1,2,0:T(8,128)(2,1)S(1)}, u32[]{:S(2)}, u32[]{:S(2)}) collective-permute-start(bf16[2,320,1,256]{3,1,2,0:T(8,128)(2,1)S(1)} %collective-permute-done.24), channel_id=1, source_target_pairs={{0,16},{16,32},{32,48},{48,64},{64,80},{80,96},{96,112},{112,128},... | collective-permute-start | bytes 983048 | tf_op jit(solution)/shard_map/ppermute | solution.py:210
  162.1 9.0 %collective-permute-start.29 = (bf16[2,320,1,256]{3,1,2,0:T(8,128)(2,1)S(1)}, bf16[2,320,1,256]{3,1,2,0:T(8,128)(2,1)S(1)}, u32[]{:S(2)}, u32[]{:S(2)}) collective-permute-start(bf16[2,320,1,256]{3,1,2,0:T(8,128)(2,1)S(1)} %collective-permute-done.27), channel_id=1, source_target_pairs={{0,240},{16,0},{32,16},{48,32},{64,48},{80,64},{96,80},{112,96},{1... | collective-permute-start | bytes 983048 | tf_op jit(solution)/shard_map/ppermute | solution.py:213
  168.0 10.6 %collective-permute-start.28 = (bf16[2,320,1,256]{3,1,2,0:T(8,128)(2,1)S(1)}, bf16[2,320,1,256]{3,1,2,0:T(8,128)(2,1)S(1)}, u32[]{:S(2)}, u32[]{:S(2)}) collective-permute-start(bf16[2,320,1,256]{3,1,2,0:T(8,128)(2,1)S(1)} %collective-permute-done.26), channel_id=1, source_target_pairs={{0,16},{16,32},{32,48},{48,64},{64,80},{80,96},{96,112},{112,128},... | collective-permute-start | bytes 983048 | tf_op jit(solution)/shard_map/ppermute | solution.py:210
  173.1 9.0 %collective-permute-start.30 = (bf16[2,320,1,256]{3,1,2,0:T(8,128)(2,1)S(1)}, bf16[2,320,1,256]{3,1,2,0:T(8,128)(2,1)S(1)}, u32[]{:S(2)}, u32[]{:S(2)}) collective-permute-start(bf16[2,320,1,256]{3,1,2,0:T(8,128)(2,1)S(1)} %collective-permute-done.29), channel_id=1, source_target_pairs={{0,240},{16,0},{32,16},{48,32},{64,48},{80,64},{96,80},{112,96},{1... | collective-permute-start | bytes 983048 | tf_op jit(solution)/shard_map/ppermute | solution.py:213
  178.5 9.0 %collective-permute-start.31 = (bf16[2,320,1,256]{3,1,2,0:T(8,128)(2,1)S(1)}, bf16[2,320,1,256]{3,1,2,0:T(8,128)(2,1)S(1)}, u32[]{:S(2)}, u32[]{:S(2)}) collective-permute-start(bf16[2,320,1,256]{3,1,2,0:T(8,128)(2,1)S(1)} %collective-permute-done.28), channel_id=1, source_target_pairs={{0,16},{16,32},{32,48},{48,64},{64,80},{80,96},{96,112},{112,128},... | collective-permute-start | bytes 983048 | tf_op jit(solution)/shard_map/ppermute | solution.py:210
  190.3 24.7 %collective-permute-start.36 = (bf16[160,1536]{1,0:T(8,128)(2,1)S(1)}, bf16[160,1536]{1,0:T(8,128)(2,1)S(1)}, u32[]{:S(2)}, u32[]{:S(2)}) collective-permute-start(bf16[160,1536]{1,0:T(8,128)(2,1)S(1)} %dynamic-slice_convert_fusion), channel_id=1, source_target_pairs={{0,1},{1,0},{2,3},{3,2},{4,5},{5,4},{6,7},{7,6},{8,9},{9,8},{10,11... | collective-permute-start | bytes 1474568 | tf_op jit(solution)/shard_map/ppermute | solution.py:71
  215.2 8.9 %collective-permute-start.37 = (bf16[160,768]{1,0:T(8,128)(2,1)S(1)}, bf16[160,768]{1,0:T(8,128)(2,1)S(1)}, u32[]{:S(2)}, u32[]{:S(2)}) collective-permute-start(bf16[160,768]{1,0:T(8,128)(2,1)S(1)} %dynamic-slice_convert_fusion.2), channel_id=1, source_target_pairs={{0,2},{1,3},{2,0},{3,1},{4,6},{5,7},{6,4},{7,5},{8,10},{9,11},{10,... | collective-permute-start | bytes 737288 | tf_op jit(solution)/shard_map/ppermute | solution.py:71
  218.5 10.3 %collective-permute-start.33 = (bf16[160,768]{1,0:T(8,128)(2,1)S(1)}, bf16[160,768]{1,0:T(8,128)(2,1)S(1)}, u32[]{:S(2)}, u32[]{:S(2)}) collective-permute-start(bf16[160,768]{1,0:T(8,128)(2,1)S(1)} %dynamic-slice_convert_fusion.3), channel_id=1, source_target_pairs={{0,8},{1,9},{2,10},{3,11},{4,12},{5,13},{6,14},{7,15},{8,0},{9,1},... | collective-permute-start | bytes 737288 | tf_op jit(solution)/shard_map/ppermute | solution.py:71
  (17 other events, 133.8 us)

commit v8 on v7

--- a/solution.py
+++ b/solution.py
@@ -59,20 +59,42 @@
     return gathered.reshape((2 * ring * block.shape[0],) + block.shape[1:])
 
 
-def halving_scatter(partial, axis, order):
+def halving_scatter(parts, axis, orders):
     size = lax.axis_size(axis)
     position = lax.axis_index(axis)
-    state = partial
-    for bit in order:
-        half = state.shape[1] // 2
-        mine = (position >> bit) & 1
-        keep = lax.dynamic_slice_in_dim(state, mine * half, half, 1)
-        send = lax.dynamic_slice_in_dim(state, (1 - mine) * half, half, 1)
-        got = lax.ppermute(
-            send.astype(jnp.bfloat16), axis, [(i, i ^ (1 << bit)) for i in range(size)]
-        )
-        state = keep + got.astype(jnp.float32)
-    return state
+    states = list(parts)
+    for stage in range(len(orders[0])):
+        keeps = []
+        sends = []
+        for index, state in enumerate(states):
+            bit = orders[index][stage]
+            half = state.shape[1] // 2
+            mine = (position >> bit) & 1
+            keeps.append(lax.dynamic_slice_in_dim(state, mine * half, half, 1))
+            sends.append(lax.dynamic_slice_in_dim(state, (1 - mine) * half, half, 1))
+        stage_bits = [order[stage] for order in orders]
+        if len(set(stage_bits)) == 1:
+            bit = stage_bits[0]
+            joined = lax.ppermute(
+                jnp.concatenate(sends, axis=0).astype(jnp.bfloat16),
+                axis,
+                [(i, i ^ (1 << bit)) for i in range(size)],
+            )
+            bounds = [0]
+            for send in sends:
+                bounds.append(bounds[-1] + send.shape[0])
+            got = [joined[bounds[i] : bounds[i + 1]] for i in range(len(sends))]
+        else:
+            got = [
+                lax.ppermute(
+                    send.astype(jnp.bfloat16),
+                    axis,
+                    [(i, i ^ (1 << bit)) for i in range(size)],
+                )
+                for send, bit in zip(sends, stage_bits)
+            ]
+        states = [keep + g.astype(jnp.float32) for keep, g in zip(keeps, got)]
+    return states
 
 
 def attend_piece(state_now, kv_piece, key_frame, queries, query_frame, query_first, head_dim):
@@ -223,21 +245,26 @@
     bits = size.bit_length() - 1
     middle = list(range(1, bits - 1))
     half_rows = tok_rows // 2
-    orders = [[0, bits - 1] + middle, [0] + middle + [bits - 1]]
-    head_parts = []
+    if bits == 4:
+        orders = [[0, 3, 1, 2], [0, 1, 3, 2]]
+    else:
+        orders = [[0, bits - 1] + middle, [0] + middle + [bits - 1]]
+    partials = []
     for part, order in enumerate(orders):
         by_bit = o_piece.reshape((2,) * bits + (full_rows // size,) + o_piece.shape[1:])
         permuted = jnp.transpose(
             by_bit,
             [bits - 1 - bit for bit in order] + list(range(bits, by_bit.ndim)),
         )
-        partial_out = jnp.einsum(
-            "nhe,rhe->nr",
-            attended[part * half_rows : (part + 1) * half_rows],
-            permuted.reshape(o_piece.shape),
-            preferred_element_type=jnp.float32,
+        partials.append(
+            jnp.einsum(
+                "nhe,rhe->nr",
+                attended[part * half_rows : (part + 1) * half_rows],
+                permuted.reshape(o_piece.shape),
+                preferred_element_type=jnp.float32,
+            )
         )
-        head_parts.append(halving_scatter(partial_out, "fsdp", order))
+    head_parts = halving_scatter(partials, "fsdp", orders)
     head_total = jnp.concatenate(head_parts, axis=0)
     own_chan = lax.dynamic_slice_in_dim(latents, column * chan_here, chan_here, 1)
     before = passed_along(own_chan, "ctx", 1)

time: 247 us -> 255 us (1.032)
  the two profiles are of different devices: /device:TPU:1 before, /device:TPU:16 now
where the time goes in v8:
time: 255 us; the launch traced here: 254 us
  starting transfers between devices  141 us (55%)
  waiting for transfers between devices  67 us (26%)
  other arithmetic  17.3 us (7%)
  matrix products  15.6 us (6%)
  local copies, waits for them, and re-layouts  10.6 us (4%)
    ppermute x7, starting transfers between devices, ring_pieces(): behind = lax.ppermute(behind, axis, backward)  39 us
    ppermute x7, starting transfers between devices, per_device(): behind = lax.ppermute(behind, 'ctx', backward)  35.2 us
    ppermute x8, waiting for transfers between devices, ring_pieces(): ahead = lax.ppermute(ahead, axis, forward)  23 us
    ppermute x8, starting transfers between devices, per_device(): ahead = lax.ppermute(ahead, 'ctx', forward)  17.6 us
    ppermute x8, starting transfers between devices, ring_pieces(): ahead = lax.ppermute(ahead, axis, forward)  15.3 us
    ppermute x4, starting transfers between devices, halving_scatter(): lax.ppermute(send.astype(jnp.bfloat16), axis, [(i, i ^ 1 << bit) for i in...  13.8 us
    ppermute x8, waiting for transfers between devices, per_device(): ahead = lax.ppermute(ahead, 'ctx', forward)  11.9 us
    ppermute x1, waiting for transfers between devices, passed_along(): return lax.ppermute(block, axis, route)  9.93 us
  transfers between devices with their start and end apart: 39, of which 23 were waited for; matrix products, arithmetic and copies ran while one was open for 10% of the time, Pallas kernels for 0%

profile of v8, /device:TPU:16, one launch (start us, length us, event | category | flops | bytes accessed | tf_op | source)
XLA Modules:
  0.0 253.7 jit_solution(5609044734055724666)
XLA Ops:
  2.3 7.6 %collective-permute-start = (bf16[104,512]{1,0:T(8,128)(2,1)S(1)}, bf16[104,512]{1,0:T(8,128)(2,1)S(1)}, u32[]{:S(2)}, u32[]{:S(2)}) collective-permute-start(bf16[104,512]{1,0:T(8,128)(2,1)S(1)} %get-tuple-element.159), channel_id=1, source_target_pairs={{0,256},{16,272},{32,288},{48,304},{64,320},{80,336},{96,352},{112... | collective-permute-start | bytes 319496 | tf_op jit(solution)/shard_map/ppermute | solution.py:34
  16.4 7.4 %collective-permute-start.2 = (bf16[2,104,512]{2,1,0:T(8,128)(2,1)S(1)}, bf16[2,104,512]{2,1,0:T(8,128)(2,1)S(1)}, u32[]{:S(2)}, u32[]{:S(2)}) collective-permute-start(bf16[2,104,512]{2,1,0:T(8,128)(2,1)S(1)} %maximum_select_fusion.2), channel_id=1, source_target_pairs={{0,240},{16,0},{32,16},{48,32},{64,48},{80,64},{96,80},{112,96},{1... | collective-permute-start | bytes 638984 | tf_op jit(solution)/shard_map/ppermute | solution.py:48
  27.9 5.1 %collective-permute-start.4 = (bf16[2,104,512]{2,1,0:T(8,128)(2,1)S(1)}, bf16[2,104,512]{2,1,0:T(8,128)(2,1)S(1)}, u32[]{:S(2)}, u32[]{:S(2)}) collective-permute-start(bf16[2,104,512]{2,1,0:T(8,128)(2,1)S(1)} %collective-permute-done.2), channel_id=1, source_target_pairs={{0,240},{16,0},{32,16},{48,32},{64,48},{80,64},{96,80},{112,96},{1... | collective-permute-start | bytes 638984 | tf_op jit(solution)/shard_map/ppermute | solution.py:48
  36.8 5.1 %collective-permute-start.6 = (bf16[2,104,512]{2,1,0:T(8,128)(2,1)S(1)}, bf16[2,104,512]{2,1,0:T(8,128)(2,1)S(1)}, u32[]{:S(2)}, u32[]{:S(2)}) collective-permute-start(bf16[2,104,512]{2,1,0:T(8,128)(2,1)S(1)} %collective-permute-done.4), channel_id=1, source_target_pairs={{0,240},{16,0},{32,16},{48,32},{64,48},{80,64},{96,80},{112,96},{1... | collective-permute-start | bytes 638984 | tf_op jit(solution)/shard_map/ppermute | solution.py:48
  45.7 5.1 %collective-permute-start.8 = (bf16[2,104,512]{2,1,0:T(8,128)(2,1)S(1)}, bf16[2,104,512]{2,1,0:T(8,128)(2,1)S(1)}, u32[]{:S(2)}, u32[]{:S(2)}) collective-permute-start(bf16[2,104,512]{2,1,0:T(8,128)(2,1)S(1)} %collective-permute-done.6), channel_id=1, source_target_pairs={{0,240},{16,0},{32,16},{48,32},{64,48},{80,64},{96,80},{112,96},{1... | collective-permute-start | bytes 638984 | tf_op jit(solution)/shard_map/ppermute | solution.py:48
  54.7 5.1 %collective-permute-start.10 = (bf16[2,104,512]{2,1,0:T(8,128)(2,1)S(1)}, bf16[2,104,512]{2,1,0:T(8,128)(2,1)S(1)}, u32[]{:S(2)}, u32[]{:S(2)}) collective-permute-start(bf16[2,104,512]{2,1,0:T(8,128)(2,1)S(1)} %collective-permute-done.8), channel_id=1, source_target_pairs={{0,240},{16,0},{32,16},{48,32},{64,48},{80,64},{96,80},{112,96},{1... | collective-permute-start | bytes 638984 | tf_op jit(solution)/shard_map/ppermute | solution.py:48
  59.9 2.6 %collective-permute-done.9 = bf16[2,104,512]{2,1,0:T(8,128)(2,1)S(1)} collective-permute-done((bf16[2,104,512]{2,1,0:T(8,128)(2,1)S(1)}, bf16[2,104,512]{2,1,0:T(8,128)(2,1)S(1)}, u32[]{:S(2)}, u32[]{:S(2)}) %collective-permute-start.9) | collective-permute-done | bytes 213024 | tf_op jit(solution)/shard_map/ppermute | solution.py:45
  64.4 5.4 %collective-permute-start.12 = (bf16[2,104,512]{2,1,0:T(8,128)(2,1)S(1)}, bf16[2,104,512]{2,1,0:T(8,128)(2,1)S(1)}, u32[]{:S(2)}, u32[]{:S(2)}) collective-permute-start(bf16[2,104,512]{2,1,0:T(8,128)(2,1)S(1)} %collective-permute-done.10), channel_id=1, source_target_pairs={{0,240},{16,0},{32,16},{48,32},{64,48},{80,64},{96,80},{112,96},{1... | collective-permute-start | bytes 638984 | tf_op jit(solution)/shard_map/ppermute | solution.py:48
  70.0 3.5 %collective-permute-done.11 = bf16[2,104,512]{2,1,0:T(8,128)(2,1)S(1)} collective-permute-done((bf16[2,104,512]{2,1,0:T(8,128)(2,1)S(1)}, bf16[2,104,512]{2,1,0:T(8,128)(2,1)S(1)}, u32[]{:S(2)}, u32[]{:S(2)}) %collective-permute-start.11) | collective-permute-done | bytes 213024 | tf_op jit(solution)/shard_map/ppermute | solution.py:45
  75.5 5.6 %collective-permute-start.14 = (bf16[2,104,512]{2,1,0:T(8,128)(2,1)S(1)}, bf16[2,104,512]{2,1,0:T(8,128)(2,1)S(1)}, u32[]{:S(2)}, u32[]{:S(2)}) collective-permute-start(bf16[2,104,512]{2,1,0:T(8,128)(2,1)S(1)} %collective-permute-done.12), channel_id=1, source_target_pairs={{0,240},{16,0},{32,16},{48,32},{64,48},{80,64},{96,80},{112,96},{1... | collective-permute-start | bytes 638984 | tf_op jit(solution)/shard_map/ppermute | solution.py:48
  81.2 2.6 %collective-permute-done.13 = bf16[2,104,512]{2,1,0:T(8,128)(2,1)S(1)} collective-permute-done((bf16[2,104,512]{2,1,0:T(8,128)(2,1)S(1)}, bf16[2,104,512]{2,1,0:T(8,128)(2,1)S(1)}, u32[]{:S(2)}, u32[]{:S(2)}) %collective-permute-start.13) | collective-permute-done | bytes 213024 | tf_op jit(solution)/shard_map/ppermute | solution.py:45
  85.8 7.0 %collective-permute-done.15 = bf16[2,104,512]{2,1,0:T(8,128)(2,1)S(1)} collective-permute-done((bf16[2,104,512]{2,1,0:T(8,128)(2,1)S(1)}, bf16[2,104,512]{2,1,0:T(8,128)(2,1)S(1)}, u32[]{:S(2)}, u32[]{:S(2)}) %collective-permute-start.15) | collective-permute-done | bytes 213024 | tf_op jit(solution)/shard_map/ppermute | solution.py:45
  100.4 3.4 %collective-permute-start.16 = (bf16[320,1,256]{2,0,1:T(8,128)(2,1)S(1)}, bf16[320,1,256]{2,0,1:T(8,128)(2,1)S(1)}, u32[]{:S(2)}, u32[]{:S(2)}) collective-permute-start(bf16[320,1,256]{2,0,1:T(8,128)(2,1)S(1)} %get-tuple-element.154), channel_id=1, source_target_pairs={{0,256},{16,272},{32,288},{48,304},{64,320},{80,336},{96,352},{112... | collective-permute-start | bytes 491528 | tf_op jit(solution)/shard_map/ppermute | solution.py:201
  105.5 3.6 %collective-permute-done.16 = bf16[320,1,256]{2,0,1:T(8,128)(2,1)S(1)} collective-permute-done((bf16[320,1,256]{2,0,1:T(8,128)(2,1)S(1)}, bf16[320,1,256]{2,0,1:T(8,128)(2,1)S(1)}, u32[]{:S(2)}, u32[]{:S(2)}) %collective-permute-start.16) | collective-permute-done | bytes 163872 | tf_op jit(solution)/shard_map/ppermute | solution.py:201
  111.1 3.9 %collective-permute-start.17 = (bf16[2,320,1,256]{3,1,2,0:T(8,128)(2,1)S(1)}, bf16[2,320,1,256]{3,1,2,0:T(8,128)(2,1)S(1)}, u32[]{:S(2)}, u32[]{:S(2)}) collective-permute-start(bf16[2,320,1,256]{3,1,2,0:T(8,128)(2,1)S(1)} %maximum_select_fusion), channel_id=1, source_target_pairs={{0,16},{16,32},{32,48},{48,64},{64,80},{80,96},{96,112},{112,128},... | collective-permute-start | bytes 983048 | tf_op jit(solution)/shard_map/ppermute | solution.py:232
  116.3 5.7 %collective-permute-done.17 = bf16[2,320,1,256]{3,1,2,0:T(8,128)(2,1)S(1)} collective-permute-done((bf16[2,320,1,256]{3,1,2,0:T(8,128)(2,1)S(1)}, bf16[2,320,1,256]{3,1,2,0:T(8,128)(2,1)S(1)}, u32[]{:S(2)}, u32[]{:S(2)}) %collective-permute-start.17) | collective-permute-done | bytes 327712 | tf_op jit(solution)/shard_map/ppermute | solution.py:232
  125.6 5.3 %collective-permute-start.21 = (bf16[2,320,1,256]{3,1,2,0:T(8,128)(2,1)S(1)}, bf16[2,320,1,256]{3,1,2,0:T(8,128)(2,1)S(1)}, u32[]{:S(2)}, u32[]{:S(2)}) collective-permute-start(bf16[2,320,1,256]{3,1,2,0:T(8,128)(2,1)S(1)} %collective-permute-done.19), channel_id=1, source_target_pairs={{0,240},{16,0},{32,16},{48,32},{64,48},{80,64},{96,80},{112,96},{1... | collective-permute-start | bytes 983048 | tf_op jit(solution)/shard_map/ppermute | solution.py:235
  137.0 5.6 %collective-permute-start.23 = (bf16[2,320,1,256]{3,1,2,0:T(8,128)(2,1)S(1)}, bf16[2,320,1,256]{3,1,2,0:T(8,128)(2,1)S(1)}, u32[]{:S(2)}, u32[]{:S(2)}) collective-permute-start(bf16[2,320,1,256]{3,1,2,0:T(8,128)(2,1)S(1)} %collective-permute-done.21), channel_id=1, source_target_pairs={{0,240},{16,0},{32,16},{48,32},{64,48},{80,64},{96,80},{112,96},{1... | collective-permute-start | bytes 983048 | tf_op jit(solution)/shard_map/ppermute | solution.py:235
  148.7 5.6 %collective-permute-start.25 = (bf16[2,320,1,256]{3,1,2,0:T(8,128)(2,1)S(1)}, bf16[2,320,1,256]{3,1,2,0:T(8,128)(2,1)S(1)}, u32[]{:S(2)}, u32[]{:S(2)}) collective-permute-start(bf16[2,320,1,256]{3,1,2,0:T(8,128)(2,1)S(1)} %collective-permute-done.23), channel_id=1, source_target_pairs={{0,240},{16,0},{32,16},{48,32},{64,48},{80,64},{96,80},{112,96},{1... | collective-permute-start | bytes 983048 | tf_op jit(solution)/shard_map/ppermute | solution.py:235
  160.5 5.6 %collective-permute-start.27 = (bf16[2,320,1,256]{3,1,2,0:T(8,128)(2,1)S(1)}, bf16[2,320,1,256]{3,1,2,0:T(8,128)(2,1)S(1)}, u32[]{:S(2)}, u32[]{:S(2)}) collective-permute-start(bf16[2,320,1,256]{3,1,2,0:T(8,128)(2,1)S(1)} %collective-permute-done.25), channel_id=1, source_target_pairs={{0,240},{16,0},{32,16},{48,32},{64,48},{80,64},{96,80},{112,96},{1... | collective-permute-start | bytes 983048 | tf_op jit(solution)/shard_map/ppermute | solution.py:235
  172.2 5.6 %collective-permute-start.29 = (bf16[2,320,1,256]{3,1,2,0:T(8,128)(2,1)S(1)}, bf16[2,320,1,256]{3,1,2,0:T(8,128)(2,1)S(1)}, u32[]{:S(2)}, u32[]{:S(2)}) collective-permute-start(bf16[2,320,1,256]{3,1,2,0:T(8,128)(2,1)S(1)} %collective-permute-done.27), channel_id=1, source_target_pairs={{0,240},{16,0},{32,16},{48,32},{64,48},{80,64},{96,80},{112,96},{1... | collective-permute-start | bytes 983048 | tf_op jit(solution)/shard_map/ppermute | solution.py:235
  184.3 5.6 %collective-permute-start.30 = (bf16[2,320,1,256]{3,1,2,0:T(8,128)(2,1)S(1)}, bf16[2,320,1,256]{3,1,2,0:T(8,128)(2,1)S(1)}, u32[]{:S(2)}, u32[]{:S(2)}) collective-permute-start(bf16[2,320,1,256]{3,1,2,0:T(8,128)(2,1)S(1)} %collective-permute-done.29), channel_id=1, source_target_pairs={{0,240},{16,0},{32,16},{48,32},{64,48},{80,64},{96,80},{112,96},{1... | collective-permute-start | bytes 983048 | tf_op jit(solution)/shard_map/ppermute | solution.py:235
  194.9 5.6 %collective-permute-done.31 = bf16[2,320,1,256]{3,1,2,0:T(8,128)(2,1)S(1)} collective-permute-done((bf16[2,320,1,256]{3,1,2,0:T(8,128)(2,1)S(1)}, bf16[2,320,1,256]{3,1,2,0:T(8,128)(2,1)S(1)}, u32[]{:S(2)}, u32[]{:S(2)}) %collective-permute-start.31) | collective-permute-done | bytes 327712 | tf_op jit(solution)/shard_map/ppermute | solution.py:232
  211.3 9.9 %collective-permute-done.38 = bf16[320,192]{1,0:T(8,128)(2,1)S(1)} collective-permute-done((bf16[320,192]{1,0:T(8,128)(2,1)S(1)}, bf16[320,192]{1,0:T(8,128)(2,1)S(1)}, u32[]{:S(2)}, u32[]{:S(2)}) %collective-permute-start.38) | collective-permute-done | bytes 122912 | tf_op jit(solution)/shard_map/ppermute | solution.py:19
  222.8 3.4 %collective-permute-start.35 = (bf16[160,768]{1,0:T(8,128)(2,1)S(1)}, bf16[160,768]{1,0:T(8,128)(2,1)S(1)}, u32[]{:S(2)}, u32[]{:S(2)}) collective-permute-start(bf16[160,768]{1,0:T(8,128)(2,1)S(1)} %dynamic-slice_convert_fusion.2), channel_id=1, source_target_pairs={{0,2},{1,3},{2,0},{3,1},{4,6},{5,7},{6,4},{7,5},{8,10},{9,11},{10,... | collective-permute-start | bytes 737288 | tf_op jit(solution)/shard_map/ppermute | solution.py:89
  226.3 3.6 %collective-permute-start.33 = (bf16[160,768]{1,0:T(8,128)(2,1)S(1)}, bf16[160,768]{1,0:T(8,128)(2,1)S(1)}, u32[]{:S(2)}, u32[]{:S(2)}) collective-permute-start(bf16[160,768]{1,0:T(8,128)(2,1)S(1)} %dynamic-slice_convert_fusion.3), channel_id=1, source_target_pairs={{0,8},{1,9},{2,10},{3,11},{4,12},{5,13},{6,14},{7,15},{8,0},{9,1},... | collective-permute-start | bytes 737288 | tf_op jit(solution)/shard_map/ppermute | solution.py:89
  229.8 2.4 collective-permute-done.35
  232.3 3.6 %collective-permute-start.36 = (bf16[160,384]{1,0:T(8,128)(2,1)S(1)}, bf16[160,384]{1,0:T(8,128)(2,1)S(1)}, u32[]{:S(2)}, u32[]{:S(2)}) collective-permute-start(bf16[160,384]{1,0:T(8,128)(2,1)S(1)} %dynamic-slice_convert_fusion.4), channel_id=1, source_target_pairs={{0,8},{1,9},{2,10},{3,11},{4,12},{5,13},{6,14},{7,15},{8,0},{9,1},... | collective-permute-start | bytes 368648 | tf_op jit(solution)/shard_map/ppermute | solution.py:89
  236.0 3.4 %collective-permute-start.34 = (bf16[160,384]{1,0:T(8,128)(2,1)S(1)}, bf16[160,384]{1,0:T(8,128)(2,1)S(1)}, u32[]{:S(2)}, u32[]{:S(2)}) collective-permute-start(bf16[160,384]{1,0:T(8,128)(2,1)S(1)} %dynamic-slice_convert_fusion.5), channel_id=1, source_target_pairs={{0,2},{1,3},{2,0},{3,1},{4,6},{5,7},{6,4},{7,5},{8,10},{9,11},{10,... | collective-permute-start | bytes 368648 | tf_op jit(solution)/shard_map/ppermute | solution.py:89
  239.5 3.3 %collective-permute-done.34 = bf16[160,384]{1,0:T(8,128)(2,1)S(1)} collective-permute-done((bf16[160,384]{1,0:T(8,128)(2,1)S(1)}, bf16[160,384]{1,0:T(8,128)(2,1)S(1)}, u32[]{:S(2)}, u32[]{:S(2)}) %collective-permute-start.34) | collective-permute-done | bytes 122912 | tf_op jit(solution)/shard_map/ppermute | solution.py:89
  243.0 4.9 %collective-permute-start.37 = (bf16[320,192]{1,0:T(8,128)(2,1)S(1)}, bf16[320,192]{1,0:T(8,128)(2,1)S(1)}, u32[]{:S(2)}, u32[]{:S(2)}) collective-permute-start(bf16[320,192]{1,0:T(8,128)(2,1)S(1)} %pad_maximum_fusion.1), channel_id=1, source_target_pairs={{0,4},{1,5},{2,6},{3,7},{4,0},{5,1},{6,2},{7,3},{8,12},{9,13},{10,... | collective-permute-start | bytes 368648 | tf_op jit(solution)/shard_map/ppermute | solution.py:78
  248.7 3.0 %collective-permute-done.37 = bf16[320,192]{1,0:T(8,128)(2,1)S(1)} collective-permute-done((bf16[320,192]{1,0:T(8,128)(2,1)S(1)}, bf16[320,192]{1,0:T(8,128)(2,1)S(1)}, u32[]{:S(2)}, u32[]{:S(2)}) %collective-permute-start.37) | collective-permute-done | bytes 122912 | tf_op jit(solution)/shard_map/ppermute | solution.py:78
  (234 shorter events, 96.0 us)
Async XLA Ops:
  2.3 12.1 %collective-permute-start = (bf16[104,512]{1,0:T(8,128)(2,1)S(1)}, bf16[104,512]{1,0:T(8,128)(2,1)S(1)}, u32[]{:S(2)}, u32[]{:S(2)}) collective-permute-start(bf16[104,512]{1,0:T(8,128)(2,1)S(1)} %get-tuple-element.159), channel_id=1, source_target_pairs={{0,256},{16,272},{32,288},{48,304},{64,320},{80,336},{96,352},{112... | collective-permute-start | bytes 319496 | tf_op jit(solution)/shard_map/ppermute | solution.py:34
  14.4 11.5 %collective-permute-start.1 = (bf16[2,104,512]{2,1,0:T(8,128)(2,1)S(1)}, bf16[2,104,512]{2,1,0:T(8,128)(2,1)S(1)}, u32[]{:S(2)}, u32[]{:S(2)}) collective-permute-start(bf16[2,104,512]{2,1,0:T(8,128)(2,1)S(1)} %maximum_select_fusion.2), channel_id=1, source_target_pairs={{0,16},{16,32},{32,48},{48,64},{64,80},{80,96},{96,112},{112,128},... | collective-permute-start | bytes 638984 | tf_op jit(solution)/shard_map/ppermute | solution.py:45
  16.4 11.5 %collective-permute-start.2 = (bf16[2,104,512]{2,1,0:T(8,128)(2,1)S(1)}, bf16[2,104,512]{2,1,0:T(8,128)(2,1)S(1)}, u32[]{:S(2)}, u32[]{:S(2)}) collective-permute-start(bf16[2,104,512]{2,1,0:T(8,128)(2,1)S(1)} %maximum_select_fusion.2), channel_id=1, source_target_pairs={{0,240},{16,0},{32,16},{48,32},{64,48},{80,64},{96,80},{112,96},{1... | collective-permute-start | bytes 638984 | tf_op jit(solution)/shard_map/ppermute | solution.py:48
  25.9 8.9 %collective-permute-start.3 = (bf16[2,104,512]{2,1,0:T(8,128)(2,1)S(1)}, bf16[2,104,512]{2,1,0:T(8,128)(2,1)S(1)}, u32[]{:S(2)}, u32[]{:S(2)}) collective-permute-start(bf16[2,104,512]{2,1,0:T(8,128)(2,1)S(1)} %collective-permute-done.1), channel_id=1, source_target_pairs={{0,16},{16,32},{32,48},{48,64},{64,80},{80,96},{96,112},{112,128},... | collective-permute-start | bytes 638984 | tf_op jit(solution)/shard_map/ppermute | solution.py:45
  34.9 8.9 %collective-permute-start.5 = (bf16[2,104,512]{2,1,0:T(8,128)(2,1)S(1)}, bf16[2,104,512]{2,1,0:T(8,128)(2,1)S(1)}, u32[]{:S(2)}, u32[]{:S(2)}) collective-permute-start(bf16[2,104,512]{2,1,0:T(8,128)(2,1)S(1)} %collective-permute-done.3), channel_id=1, source_target_pairs={{0,16},{16,32},{32,48},{48,64},{64,80},{80,96},{96,112},{112,128},... | collective-permute-start | bytes 638984 | tf_op jit(solution)/shard_map/ppermute | solution.py:45
  43.8 8.9 %collective-permute-start.7 = (bf16[2,104,512]{2,1,0:T(8,128)(2,1)S(1)}, bf16[2,104,512]{2,1,0:T(8,128)(2,1)S(1)}, u32[]{:S(2)}, u32[]{:S(2)}) collective-permute-start(bf16[2,104,512]{2,1,0:T(8,128)(2,1)S(1)} %collective-permute-done.5), channel_id=1, source_target_pairs={{0,16},{16,32},{32,48},{48,64},{64,80},{80,96},{96,112},{112,128},... | collective-permute-start | bytes 638984 | tf_op jit(solution)/shard_map/ppermute | solution.py:45
  52.8 9.8 %collective-permute-start.9 = (bf16[2,104,512]{2,1,0:T(8,128)(2,1)S(1)}, bf16[2,104,512]{2,1,0:T(8,128)(2,1)S(1)}, u32[]{:S(2)}, u32[]{:S(2)}) collective-permute-start(bf16[2,104,512]{2,1,0:T(8,128)(2,1)S(1)} %collective-permute-done.7), channel_id=1, source_target_pairs={{0,16},{16,32},{32,48},{48,64},{64,80},{80,96},{96,112},{112,128},... | collective-permute-start | bytes 638984 | tf_op jit(solution)/shard_map/ppermute | solution.py:45
  54.7 9.7 %collective-permute-start.10 = (bf16[2,104,512]{2,1,0:T(8,128)(2,1)S(1)}, bf16[2,104,512]{2,1,0:T(8,128)(2,1)S(1)}, u32[]{:S(2)}, u32[]{:S(2)}) collective-permute-start(bf16[2,104,512]{2,1,0:T(8,128)(2,1)S(1)} %collective-permute-done.8), channel_id=1, source_target_pairs={{0,240},{16,0},{32,16},{48,32},{64,48},{80,64},{96,80},{112,96},{1... | collective-permute-start | bytes 638984 | tf_op jit(solution)/shard_map/ppermute | solution.py:48
  62.5 10.9 %collective-permute-start.11 = (bf16[2,104,512]{2,1,0:T(8,128)(2,1)S(1)}, bf16[2,104,512]{2,1,0:T(8,128)(2,1)S(1)}, u32[]{:S(2)}, u32[]{:S(2)}) collective-permute-start(bf16[2,104,512]{2,1,0:T(8,128)(2,1)S(1)} %collective-permute-done.9), channel_id=1, source_target_pairs={{0,16},{16,32},{32,48},{48,64},{64,80},{80,96},{96,112},{112,128},... | collective-permute-start | bytes 638984 | tf_op jit(solution)/shard_map/ppermute | solution.py:45
  64.4 11.1 %collective-permute-start.12 = (bf16[2,104,512]{2,1,0:T(8,128)(2,1)S(1)}, bf16[2,104,512]{2,1,0:T(8,128)(2,1)S(1)}, u32[]{:S(2)}, u32[]{:S(2)}) collective-permute-start(bf16[2,104,512]{2,1,0:T(8,128)(2,1)S(1)} %collective-permute-done.10), channel_id=1, source_target_pairs={{0,240},{16,0},{32,16},{48,32},{64,48},{80,64},{96,80},{112,96},{1... | collective-permute-start | bytes 638984 | tf_op jit(solution)/shard_map/ppermute | solution.py:48
  73.4 10.4 %collective-permute-start.13 = (bf16[2,104,512]{2,1,0:T(8,128)(2,1)S(1)}, bf16[2,104,512]{2,1,0:T(8,128)(2,1)S(1)}, u32[]{:S(2)}, u32[]{:S(2)}) collective-permute-start(bf16[2,104,512]{2,1,0:T(8,128)(2,1)S(1)} %collective-permute-done.11), channel_id=1, source_target_pairs={{0,16},{16,32},{32,48},{48,64},{64,80},{80,96},{96,112},{112,128},... | collective-permute-start | bytes 638984 | tf_op jit(solution)/shard_map/ppermute | solution.py:45
  75.5 10.2 %collective-permute-start.14 = (bf16[2,104,512]{2,1,0:T(8,128)(2,1)S(1)}, bf16[2,104,512]{2,1,0:T(8,128)(2,1)S(1)}, u32[]{:S(2)}, u32[]{:S(2)}) collective-permute-start(bf16[2,104,512]{2,1,0:T(8,128)(2,1)S(1)} %collective-permute-done.12), channel_id=1, source_target_pairs={{0,240},{16,0},{32,16},{48,32},{64,48},{80,64},{96,80},{112,96},{1... | collective-permute-start | bytes 638984 | tf_op jit(solution)/shard_map/ppermute | solution.py:48
  83.8 8.9 %collective-permute-start.15 = (bf16[2,104,512]{2,1,0:T(8,128)(2,1)S(1)}, bf16[2,104,512]{2,1,0:T(8,128)(2,1)S(1)}, u32[]{:S(2)}, u32[]{:S(2)}) collective-permute-start(bf16[2,104,512]{2,1,0:T(8,128)(2,1)S(1)} %collective-permute-done.13), channel_id=1, source_target_pairs={{0,16},{16,32},{32,48},{48,64},{64,80},{80,96},{96,112},{112,128},... | collective-permute-start | bytes 638984 | tf_op jit(solution)/shard_map/ppermute | solution.py:45
  109.2 14.8 %collective-permute-start.19 = (bf16[2,320,1,256]{3,1,2,0:T(8,128)(2,1)S(1)}, bf16[2,320,1,256]{3,1,2,0:T(8,128)(2,1)S(1)}, u32[]{:S(2)}, u32[]{:S(2)}) collective-permute-start(bf16[2,320,1,256]{3,1,2,0:T(8,128)(2,1)S(1)} %maximum_select_fusion), channel_id=1, source_target_pairs={{0,240},{16,0},{32,16},{48,32},{64,48},{80,64},{96,80},{112,96},{1... | collective-permute-start | bytes 983048 | tf_op jit(solution)/shard_map/ppermute | solution.py:235
  111.1 11.0 %collective-permute-start.17 = (bf16[2,320,1,256]{3,1,2,0:T(8,128)(2,1)S(1)}, bf16[2,320,1,256]{3,1,2,0:T(8,128)(2,1)S(1)}, u32[]{:S(2)}, u32[]{:S(2)}) collective-permute-start(bf16[2,320,1,256]{3,1,2,0:T(8,128)(2,1)S(1)} %maximum_select_fusion), channel_id=1, source_target_pairs={{0,16},{16,32},{32,48},{48,64},{64,80},{80,96},{96,112},{112,128},... | collective-permute-start | bytes 983048 | tf_op jit(solution)/shard_map/ppermute | solution.py:232
  122.1 10.2 %collective-permute-start.18 = (bf16[2,320,1,256]{3,1,2,0:T(8,128)(2,1)S(1)}, bf16[2,320,1,256]{3,1,2,0:T(8,128)(2,1)S(1)}, u32[]{:S(2)}, u32[]{:S(2)}) collective-permute-start(bf16[2,320,1,256]{3,1,2,0:T(8,128)(2,1)S(1)} %collective-permute-done.17), channel_id=1, source_target_pairs={{0,16},{16,32},{32,48},{48,64},{64,80},{80,96},{96,112},{112,128},... | collective-permute-start | bytes 983048 | tf_op jit(solution)/shard_map/ppermute | solution.py:232
  125.6 9.8 %collective-permute-start.21 = (bf16[2,320,1,256]{3,1,2,0:T(8,128)(2,1)S(1)}, bf16[2,320,1,256]{3,1,2,0:T(8,128)(2,1)S(1)}, u32[]{:S(2)}, u32[]{:S(2)}) collective-permute-start(bf16[2,320,1,256]{3,1,2,0:T(8,128)(2,1)S(1)} %collective-permute-done.19), channel_id=1, source_target_pairs={{0,240},{16,0},{32,16},{48,32},{64,48},{80,64},{96,80},{112,96},{1... | collective-permute-start | bytes 983048 | tf_op jit(solution)/shard_map/ppermute | solution.py:235
  132.2 11.1 %collective-permute-start.20 = (bf16[2,320,1,256]{3,1,2,0:T(8,128)(2,1)S(1)}, bf16[2,320,1,256]{3,1,2,0:T(8,128)(2,1)S(1)}, u32[]{:S(2)}, u32[]{:S(2)}) collective-permute-start(bf16[2,320,1,256]{3,1,2,0:T(8,128)(2,1)S(1)} %collective-permute-done.18), channel_id=1, source_target_pairs={{0,16},{16,32},{32,48},{48,64},{64,80},{80,96},{96,112},{112,128},... | collective-permute-start | bytes 983048 | tf_op jit(solution)/shard_map/ppermute | solution.py:232
  137.0 10.2 %collective-permute-start.23 = (bf16[2,320,1,256]{3,1,2,0:T(8,128)(2,1)S(1)}, bf16[2,320,1,256]{3,1,2,0:T(8,128)(2,1)S(1)}, u32[]{:S(2)}, u32[]{:S(2)}) collective-permute-start(bf16[2,320,1,256]{3,1,2,0:T(8,128)(2,1)S(1)} %collective-permute-done.21), channel_id=1, source_target_pairs={{0,240},{16,0},{32,16},{48,32},{64,48},{80,64},{96,80},{112,96},{1... | collective-permute-start | bytes 983048 | tf_op jit(solution)/shard_map/ppermute | solution.py:235
  143.4 11.7 %collective-permute-start.22 = (bf16[2,320,1,256]{3,1,2,0:T(8,128)(2,1)S(1)}, bf16[2,320,1,256]{3,1,2,0:T(8,128)(2,1)S(1)}, u32[]{:S(2)}, u32[]{:S(2)}) collective-permute-start(bf16[2,320,1,256]{3,1,2,0:T(8,128)(2,1)S(1)} %collective-permute-done.20), channel_id=1, source_target_pairs={{0,16},{16,32},{32,48},{48,64},{64,80},{80,96},{96,112},{112,128},... | collective-permute-start | bytes 983048 | tf_op jit(solution)/shard_map/ppermute | solution.py:232
  148.7 10.2 %collective-permute-start.25 = (bf16[2,320,1,256]{3,1,2,0:T(8,128)(2,1)S(1)}, bf16[2,320,1,256]{3,1,2,0:T(8,128)(2,1)S(1)}, u32[]{:S(2)}, u32[]{:S(2)}) collective-permute-start(bf16[2,320,1,256]{3,1,2,0:T(8,128)(2,1)S(1)} %collective-permute-done.23), channel_id=1, source_target_pairs={{0,240},{16,0},{32,16},{48,32},{64,48},{80,64},{96,80},{112,96},{1... | collective-permute-start | bytes 983048 | tf_op jit(solution)/shard_map/ppermute | solution.py:235
  155.1 11.7 %collective-permute-start.24 = (bf16[2,320,1,256]{3,1,2,0:T(8,128)(2,1)S(1)}, bf16[2,320,1,256]{3,1,2,0:T(8,128)(2,1)S(1)}, u32[]{:S(2)}, u32[]{:S(2)}) collective-permute-start(bf16[2,320,1,256]{3,1,2,0:T(8,128)(2,1)S(1)} %collective-permute-done.22), channel_id=1, source_target_pairs={{0,16},{16,32},{32,48},{48,64},{64,80},{80,96},{96,112},{112,128},... | collective-permute-start | bytes 983048 | tf_op jit(solution)/shard_map/ppermute | solution.py:232
  160.5 10.2 %collective-permute-start.27 = (bf16[2,320,1,256]{3,1,2,0:T(8,128)(2,1)S(1)}, bf16[2,320,1,256]{3,1,2,0:T(8,128)(2,1)S(1)}, u32[]{:S(2)}, u32[]{:S(2)}) collective-permute-start(bf16[2,320,1,256]{3,1,2,0:T(8,128)(2,1)S(1)} %collective-permute-done.25), channel_id=1, source_target_pairs={{0,240},{16,0},{32,16},{48,32},{64,48},{80,64},{96,80},{112,96},{1... | collective-permute-start | bytes 983048 | tf_op jit(solution)/shard_map/ppermute | solution.py:235
  166.9 11.7 %collective-permute-start.26 = (bf16[2,320,1,256]{3,1,2,0:T(8,128)(2,1)S(1)}, bf16[2,320,1,256]{3,1,2,0:T(8,128)(2,1)S(1)}, u32[]{:S(2)}, u32[]{:S(2)}) collective-permute-start(bf16[2,320,1,256]{3,1,2,0:T(8,128)(2,1)S(1)} %collective-permute-done.24), channel_id=1, source_target_pairs={{0,16},{16,32},{32,48},{48,64},{64,80},{80,96},{96,112},{112,128},... | collective-permute-start | bytes 983048 | tf_op jit(solution)/shard_map/ppermute | solution.py:232
  172.2 10.2 %collective-permute-start.29 = (bf16[2,320,1,256]{3,1,2,0:T(8,128)(2,1)S(1)}, bf16[2,320,1,256]{3,1,2,0:T(8,128)(2,1)S(1)}, u32[]{:S(2)}, u32[]{:S(2)}) collective-permute-start(bf16[2,320,1,256]{3,1,2,0:T(8,128)(2,1)S(1)} %collective-permute-done.27), channel_id=1, source_target_pairs={{0,240},{16,0},{32,16},{48,32},{64,48},{80,64},{96,80},{112,96},{1... | collective-permute-start | bytes 983048 | tf_op jit(solution)/shard_map/ppermute | solution.py:235
  178.6 11.7 %collective-permute-start.28 = (bf16[2,320,1,256]{3,1,2,0:T(8,128)(2,1)S(1)}, bf16[2,320,1,256]{3,1,2,0:T(8,128)(2,1)S(1)}, u32[]{:S(2)}, u32[]{:S(2)}) collective-permute-start(bf16[2,320,1,256]{3,1,2,0:T(8,128)(2,1)S(1)} %collective-permute-done.26), channel_id=1, source_target_pairs={{0,16},{16,32},{32,48},{48,64},{64,80},{80,96},{96,112},{112,128},... | collective-permute-start | bytes 983048 | tf_op jit(solution)/shard_map/ppermute | solution.py:232
  184.3 10.2 %collective-permute-start.30 = (bf16[2,320,1,256]{3,1,2,0:T(8,128)(2,1)S(1)}, bf16[2,320,1,256]{3,1,2,0:T(8,128)(2,1)S(1)}, u32[]{:S(2)}, u32[]{:S(2)}) collective-permute-start(bf16[2,320,1,256]{3,1,2,0:T(8,128)(2,1)S(1)} %collective-permute-done.29), channel_id=1, source_target_pairs={{0,240},{16,0},{32,16},{48,32},{64,48},{80,64},{96,80},{112,96},{1... | collective-permute-start | bytes 983048 | tf_op jit(solution)/shard_map/ppermute | solution.py:235
  190.3 10.2 %collective-permute-start.31 = (bf16[2,320,1,256]{3,1,2,0:T(8,128)(2,1)S(1)}, bf16[2,320,1,256]{3,1,2,0:T(8,128)(2,1)S(1)}, u32[]{:S(2)}, u32[]{:S(2)}) collective-permute-start(bf16[2,320,1,256]{3,1,2,0:T(8,128)(2,1)S(1)} %collective-permute-done.28), channel_id=1, source_target_pairs={{0,16},{16,32},{32,48},{48,64},{64,80},{80,96},{96,112},{112,128},... | collective-permute-start | bytes 983048 | tf_op jit(solution)/shard_map/ppermute | solution.py:232
  206.1 15.2 %collective-permute-start.32 = (bf16[320,1536]{1,0:T(8,128)(2,1)}, bf16[320,1536]{1,0:T(8,128)(2,1)S(1)}, u32[]{:S(2)}, u32[]{:S(2)}) collective-permute-start(bf16[320,1536]{1,0:T(8,128)(2,1)} %pad_maximum_fusion), channel_id=1, source_target_pairs={{0,1},{1,0},{2,3},{3,2},{4,5},{5,4},{6,7},{7,6},{8,9},{9,8},{10,11... | collective-permute-start | bytes 2949128 | tf_op jit(solution)/shard_map/ppermute | solution.py:78
  209.1 12.1 %collective-permute-start.38 = (bf16[320,192]{1,0:T(8,128)(2,1)S(1)}, bf16[320,192]{1,0:T(8,128)(2,1)S(1)}, u32[]{:S(2)}, u32[]{:S(2)}) collective-permute-start(bf16[320,192]{1,0:T(8,128)(2,1)S(1)} %constant_dynamic-slice_fusion), channel_id=1, source_target_pairs={{0,16},{16,32},{32,48},{48,64},{64,80},{80,96},{96,112},{112,128},... | collective-permute-start | bytes 368648 | tf_op jit(solution)/shard_map/ppermute | solution.py:19
  222.8 9.5 %collective-permute-start.35 = (bf16[160,768]{1,0:T(8,128)(2,1)S(1)}, bf16[160,768]{1,0:T(8,128)(2,1)S(1)}, u32[]{:S(2)}, u32[]{:S(2)}) collective-permute-start(bf16[160,768]{1,0:T(8,128)(2,1)S(1)} %dynamic-slice_convert_fusion.2), channel_id=1, source_target_pairs={{0,2},{1,3},{2,0},{3,1},{4,6},{5,7},{6,4},{7,5},{8,10},{9,11},{10,... | collective-permute-start | bytes 737288 | tf_op jit(solution)/shard_map/ppermute | solution.py:89
  226.3 9.6 %collective-permute-start.33 = (bf16[160,768]{1,0:T(8,128)(2,1)S(1)}, bf16[160,768]{1,0:T(8,128)(2,1)S(1)}, u32[]{:S(2)}, u32[]{:S(2)}) collective-permute-start(bf16[160,768]{1,0:T(8,128)(2,1)S(1)} %dynamic-slice_convert_fusion.3), channel_id=1, source_target_pairs={{0,8},{1,9},{2,10},{3,11},{4,12},{5,13},{6,14},{7,15},{8,0},{9,1},... | collective-permute-start | bytes 737288 | tf_op jit(solution)/shard_map/ppermute | solution.py:89
  (16 other events, 99.5 us)

commit v9 on v7

--- a/solution.py
+++ b/solution.py
@@ -38,23 +38,33 @@
     ring_pos = position % ring
     forward = [(y * ring + a, y * ring + (a + 1) % ring) for y in range(2) for a in range(ring)]
     backward = [(y * ring + a, y * ring + (a - 1) % ring) for y in range(2) for a in range(ring)]
-    pieces = [(pair, ring_pos)]
+    pieces = [(pair, ring_pos, (0, 1))]
     ahead = pair
     behind = pair
     for step in range(1, ring // 2 + 1):
+        source = (ring_pos - step) % ring
+        if 2 * step == ring:
+            ahead = lax.ppermute(ahead[:1], axis, forward)
+            behind = lax.ppermute(behind[1:], axis, backward)
+            pieces.append((ahead, source, (0,)))
+            pieces.append((behind, source, (1,)))
+            break
         ahead = lax.ppermute(ahead, axis, forward)
-        pieces.append((ahead, (ring_pos - step) % ring))
+        pieces.append((ahead, source, (0, 1)))
         if step < ring - ring // 2:
             behind = lax.ppermute(behind, axis, backward)
-            pieces.append((behind, (ring_pos + step) % ring))
+            pieces.append((behind, (ring_pos + step) % ring, (0, 1)))
     return pieces, ring
 
 
 def ring_gather(block, axis):
     pieces, ring = ring_pieces(block, axis)
     gathered = jnp.zeros((ring,) + pieces[0][0].shape, block.dtype)
-    for piece, source in pieces:
-        gathered = lax.dynamic_update_index_in_dim(gathered, piece, source, 0)
+    zero = jnp.zeros((), jnp.int32)
+    for piece, source, halves in pieces:
+        gathered = lax.dynamic_update_slice(
+            gathered, piece[None], (source, halves[0]) + (zero,) * block.ndim
+        )
     gathered = jnp.swapaxes(gathered, 0, 1)
     return gathered.reshape((2 * ring * block.shape[0],) + block.shape[1:])
 
@@ -185,16 +195,14 @@
     backward = [(y * ring + a, y * ring + (a - 1) % ring) for y in range(2) for a in range(ring)]
     token_ids = jnp.arange(tok_rows, dtype=jnp.int32)
 
-    def fold(state_in, piece, source):
+    def fold(state_in, piece, source, halves):
         key_frame = (
-            jnp.concatenate(
-                [source * tok_rows + token_ids, (ring + source) * tok_rows + token_ids]
-            )
+            jnp.concatenate([(half * ring + source) * tok_rows + token_ids for half in halves])
             // frame_size
         )
         return attend_piece(
             state_in,
-            piece.reshape((2 * tok_rows,) + piece.shape[2:]),
+            piece.reshape((len(halves) * tok_rows,) + piece.shape[2:]),
             key_frame,
             queries,
             query_frame,
@@ -204,19 +212,25 @@
 
     ahead = pair
     behind = pair
-    waiting = [(pair, ring_pos)]
+    waiting = [(pair, ring_pos, (0, 1))]
     for step in range(1, ring // 2 + 1):
         ahead, state = lax.optimization_barrier((ahead, state))
-        ahead = lax.ppermute(ahead, "ctx", forward)
-        arrived = [(ahead, (ring_pos - step) % ring)]
-        if step < ring - ring // 2:
-            behind = lax.ppermute(behind, "ctx", backward)
-            arrived.append((behind, (ring_pos + step) % ring))
-        for piece, source in waiting:
-            state = fold(state, piece, source)
+        source = (ring_pos - step) % ring
+        if 2 * step == ring:
+            ahead = lax.ppermute(ahead[:1], "ctx", forward)
+            behind = lax.ppermute(behind[1:], "ctx", backward)
+            arrived = [(ahead, source, (0,)), (behind, source, (1,))]
+        else:
+            ahead = lax.ppermute(ahead, "ctx", forward)
+            arrived = [(ahead, source, (0, 1))]
+            if step < ring - ring // 2:
+                behind = lax.ppermute(behind, "ctx", backward)
+                arrived.append((behind, (ring_pos + step) % ring, (0, 1)))
+        for piece, where, halves in waiting:
+            state = fold(state, piece, where, halves)
         waiting = arrived
-    for piece, source in waiting:
-        state = fold(state, piece, source)
+    for piece, where, halves in waiting:
+        state = fold(state, piece, where, halves)
     run_max, run_sum, accumulated = state
     attended = (accumulated / run_sum[..., None]).astype(jnp.bfloat16)
     size = lax.axis_size("fsdp")

time: 247 us -> 259 us (1.049)
  starting transfers between devices: 155 us -> 168 us
    ppermute x0 -> x4, starting transfers between devices: none -> 13.7 us  [the longest x1 5.02 us: per_device(): behind = lax.ppermute(behind[1:], 'ctx', backward)]
    ppermute x0 -> x4, waiting for transfers between devices: none -> 7.88 us  [the longest x1 5.04 us: per_device(): ahead = lax.ppermute(ahead[:1], 'ctx', forward)]
    ppermute x8 -> x7, waiting for transfers between devices: 18.7 us -> 11 us  [ring_pieces(): ahead = lax.ppermute(ahead, axis, forward)]
    ppermute x8 -> x7, waiting for transfers between devices: 12.3 us -> 7.87 us  [per_device(): ahead = lax.ppermute(ahead, 'ctx', forward)]
    ppermute x7, starting transfers between devices: 31.4 us -> 35.2 us  [per_device(): behind = lax.ppermute(behind, 'ctx', backward)]
    ppermute x8 -> x7, starting transfers between devices: 17.4 us -> 13.8 us  [per_device(): ahead = lax.ppermute(ahead, 'ctx', forward)]
    ppermute x7, waiting for transfers between devices: 4.62 us -> 7.59 us  [per_device(): behind = lax.ppermute(behind, 'ctx', backward)]
    ppermute x8 -> x7, starting transfers between devices: 16.9 us -> 15 us  [ring_pieces(): ahead = lax.ppermute(ahead, axis, forward)]
  transfers between devices with their start and end apart: 41 -> 43, of which waited for: 22 -> 24; matrix products, arithmetic and copies ran while one was open for 11% -> 11% of each run, Pallas kernels for 0% -> 0%
where the time goes in v9:
time: 259 us; the launch traced here: 255 us
  starting transfers between devices  168 us (65%)
  waiting for transfers between devices  44.6 us (17%)
  matrix products  16 us (6%)
  other arithmetic  14.6 us (6%)
  local copies, waits for them, and re-layouts  9.35 us (4%)
  between operations  2.67 us (1%)
    ppermute x8, starting transfers between devices, halving_scatter(): lax.ppermute(send.astype(jnp.bfloat16), axis, [(i, i ^ 1 << bit) for i in...  43.7 us
    ppermute x7, starting transfers between devices, ring_pieces(): behind = lax.ppermute(behind, axis, backward)  35.3 us
    ppermute x7, starting transfers between devices, per_device(): behind = lax.ppermute(behind, 'ctx', backward)  35.2 us
    ppermute x7, starting transfers between devices, ring_pieces(): ahead = lax.ppermute(ahead, axis, forward)  15 us
    ppermute x7, starting transfers between devices, per_device(): ahead = lax.ppermute(ahead, 'ctx', forward)  13.8 us
    ppermute x7, waiting for transfers between devices, ring_pieces(): ahead = lax.ppermute(ahead, axis, forward)  11 us
    ppermute x7, waiting for transfers between devices, per_device(): ahead = lax.ppermute(ahead, 'ctx', forward)  7.87 us
    ppermute x7, waiting for transfers between devices, per_device(): behind = lax.ppermute(behind, 'ctx', backward)  7.59 us
  transfers between devices with their start and end apart: 43, of which 24 were waited for; matrix products, arithmetic and copies ran while one was open for 11% of the time, Pallas kernels for 0%

profile of v9, /device:TPU:1, one launch (start us, length us, event | category | flops | bytes accessed | tf_op | source)
XLA Modules:
  0.0 255.1 jit_solution(12405050938672911919)
XLA Ops:
  2.3 5.7 %collective-permute-start = (bf16[104,512]{1,0:T(8,128)(2,1)S(1)}, bf16[104,512]{1,0:T(8,128)(2,1)S(1)}, u32[]{:S(2)}, u32[]{:S(2)}) collective-permute-start(bf16[104,512]{1,0:T(8,128)(2,1)S(1)} %get-tuple-element.159), channel_id=1, source_target_pairs={{0,256},{16,272},{32,288},{48,304},{64,320},{80,336},{96,352},{112... | collective-permute-start | bytes 319496 | tf_op jit(solution)/shard_map/ppermute | solution.py:34
  9.1 3.6 %collective-permute-start.42 = (bf16[320,192]{1,0:T(8,128)(2,1)S(1)}, bf16[320,192]{1,0:T(8,128)(2,1)S(1)}, u32[]{:S(2)}, u32[]{:S(2)}) collective-permute-start(bf16[320,192]{1,0:T(8,128)(2,1)S(1)} %constant_dynamic-slice_fusion), channel_id=1, source_target_pairs={{0,16},{16,32},{32,48},{48,64},{64,80},{80,96},{96,112},{112,128},... | collective-permute-start | bytes 368648 | tf_op jit(solution)/shard_map/ppermute | solution.py:19
  18.3 3.5 %collective-permute-start.1 = (bf16[2,104,512]{2,1,0:T(8,128)(2,1)S(1)}, bf16[2,104,512]{2,1,0:T(8,128)(2,1)S(1)}, u32[]{:S(2)}, u32[]{:S(2)}) collective-permute-start(bf16[2,104,512]{2,1,0:T(8,128)(2,1)S(1)} %maximum_select_fusion.2), channel_id=1, source_target_pairs={{0,16},{16,32},{32,48},{48,64},{64,80},{80,96},{96,112},{112,128},... | collective-permute-start | bytes 638984 | tf_op jit(solution)/shard_map/ppermute | solution.py:52
  21.9 7.9 %collective-permute-start.2 = (bf16[2,104,512]{2,1,0:T(8,128)(2,1)S(1)}, bf16[2,104,512]{2,1,0:T(8,128)(2,1)S(1)}, u32[]{:S(2)}, u32[]{:S(2)}) collective-permute-start(bf16[2,104,512]{2,1,0:T(8,128)(2,1)S(1)} %maximum_select_fusion.2), channel_id=1, source_target_pairs={{0,240},{16,0},{32,16},{48,32},{64,48},{80,64},{96,80},{112,96},{1... | collective-permute-start | bytes 638984 | tf_op jit(solution)/shard_map/ppermute | solution.py:55
  30.2 2.3 collective-permute-done.1
  34.4 4.6 %collective-permute-start.4 = (bf16[2,104,512]{2,1,0:T(8,128)(2,1)S(1)}, bf16[2,104,512]{2,1,0:T(8,128)(2,1)S(1)}, u32[]{:S(2)}, u32[]{:S(2)}) collective-permute-start(bf16[2,104,512]{2,1,0:T(8,128)(2,1)S(1)} %collective-permute-done.2), channel_id=1, source_target_pairs={{0,240},{16,0},{32,16},{48,32},{64,48},{80,64},{96,80},{112,96},{1... | collective-permute-start | bytes 638984 | tf_op jit(solution)/shard_map/ppermute | solution.py:55
  42.7 4.6 %collective-permute-start.6 = (bf16[2,104,512]{2,1,0:T(8,128)(2,1)S(1)}, bf16[2,104,512]{2,1,0:T(8,128)(2,1)S(1)}, u32[]{:S(2)}, u32[]{:S(2)}) collective-permute-start(bf16[2,104,512]{2,1,0:T(8,128)(2,1)S(1)} %collective-permute-done.4), channel_id=1, source_target_pairs={{0,240},{16,0},{32,16},{48,32},{64,48},{80,64},{96,80},{112,96},{1... | collective-permute-start | bytes 638984 | tf_op jit(solution)/shard_map/ppermute | solution.py:55
  50.5 4.6 %collective-permute-start.8 = (bf16[2,104,512]{2,1,0:T(8,128)(2,1)S(1)}, bf16[2,104,512]{2,1,0:T(8,128)(2,1)S(1)}, u32[]{:S(2)}, u32[]{:S(2)}) collective-permute-start(bf16[2,104,512]{2,1,0:T(8,128)(2,1)S(1)} %collective-permute-done.6), channel_id=1, source_target_pairs={{0,240},{16,0},{32,16},{48,32},{64,48},{80,64},{96,80},{112,96},{1... | collective-permute-start | bytes 638984 | tf_op jit(solution)/shard_map/ppermute | solution.py:55
  58.3 4.6 %collective-permute-start.10 = (bf16[2,104,512]{2,1,0:T(8,128)(2,1)S(1)}, bf16[2,104,512]{2,1,0:T(8,128)(2,1)S(1)}, u32[]{:S(2)}, u32[]{:S(2)}) collective-permute-start(bf16[2,104,512]{2,1,0:T(8,128)(2,1)S(1)} %collective-permute-done.8), channel_id=1, source_target_pairs={{0,240},{16,0},{32,16},{48,32},{64,48},{80,64},{96,80},{112,96},{1... | collective-permute-start | bytes 638984 | tf_op jit(solution)/shard_map/ppermute | solution.py:55
  66.1 4.6 %collective-permute-start.12 = (bf16[2,104,512]{2,1,0:T(8,128)(2,1)S(1)}, bf16[2,104,512]{2,1,0:T(8,128)(2,1)S(1)}, u32[]{:S(2)}, u32[]{:S(2)}) collective-permute-start(bf16[2,104,512]{2,1,0:T(8,128)(2,1)S(1)} %collective-permute-done.10), channel_id=1, source_target_pairs={{0,240},{16,0},{32,16},{48,32},{64,48},{80,64},{96,80},{112,96},{1... | collective-permute-start | bytes 638984 | tf_op jit(solution)/shard_map/ppermute | solution.py:55
  73.8 4.6 %collective-permute-start.14 = (bf16[2,104,512]{2,1,0:T(8,128)(2,1)S(1)}, bf16[2,104,512]{2,1,0:T(8,128)(2,1)S(1)}, u32[]{:S(2)}, u32[]{:S(2)}) collective-permute-start(bf16[2,104,512]{2,1,0:T(8,128)(2,1)S(1)} %collective-permute-done.12), channel_id=1, source_target_pairs={{0,240},{16,0},{32,16},{48,32},{64,48},{80,64},{96,80},{112,96},{1... | collective-permute-start | bytes 638984 | tf_op jit(solution)/shard_map/ppermute | solution.py:55
  82.5 4.8 %collective-permute-start.16 = (bf16[1,104,512]{2,1,0:T(8,128)(2,1)S(1)}, bf16[1,104,512]{2,1,0:T(8,128)(2,1)S(1)}, u32[]{:S(2)}, u32[]{:S(2)}) collective-permute-start(bf16[1,104,512]{2,1,0:T(8,128)(2,1)S(1)} %slice.443), channel_id=1, source_target_pairs={{0,240},{16,0},{32,16},{48,32},{64,48},{80,64},{96,80},{112,96},{1... | collective-permute-start | bytes 319496 | tf_op jit(solution)/shard_map/ppermute | solution.py:48
  101.9 3.5 %collective-permute-done.17 = bf16[320,1,256]{2,0,1:T(8,128)(2,1)S(1)} collective-permute-done((bf16[320,1,256]{2,0,1:T(8,128)(2,1)S(1)}, bf16[320,1,256]{2,0,1:T(8,128)(2,1)S(1)}, u32[]{:S(2)}, u32[]{:S(2)}) %collective-permute-start.17) | collective-permute-done | bytes 163872 | tf_op jit(solution)/shard_map/ppermute | solution.py:189
  105.4 5.3 %collective-permute-start.20 = (bf16[2,320,1,256]{3,1,2,0:T(8,128)(2,1)S(1)}, bf16[2,320,1,256]{3,1,2,0:T(8,128)(2,1)S(1)}, u32[]{:S(2)}, u32[]{:S(2)}) collective-permute-start(bf16[2,320,1,256]{3,1,2,0:T(8,128)(2,1)S(1)} %maximum_select_fusion), channel_id=1, source_target_pairs={{0,240},{16,0},{32,16},{48,32},{64,48},{80,64},{96,80},{112,96},{1... | collective-permute-start | bytes 983048 | tf_op jit(solution)/shard_map/ppermute | solution.py:227
  114.0 5.8 %collective-permute-done.18 = bf16[2,320,1,256]{3,1,2,0:T(8,128)(2,1)S(1)} collective-permute-done((bf16[2,320,1,256]{3,1,2,0:T(8,128)(2,1)S(1)}, bf16[2,320,1,256]{3,1,2,0:T(8,128)(2,1)S(1)}, u32[]{:S(2)}, u32[]{:S(2)}) %collective-permute-start.18) | collective-permute-done | bytes 327712 | tf_op jit(solution)/shard_map/ppermute | solution.py:224
  123.4 4.6 %collective-permute-start.22 = (bf16[2,320,1,256]{3,1,2,0:T(8,128)(2,1)S(1)}, bf16[2,320,1,256]{3,1,2,0:T(8,128)(2,1)S(1)}, u32[]{:S(2)}, u32[]{:S(2)}) collective-permute-start(bf16[2,320,1,256]{3,1,2,0:T(8,128)(2,1)S(1)} %collective-permute-done.20), channel_id=1, source_target_pairs={{0,240},{16,0},{32,16},{48,32},{64,48},{80,64},{96,80},{112,96},{1... | collective-permute-start | bytes 983048 | tf_op jit(solution)/shard_map/ppermute | solution.py:227
  133.8 4.8 %collective-permute-start.24 = (bf16[2,320,1,256]{3,1,2,0:T(8,128)(2,1)S(1)}, bf16[2,320,1,256]{3,1,2,0:T(8,128)(2,1)S(1)}, u32[]{:S(2)}, u32[]{:S(2)}) collective-permute-start(bf16[2,320,1,256]{3,1,2,0:T(8,128)(2,1)S(1)} %collective-permute-done.22), channel_id=1, source_target_pairs={{0,240},{16,0},{32,16},{48,32},{64,48},{80,64},{96,80},{112,96},{1... | collective-permute-start | bytes 983048 | tf_op jit(solution)/shard_map/ppermute | solution.py:227
  144.2 5.4 %collective-permute-start.26 = (bf16[2,320,1,256]{3,1,2,0:T(8,128)(2,1)S(1)}, bf16[2,320,1,256]{3,1,2,0:T(8,128)(2,1)S(1)}, u32[]{:S(2)}, u32[]{:S(2)}) collective-permute-start(bf16[2,320,1,256]{3,1,2,0:T(8,128)(2,1)S(1)} %collective-permute-done.24), channel_id=1, source_target_pairs={{0,240},{16,0},{32,16},{48,32},{64,48},{80,64},{96,80},{112,96},{1... | collective-permute-start | bytes 983048 | tf_op jit(solution)/shard_map/ppermute | solution.py:227
  155.1 5.0 %collective-permute-start.28 = (bf16[2,320,1,256]{3,1,2,0:T(8,128)(2,1)S(1)}, bf16[2,320,1,256]{3,1,2,0:T(8,128)(2,1)S(1)}, u32[]{:S(2)}, u32[]{:S(2)}) collective-permute-start(bf16[2,320,1,256]{3,1,2,0:T(8,128)(2,1)S(1)} %collective-permute-done.26), channel_id=1, source_target_pairs={{0,240},{16,0},{32,16},{48,32},{64,48},{80,64},{96,80},{112,96},{1... | collective-permute-start | bytes 983048 | tf_op jit(solution)/shard_map/ppermute | solution.py:227
  165.7 5.0 %collective-permute-start.30 = (bf16[2,320,1,256]{3,1,2,0:T(8,128)(2,1)S(1)}, bf16[2,320,1,256]{3,1,2,0:T(8,128)(2,1)S(1)}, u32[]{:S(2)}, u32[]{:S(2)}) collective-permute-start(bf16[2,320,1,256]{3,1,2,0:T(8,128)(2,1)S(1)} %collective-permute-done.28), channel_id=1, source_target_pairs={{0,240},{16,0},{32,16},{48,32},{64,48},{80,64},{96,80},{112,96},{1... | collective-permute-start | bytes 983048 | tf_op jit(solution)/shard_map/ppermute | solution.py:227
  176.3 5.0 %collective-permute-start.31 = (bf16[2,320,1,256]{3,1,2,0:T(8,128)(2,1)S(1)}, bf16[2,320,1,256]{3,1,2,0:T(8,128)(2,1)S(1)}, u32[]{:S(2)}, u32[]{:S(2)}) collective-permute-start(bf16[2,320,1,256]{3,1,2,0:T(8,128)(2,1)S(1)} %collective-permute-done.30), channel_id=1, source_target_pairs={{0,240},{16,0},{32,16},{48,32},{64,48},{80,64},{96,80},{112,96},{1... | collective-permute-start | bytes 983048 | tf_op jit(solution)/shard_map/ppermute | solution.py:227
  182.1 3.2 %collective-permute-done.31 = bf16[2,320,1,256]{3,1,2,0:T(8,128)(2,1)S(1)} collective-permute-done((bf16[2,320,1,256]{3,1,2,0:T(8,128)(2,1)S(1)}, bf16[2,320,1,256]{3,1,2,0:T(8,128)(2,1)S(1)}, u32[]{:S(2)}, u32[]{:S(2)}) %collective-permute-start.31) | collective-permute-done | bytes 327712 | tf_op jit(solution)/shard_map/ppermute | solution.py:227
  185.3 5.0 %collective-permute-start.33 = (bf16[1,320,1,256]{3,1,2,0:T(8,128)(2,1)S(1)}, bf16[1,320,1,256]{3,1,2,0:T(8,128)(2,1)S(1)}, u32[]{:S(2)}, u32[]{:S(2)}) collective-permute-start(bf16[1,320,1,256]{3,1,2,0:T(8,128)(2,1)S(1)} %slice.485), channel_id=1, source_target_pairs={{0,240},{16,0},{32,16},{48,32},{64,48},{80,64},{96,80},{112,96},{1... | collective-permute-start | bytes 491528 | tf_op jit(solution)/shard_map/ppermute | solution.py:221
  194.6 5.0 %collective-permute-done.32 = bf16[1,320,1,256]{3,1,2,0:T(8,128)(2,1)S(1)} collective-permute-done((bf16[1,320,1,256]{3,1,2,0:T(8,128)(2,1)S(1)}, bf16[1,320,1,256]{3,1,2,0:T(8,128)(2,1)S(1)}, u32[]{:S(2)}, u32[]{:S(2)}) %collective-permute-start.32) | collective-permute-done | bytes 163872 | tf_op jit(solution)/shard_map/ppermute | solution.py:220
  202.0 23.2 %collective-permute-start.38 = (bf16[160,1536]{1,0:T(8,128)(2,1)S(1)}, bf16[160,1536]{1,0:T(8,128)(2,1)S(1)}, u32[]{:S(2)}, u32[]{:S(2)}) collective-permute-start(bf16[160,1536]{1,0:T(8,128)(2,1)S(1)} %dynamic-slice_convert_fusion), channel_id=1, source_target_pairs={{0,1},{1,0},{2,3},{3,2},{4,5},{5,4},{6,7},{7,6},{8,9},{9,8},{10,11... | collective-permute-start | bytes 1474568 | tf_op jit(solution)/shard_map/ppermute | solution.py:81
  227.8 3.1 %collective-permute-start.39 = (bf16[160,768]{1,0:T(8,128)(2,1)S(1)}, bf16[160,768]{1,0:T(8,128)(2,1)S(1)}, u32[]{:S(2)}, u32[]{:S(2)}) collective-permute-start(bf16[160,768]{1,0:T(8,128)(2,1)S(1)} %dynamic-slice_convert_fusion.2), channel_id=1, source_target_pairs={{0,2},{1,3},{2,0},{3,1},{4,6},{5,7},{6,4},{7,5},{8,10},{9,11},{10,... | collective-permute-start | bytes 737288 | tf_op jit(solution)/shard_map/ppermute | solution.py:81
  231.1 2.3 collective-permute-start.35
  233.4 3.3 %collective-permute-done.39 = bf16[160,768]{1,0:T(8,128)(2,1)S(1)} collective-permute-done((bf16[160,768]{1,0:T(8,128)(2,1)S(1)}, bf16[160,768]{1,0:T(8,128)(2,1)S(1)}, u32[]{:S(2)}, u32[]{:S(2)}) %collective-permute-start.39) | collective-permute-done | bytes 245792 | tf_op jit(solution)/shard_map/ppermute | solution.py:81
  236.8 4.6 %collective-permute-start.40 = (bf16[160,384]{1,0:T(8,128)(2,1)S(1)}, bf16[160,384]{1,0:T(8,128)(2,1)S(1)}, u32[]{:S(2)}, u32[]{:S(2)}) collective-permute-start(bf16[160,384]{1,0:T(8,128)(2,1)S(1)} %dynamic-slice_convert_fusion.4), channel_id=1, source_target_pairs={{0,4},{1,5},{2,6},{3,7},{4,0},{5,1},{6,2},{7,3},{8,12},{9,13},{10,... | collective-permute-start | bytes 368648 | tf_op jit(solution)/shard_map/ppermute | solution.py:81
  244.1 2.3 collective-permute-start.41
  247.4 4.0 %collective-permute-start.37 = (bf16[160,192]{1,0:T(8,128)(2,1)S(1)}, bf16[160,192]{1,0:T(8,128)(2,1)S(1)}, u32[]{:S(2)}, u32[]{:S(2)}) collective-permute-start(bf16[160,192]{1,0:T(8,128)(2,1)S(1)} %dynamic-slice_convert_fusion.7), channel_id=1, source_target_pairs={{0,4},{1,5},{2,6},{3,7},{4,0},{5,1},{6,2},{7,3},{8,12},{9,13},{10,... | collective-permute-start | bytes 184328 | tf_op jit(solution)/shard_map/ppermute | solution.py:81
  251.5 2.5 collective-permute-done.37
  (251 shorter events, 94.1 us)
Async XLA Ops:
  2.3 15.9 %collective-permute-start = (bf16[104,512]{1,0:T(8,128)(2,1)S(1)}, bf16[104,512]{1,0:T(8,128)(2,1)S(1)}, u32[]{:S(2)}, u32[]{:S(2)}) collective-permute-start(bf16[104,512]{1,0:T(8,128)(2,1)S(1)} %get-tuple-element.159), channel_id=1, source_target_pairs={{0,256},{16,272},{32,288},{48,304},{64,320},{80,336},{96,352},{112... | collective-permute-start | bytes 319496 | tf_op jit(solution)/shard_map/ppermute | solution.py:34
  9.1 21.0 %collective-permute-start.42 = (bf16[320,192]{1,0:T(8,128)(2,1)S(1)}, bf16[320,192]{1,0:T(8,128)(2,1)S(1)}, u32[]{:S(2)}, u32[]{:S(2)}) collective-permute-start(bf16[320,192]{1,0:T(8,128)(2,1)S(1)} %constant_dynamic-slice_fusion), channel_id=1, source_target_pairs={{0,16},{16,32},{32,48},{48,64},{64,80},{80,96},{96,112},{112,128},... | collective-permute-start | bytes 368648 | tf_op jit(solution)/shard_map/ppermute | solution.py:19
  18.3 14.1 %collective-permute-start.1 = (bf16[2,104,512]{2,1,0:T(8,128)(2,1)S(1)}, bf16[2,104,512]{2,1,0:T(8,128)(2,1)S(1)}, u32[]{:S(2)}, u32[]{:S(2)}) collective-permute-start(bf16[2,104,512]{2,1,0:T(8,128)(2,1)S(1)} %maximum_select_fusion.2), channel_id=1, source_target_pairs={{0,16},{16,32},{32,48},{48,64},{64,80},{80,96},{96,112},{112,128},... | collective-permute-start | bytes 638984 | tf_op jit(solution)/shard_map/ppermute | solution.py:52
  21.9 12.5 %collective-permute-start.2 = (bf16[2,104,512]{2,1,0:T(8,128)(2,1)S(1)}, bf16[2,104,512]{2,1,0:T(8,128)(2,1)S(1)}, u32[]{:S(2)}, u32[]{:S(2)}) collective-permute-start(bf16[2,104,512]{2,1,0:T(8,128)(2,1)S(1)} %maximum_select_fusion.2), channel_id=1, source_target_pairs={{0,240},{16,0},{32,16},{48,32},{64,48},{80,64},{96,80},{112,96},{1... | collective-permute-start | bytes 638984 | tf_op jit(solution)/shard_map/ppermute | solution.py:55
  32.5 8.3 %collective-permute-start.3 = (bf16[2,104,512]{2,1,0:T(8,128)(2,1)S(1)}, bf16[2,104,512]{2,1,0:T(8,128)(2,1)S(1)}, u32[]{:S(2)}, u32[]{:S(2)}) collective-permute-start(bf16[2,104,512]{2,1,0:T(8,128)(2,1)S(1)} %collective-permute-done.1), channel_id=1, source_target_pairs={{0,16},{16,32},{32,48},{48,64},{64,80},{80,96},{96,112},{112,128},... | collective-permute-start | bytes 638984 | tf_op jit(solution)/shard_map/ppermute | solution.py:52
  34.4 8.3 %collective-permute-start.4 = (bf16[2,104,512]{2,1,0:T(8,128)(2,1)S(1)}, bf16[2,104,512]{2,1,0:T(8,128)(2,1)S(1)}, u32[]{:S(2)}, u32[]{:S(2)}) collective-permute-start(bf16[2,104,512]{2,1,0:T(8,128)(2,1)S(1)} %collective-permute-done.2), channel_id=1, source_target_pairs={{0,240},{16,0},{32,16},{48,32},{64,48},{80,64},{96,80},{112,96},{1... | collective-permute-start | bytes 638984 | tf_op jit(solution)/shard_map/ppermute | solution.py:55
  40.8 7.8 %collective-permute-start.5 = (bf16[2,104,512]{2,1,0:T(8,128)(2,1)S(1)}, bf16[2,104,512]{2,1,0:T(8,128)(2,1)S(1)}, u32[]{:S(2)}, u32[]{:S(2)}) collective-permute-start(bf16[2,104,512]{2,1,0:T(8,128)(2,1)S(1)} %collective-permute-done.3), channel_id=1, source_target_pairs={{0,16},{16,32},{32,48},{48,64},{64,80},{80,96},{96,112},{112,128},... | collective-permute-start | bytes 638984 | tf_op jit(solution)/shard_map/ppermute | solution.py:52
  48.5 7.8 %collective-permute-start.7 = (bf16[2,104,512]{2,1,0:T(8,128)(2,1)S(1)}, bf16[2,104,512]{2,1,0:T(8,128)(2,1)S(1)}, u32[]{:S(2)}, u32[]{:S(2)}) collective-permute-start(bf16[2,104,512]{2,1,0:T(8,128)(2,1)S(1)} %collective-permute-done.5), channel_id=1, source_target_pairs={{0,16},{16,32},{32,48},{48,64},{64,80},{80,96},{96,112},{112,128},... | collective-permute-start | bytes 638984 | tf_op jit(solution)/shard_map/ppermute | solution.py:52
  56.3 7.8 %collective-permute-start.9 = (bf16[2,104,512]{2,1,0:T(8,128)(2,1)S(1)}, bf16[2,104,512]{2,1,0:T(8,128)(2,1)S(1)}, u32[]{:S(2)}, u32[]{:S(2)}) collective-permute-start(bf16[2,104,512]{2,1,0:T(8,128)(2,1)S(1)} %collective-permute-done.7), channel_id=1, source_target_pairs={{0,16},{16,32},{32,48},{48,64},{64,80},{80,96},{96,112},{112,128},... | collective-permute-start | bytes 638984 | tf_op jit(solution)/shard_map/ppermute | solution.py:52
  64.1 7.8 %collective-permute-start.11 = (bf16[2,104,512]{2,1,0:T(8,128)(2,1)S(1)}, bf16[2,104,512]{2,1,0:T(8,128)(2,1)S(1)}, u32[]{:S(2)}, u32[]{:S(2)}) collective-permute-start(bf16[2,104,512]{2,1,0:T(8,128)(2,1)S(1)} %collective-permute-done.9), channel_id=1, source_target_pairs={{0,16},{16,32},{32,48},{48,64},{64,80},{80,96},{96,112},{112,128},... | collective-permute-start | bytes 638984 | tf_op jit(solution)/shard_map/ppermute | solution.py:52
  71.9 8.7 %collective-permute-start.13 = (bf16[2,104,512]{2,1,0:T(8,128)(2,1)S(1)}, bf16[2,104,512]{2,1,0:T(8,128)(2,1)S(1)}, u32[]{:S(2)}, u32[]{:S(2)}) collective-permute-start(bf16[2,104,512]{2,1,0:T(8,128)(2,1)S(1)} %collective-permute-done.11), channel_id=1, source_target_pairs={{0,16},{16,32},{32,48},{48,64},{64,80},{80,96},{96,112},{112,128},... | collective-permute-start | bytes 638984 | tf_op jit(solution)/shard_map/ppermute | solution.py:52
  73.8 8.7 %collective-permute-start.14 = (bf16[2,104,512]{2,1,0:T(8,128)(2,1)S(1)}, bf16[2,104,512]{2,1,0:T(8,128)(2,1)S(1)}, u32[]{:S(2)}, u32[]{:S(2)}) collective-permute-start(bf16[2,104,512]{2,1,0:T(8,128)(2,1)S(1)} %collective-permute-done.12), channel_id=1, source_target_pairs={{0,240},{16,0},{32,16},{48,32},{64,48},{80,64},{96,80},{112,96},{1... | collective-permute-start | bytes 638984 | tf_op jit(solution)/shard_map/ppermute | solution.py:55
  80.6 8.1 %collective-permute-start.15 = (bf16[1,104,512]{2,1,0:T(8,128)(2,1)S(1)}, bf16[1,104,512]{2,1,0:T(8,128)(2,1)S(1)}, u32[]{:S(2)}, u32[]{:S(2)}) collective-permute-start(bf16[1,104,512]{2,1,0:T(8,128)(2,1)S(1)} %slice.442), channel_id=1, source_target_pairs={{0,16},{16,32},{32,48},{48,64},{64,80},{80,96},{96,112},{112,128},... | collective-permute-start | bytes 319496 | tf_op jit(solution)/shard_map/ppermute | solution.py:47
  105.4 16.5 %collective-permute-start.20 = (bf16[2,320,1,256]{3,1,2,0:T(8,128)(2,1)S(1)}, bf16[2,320,1,256]{3,1,2,0:T(8,128)(2,1)S(1)}, u32[]{:S(2)}, u32[]{:S(2)}) collective-permute-start(bf16[2,320,1,256]{3,1,2,0:T(8,128)(2,1)S(1)} %maximum_select_fusion), channel_id=1, source_target_pairs={{0,240},{16,0},{32,16},{48,32},{64,48},{80,64},{96,80},{112,96},{1... | collective-permute-start | bytes 983048 | tf_op jit(solution)/shard_map/ppermute | solution.py:227
  110.8 9.0 %collective-permute-start.18 = (bf16[2,320,1,256]{3,1,2,0:T(8,128)(2,1)S(1)}, bf16[2,320,1,256]{3,1,2,0:T(8,128)(2,1)S(1)}, u32[]{:S(2)}, u32[]{:S(2)}) collective-permute-start(bf16[2,320,1,256]{3,1,2,0:T(8,128)(2,1)S(1)} %maximum_select_fusion), channel_id=1, source_target_pairs={{0,16},{16,32},{32,48},{48,64},{64,80},{80,96},{96,112},{112,128},... | collective-permute-start | bytes 983048 | tf_op jit(solution)/shard_map/ppermute | solution.py:224
  119.8 10.5 %collective-permute-start.19 = (bf16[2,320,1,256]{3,1,2,0:T(8,128)(2,1)S(1)}, bf16[2,320,1,256]{3,1,2,0:T(8,128)(2,1)S(1)}, u32[]{:S(2)}, u32[]{:S(2)}) collective-permute-start(bf16[2,320,1,256]{3,1,2,0:T(8,128)(2,1)S(1)} %collective-permute-done.18), channel_id=1, source_target_pairs={{0,16},{16,32},{32,48},{48,64},{64,80},{80,96},{96,112},{112,128},... | collective-permute-start | bytes 983048 | tf_op jit(solution)/shard_map/ppermute | solution.py:224
  123.4 8.8 %collective-permute-start.22 = (bf16[2,320,1,256]{3,1,2,0:T(8,128)(2,1)S(1)}, bf16[2,320,1,256]{3,1,2,0:T(8,128)(2,1)S(1)}, u32[]{:S(2)}, u32[]{:S(2)}) collective-permute-start(bf16[2,320,1,256]{3,1,2,0:T(8,128)(2,1)S(1)} %collective-permute-done.20), channel_id=1, source_target_pairs={{0,240},{16,0},{32,16},{48,32},{64,48},{80,64},{96,80},{112,96},{1... | collective-permute-start | bytes 983048 | tf_op jit(solution)/shard_map/ppermute | solution.py:227
  130.3 9.6 %collective-permute-start.21 = (bf16[2,320,1,256]{3,1,2,0:T(8,128)(2,1)S(1)}, bf16[2,320,1,256]{3,1,2,0:T(8,128)(2,1)S(1)}, u32[]{:S(2)}, u32[]{:S(2)}) collective-permute-start(bf16[2,320,1,256]{3,1,2,0:T(8,128)(2,1)S(1)} %collective-permute-done.19), channel_id=1, source_target_pairs={{0,16},{16,32},{32,48},{48,64},{64,80},{80,96},{96,112},{112,128},... | collective-permute-start | bytes 983048 | tf_op jit(solution)/shard_map/ppermute | solution.py:224
  133.8 8.8 %collective-permute-start.24 = (bf16[2,320,1,256]{3,1,2,0:T(8,128)(2,1)S(1)}, bf16[2,320,1,256]{3,1,2,0:T(8,128)(2,1)S(1)}, u32[]{:S(2)}, u32[]{:S(2)}) collective-permute-start(bf16[2,320,1,256]{3,1,2,0:T(8,128)(2,1)S(1)} %collective-permute-done.22), channel_id=1, source_target_pairs={{0,240},{16,0},{32,16},{48,32},{64,48},{80,64},{96,80},{112,96},{1... | collective-permute-start | bytes 983048 | tf_op jit(solution)/shard_map/ppermute | solution.py:227
  140.0 10.4 %collective-permute-start.23 = (bf16[2,320,1,256]{3,1,2,0:T(8,128)(2,1)S(1)}, bf16[2,320,1,256]{3,1,2,0:T(8,128)(2,1)S(1)}, u32[]{:S(2)}, u32[]{:S(2)}) collective-permute-start(bf16[2,320,1,256]{3,1,2,0:T(8,128)(2,1)S(1)} %collective-permute-done.21), channel_id=1, source_target_pairs={{0,16},{16,32},{32,48},{48,64},{64,80},{80,96},{96,112},{112,128},... | collective-permute-start | bytes 983048 | tf_op jit(solution)/shard_map/ppermute | solution.py:224
  144.2 9.4 %collective-permute-start.26 = (bf16[2,320,1,256]{3,1,2,0:T(8,128)(2,1)S(1)}, bf16[2,320,1,256]{3,1,2,0:T(8,128)(2,1)S(1)}, u32[]{:S(2)}, u32[]{:S(2)}) collective-permute-start(bf16[2,320,1,256]{3,1,2,0:T(8,128)(2,1)S(1)} %collective-permute-done.24), channel_id=1, source_target_pairs={{0,240},{16,0},{32,16},{48,32},{64,48},{80,64},{96,80},{112,96},{1... | collective-permute-start | bytes 983048 | tf_op jit(solution)/shard_map/ppermute | solution.py:227
  150.3 10.6 %collective-permute-start.25 = (bf16[2,320,1,256]{3,1,2,0:T(8,128)(2,1)S(1)}, bf16[2,320,1,256]{3,1,2,0:T(8,128)(2,1)S(1)}, u32[]{:S(2)}, u32[]{:S(2)}) collective-permute-start(bf16[2,320,1,256]{3,1,2,0:T(8,128)(2,1)S(1)} %collective-permute-done.23), channel_id=1, source_target_pairs={{0,16},{16,32},{32,48},{48,64},{64,80},{80,96},{96,112},{112,128},... | collective-permute-start | bytes 983048 | tf_op jit(solution)/shard_map/ppermute | solution.py:224
  155.1 9.0 %collective-permute-start.28 = (bf16[2,320,1,256]{3,1,2,0:T(8,128)(2,1)S(1)}, bf16[2,320,1,256]{3,1,2,0:T(8,128)(2,1)S(1)}, u32[]{:S(2)}, u32[]{:S(2)}) collective-permute-start(bf16[2,320,1,256]{3,1,2,0:T(8,128)(2,1)S(1)} %collective-permute-done.26), channel_id=1, source_target_pairs={{0,240},{16,0},{32,16},{48,32},{64,48},{80,64},{96,80},{112,96},{1... | collective-permute-start | bytes 983048 | tf_op jit(solution)/shard_map/ppermute | solution.py:227
  160.9 10.6 %collective-permute-start.27 = (bf16[2,320,1,256]{3,1,2,0:T(8,128)(2,1)S(1)}, bf16[2,320,1,256]{3,1,2,0:T(8,128)(2,1)S(1)}, u32[]{:S(2)}, u32[]{:S(2)}) collective-permute-start(bf16[2,320,1,256]{3,1,2,0:T(8,128)(2,1)S(1)} %collective-permute-done.25), channel_id=1, source_target_pairs={{0,16},{16,32},{32,48},{48,64},{64,80},{80,96},{96,112},{112,128},... | collective-permute-start | bytes 983048 | tf_op jit(solution)/shard_map/ppermute | solution.py:224
  165.7 9.0 %collective-permute-start.30 = (bf16[2,320,1,256]{3,1,2,0:T(8,128)(2,1)S(1)}, bf16[2,320,1,256]{3,1,2,0:T(8,128)(2,1)S(1)}, u32[]{:S(2)}, u32[]{:S(2)}) collective-permute-start(bf16[2,320,1,256]{3,1,2,0:T(8,128)(2,1)S(1)} %collective-permute-done.28), channel_id=1, source_target_pairs={{0,240},{16,0},{32,16},{48,32},{64,48},{80,64},{96,80},{112,96},{1... | collective-permute-start | bytes 983048 | tf_op jit(solution)/shard_map/ppermute | solution.py:227
  171.5 18.8 %collective-permute-start.29 = (bf16[2,320,1,256]{3,1,2,0:T(8,128)(2,1)S(1)}, bf16[2,320,1,256]{3,1,2,0:T(8,128)(2,1)S(1)}, u32[]{:S(2)}, u32[]{:S(2)}) collective-permute-start(bf16[2,320,1,256]{3,1,2,0:T(8,128)(2,1)S(1)} %collective-permute-done.27), channel_id=1, source_target_pairs={{0,16},{16,32},{32,48},{48,64},{64,80},{80,96},{96,112},{112,128},... | collective-permute-start | bytes 983048 | tf_op jit(solution)/shard_map/ppermute | solution.py:224
  176.3 9.0 %collective-permute-start.31 = (bf16[2,320,1,256]{3,1,2,0:T(8,128)(2,1)S(1)}, bf16[2,320,1,256]{3,1,2,0:T(8,128)(2,1)S(1)}, u32[]{:S(2)}, u32[]{:S(2)}) collective-permute-start(bf16[2,320,1,256]{3,1,2,0:T(8,128)(2,1)S(1)} %collective-permute-done.30), channel_id=1, source_target_pairs={{0,240},{16,0},{32,16},{48,32},{64,48},{80,64},{96,80},{112,96},{1... | collective-permute-start | bytes 983048 | tf_op jit(solution)/shard_map/ppermute | solution.py:227
  185.3 9.1 %collective-permute-start.33 = (bf16[1,320,1,256]{3,1,2,0:T(8,128)(2,1)S(1)}, bf16[1,320,1,256]{3,1,2,0:T(8,128)(2,1)S(1)}, u32[]{:S(2)}, u32[]{:S(2)}) collective-permute-start(bf16[1,320,1,256]{3,1,2,0:T(8,128)(2,1)S(1)} %slice.485), channel_id=1, source_target_pairs={{0,240},{16,0},{32,16},{48,32},{64,48},{80,64},{96,80},{112,96},{1... | collective-permute-start | bytes 491528 | tf_op jit(solution)/shard_map/ppermute | solution.py:221
  190.4 9.3 %collective-permute-start.32 = (bf16[1,320,1,256]{3,1,2,0:T(8,128)(2,1)S(1)}, bf16[1,320,1,256]{3,1,2,0:T(8,128)(2,1)S(1)}, u32[]{:S(2)}, u32[]{:S(2)}) collective-permute-start(bf16[1,320,1,256]{3,1,2,0:T(8,128)(2,1)S(1)} %slice.376), channel_id=1, source_target_pairs={{0,16},{16,32},{32,48},{48,64},{64,80},{80,96},{96,112},{112,128},... | collective-permute-start | bytes 491528 | tf_op jit(solution)/shard_map/ppermute | solution.py:220
  202.0 25.7 %collective-permute-start.38 = (bf16[160,1536]{1,0:T(8,128)(2,1)S(1)}, bf16[160,1536]{1,0:T(8,128)(2,1)S(1)}, u32[]{:S(2)}, u32[]{:S(2)}) collective-permute-start(bf16[160,1536]{1,0:T(8,128)(2,1)S(1)} %dynamic-slice_convert_fusion), channel_id=1, source_target_pairs={{0,1},{1,0},{2,3},{3,2},{4,5},{5,4},{6,7},{7,6},{8,9},{9,8},{10,11... | collective-permute-start | bytes 1474568 | tf_op jit(solution)/shard_map/ppermute | solution.py:81
  227.8 8.9 %collective-permute-start.39 = (bf16[160,768]{1,0:T(8,128)(2,1)S(1)}, bf16[160,768]{1,0:T(8,128)(2,1)S(1)}, u32[]{:S(2)}, u32[]{:S(2)}) collective-permute-start(bf16[160,768]{1,0:T(8,128)(2,1)S(1)} %dynamic-slice_convert_fusion.2), channel_id=1, source_target_pairs={{0,2},{1,3},{2,0},{3,1},{4,6},{5,7},{6,4},{7,5},{8,10},{9,11},{10,... | collective-permute-start | bytes 737288 | tf_op jit(solution)/shard_map/ppermute | solution.py:81
  231.1 10.4 %collective-permute-start.35 = (bf16[160,768]{1,0:T(8,128)(2,1)S(1)}, bf16[160,768]{1,0:T(8,128)(2,1)S(1)}, u32[]{:S(2)}, u32[]{:S(2)}) collective-permute-start(bf16[160,768]{1,0:T(8,128)(2,1)S(1)} %dynamic-slice_convert_fusion.3), channel_id=1, source_target_pairs={{0,8},{1,9},{2,10},{3,11},{4,12},{5,13},{6,14},{7,15},{8,0},{9,1},... | collective-permute-start | bytes 737288 | tf_op jit(solution)/shard_map/ppermute | solution.py:81
  (20 other events, 152.5 us)

commit v10 on v7

--- a/solution.py
+++ b/solution.py
@@ -38,23 +38,33 @@
     ring_pos = position % ring
     forward = [(y * ring + a, y * ring + (a + 1) % ring) for y in range(2) for a in range(ring)]
     backward = [(y * ring + a, y * ring + (a - 1) % ring) for y in range(2) for a in range(ring)]
-    pieces = [(pair, ring_pos)]
+    pieces = [(pair, ring_pos, (0, 1))]
     ahead = pair
     behind = pair
     for step in range(1, ring // 2 + 1):
+        source = (ring_pos - step) % ring
+        if 2 * step == ring:
+            ahead = lax.ppermute(ahead[:1], axis, forward)
+            behind = lax.ppermute(behind[1:], axis, backward)
+            pieces.append((ahead, source, (0,)))
+            pieces.append((behind, source, (1,)))
+            break
         ahead = lax.ppermute(ahead, axis, forward)
-        pieces.append((ahead, (ring_pos - step) % ring))
+        pieces.append((ahead, source, (0, 1)))
         if step < ring - ring // 2:
             behind = lax.ppermute(behind, axis, backward)
-            pieces.append((behind, (ring_pos + step) % ring))
+            pieces.append((behind, (ring_pos + step) % ring, (0, 1)))
     return pieces, ring
 
 
 def ring_gather(block, axis):
     pieces, ring = ring_pieces(block, axis)
     gathered = jnp.zeros((ring,) + pieces[0][0].shape, block.dtype)
-    for piece, source in pieces:
-        gathered = lax.dynamic_update_index_in_dim(gathered, piece, source, 0)
+    zero = jnp.zeros((), jnp.int32)
+    for piece, source, halves in pieces:
+        gathered = lax.dynamic_update_slice(
+            gathered, piece[None], (source, halves[0]) + (zero,) * block.ndim
+        )
     gathered = jnp.swapaxes(gathered, 0, 1)
     return gathered.reshape((2 * ring * block.shape[0],) + block.shape[1:])
 

time: 247 us -> 250 us (1.012)
  starting transfers between devices: 155 us -> 162 us
  waiting for transfers between devices: 45.9 us -> 42 us
    ppermute x8 -> x7, waiting for transfers between devices: 18.7 us -> 11 us  [ring_pieces(): ahead = lax.ppermute(ahead, axis, forward)]
    ppermute x0 -> x2, starting transfers between devices: none -> 6.76 us  [the longest x1 4.84 us: ring_pieces(): behind = lax.ppermute(behind[1:], axis, backward)]
    ppermute x7, starting transfers between devices: 31.4 us -> 35.1 us  [per_device(): behind = lax.ppermute(behind, 'ctx', backward)]
    ppermute x0 -> x2, waiting for transfers between devices: none -> 2.69 us  [the longest x1 1.46 us: ring_pieces(): behind = lax.ppermute(behind[1:], axis, backward)]
    ppermute x8 -> x7, starting transfers between devices: 16.9 us -> 15 us  [ring_pieces(): ahead = lax.ppermute(ahead, axis, forward)]
  transfers between devices with their start and end apart: 41 -> 42, of which waited for: 22 -> 23; matrix products, arithmetic and copies ran while one was open for 11% -> 11% of each run, Pallas kernels for 0% -> 0%
where the time goes in v10:
time: 250 us; the launch traced here: 246 us
  starting transfers between devices  162 us (65%)
  waiting for transfers between devices  42 us (17%)
  matrix products  15.6 us (6%)
  other arithmetic  14.1 us (6%)
  local copies, waits for them, and re-layouts  9.34 us (4%)
  between operations  2.64 us (1%)
    ppermute x8, starting transfers between devices, halving_scatter(): lax.ppermute(send.astype(jnp.bfloat16), axis, [(i, i ^ 1 << bit) for i in...  42.9 us
    ppermute x7, starting transfers between devices, ring_pieces(): behind = lax.ppermute(behind, axis, backward)  35.3 us
    ppermute x7, starting transfers between devices, per_device(): behind = lax.ppermute(behind, 'ctx', backward)  35.1 us
    ppermute x8, starting transfers between devices, per_device(): ahead = lax.ppermute(ahead, 'ctx', forward)  15.7 us
    ppermute x7, starting transfers between devices, ring_pieces(): ahead = lax.ppermute(ahead, axis, forward)  15 us
    ppermute x8, waiting for transfers between devices, per_device(): ahead = lax.ppermute(ahead, 'ctx', forward)  12.9 us
    ppermute x7, waiting for transfers between devices, ring_pieces(): ahead = lax.ppermute(ahead, axis, forward)  11 us
    dot_general x16, matrix products, attend_piece(): jnp.einsum('nhe,mhe->nhm', queries, key_part, preferred_element_type=jnp....  7.03 us
  transfers between devices with their start and end apart: 42, of which 23 were waited for; matrix products, arithmetic and copies ran while one was open for 11% of the time, Pallas kernels for 0%

profile of v10, /device:TPU:1, one launch (start us, length us, event | category | flops | bytes accessed | tf_op | source)
XLA Modules:
  0.0 245.6 jit_solution(11424587041127203119)
XLA Ops:
  2.3 5.7 %collective-permute-start = (bf16[104,512]{1,0:T(8,128)(2,1)S(1)}, bf16[104,512]{1,0:T(8,128)(2,1)S(1)}, u32[]{:S(2)}, u32[]{:S(2)}) collective-permute-start(bf16[104,512]{1,0:T(8,128)(2,1)S(1)} %get-tuple-element.155), channel_id=1, source_target_pairs={{0,256},{16,272},{32,288},{48,304},{64,320},{80,336},{96,352},{112... | collective-permute-start | bytes 319496 | tf_op jit(solution)/shard_map/ppermute | solution.py:34
  9.1 3.6 %collective-permute-start.41 = (bf16[320,192]{1,0:T(8,128)(2,1)S(1)}, bf16[320,192]{1,0:T(8,128)(2,1)S(1)}, u32[]{:S(2)}, u32[]{:S(2)}) collective-permute-start(bf16[320,192]{1,0:T(8,128)(2,1)S(1)} %constant_dynamic-slice_fusion), channel_id=1, source_target_pairs={{0,16},{16,32},{32,48},{48,64},{64,80},{80,96},{96,112},{112,128},... | collective-permute-start | bytes 368648 | tf_op jit(solution)/shard_map/ppermute | solution.py:19
  17.8 3.5 %collective-permute-start.1 = (bf16[2,104,512]{2,1,0:T(8,128)(2,1)S(1)}, bf16[2,104,512]{2,1,0:T(8,128)(2,1)S(1)}, u32[]{:S(2)}, u32[]{:S(2)}) collective-permute-start(bf16[2,104,512]{2,1,0:T(8,128)(2,1)S(1)} %maximum_select_fusion.2), channel_id=1, source_target_pairs={{0,16},{16,32},{32,48},{48,64},{64,80},{80,96},{96,112},{112,128},... | collective-permute-start | bytes 638984 | tf_op jit(solution)/shard_map/ppermute | solution.py:52
  21.3 7.9 %collective-permute-start.2 = (bf16[2,104,512]{2,1,0:T(8,128)(2,1)S(1)}, bf16[2,104,512]{2,1,0:T(8,128)(2,1)S(1)}, u32[]{:S(2)}, u32[]{:S(2)}) collective-permute-start(bf16[2,104,512]{2,1,0:T(8,128)(2,1)S(1)} %maximum_select_fusion.2), channel_id=1, source_target_pairs={{0,240},{16,0},{32,16},{48,32},{64,48},{80,64},{96,80},{112,96},{1... | collective-permute-start | bytes 638984 | tf_op jit(solution)/shard_map/ppermute | solution.py:55
  29.7 2.3 collective-permute-done.1
  33.9 4.6 %collective-permute-start.4 = (bf16[2,104,512]{2,1,0:T(8,128)(2,1)S(1)}, bf16[2,104,512]{2,1,0:T(8,128)(2,1)S(1)}, u32[]{:S(2)}, u32[]{:S(2)}) collective-permute-start(bf16[2,104,512]{2,1,0:T(8,128)(2,1)S(1)} %collective-permute-done.2), channel_id=1, source_target_pairs={{0,240},{16,0},{32,16},{48,32},{64,48},{80,64},{96,80},{112,96},{1... | collective-permute-start | bytes 638984 | tf_op jit(solution)/shard_map/ppermute | solution.py:55
  42.2 4.6 %collective-permute-start.6 = (bf16[2,104,512]{2,1,0:T(8,128)(2,1)S(1)}, bf16[2,104,512]{2,1,0:T(8,128)(2,1)S(1)}, u32[]{:S(2)}, u32[]{:S(2)}) collective-permute-start(bf16[2,104,512]{2,1,0:T(8,128)(2,1)S(1)} %collective-permute-done.4), channel_id=1, source_target_pairs={{0,240},{16,0},{32,16},{48,32},{64,48},{80,64},{96,80},{112,96},{1... | collective-permute-start | bytes 638984 | tf_op jit(solution)/shard_map/ppermute | solution.py:55
  49.9 4.6 %collective-permute-start.8 = (bf16[2,104,512]{2,1,0:T(8,128)(2,1)S(1)}, bf16[2,104,512]{2,1,0:T(8,128)(2,1)S(1)}, u32[]{:S(2)}, u32[]{:S(2)}) collective-permute-start(bf16[2,104,512]{2,1,0:T(8,128)(2,1)S(1)} %collective-permute-done.6), channel_id=1, source_target_pairs={{0,240},{16,0},{32,16},{48,32},{64,48},{80,64},{96,80},{112,96},{1... | collective-permute-start | bytes 638984 | tf_op jit(solution)/shard_map/ppermute | solution.py:55
  57.7 4.6 %collective-permute-start.10 = (bf16[2,104,512]{2,1,0:T(8,128)(2,1)S(1)}, bf16[2,104,512]{2,1,0:T(8,128)(2,1)S(1)}, u32[]{:S(2)}, u32[]{:S(2)}) collective-permute-start(bf16[2,104,512]{2,1,0:T(8,128)(2,1)S(1)} %collective-permute-done.8), channel_id=1, source_target_pairs={{0,240},{16,0},{32,16},{48,32},{64,48},{80,64},{96,80},{112,96},{1... | collective-permute-start | bytes 638984 | tf_op jit(solution)/shard_map/ppermute | solution.py:55
  65.5 4.6 %collective-permute-start.12 = (bf16[2,104,512]{2,1,0:T(8,128)(2,1)S(1)}, bf16[2,104,512]{2,1,0:T(8,128)(2,1)S(1)}, u32[]{:S(2)}, u32[]{:S(2)}) collective-permute-start(bf16[2,104,512]{2,1,0:T(8,128)(2,1)S(1)} %collective-permute-done.10), channel_id=1, source_target_pairs={{0,240},{16,0},{32,16},{48,32},{64,48},{80,64},{96,80},{112,96},{1... | collective-permute-start | bytes 638984 | tf_op jit(solution)/shard_map/ppermute | solution.py:55
  73.3 4.6 %collective-permute-start.14 = (bf16[2,104,512]{2,1,0:T(8,128)(2,1)S(1)}, bf16[2,104,512]{2,1,0:T(8,128)(2,1)S(1)}, u32[]{:S(2)}, u32[]{:S(2)}) collective-permute-start(bf16[2,104,512]{2,1,0:T(8,128)(2,1)S(1)} %collective-permute-done.12), channel_id=1, source_target_pairs={{0,240},{16,0},{32,16},{48,32},{64,48},{80,64},{96,80},{112,96},{1... | collective-permute-start | bytes 638984 | tf_op jit(solution)/shard_map/ppermute | solution.py:55
  82.0 4.8 %collective-permute-start.16 = (bf16[1,104,512]{2,1,0:T(8,128)(2,1)S(1)}, bf16[1,104,512]{2,1,0:T(8,128)(2,1)S(1)}, u32[]{:S(2)}, u32[]{:S(2)}) collective-permute-start(bf16[1,104,512]{2,1,0:T(8,128)(2,1)S(1)} %slice.427), channel_id=1, source_target_pairs={{0,240},{16,0},{32,16},{48,32},{64,48},{80,64},{96,80},{112,96},{1... | collective-permute-start | bytes 319496 | tf_op jit(solution)/shard_map/ppermute | solution.py:48
  101.4 3.5 %collective-permute-done.17 = bf16[320,1,256]{2,0,1:T(8,128)(2,1)S(1)} collective-permute-done((bf16[320,1,256]{2,0,1:T(8,128)(2,1)S(1)}, bf16[320,1,256]{2,0,1:T(8,128)(2,1)S(1)}, u32[]{:S(2)}, u32[]{:S(2)}) %collective-permute-start.17) | collective-permute-done | bytes 163872 | tf_op jit(solution)/shard_map/ppermute | solution.py:189
  104.9 5.3 %collective-permute-start.20 = (bf16[2,320,1,256]{3,1,2,0:T(8,128)(2,1)S(1)}, bf16[2,320,1,256]{3,1,2,0:T(8,128)(2,1)S(1)}, u32[]{:S(2)}, u32[]{:S(2)}) collective-permute-start(bf16[2,320,1,256]{3,1,2,0:T(8,128)(2,1)S(1)} %maximum_select_fusion), channel_id=1, source_target_pairs={{0,240},{16,0},{32,16},{48,32},{64,48},{80,64},{96,80},{112,96},{1... | collective-permute-start | bytes 983048 | tf_op jit(solution)/shard_map/ppermute | solution.py:223
  113.5 5.8 %collective-permute-done.18 = bf16[2,320,1,256]{3,1,2,0:T(8,128)(2,1)S(1)} collective-permute-done((bf16[2,320,1,256]{3,1,2,0:T(8,128)(2,1)S(1)}, bf16[2,320,1,256]{3,1,2,0:T(8,128)(2,1)S(1)}, u32[]{:S(2)}, u32[]{:S(2)}) %collective-permute-start.18) | collective-permute-done | bytes 327712 | tf_op jit(solution)/shard_map/ppermute | solution.py:220
  122.9 4.6 %collective-permute-start.22 = (bf16[2,320,1,256]{3,1,2,0:T(8,128)(2,1)S(1)}, bf16[2,320,1,256]{3,1,2,0:T(8,128)(2,1)S(1)}, u32[]{:S(2)}, u32[]{:S(2)}) collective-permute-start(bf16[2,320,1,256]{3,1,2,0:T(8,128)(2,1)S(1)} %collective-permute-done.20), channel_id=1, source_target_pairs={{0,240},{16,0},{32,16},{48,32},{64,48},{80,64},{96,80},{112,96},{1... | collective-permute-start | bytes 983048 | tf_op jit(solution)/shard_map/ppermute | solution.py:223
  133.3 4.8 %collective-permute-start.24 = (bf16[2,320,1,256]{3,1,2,0:T(8,128)(2,1)S(1)}, bf16[2,320,1,256]{3,1,2,0:T(8,128)(2,1)S(1)}, u32[]{:S(2)}, u32[]{:S(2)}) collective-permute-start(bf16[2,320,1,256]{3,1,2,0:T(8,128)(2,1)S(1)} %collective-permute-done.22), channel_id=1, source_target_pairs={{0,240},{16,0},{32,16},{48,32},{64,48},{80,64},{96,80},{112,96},{1... | collective-permute-start | bytes 983048 | tf_op jit(solution)/shard_map/ppermute | solution.py:223
  143.6 5.4 %collective-permute-start.26 = (bf16[2,320,1,256]{3,1,2,0:T(8,128)(2,1)S(1)}, bf16[2,320,1,256]{3,1,2,0:T(8,128)(2,1)S(1)}, u32[]{:S(2)}, u32[]{:S(2)}) collective-permute-start(bf16[2,320,1,256]{3,1,2,0:T(8,128)(2,1)S(1)} %collective-permute-done.24), channel_id=1, source_target_pairs={{0,240},{16,0},{32,16},{48,32},{64,48},{80,64},{96,80},{112,96},{1... | collective-permute-start | bytes 983048 | tf_op jit(solution)/shard_map/ppermute | solution.py:223
  154.6 5.0 %collective-permute-start.28 = (bf16[2,320,1,256]{3,1,2,0:T(8,128)(2,1)S(1)}, bf16[2,320,1,256]{3,1,2,0:T(8,128)(2,1)S(1)}, u32[]{:S(2)}, u32[]{:S(2)}) collective-permute-start(bf16[2,320,1,256]{3,1,2,0:T(8,128)(2,1)S(1)} %collective-permute-done.26), channel_id=1, source_target_pairs={{0,240},{16,0},{32,16},{48,32},{64,48},{80,64},{96,80},{112,96},{1... | collective-permute-start | bytes 983048 | tf_op jit(solution)/shard_map/ppermute | solution.py:223
  165.1 5.0 %collective-permute-start.30 = (bf16[2,320,1,256]{3,1,2,0:T(8,128)(2,1)S(1)}, bf16[2,320,1,256]{3,1,2,0:T(8,128)(2,1)S(1)}, u32[]{:S(2)}, u32[]{:S(2)}) collective-permute-start(bf16[2,320,1,256]{3,1,2,0:T(8,128)(2,1)S(1)} %collective-permute-done.28), channel_id=1, source_target_pairs={{0,240},{16,0},{32,16},{48,32},{64,48},{80,64},{96,80},{112,96},{1... | collective-permute-start | bytes 983048 | tf_op jit(solution)/shard_map/ppermute | solution.py:223
  171.0 2.1 collective-permute-start.29
  176.1 5.0 %collective-permute-start.31 = (bf16[2,320,1,256]{3,1,2,0:T(8,128)(2,1)S(1)}, bf16[2,320,1,256]{3,1,2,0:T(8,128)(2,1)S(1)}, u32[]{:S(2)}, u32[]{:S(2)}) collective-permute-start(bf16[2,320,1,256]{3,1,2,0:T(8,128)(2,1)S(1)} %collective-permute-done.30), channel_id=1, source_target_pairs={{0,240},{16,0},{32,16},{48,32},{64,48},{80,64},{96,80},{112,96},{1... | collective-permute-start | bytes 983048 | tf_op jit(solution)/shard_map/ppermute | solution.py:223
  185.6 5.0 %collective-permute-done.32 = bf16[2,320,1,256]{3,1,2,0:T(8,128)(2,1)S(1)} collective-permute-done((bf16[2,320,1,256]{3,1,2,0:T(8,128)(2,1)S(1)}, bf16[2,320,1,256]{3,1,2,0:T(8,128)(2,1)S(1)}, u32[]{:S(2)}, u32[]{:S(2)}) %collective-permute-start.32) | collective-permute-done | bytes 327712 | tf_op jit(solution)/shard_map/ppermute | solution.py:220
  193.3 22.4 %collective-permute-start.37 = (bf16[160,1536]{1,0:T(8,128)(2,1)S(1)}, bf16[160,1536]{1,0:T(8,128)(2,1)S(1)}, u32[]{:S(2)}, u32[]{:S(2)}) collective-permute-start(bf16[160,1536]{1,0:T(8,128)(2,1)S(1)} %dynamic-slice_convert_fusion), channel_id=1, source_target_pairs={{0,1},{1,0},{2,3},{3,2},{4,5},{5,4},{6,7},{7,6},{8,9},{9,8},{10,11... | collective-permute-start | bytes 1474568 | tf_op jit(solution)/shard_map/ppermute | solution.py:81
  218.3 3.1 %collective-permute-start.38 = (bf16[160,768]{1,0:T(8,128)(2,1)S(1)}, bf16[160,768]{1,0:T(8,128)(2,1)S(1)}, u32[]{:S(2)}, u32[]{:S(2)}) collective-permute-start(bf16[160,768]{1,0:T(8,128)(2,1)S(1)} %dynamic-slice_convert_fusion.2), channel_id=1, source_target_pairs={{0,2},{1,3},{2,0},{3,1},{4,6},{5,7},{6,4},{7,5},{8,10},{9,11},{10,... | collective-permute-start | bytes 737288 | tf_op jit(solution)/shard_map/ppermute | solution.py:81
  221.6 2.3 collective-permute-start.34
  223.9 3.3 %collective-permute-done.38 = bf16[160,768]{1,0:T(8,128)(2,1)S(1)} collective-permute-done((bf16[160,768]{1,0:T(8,128)(2,1)S(1)}, bf16[160,768]{1,0:T(8,128)(2,1)S(1)}, u32[]{:S(2)}, u32[]{:S(2)}) %collective-permute-start.38) | collective-permute-done | bytes 245792 | tf_op jit(solution)/shard_map/ppermute | solution.py:81
  227.3 4.6 %collective-permute-start.39 = (bf16[160,384]{1,0:T(8,128)(2,1)S(1)}, bf16[160,384]{1,0:T(8,128)(2,1)S(1)}, u32[]{:S(2)}, u32[]{:S(2)}) collective-permute-start(bf16[160,384]{1,0:T(8,128)(2,1)S(1)} %dynamic-slice_convert_fusion.4), channel_id=1, source_target_pairs={{0,4},{1,5},{2,6},{3,7},{4,0},{5,1},{6,2},{7,3},{8,12},{9,13},{10,... | collective-permute-start | bytes 368648 | tf_op jit(solution)/shard_map/ppermute | solution.py:81
  232.1 2.2 collective-permute-start.35
  234.6 2.3 collective-permute-start.40
  237.8 4.0 %collective-permute-start.36 = (bf16[160,192]{1,0:T(8,128)(2,1)S(1)}, bf16[160,192]{1,0:T(8,128)(2,1)S(1)}, u32[]{:S(2)}, u32[]{:S(2)}) collective-permute-start(bf16[160,192]{1,0:T(8,128)(2,1)S(1)} %dynamic-slice_convert_fusion.7), channel_id=1, source_target_pairs={{0,4},{1,5},{2,6},{3,7},{4,0},{5,1},{6,2},{7,3},{8,12},{9,13},{10,... | collective-permute-start | bytes 184328 | tf_op jit(solution)/shard_map/ppermute | solution.py:81
  242.0 2.5 %collective-permute-done.36 = bf16[160,192]{1,0:T(8,128)(2,1)S(1)} collective-permute-done((bf16[160,192]{1,0:T(8,128)(2,1)S(1)}, bf16[160,192]{1,0:T(8,128)(2,1)S(1)}, u32[]{:S(2)}, u32[]{:S(2)}) %collective-permute-start.36) | collective-permute-done | bytes 61472 | tf_op jit(solution)/shard_map/ppermute | solution.py:81
  (241 shorter events, 89.4 us)
Async XLA Ops:
  2.3 15.4 %collective-permute-start = (bf16[104,512]{1,0:T(8,128)(2,1)S(1)}, bf16[104,512]{1,0:T(8,128)(2,1)S(1)}, u32[]{:S(2)}, u32[]{:S(2)}) collective-permute-start(bf16[104,512]{1,0:T(8,128)(2,1)S(1)} %get-tuple-element.155), channel_id=1, source_target_pairs={{0,256},{16,272},{32,288},{48,304},{64,320},{80,336},{96,352},{112... | collective-permute-start | bytes 319496 | tf_op jit(solution)/shard_map/ppermute | solution.py:34
  9.1 20.4 %collective-permute-start.41 = (bf16[320,192]{1,0:T(8,128)(2,1)S(1)}, bf16[320,192]{1,0:T(8,128)(2,1)S(1)}, u32[]{:S(2)}, u32[]{:S(2)}) collective-permute-start(bf16[320,192]{1,0:T(8,128)(2,1)S(1)} %constant_dynamic-slice_fusion), channel_id=1, source_target_pairs={{0,16},{16,32},{32,48},{48,64},{64,80},{80,96},{96,112},{112,128},... | collective-permute-start | bytes 368648 | tf_op jit(solution)/shard_map/ppermute | solution.py:19
  17.8 14.1 %collective-permute-start.1 = (bf16[2,104,512]{2,1,0:T(8,128)(2,1)S(1)}, bf16[2,104,512]{2,1,0:T(8,128)(2,1)S(1)}, u32[]{:S(2)}, u32[]{:S(2)}) collective-permute-start(bf16[2,104,512]{2,1,0:T(8,128)(2,1)S(1)} %maximum_select_fusion.2), channel_id=1, source_target_pairs={{0,16},{16,32},{32,48},{48,64},{64,80},{80,96},{96,112},{112,128},... | collective-permute-start | bytes 638984 | tf_op jit(solution)/shard_map/ppermute | solution.py:52
  21.3 12.5 %collective-permute-start.2 = (bf16[2,104,512]{2,1,0:T(8,128)(2,1)S(1)}, bf16[2,104,512]{2,1,0:T(8,128)(2,1)S(1)}, u32[]{:S(2)}, u32[]{:S(2)}) collective-permute-start(bf16[2,104,512]{2,1,0:T(8,128)(2,1)S(1)} %maximum_select_fusion.2), channel_id=1, source_target_pairs={{0,240},{16,0},{32,16},{48,32},{64,48},{80,64},{96,80},{112,96},{1... | collective-permute-start | bytes 638984 | tf_op jit(solution)/shard_map/ppermute | solution.py:55
  31.9 8.3 %collective-permute-start.3 = (bf16[2,104,512]{2,1,0:T(8,128)(2,1)S(1)}, bf16[2,104,512]{2,1,0:T(8,128)(2,1)S(1)}, u32[]{:S(2)}, u32[]{:S(2)}) collective-permute-start(bf16[2,104,512]{2,1,0:T(8,128)(2,1)S(1)} %collective-permute-done.1), channel_id=1, source_target_pairs={{0,16},{16,32},{32,48},{48,64},{64,80},{80,96},{96,112},{112,128},... | collective-permute-start | bytes 638984 | tf_op jit(solution)/shard_map/ppermute | solution.py:52
  33.9 8.3 %collective-permute-start.4 = (bf16[2,104,512]{2,1,0:T(8,128)(2,1)S(1)}, bf16[2,104,512]{2,1,0:T(8,128)(2,1)S(1)}, u32[]{:S(2)}, u32[]{:S(2)}) collective-permute-start(bf16[2,104,512]{2,1,0:T(8,128)(2,1)S(1)} %collective-permute-done.2), channel_id=1, source_target_pairs={{0,240},{16,0},{32,16},{48,32},{64,48},{80,64},{96,80},{112,96},{1... | collective-permute-start | bytes 638984 | tf_op jit(solution)/shard_map/ppermute | solution.py:55
  40.2 7.8 %collective-permute-start.5 = (bf16[2,104,512]{2,1,0:T(8,128)(2,1)S(1)}, bf16[2,104,512]{2,1,0:T(8,128)(2,1)S(1)}, u32[]{:S(2)}, u32[]{:S(2)}) collective-permute-start(bf16[2,104,512]{2,1,0:T(8,128)(2,1)S(1)} %collective-permute-done.3), channel_id=1, source_target_pairs={{0,16},{16,32},{32,48},{48,64},{64,80},{80,96},{96,112},{112,128},... | collective-permute-start | bytes 638984 | tf_op jit(solution)/shard_map/ppermute | solution.py:52
  42.2 7.8 %collective-permute-start.6 = (bf16[2,104,512]{2,1,0:T(8,128)(2,1)S(1)}, bf16[2,104,512]{2,1,0:T(8,128)(2,1)S(1)}, u32[]{:S(2)}, u32[]{:S(2)}) collective-permute-start(bf16[2,104,512]{2,1,0:T(8,128)(2,1)S(1)} %collective-permute-done.4), channel_id=1, source_target_pairs={{0,240},{16,0},{32,16},{48,32},{64,48},{80,64},{96,80},{112,96},{1... | collective-permute-start | bytes 638984 | tf_op jit(solution)/shard_map/ppermute | solution.py:55
  48.0 7.8 %collective-permute-start.7 = (bf16[2,104,512]{2,1,0:T(8,128)(2,1)S(1)}, bf16[2,104,512]{2,1,0:T(8,128)(2,1)S(1)}, u32[]{:S(2)}, u32[]{:S(2)}) collective-permute-start(bf16[2,104,512]{2,1,0:T(8,128)(2,1)S(1)} %collective-permute-done.5), channel_id=1, source_target_pairs={{0,16},{16,32},{32,48},{48,64},{64,80},{80,96},{96,112},{112,128},... | collective-permute-start | bytes 638984 | tf_op jit(solution)/shard_map/ppermute | solution.py:52
  55.8 7.8 %collective-permute-start.9 = (bf16[2,104,512]{2,1,0:T(8,128)(2,1)S(1)}, bf16[2,104,512]{2,1,0:T(8,128)(2,1)S(1)}, u32[]{:S(2)}, u32[]{:S(2)}) collective-permute-start(bf16[2,104,512]{2,1,0:T(8,128)(2,1)S(1)} %collective-permute-done.7), channel_id=1, source_target_pairs={{0,16},{16,32},{32,48},{48,64},{64,80},{80,96},{96,112},{112,128},... | collective-permute-start | bytes 638984 | tf_op jit(solution)/shard_map/ppermute | solution.py:52
  63.6 7.8 %collective-permute-start.11 = (bf16[2,104,512]{2,1,0:T(8,128)(2,1)S(1)}, bf16[2,104,512]{2,1,0:T(8,128)(2,1)S(1)}, u32[]{:S(2)}, u32[]{:S(2)}) collective-permute-start(bf16[2,104,512]{2,1,0:T(8,128)(2,1)S(1)} %collective-permute-done.9), channel_id=1, source_target_pairs={{0,16},{16,32},{32,48},{48,64},{64,80},{80,96},{96,112},{112,128},... | collective-permute-start | bytes 638984 | tf_op jit(solution)/shard_map/ppermute | solution.py:52
  71.4 8.7 %collective-permute-start.13 = (bf16[2,104,512]{2,1,0:T(8,128)(2,1)S(1)}, bf16[2,104,512]{2,1,0:T(8,128)(2,1)S(1)}, u32[]{:S(2)}, u32[]{:S(2)}) collective-permute-start(bf16[2,104,512]{2,1,0:T(8,128)(2,1)S(1)} %collective-permute-done.11), channel_id=1, source_target_pairs={{0,16},{16,32},{32,48},{48,64},{64,80},{80,96},{96,112},{112,128},... | collective-permute-start | bytes 638984 | tf_op jit(solution)/shard_map/ppermute | solution.py:52
  73.3 8.7 %collective-permute-start.14 = (bf16[2,104,512]{2,1,0:T(8,128)(2,1)S(1)}, bf16[2,104,512]{2,1,0:T(8,128)(2,1)S(1)}, u32[]{:S(2)}, u32[]{:S(2)}) collective-permute-start(bf16[2,104,512]{2,1,0:T(8,128)(2,1)S(1)} %collective-permute-done.12), channel_id=1, source_target_pairs={{0,240},{16,0},{32,16},{48,32},{64,48},{80,64},{96,80},{112,96},{1... | collective-permute-start | bytes 638984 | tf_op jit(solution)/shard_map/ppermute | solution.py:55
  80.1 8.1 %collective-permute-start.15 = (bf16[1,104,512]{2,1,0:T(8,128)(2,1)S(1)}, bf16[1,104,512]{2,1,0:T(8,128)(2,1)S(1)}, u32[]{:S(2)}, u32[]{:S(2)}) collective-permute-start(bf16[1,104,512]{2,1,0:T(8,128)(2,1)S(1)} %slice.426), channel_id=1, source_target_pairs={{0,16},{16,32},{32,48},{48,64},{64,80},{80,96},{96,112},{112,128},... | collective-permute-start | bytes 319496 | tf_op jit(solution)/shard_map/ppermute | solution.py:47
  104.9 16.5 %collective-permute-start.20 = (bf16[2,320,1,256]{3,1,2,0:T(8,128)(2,1)S(1)}, bf16[2,320,1,256]{3,1,2,0:T(8,128)(2,1)S(1)}, u32[]{:S(2)}, u32[]{:S(2)}) collective-permute-start(bf16[2,320,1,256]{3,1,2,0:T(8,128)(2,1)S(1)} %maximum_select_fusion), channel_id=1, source_target_pairs={{0,240},{16,0},{32,16},{48,32},{64,48},{80,64},{96,80},{112,96},{1... | collective-permute-start | bytes 983048 | tf_op jit(solution)/shard_map/ppermute | solution.py:223
  110.2 9.0 %collective-permute-start.18 = (bf16[2,320,1,256]{3,1,2,0:T(8,128)(2,1)S(1)}, bf16[2,320,1,256]{3,1,2,0:T(8,128)(2,1)S(1)}, u32[]{:S(2)}, u32[]{:S(2)}) collective-permute-start(bf16[2,320,1,256]{3,1,2,0:T(8,128)(2,1)S(1)} %maximum_select_fusion), channel_id=1, source_target_pairs={{0,16},{16,32},{32,48},{48,64},{64,80},{80,96},{96,112},{112,128},... | collective-permute-start | bytes 983048 | tf_op jit(solution)/shard_map/ppermute | solution.py:220
  119.3 10.6 %collective-permute-start.19 = (bf16[2,320,1,256]{3,1,2,0:T(8,128)(2,1)S(1)}, bf16[2,320,1,256]{3,1,2,0:T(8,128)(2,1)S(1)}, u32[]{:S(2)}, u32[]{:S(2)}) collective-permute-start(bf16[2,320,1,256]{3,1,2,0:T(8,128)(2,1)S(1)} %collective-permute-done.18), channel_id=1, source_target_pairs={{0,16},{16,32},{32,48},{48,64},{64,80},{80,96},{96,112},{112,128},... | collective-permute-start | bytes 983048 | tf_op jit(solution)/shard_map/ppermute | solution.py:220
  122.9 8.8 %collective-permute-start.22 = (bf16[2,320,1,256]{3,1,2,0:T(8,128)(2,1)S(1)}, bf16[2,320,1,256]{3,1,2,0:T(8,128)(2,1)S(1)}, u32[]{:S(2)}, u32[]{:S(2)}) collective-permute-start(bf16[2,320,1,256]{3,1,2,0:T(8,128)(2,1)S(1)} %collective-permute-done.20), channel_id=1, source_target_pairs={{0,240},{16,0},{32,16},{48,32},{64,48},{80,64},{96,80},{112,96},{1... | collective-permute-start | bytes 983048 | tf_op jit(solution)/shard_map/ppermute | solution.py:223
  129.8 9.6 %collective-permute-start.21 = (bf16[2,320,1,256]{3,1,2,0:T(8,128)(2,1)S(1)}, bf16[2,320,1,256]{3,1,2,0:T(8,128)(2,1)S(1)}, u32[]{:S(2)}, u32[]{:S(2)}) collective-permute-start(bf16[2,320,1,256]{3,1,2,0:T(8,128)(2,1)S(1)} %collective-permute-done.19), channel_id=1, source_target_pairs={{0,16},{16,32},{32,48},{48,64},{64,80},{80,96},{96,112},{112,128},... | collective-permute-start | bytes 983048 | tf_op jit(solution)/shard_map/ppermute | solution.py:220
  133.3 8.8 %collective-permute-start.24 = (bf16[2,320,1,256]{3,1,2,0:T(8,128)(2,1)S(1)}, bf16[2,320,1,256]{3,1,2,0:T(8,128)(2,1)S(1)}, u32[]{:S(2)}, u32[]{:S(2)}) collective-permute-start(bf16[2,320,1,256]{3,1,2,0:T(8,128)(2,1)S(1)} %collective-permute-done.22), channel_id=1, source_target_pairs={{0,240},{16,0},{32,16},{48,32},{64,48},{80,64},{96,80},{112,96},{1... | collective-permute-start | bytes 983048 | tf_op jit(solution)/shard_map/ppermute | solution.py:223
  139.5 10.4 %collective-permute-start.23 = (bf16[2,320,1,256]{3,1,2,0:T(8,128)(2,1)S(1)}, bf16[2,320,1,256]{3,1,2,0:T(8,128)(2,1)S(1)}, u32[]{:S(2)}, u32[]{:S(2)}) collective-permute-start(bf16[2,320,1,256]{3,1,2,0:T(8,128)(2,1)S(1)} %collective-permute-done.21), channel_id=1, source_target_pairs={{0,16},{16,32},{32,48},{48,64},{64,80},{80,96},{96,112},{112,128},... | collective-permute-start | bytes 983048 | tf_op jit(solution)/shard_map/ppermute | solution.py:220
  143.6 9.4 %collective-permute-start.26 = (bf16[2,320,1,256]{3,1,2,0:T(8,128)(2,1)S(1)}, bf16[2,320,1,256]{3,1,2,0:T(8,128)(2,1)S(1)}, u32[]{:S(2)}, u32[]{:S(2)}) collective-permute-start(bf16[2,320,1,256]{3,1,2,0:T(8,128)(2,1)S(1)} %collective-permute-done.24), channel_id=1, source_target_pairs={{0,240},{16,0},{32,16},{48,32},{64,48},{80,64},{96,80},{112,96},{1... | collective-permute-start | bytes 983048 | tf_op jit(solution)/shard_map/ppermute | solution.py:223
  149.8 10.6 %collective-permute-start.25 = (bf16[2,320,1,256]{3,1,2,0:T(8,128)(2,1)S(1)}, bf16[2,320,1,256]{3,1,2,0:T(8,128)(2,1)S(1)}, u32[]{:S(2)}, u32[]{:S(2)}) collective-permute-start(bf16[2,320,1,256]{3,1,2,0:T(8,128)(2,1)S(1)} %collective-permute-done.23), channel_id=1, source_target_pairs={{0,16},{16,32},{32,48},{48,64},{64,80},{80,96},{96,112},{112,128},... | collective-permute-start | bytes 983048 | tf_op jit(solution)/shard_map/ppermute | solution.py:220
  154.6 9.0 %collective-permute-start.28 = (bf16[2,320,1,256]{3,1,2,0:T(8,128)(2,1)S(1)}, bf16[2,320,1,256]{3,1,2,0:T(8,128)(2,1)S(1)}, u32[]{:S(2)}, u32[]{:S(2)}) collective-permute-start(bf16[2,320,1,256]{3,1,2,0:T(8,128)(2,1)S(1)} %collective-permute-done.26), channel_id=1, source_target_pairs={{0,240},{16,0},{32,16},{48,32},{64,48},{80,64},{96,80},{112,96},{1... | collective-permute-start | bytes 983048 | tf_op jit(solution)/shard_map/ppermute | solution.py:223
  160.4 10.6 %collective-permute-start.27 = (bf16[2,320,1,256]{3,1,2,0:T(8,128)(2,1)S(1)}, bf16[2,320,1,256]{3,1,2,0:T(8,128)(2,1)S(1)}, u32[]{:S(2)}, u32[]{:S(2)}) collective-permute-start(bf16[2,320,1,256]{3,1,2,0:T(8,128)(2,1)S(1)} %collective-permute-done.25), channel_id=1, source_target_pairs={{0,16},{16,32},{32,48},{48,64},{64,80},{80,96},{96,112},{112,128},... | collective-permute-start | bytes 983048 | tf_op jit(solution)/shard_map/ppermute | solution.py:220
  165.1 9.0 %collective-permute-start.30 = (bf16[2,320,1,256]{3,1,2,0:T(8,128)(2,1)S(1)}, bf16[2,320,1,256]{3,1,2,0:T(8,128)(2,1)S(1)}, u32[]{:S(2)}, u32[]{:S(2)}) collective-permute-start(bf16[2,320,1,256]{3,1,2,0:T(8,128)(2,1)S(1)} %collective-permute-done.28), channel_id=1, source_target_pairs={{0,240},{16,0},{32,16},{48,32},{64,48},{80,64},{96,80},{112,96},{1... | collective-permute-start | bytes 983048 | tf_op jit(solution)/shard_map/ppermute | solution.py:223
  171.0 10.6 %collective-permute-start.29 = (bf16[2,320,1,256]{3,1,2,0:T(8,128)(2,1)S(1)}, bf16[2,320,1,256]{3,1,2,0:T(8,128)(2,1)S(1)}, u32[]{:S(2)}, u32[]{:S(2)}) collective-permute-start(bf16[2,320,1,256]{3,1,2,0:T(8,128)(2,1)S(1)} %collective-permute-done.27), channel_id=1, source_target_pairs={{0,16},{16,32},{32,48},{48,64},{64,80},{80,96},{96,112},{112,128},... | collective-permute-start | bytes 983048 | tf_op jit(solution)/shard_map/ppermute | solution.py:220
  176.1 9.0 %collective-permute-start.31 = (bf16[2,320,1,256]{3,1,2,0:T(8,128)(2,1)S(1)}, bf16[2,320,1,256]{3,1,2,0:T(8,128)(2,1)S(1)}, u32[]{:S(2)}, u32[]{:S(2)}) collective-permute-start(bf16[2,320,1,256]{3,1,2,0:T(8,128)(2,1)S(1)} %collective-permute-done.30), channel_id=1, source_target_pairs={{0,240},{16,0},{32,16},{48,32},{64,48},{80,64},{96,80},{112,96},{1... | collective-permute-start | bytes 983048 | tf_op jit(solution)/shard_map/ppermute | solution.py:223
  181.6 9.0 %collective-permute-start.32 = (bf16[2,320,1,256]{3,1,2,0:T(8,128)(2,1)S(1)}, bf16[2,320,1,256]{3,1,2,0:T(8,128)(2,1)S(1)}, u32[]{:S(2)}, u32[]{:S(2)}) collective-permute-start(bf16[2,320,1,256]{3,1,2,0:T(8,128)(2,1)S(1)} %collective-permute-done.29), channel_id=1, source_target_pairs={{0,16},{16,32},{32,48},{48,64},{64,80},{80,96},{96,112},{112,128},... | collective-permute-start | bytes 983048 | tf_op jit(solution)/shard_map/ppermute | solution.py:220
  193.3 24.8 %collective-permute-start.37 = (bf16[160,1536]{1,0:T(8,128)(2,1)S(1)}, bf16[160,1536]{1,0:T(8,128)(2,1)S(1)}, u32[]{:S(2)}, u32[]{:S(2)}) collective-permute-start(bf16[160,1536]{1,0:T(8,128)(2,1)S(1)} %dynamic-slice_convert_fusion), channel_id=1, source_target_pairs={{0,1},{1,0},{2,3},{3,2},{4,5},{5,4},{6,7},{7,6},{8,9},{9,8},{10,11... | collective-permute-start | bytes 1474568 | tf_op jit(solution)/shard_map/ppermute | solution.py:81
  218.3 8.9 %collective-permute-start.38 = (bf16[160,768]{1,0:T(8,128)(2,1)S(1)}, bf16[160,768]{1,0:T(8,128)(2,1)S(1)}, u32[]{:S(2)}, u32[]{:S(2)}) collective-permute-start(bf16[160,768]{1,0:T(8,128)(2,1)S(1)} %dynamic-slice_convert_fusion.2), channel_id=1, source_target_pairs={{0,2},{1,3},{2,0},{3,1},{4,6},{5,7},{6,4},{7,5},{8,10},{9,11},{10,... | collective-permute-start | bytes 737288 | tf_op jit(solution)/shard_map/ppermute | solution.py:81
  221.6 10.4 %collective-permute-start.34 = (bf16[160,768]{1,0:T(8,128)(2,1)S(1)}, bf16[160,768]{1,0:T(8,128)(2,1)S(1)}, u32[]{:S(2)}, u32[]{:S(2)}) collective-permute-start(bf16[160,768]{1,0:T(8,128)(2,1)S(1)} %dynamic-slice_convert_fusion.3), channel_id=1, source_target_pairs={{0,8},{1,9},{2,10},{3,11},{4,12},{5,13},{6,14},{7,15},{8,0},{9,1},... | collective-permute-start | bytes 737288 | tf_op jit(solution)/shard_map/ppermute | solution.py:81
  (18 other events, 141.3 us)

commit v11 on v7

--- a/solution.py
+++ b/solution.py
@@ -185,13 +185,10 @@
     backward = [(y * ring + a, y * ring + (a - 1) % ring) for y in range(2) for a in range(ring)]
     token_ids = jnp.arange(tok_rows, dtype=jnp.int32)
 
+    frame_pattern = jnp.concatenate([token_ids, ring * tok_rows + token_ids]) // frame_size
+
     def fold(state_in, piece, source):
-        key_frame = (
-            jnp.concatenate(
-                [source * tok_rows + token_ids, (ring + source) * tok_rows + token_ids]
-            )
-            // frame_size
-        )
+        key_frame = source * frames_here + frame_pattern
         return attend_piece(
             state_in,
             piece.reshape((2 * tok_rows,) + piece.shape[2:]),

time: 247 us -> 245 us (level)
  transfers between devices with their start and end apart: 41 -> 41, of which waited for: 22 -> 22; matrix products, arithmetic and copies ran while one was open for 11% -> 10% of each run, Pallas kernels for 0% -> 0%
where the time goes in v11:
time: 245 us; the launch traced here: 241 us
  starting transfers between devices  155 us (63%)
  waiting for transfers between devices  45.9 us (19%)
  matrix products  15.6 us (6%)
  other arithmetic  12.8 us (5%)
  local copies, waits for them, and re-layouts  9.32 us (4%)
    ppermute x8, starting transfers between devices, halving_scatter(): lax.ppermute(send.astype(jnp.bfloat16), axis, [(i, i ^ 1 << bit) for i in...  42.8 us
    ppermute x7, starting transfers between devices, ring_pieces(): behind = lax.ppermute(behind, axis, backward)  35.3 us
    ppermute x7, starting transfers between devices, per_device(): behind = lax.ppermute(behind, 'ctx', backward)  31.4 us
    ppermute x8, waiting for transfers between devices, ring_pieces(): ahead = lax.ppermute(ahead, axis, forward)  18.7 us
    ppermute x8, starting transfers between devices, per_device(): ahead = lax.ppermute(ahead, 'ctx', forward)  17.4 us
    ppermute x8, starting transfers between devices, ring_pieces(): ahead = lax.ppermute(ahead, axis, forward)  16.9 us
    ppermute x8, waiting for transfers between devices, per_device(): ahead = lax.ppermute(ahead, 'ctx', forward)  12.3 us
    dot_general x16, matrix products, attend_piece(): jnp.einsum('nhe,mhe->nhm', queries, key_part, preferred_element_type=jnp....  7.02 us
  transfers between devices with their start and end apart: 41, of which 22 were waited for; matrix products, arithmetic and copies ran while one was open for 10% of the time, Pallas kernels for 0%

profile of v11, /device:TPU:1, one launch (start us, length us, event | category | flops | bytes accessed | tf_op | source)
XLA Modules:
  0.0 240.9 jit_solution(4981418167014281751)
XLA Ops:
  2.3 5.7 %collective-permute-start = (bf16[104,512]{1,0:T(8,128)(2,1)S(1)}, bf16[104,512]{1,0:T(8,128)(2,1)S(1)}, u32[]{:S(2)}, u32[]{:S(2)}) collective-permute-start(bf16[104,512]{1,0:T(8,128)(2,1)S(1)} %get-tuple-element.157), channel_id=1, source_target_pairs={{0,256},{16,272},{32,288},{48,304},{64,320},{80,336},{96,352},{112... | collective-permute-start | bytes 319496 | tf_op jit(solution)/shard_map/ppermute | solution.py:34
  9.1 3.6 %collective-permute-start.40 = (bf16[320,192]{1,0:T(8,128)(2,1)S(1)}, bf16[320,192]{1,0:T(8,128)(2,1)S(1)}, u32[]{:S(2)}, u32[]{:S(2)}) collective-permute-start(bf16[320,192]{1,0:T(8,128)(2,1)S(1)} %constant_dynamic-slice_fusion), channel_id=1, source_target_pairs={{0,16},{16,32},{32,48},{48,64},{64,80},{80,96},{96,112},{112,128},... | collective-permute-start | bytes 368648 | tf_op jit(solution)/shard_map/ppermute | solution.py:19
  16.3 3.5 %collective-permute-start.1 = (bf16[2,104,512]{2,1,0:T(8,128)(2,1)S(1)}, bf16[2,104,512]{2,1,0:T(8,128)(2,1)S(1)}, u32[]{:S(2)}, u32[]{:S(2)}) collective-permute-start(bf16[2,104,512]{2,1,0:T(8,128)(2,1)S(1)} %maximum_select_fusion.2), channel_id=1, source_target_pairs={{0,16},{16,32},{32,48},{48,64},{64,80},{80,96},{96,112},{112,128},... | collective-permute-start | bytes 638984 | tf_op jit(solution)/shard_map/ppermute | solution.py:45
  19.8 7.9 %collective-permute-start.2 = (bf16[2,104,512]{2,1,0:T(8,128)(2,1)S(1)}, bf16[2,104,512]{2,1,0:T(8,128)(2,1)S(1)}, u32[]{:S(2)}, u32[]{:S(2)}) collective-permute-start(bf16[2,104,512]{2,1,0:T(8,128)(2,1)S(1)} %maximum_select_fusion.2), channel_id=1, source_target_pairs={{0,240},{16,0},{32,16},{48,32},{64,48},{80,64},{96,80},{112,96},{1... | collective-permute-start | bytes 638984 | tf_op jit(solution)/shard_map/ppermute | solution.py:48
  28.1 2.3 collective-permute-done.1
  32.3 4.6 %collective-permute-start.4 = (bf16[2,104,512]{2,1,0:T(8,128)(2,1)S(1)}, bf16[2,104,512]{2,1,0:T(8,128)(2,1)S(1)}, u32[]{:S(2)}, u32[]{:S(2)}) collective-permute-start(bf16[2,104,512]{2,1,0:T(8,128)(2,1)S(1)} %collective-permute-done.2), channel_id=1, source_target_pairs={{0,240},{16,0},{32,16},{48,32},{64,48},{80,64},{96,80},{112,96},{1... | collective-permute-start | bytes 638984 | tf_op jit(solution)/shard_map/ppermute | solution.py:48
  40.6 4.6 %collective-permute-start.6 = (bf16[2,104,512]{2,1,0:T(8,128)(2,1)S(1)}, bf16[2,104,512]{2,1,0:T(8,128)(2,1)S(1)}, u32[]{:S(2)}, u32[]{:S(2)}) collective-permute-start(bf16[2,104,512]{2,1,0:T(8,128)(2,1)S(1)} %collective-permute-done.4), channel_id=1, source_target_pairs={{0,240},{16,0},{32,16},{48,32},{64,48},{80,64},{96,80},{112,96},{1... | collective-permute-start | bytes 638984 | tf_op jit(solution)/shard_map/ppermute | solution.py:48
  48.4 4.6 %collective-permute-start.8 = (bf16[2,104,512]{2,1,0:T(8,128)(2,1)S(1)}, bf16[2,104,512]{2,1,0:T(8,128)(2,1)S(1)}, u32[]{:S(2)}, u32[]{:S(2)}) collective-permute-start(bf16[2,104,512]{2,1,0:T(8,128)(2,1)S(1)} %collective-permute-done.6), channel_id=1, source_target_pairs={{0,240},{16,0},{32,16},{48,32},{64,48},{80,64},{96,80},{112,96},{1... | collective-permute-start | bytes 638984 | tf_op jit(solution)/shard_map/ppermute | solution.py:48
  56.2 4.6 %collective-permute-start.10 = (bf16[2,104,512]{2,1,0:T(8,128)(2,1)S(1)}, bf16[2,104,512]{2,1,0:T(8,128)(2,1)S(1)}, u32[]{:S(2)}, u32[]{:S(2)}) collective-permute-start(bf16[2,104,512]{2,1,0:T(8,128)(2,1)S(1)} %collective-permute-done.8), channel_id=1, source_target_pairs={{0,240},{16,0},{32,16},{48,32},{64,48},{80,64},{96,80},{112,96},{1... | collective-permute-start | bytes 638984 | tf_op jit(solution)/shard_map/ppermute | solution.py:48
  64.0 4.6 %collective-permute-start.12 = (bf16[2,104,512]{2,1,0:T(8,128)(2,1)S(1)}, bf16[2,104,512]{2,1,0:T(8,128)(2,1)S(1)}, u32[]{:S(2)}, u32[]{:S(2)}) collective-permute-start(bf16[2,104,512]{2,1,0:T(8,128)(2,1)S(1)} %collective-permute-done.10), channel_id=1, source_target_pairs={{0,240},{16,0},{32,16},{48,32},{64,48},{80,64},{96,80},{112,96},{1... | collective-permute-start | bytes 638984 | tf_op jit(solution)/shard_map/ppermute | solution.py:48
  71.8 4.6 %collective-permute-start.14 = (bf16[2,104,512]{2,1,0:T(8,128)(2,1)S(1)}, bf16[2,104,512]{2,1,0:T(8,128)(2,1)S(1)}, u32[]{:S(2)}, u32[]{:S(2)}) collective-permute-start(bf16[2,104,512]{2,1,0:T(8,128)(2,1)S(1)} %collective-permute-done.12), channel_id=1, source_target_pairs={{0,240},{16,0},{32,16},{48,32},{64,48},{80,64},{96,80},{112,96},{1... | collective-permute-start | bytes 638984 | tf_op jit(solution)/shard_map/ppermute | solution.py:48
  80.5 7.8 %collective-permute-done.15 = bf16[2,104,512]{2,1,0:T(8,128)(2,1)S(1)} collective-permute-done((bf16[2,104,512]{2,1,0:T(8,128)(2,1)S(1)}, bf16[2,104,512]{2,1,0:T(8,128)(2,1)S(1)}, u32[]{:S(2)}, u32[]{:S(2)}) %collective-permute-start.15) | collective-permute-done | bytes 213024 | tf_op jit(solution)/shard_map/ppermute | solution.py:45
  100.0 3.5 %collective-permute-done.16 = bf16[320,1,256]{2,0,1:T(8,128)(2,1)S(1)} collective-permute-done((bf16[320,1,256]{2,0,1:T(8,128)(2,1)S(1)}, bf16[320,1,256]{2,0,1:T(8,128)(2,1)S(1)}, u32[]{:S(2)}, u32[]{:S(2)}) %collective-permute-start.16) | collective-permute-done | bytes 163872 | tf_op jit(solution)/shard_map/ppermute | solution.py:179
  105.5 3.4 %collective-permute-start.17 = (bf16[2,320,1,256]{3,1,2,0:T(8,128)(2,1)S(1)}, bf16[2,320,1,256]{3,1,2,0:T(8,128)(2,1)S(1)}, u32[]{:S(2)}, u32[]{:S(2)}) collective-permute-start(bf16[2,320,1,256]{3,1,2,0:T(8,128)(2,1)S(1)} %maximum_select_fusion), channel_id=1, source_target_pairs={{0,16},{16,32},{32,48},{48,64},{64,80},{80,96},{96,112},{112,128},... | collective-permute-start | bytes 983048 | tf_op jit(solution)/shard_map/ppermute | solution.py:207
  110.2 4.3 %collective-permute-done.17 = bf16[2,320,1,256]{3,1,2,0:T(8,128)(2,1)S(1)} collective-permute-done((bf16[2,320,1,256]{3,1,2,0:T(8,128)(2,1)S(1)}, bf16[2,320,1,256]{3,1,2,0:T(8,128)(2,1)S(1)}, u32[]{:S(2)}, u32[]{:S(2)}) %collective-permute-start.17) | collective-permute-done | bytes 327712 | tf_op jit(solution)/shard_map/ppermute | solution.py:207
  114.5 2.3 collective-permute-start.18
  118.4 4.3 %collective-permute-start.21 = (bf16[2,320,1,256]{3,1,2,0:T(8,128)(2,1)S(1)}, bf16[2,320,1,256]{3,1,2,0:T(8,128)(2,1)S(1)}, u32[]{:S(2)}, u32[]{:S(2)}) collective-permute-start(bf16[2,320,1,256]{3,1,2,0:T(8,128)(2,1)S(1)} %collective-permute-done.19), channel_id=1, source_target_pairs={{0,240},{16,0},{32,16},{48,32},{64,48},{80,64},{96,80},{112,96},{1... | collective-permute-start | bytes 983048 | tf_op jit(solution)/shard_map/ppermute | solution.py:210
  128.9 4.6 %collective-permute-start.23 = (bf16[2,320,1,256]{3,1,2,0:T(8,128)(2,1)S(1)}, bf16[2,320,1,256]{3,1,2,0:T(8,128)(2,1)S(1)}, u32[]{:S(2)}, u32[]{:S(2)}) collective-permute-start(bf16[2,320,1,256]{3,1,2,0:T(8,128)(2,1)S(1)} %collective-permute-done.21), channel_id=1, source_target_pairs={{0,240},{16,0},{32,16},{48,32},{64,48},{80,64},{96,80},{112,96},{1... | collective-permute-start | bytes 983048 | tf_op jit(solution)/shard_map/ppermute | solution.py:210
  139.0 5.5 %collective-permute-start.25 = (bf16[2,320,1,256]{3,1,2,0:T(8,128)(2,1)S(1)}, bf16[2,320,1,256]{3,1,2,0:T(8,128)(2,1)S(1)}, u32[]{:S(2)}, u32[]{:S(2)}) collective-permute-start(bf16[2,320,1,256]{3,1,2,0:T(8,128)(2,1)S(1)} %collective-permute-done.23), channel_id=1, source_target_pairs={{0,240},{16,0},{32,16},{48,32},{64,48},{80,64},{96,80},{112,96},{1... | collective-permute-start | bytes 983048 | tf_op jit(solution)/shard_map/ppermute | solution.py:210
  150.0 5.0 %collective-permute-start.27 = (bf16[2,320,1,256]{3,1,2,0:T(8,128)(2,1)S(1)}, bf16[2,320,1,256]{3,1,2,0:T(8,128)(2,1)S(1)}, u32[]{:S(2)}, u32[]{:S(2)}) collective-permute-start(bf16[2,320,1,256]{3,1,2,0:T(8,128)(2,1)S(1)} %collective-permute-done.25), channel_id=1, source_target_pairs={{0,240},{16,0},{32,16},{48,32},{64,48},{80,64},{96,80},{112,96},{1... | collective-permute-start | bytes 983048 | tf_op jit(solution)/shard_map/ppermute | solution.py:210
  160.6 5.0 %collective-permute-start.29 = (bf16[2,320,1,256]{3,1,2,0:T(8,128)(2,1)S(1)}, bf16[2,320,1,256]{3,1,2,0:T(8,128)(2,1)S(1)}, u32[]{:S(2)}, u32[]{:S(2)}) collective-permute-start(bf16[2,320,1,256]{3,1,2,0:T(8,128)(2,1)S(1)} %collective-permute-done.27), channel_id=1, source_target_pairs={{0,240},{16,0},{32,16},{48,32},{64,48},{80,64},{96,80},{112,96},{1... | collective-permute-start | bytes 983048 | tf_op jit(solution)/shard_map/ppermute | solution.py:210
  171.6 5.0 %collective-permute-start.30 = (bf16[2,320,1,256]{3,1,2,0:T(8,128)(2,1)S(1)}, bf16[2,320,1,256]{3,1,2,0:T(8,128)(2,1)S(1)}, u32[]{:S(2)}, u32[]{:S(2)}) collective-permute-start(bf16[2,320,1,256]{3,1,2,0:T(8,128)(2,1)S(1)} %collective-permute-done.29), channel_id=1, source_target_pairs={{0,240},{16,0},{32,16},{48,32},{64,48},{80,64},{96,80},{112,96},{1... | collective-permute-start | bytes 983048 | tf_op jit(solution)/shard_map/ppermute | solution.py:210
  181.0 5.0 %collective-permute-done.31 = bf16[2,320,1,256]{3,1,2,0:T(8,128)(2,1)S(1)} collective-permute-done((bf16[2,320,1,256]{3,1,2,0:T(8,128)(2,1)S(1)}, bf16[2,320,1,256]{3,1,2,0:T(8,128)(2,1)S(1)}, u32[]{:S(2)}, u32[]{:S(2)}) %collective-permute-start.31) | collective-permute-done | bytes 327712 | tf_op jit(solution)/shard_map/ppermute | solution.py:207
  188.8 22.3 %collective-permute-start.36 = (bf16[160,1536]{1,0:T(8,128)(2,1)S(1)}, bf16[160,1536]{1,0:T(8,128)(2,1)S(1)}, u32[]{:S(2)}, u32[]{:S(2)}) collective-permute-start(bf16[160,1536]{1,0:T(8,128)(2,1)S(1)} %dynamic-slice_convert_fusion), channel_id=1, source_target_pairs={{0,1},{1,0},{2,3},{3,2},{4,5},{5,4},{6,7},{7,6},{8,9},{9,8},{10,11... | collective-permute-start | bytes 1474568 | tf_op jit(solution)/shard_map/ppermute | solution.py:71
  213.6 3.1 %collective-permute-start.37 = (bf16[160,768]{1,0:T(8,128)(2,1)S(1)}, bf16[160,768]{1,0:T(8,128)(2,1)S(1)}, u32[]{:S(2)}, u32[]{:S(2)}) collective-permute-start(bf16[160,768]{1,0:T(8,128)(2,1)S(1)} %dynamic-slice_convert_fusion.2), channel_id=1, source_target_pairs={{0,2},{1,3},{2,0},{3,1},{4,6},{5,7},{6,4},{7,5},{8,10},{9,11},{10,... | collective-permute-start | bytes 737288 | tf_op jit(solution)/shard_map/ppermute | solution.py:71
  217.0 2.3 collective-permute-start.33
  219.3 3.3 %collective-permute-done.37 = bf16[160,768]{1,0:T(8,128)(2,1)S(1)} collective-permute-done((bf16[160,768]{1,0:T(8,128)(2,1)S(1)}, bf16[160,768]{1,0:T(8,128)(2,1)S(1)}, u32[]{:S(2)}, u32[]{:S(2)}) %collective-permute-start.37) | collective-permute-done | bytes 245792 | tf_op jit(solution)/shard_map/ppermute | solution.py:71
  222.6 4.7 %collective-permute-start.38 = (bf16[160,384]{1,0:T(8,128)(2,1)S(1)}, bf16[160,384]{1,0:T(8,128)(2,1)S(1)}, u32[]{:S(2)}, u32[]{:S(2)}) collective-permute-start(bf16[160,384]{1,0:T(8,128)(2,1)S(1)} %dynamic-slice_convert_fusion.4), channel_id=1, source_target_pairs={{0,4},{1,5},{2,6},{3,7},{4,0},{5,1},{6,2},{7,3},{8,12},{9,13},{10,... | collective-permute-start | bytes 368648 | tf_op jit(solution)/shard_map/ppermute | solution.py:71
  227.4 2.2 collective-permute-start.34
  229.9 2.3 collective-permute-start.39
  233.2 4.0 %collective-permute-start.35 = (bf16[160,192]{1,0:T(8,128)(2,1)S(1)}, bf16[160,192]{1,0:T(8,128)(2,1)S(1)}, u32[]{:S(2)}, u32[]{:S(2)}) collective-permute-start(bf16[160,192]{1,0:T(8,128)(2,1)S(1)} %dynamic-slice_convert_fusion.7), channel_id=1, source_target_pairs={{0,4},{1,5},{2,6},{3,7},{4,0},{5,1},{6,2},{7,3},{8,12},{9,13},{10,... | collective-permute-start | bytes 184328 | tf_op jit(solution)/shard_map/ppermute | solution.py:71
  237.3 2.6 %collective-permute-done.35 = bf16[160,192]{1,0:T(8,128)(2,1)S(1)} collective-permute-done((bf16[160,192]{1,0:T(8,128)(2,1)S(1)}, bf16[160,192]{1,0:T(8,128)(2,1)S(1)}, u32[]{:S(2)}, u32[]{:S(2)}) %collective-permute-start.35) | collective-permute-done | bytes 61472 | tf_op jit(solution)/shard_map/ppermute | solution.py:71
  (208 shorter events, 85.8 us)
Async XLA Ops:
  2.3 13.9 %collective-permute-start = (bf16[104,512]{1,0:T(8,128)(2,1)S(1)}, bf16[104,512]{1,0:T(8,128)(2,1)S(1)}, u32[]{:S(2)}, u32[]{:S(2)}) collective-permute-start(bf16[104,512]{1,0:T(8,128)(2,1)S(1)} %get-tuple-element.157), channel_id=1, source_target_pairs={{0,256},{16,272},{32,288},{48,304},{64,320},{80,336},{96,352},{112... | collective-permute-start | bytes 319496 | tf_op jit(solution)/shard_map/ppermute | solution.py:34
  9.1 18.9 %collective-permute-start.40 = (bf16[320,192]{1,0:T(8,128)(2,1)S(1)}, bf16[320,192]{1,0:T(8,128)(2,1)S(1)}, u32[]{:S(2)}, u32[]{:S(2)}) collective-permute-start(bf16[320,192]{1,0:T(8,128)(2,1)S(1)} %constant_dynamic-slice_fusion), channel_id=1, source_target_pairs={{0,16},{16,32},{32,48},{48,64},{64,80},{80,96},{96,112},{112,128},... | collective-permute-start | bytes 368648 | tf_op jit(solution)/shard_map/ppermute | solution.py:19
  16.3 14.1 %collective-permute-start.1 = (bf16[2,104,512]{2,1,0:T(8,128)(2,1)S(1)}, bf16[2,104,512]{2,1,0:T(8,128)(2,1)S(1)}, u32[]{:S(2)}, u32[]{:S(2)}) collective-permute-start(bf16[2,104,512]{2,1,0:T(8,128)(2,1)S(1)} %maximum_select_fusion.2), channel_id=1, source_target_pairs={{0,16},{16,32},{32,48},{48,64},{64,80},{80,96},{96,112},{112,128},... | collective-permute-start | bytes 638984 | tf_op jit(solution)/shard_map/ppermute | solution.py:45
  19.8 12.5 %collective-permute-start.2 = (bf16[2,104,512]{2,1,0:T(8,128)(2,1)S(1)}, bf16[2,104,512]{2,1,0:T(8,128)(2,1)S(1)}, u32[]{:S(2)}, u32[]{:S(2)}) collective-permute-start(bf16[2,104,512]{2,1,0:T(8,128)(2,1)S(1)} %maximum_select_fusion.2), channel_id=1, source_target_pairs={{0,240},{16,0},{32,16},{48,32},{64,48},{80,64},{96,80},{112,96},{1... | collective-permute-start | bytes 638984 | tf_op jit(solution)/shard_map/ppermute | solution.py:48
  30.4 8.3 %collective-permute-start.3 = (bf16[2,104,512]{2,1,0:T(8,128)(2,1)S(1)}, bf16[2,104,512]{2,1,0:T(8,128)(2,1)S(1)}, u32[]{:S(2)}, u32[]{:S(2)}) collective-permute-start(bf16[2,104,512]{2,1,0:T(8,128)(2,1)S(1)} %collective-permute-done.1), channel_id=1, source_target_pairs={{0,16},{16,32},{32,48},{48,64},{64,80},{80,96},{96,112},{112,128},... | collective-permute-start | bytes 638984 | tf_op jit(solution)/shard_map/ppermute | solution.py:45
  32.3 8.3 %collective-permute-start.4 = (bf16[2,104,512]{2,1,0:T(8,128)(2,1)S(1)}, bf16[2,104,512]{2,1,0:T(8,128)(2,1)S(1)}, u32[]{:S(2)}, u32[]{:S(2)}) collective-permute-start(bf16[2,104,512]{2,1,0:T(8,128)(2,1)S(1)} %collective-permute-done.2), channel_id=1, source_target_pairs={{0,240},{16,0},{32,16},{48,32},{64,48},{80,64},{96,80},{112,96},{1... | collective-permute-start | bytes 638984 | tf_op jit(solution)/shard_map/ppermute | solution.py:48
  38.7 7.8 %collective-permute-start.5 = (bf16[2,104,512]{2,1,0:T(8,128)(2,1)S(1)}, bf16[2,104,512]{2,1,0:T(8,128)(2,1)S(1)}, u32[]{:S(2)}, u32[]{:S(2)}) collective-permute-start(bf16[2,104,512]{2,1,0:T(8,128)(2,1)S(1)} %collective-permute-done.3), channel_id=1, source_target_pairs={{0,16},{16,32},{32,48},{48,64},{64,80},{80,96},{96,112},{112,128},... | collective-permute-start | bytes 638984 | tf_op jit(solution)/shard_map/ppermute | solution.py:45
  40.6 7.8 %collective-permute-start.6 = (bf16[2,104,512]{2,1,0:T(8,128)(2,1)S(1)}, bf16[2,104,512]{2,1,0:T(8,128)(2,1)S(1)}, u32[]{:S(2)}, u32[]{:S(2)}) collective-permute-start(bf16[2,104,512]{2,1,0:T(8,128)(2,1)S(1)} %collective-permute-done.4), channel_id=1, source_target_pairs={{0,240},{16,0},{32,16},{48,32},{64,48},{80,64},{96,80},{112,96},{1... | collective-permute-start | bytes 638984 | tf_op jit(solution)/shard_map/ppermute | solution.py:48
  46.5 7.8 %collective-permute-start.7 = (bf16[2,104,512]{2,1,0:T(8,128)(2,1)S(1)}, bf16[2,104,512]{2,1,0:T(8,128)(2,1)S(1)}, u32[]{:S(2)}, u32[]{:S(2)}) collective-permute-start(bf16[2,104,512]{2,1,0:T(8,128)(2,1)S(1)} %collective-permute-done.5), channel_id=1, source_target_pairs={{0,16},{16,32},{32,48},{48,64},{64,80},{80,96},{96,112},{112,128},... | collective-permute-start | bytes 638984 | tf_op jit(solution)/shard_map/ppermute | solution.py:45
  54.3 7.8 %collective-permute-start.9 = (bf16[2,104,512]{2,1,0:T(8,128)(2,1)S(1)}, bf16[2,104,512]{2,1,0:T(8,128)(2,1)S(1)}, u32[]{:S(2)}, u32[]{:S(2)}) collective-permute-start(bf16[2,104,512]{2,1,0:T(8,128)(2,1)S(1)} %collective-permute-done.7), channel_id=1, source_target_pairs={{0,16},{16,32},{32,48},{48,64},{64,80},{80,96},{96,112},{112,128},... | collective-permute-start | bytes 638984 | tf_op jit(solution)/shard_map/ppermute | solution.py:45
  62.1 7.8 %collective-permute-start.11 = (bf16[2,104,512]{2,1,0:T(8,128)(2,1)S(1)}, bf16[2,104,512]{2,1,0:T(8,128)(2,1)S(1)}, u32[]{:S(2)}, u32[]{:S(2)}) collective-permute-start(bf16[2,104,512]{2,1,0:T(8,128)(2,1)S(1)} %collective-permute-done.9), channel_id=1, source_target_pairs={{0,16},{16,32},{32,48},{48,64},{64,80},{80,96},{96,112},{112,128},... | collective-permute-start | bytes 638984 | tf_op jit(solution)/shard_map/ppermute | solution.py:45
  69.9 8.7 %collective-permute-start.13 = (bf16[2,104,512]{2,1,0:T(8,128)(2,1)S(1)}, bf16[2,104,512]{2,1,0:T(8,128)(2,1)S(1)}, u32[]{:S(2)}, u32[]{:S(2)}) collective-permute-start(bf16[2,104,512]{2,1,0:T(8,128)(2,1)S(1)} %collective-permute-done.11), channel_id=1, source_target_pairs={{0,16},{16,32},{32,48},{48,64},{64,80},{80,96},{96,112},{112,128},... | collective-permute-start | bytes 638984 | tf_op jit(solution)/shard_map/ppermute | solution.py:45
  71.8 8.7 %collective-permute-start.14 = (bf16[2,104,512]{2,1,0:T(8,128)(2,1)S(1)}, bf16[2,104,512]{2,1,0:T(8,128)(2,1)S(1)}, u32[]{:S(2)}, u32[]{:S(2)}) collective-permute-start(bf16[2,104,512]{2,1,0:T(8,128)(2,1)S(1)} %collective-permute-done.12), channel_id=1, source_target_pairs={{0,240},{16,0},{32,16},{48,32},{64,48},{80,64},{96,80},{112,96},{1... | collective-permute-start | bytes 638984 | tf_op jit(solution)/shard_map/ppermute | solution.py:48
  78.5 9.8 %collective-permute-start.15 = (bf16[2,104,512]{2,1,0:T(8,128)(2,1)S(1)}, bf16[2,104,512]{2,1,0:T(8,128)(2,1)S(1)}, u32[]{:S(2)}, u32[]{:S(2)}) collective-permute-start(bf16[2,104,512]{2,1,0:T(8,128)(2,1)S(1)} %collective-permute-done.13), channel_id=1, source_target_pairs={{0,16},{16,32},{32,48},{48,64},{64,80},{80,96},{96,112},{112,128},... | collective-permute-start | bytes 638984 | tf_op jit(solution)/shard_map/ppermute | solution.py:45
  103.6 13.3 %collective-permute-start.19 = (bf16[2,320,1,256]{3,1,2,0:T(8,128)(2,1)S(1)}, bf16[2,320,1,256]{3,1,2,0:T(8,128)(2,1)S(1)}, u32[]{:S(2)}, u32[]{:S(2)}) collective-permute-start(bf16[2,320,1,256]{3,1,2,0:T(8,128)(2,1)S(1)} %maximum_select_fusion), channel_id=1, source_target_pairs={{0,240},{16,0},{32,16},{48,32},{64,48},{80,64},{96,80},{112,96},{1... | collective-permute-start | bytes 983048 | tf_op jit(solution)/shard_map/ppermute | solution.py:210
  105.5 9.0 %collective-permute-start.17 = (bf16[2,320,1,256]{3,1,2,0:T(8,128)(2,1)S(1)}, bf16[2,320,1,256]{3,1,2,0:T(8,128)(2,1)S(1)}, u32[]{:S(2)}, u32[]{:S(2)}) collective-permute-start(bf16[2,320,1,256]{3,1,2,0:T(8,128)(2,1)S(1)} %maximum_select_fusion), channel_id=1, source_target_pairs={{0,16},{16,32},{32,48},{48,64},{64,80},{80,96},{96,112},{112,128},... | collective-permute-start | bytes 983048 | tf_op jit(solution)/shard_map/ppermute | solution.py:207
  114.5 10.9 %collective-permute-start.18 = (bf16[2,320,1,256]{3,1,2,0:T(8,128)(2,1)S(1)}, bf16[2,320,1,256]{3,1,2,0:T(8,128)(2,1)S(1)}, u32[]{:S(2)}, u32[]{:S(2)}) collective-permute-start(bf16[2,320,1,256]{3,1,2,0:T(8,128)(2,1)S(1)} %collective-permute-done.17), channel_id=1, source_target_pairs={{0,16},{16,32},{32,48},{48,64},{64,80},{80,96},{96,112},{112,128},... | collective-permute-start | bytes 983048 | tf_op jit(solution)/shard_map/ppermute | solution.py:207
  118.4 8.9 %collective-permute-start.21 = (bf16[2,320,1,256]{3,1,2,0:T(8,128)(2,1)S(1)}, bf16[2,320,1,256]{3,1,2,0:T(8,128)(2,1)S(1)}, u32[]{:S(2)}, u32[]{:S(2)}) collective-permute-start(bf16[2,320,1,256]{3,1,2,0:T(8,128)(2,1)S(1)} %collective-permute-done.19), channel_id=1, source_target_pairs={{0,240},{16,0},{32,16},{48,32},{64,48},{80,64},{96,80},{112,96},{1... | collective-permute-start | bytes 983048 | tf_op jit(solution)/shard_map/ppermute | solution.py:210
  125.4 9.9 %collective-permute-start.20 = (bf16[2,320,1,256]{3,1,2,0:T(8,128)(2,1)S(1)}, bf16[2,320,1,256]{3,1,2,0:T(8,128)(2,1)S(1)}, u32[]{:S(2)}, u32[]{:S(2)}) collective-permute-start(bf16[2,320,1,256]{3,1,2,0:T(8,128)(2,1)S(1)} %collective-permute-done.18), channel_id=1, source_target_pairs={{0,16},{16,32},{32,48},{48,64},{64,80},{80,96},{96,112},{112,128},... | collective-permute-start | bytes 983048 | tf_op jit(solution)/shard_map/ppermute | solution.py:207
  128.9 8.6 %collective-permute-start.23 = (bf16[2,320,1,256]{3,1,2,0:T(8,128)(2,1)S(1)}, bf16[2,320,1,256]{3,1,2,0:T(8,128)(2,1)S(1)}, u32[]{:S(2)}, u32[]{:S(2)}) collective-permute-start(bf16[2,320,1,256]{3,1,2,0:T(8,128)(2,1)S(1)} %collective-permute-done.21), channel_id=1, source_target_pairs={{0,240},{16,0},{32,16},{48,32},{64,48},{80,64},{96,80},{112,96},{1... | collective-permute-start | bytes 983048 | tf_op jit(solution)/shard_map/ppermute | solution.py:210
  135.3 9.9 %collective-permute-start.22 = (bf16[2,320,1,256]{3,1,2,0:T(8,128)(2,1)S(1)}, bf16[2,320,1,256]{3,1,2,0:T(8,128)(2,1)S(1)}, u32[]{:S(2)}, u32[]{:S(2)}) collective-permute-start(bf16[2,320,1,256]{3,1,2,0:T(8,128)(2,1)S(1)} %collective-permute-done.20), channel_id=1, source_target_pairs={{0,16},{16,32},{32,48},{48,64},{64,80},{80,96},{96,112},{112,128},... | collective-permute-start | bytes 983048 | tf_op jit(solution)/shard_map/ppermute | solution.py:207
  139.0 9.5 %collective-permute-start.25 = (bf16[2,320,1,256]{3,1,2,0:T(8,128)(2,1)S(1)}, bf16[2,320,1,256]{3,1,2,0:T(8,128)(2,1)S(1)}, u32[]{:S(2)}, u32[]{:S(2)}) collective-permute-start(bf16[2,320,1,256]{3,1,2,0:T(8,128)(2,1)S(1)} %collective-permute-done.23), channel_id=1, source_target_pairs={{0,240},{16,0},{32,16},{48,32},{64,48},{80,64},{96,80},{112,96},{1... | collective-permute-start | bytes 983048 | tf_op jit(solution)/shard_map/ppermute | solution.py:210
  145.3 10.6 %collective-permute-start.24 = (bf16[2,320,1,256]{3,1,2,0:T(8,128)(2,1)S(1)}, bf16[2,320,1,256]{3,1,2,0:T(8,128)(2,1)S(1)}, u32[]{:S(2)}, u32[]{:S(2)}) collective-permute-start(bf16[2,320,1,256]{3,1,2,0:T(8,128)(2,1)S(1)} %collective-permute-done.22), channel_id=1, source_target_pairs={{0,16},{16,32},{32,48},{48,64},{64,80},{80,96},{96,112},{112,128},... | collective-permute-start | bytes 983048 | tf_op jit(solution)/shard_map/ppermute | solution.py:207
  150.0 9.0 %collective-permute-start.27 = (bf16[2,320,1,256]{3,1,2,0:T(8,128)(2,1)S(1)}, bf16[2,320,1,256]{3,1,2,0:T(8,128)(2,1)S(1)}, u32[]{:S(2)}, u32[]{:S(2)}) collective-permute-start(bf16[2,320,1,256]{3,1,2,0:T(8,128)(2,1)S(1)} %collective-permute-done.25), channel_id=1, source_target_pairs={{0,240},{16,0},{32,16},{48,32},{64,48},{80,64},{96,80},{112,96},{1... | collective-permute-start | bytes 983048 | tf_op jit(solution)/shard_map/ppermute | solution.py:210
  155.8 10.6 %collective-permute-start.26 = (bf16[2,320,1,256]{3,1,2,0:T(8,128)(2,1)S(1)}, bf16[2,320,1,256]{3,1,2,0:T(8,128)(2,1)S(1)}, u32[]{:S(2)}, u32[]{:S(2)}) collective-permute-start(bf16[2,320,1,256]{3,1,2,0:T(8,128)(2,1)S(1)} %collective-permute-done.24), channel_id=1, source_target_pairs={{0,16},{16,32},{32,48},{48,64},{64,80},{80,96},{96,112},{112,128},... | collective-permute-start | bytes 983048 | tf_op jit(solution)/shard_map/ppermute | solution.py:207
  160.6 9.0 %collective-permute-start.29 = (bf16[2,320,1,256]{3,1,2,0:T(8,128)(2,1)S(1)}, bf16[2,320,1,256]{3,1,2,0:T(8,128)(2,1)S(1)}, u32[]{:S(2)}, u32[]{:S(2)}) collective-permute-start(bf16[2,320,1,256]{3,1,2,0:T(8,128)(2,1)S(1)} %collective-permute-done.27), channel_id=1, source_target_pairs={{0,240},{16,0},{32,16},{48,32},{64,48},{80,64},{96,80},{112,96},{1... | collective-permute-start | bytes 983048 | tf_op jit(solution)/shard_map/ppermute | solution.py:210
  166.4 10.6 %collective-permute-start.28 = (bf16[2,320,1,256]{3,1,2,0:T(8,128)(2,1)S(1)}, bf16[2,320,1,256]{3,1,2,0:T(8,128)(2,1)S(1)}, u32[]{:S(2)}, u32[]{:S(2)}) collective-permute-start(bf16[2,320,1,256]{3,1,2,0:T(8,128)(2,1)S(1)} %collective-permute-done.26), channel_id=1, source_target_pairs={{0,16},{16,32},{32,48},{48,64},{64,80},{80,96},{96,112},{112,128},... | collective-permute-start | bytes 983048 | tf_op jit(solution)/shard_map/ppermute | solution.py:207
  171.6 9.0 %collective-permute-start.30 = (bf16[2,320,1,256]{3,1,2,0:T(8,128)(2,1)S(1)}, bf16[2,320,1,256]{3,1,2,0:T(8,128)(2,1)S(1)}, u32[]{:S(2)}, u32[]{:S(2)}) collective-permute-start(bf16[2,320,1,256]{3,1,2,0:T(8,128)(2,1)S(1)} %collective-permute-done.29), channel_id=1, source_target_pairs={{0,240},{16,0},{32,16},{48,32},{64,48},{80,64},{96,80},{112,96},{1... | collective-permute-start | bytes 983048 | tf_op jit(solution)/shard_map/ppermute | solution.py:210
  177.0 9.0 %collective-permute-start.31 = (bf16[2,320,1,256]{3,1,2,0:T(8,128)(2,1)S(1)}, bf16[2,320,1,256]{3,1,2,0:T(8,128)(2,1)S(1)}, u32[]{:S(2)}, u32[]{:S(2)}) collective-permute-start(bf16[2,320,1,256]{3,1,2,0:T(8,128)(2,1)S(1)} %collective-permute-done.28), channel_id=1, source_target_pairs={{0,16},{16,32},{32,48},{48,64},{64,80},{80,96},{96,112},{112,128},... | collective-permute-start | bytes 983048 | tf_op jit(solution)/shard_map/ppermute | solution.py:207
  188.8 24.7 %collective-permute-start.36 = (bf16[160,1536]{1,0:T(8,128)(2,1)S(1)}, bf16[160,1536]{1,0:T(8,128)(2,1)S(1)}, u32[]{:S(2)}, u32[]{:S(2)}) collective-permute-start(bf16[160,1536]{1,0:T(8,128)(2,1)S(1)} %dynamic-slice_convert_fusion), channel_id=1, source_target_pairs={{0,1},{1,0},{2,3},{3,2},{4,5},{5,4},{6,7},{7,6},{8,9},{9,8},{10,11... | collective-permute-start | bytes 1474568 | tf_op jit(solution)/shard_map/ppermute | solution.py:71
  213.6 8.9 %collective-permute-start.37 = (bf16[160,768]{1,0:T(8,128)(2,1)S(1)}, bf16[160,768]{1,0:T(8,128)(2,1)S(1)}, u32[]{:S(2)}, u32[]{:S(2)}) collective-permute-start(bf16[160,768]{1,0:T(8,128)(2,1)S(1)} %dynamic-slice_convert_fusion.2), channel_id=1, source_target_pairs={{0,2},{1,3},{2,0},{3,1},{4,6},{5,7},{6,4},{7,5},{8,10},{9,11},{10,... | collective-permute-start | bytes 737288 | tf_op jit(solution)/shard_map/ppermute | solution.py:71
  217.0 10.4 %collective-permute-start.33 = (bf16[160,768]{1,0:T(8,128)(2,1)S(1)}, bf16[160,768]{1,0:T(8,128)(2,1)S(1)}, u32[]{:S(2)}, u32[]{:S(2)}) collective-permute-start(bf16[160,768]{1,0:T(8,128)(2,1)S(1)} %dynamic-slice_convert_fusion.3), channel_id=1, source_target_pairs={{0,8},{1,9},{2,10},{3,11},{4,12},{5,13},{6,14},{7,15},{8,0},{9,1},... | collective-permute-start | bytes 737288 | tf_op jit(solution)/shard_map/ppermute | solution.py:71
  (17 other events, 131.7 us)

commit v12 on v11

--- a/solution.py
+++ b/solution.py
@@ -55,8 +55,7 @@
     gathered = jnp.zeros((ring,) + pieces[0][0].shape, block.dtype)
     for piece, source in pieces:
         gathered = lax.dynamic_update_index_in_dim(gathered, piece, source, 0)
-    gathered = jnp.swapaxes(gathered, 0, 1)
-    return gathered.reshape((2 * ring * block.shape[0],) + block.shape[1:])
+    return gathered
 
 
 def halving_scatter(partial, axis, order):
@@ -146,24 +145,31 @@
         ],
         axis=0,
     )
-    gathered = ring_gather(bundle, "ctx")
-    blocks = gathered.shape[0] // bundle.shape[0]
-    gathered = gathered.reshape(blocks, rows_here + extra_rows, width)
+    stacked_blocks = ring_gather(bundle, "ctx")
+    ring = stacked_blocks.shape[0]
+    block_rows = rows_here + extra_rows
+    blocks = 2 * ring
+    gathered = jnp.swapaxes(stacked_blocks, 0, 1).reshape(blocks, block_rows, width)
     full_rows = blocks * rows_here
-    w_piece = gathered[:, :rows_here, :qkv_cols].reshape(full_rows, heads_here, qkv_width)
     o_piece = gathered[:, :rows_here, qkv_cols:].reshape(full_rows, heads_here, head_dim)
     share_bits = (
-        gathered[:, rows_here:, :]
-        .reshape(blocks, extra_rows * width)[:, :share_count]
-        .reshape(full_rows, 4)
+        stacked_blocks[:, :, rows_here:, :]
+        .reshape(ring, 2, extra_rows * width)[:, :, :share_count]
+        .reshape(ring, 2, rows_here, 4)
         .astype(jnp.float32)
     )
-    shares = share_bits[:, :2] + share_bits[:, 2:]
-
-    modulated = (normed * (1.0 + shares[:, 1]) + shares[:, 0]).astype(jnp.bfloat16)
-    projected_qkv = jnp.einsum(
-        "nr,rhc->nhc", modulated, w_piece, preferred_element_type=jnp.float32
-    ).astype(jnp.bfloat16)
+    shares = share_bits[..., :2] + share_bits[..., 2:]
+    normed_blocks = jnp.swapaxes(normed.reshape(tok_rows, 2, ring, rows_here), 1, 2)
+    modulated = (normed_blocks * (1.0 + shares[..., 1]) + shares[..., 0]).astype(jnp.bfloat16)
+    modulated = jnp.pad(modulated, ((0, 0), (0, 0), (0, 0), (0, extra_rows)))
+    projected_all = jnp.dot(
+        modulated.reshape(tok_rows, ring * 2 * block_rows),
+        stacked_blocks.reshape(ring * 2 * block_rows, width),
+        preferred_element_type=jnp.float32,
+    )
+    projected_qkv = (
+        projected_all[:, :qkv_cols].astype(jnp.bfloat16).reshape(tok_rows, heads_here, qkv_width)
+    )
     queries = projected_qkv[:, :, :head_dim]
     packed = projected_qkv[:, :, head_dim:]
     query_frame = position * frames_here + jnp.arange(tok_rows, dtype=jnp.int32) // frame_size

time: 245 us -> 255 us (1.041)
  other arithmetic: 12.8 us -> 18.4 us
  local copies, waits for them, and re-layouts: 9.32 us -> 12.5 us
    unnamed x17 -> x83, local copies, waits for them, and re-layouts: 1.04 us -> 5.24 us
    convert_element_type x1 -> x2, other arithmetic: 0.01 us -> 3.08 us  [the longest x1 3.05 us: per_device(): (normed_blocks * (1.0 + shares[..., 1]) + shares[..., 0]).astype(jnp.bflo...]
    mul x0 -> x1, other arithmetic: none -> 2.58 us  [per_device(): normed = centred * lax.rsqrt(variance + EPS)]
  transfers between devices with their start and end apart: 41 -> 41, of which waited for: 22 -> 22; matrix products, arithmetic and copies ran while one was open for 10% -> 12% of each run, Pallas kernels for 0% -> 0%
where the time goes in v12:
time: 255 us; the launch traced here: 252 us
  starting transfers between devices  154 us (60%)
  waiting for transfers between devices  47.7 us (19%)
  other arithmetic  18.4 us (7%)
  matrix products  16.2 us (6%)
  local copies, waits for them, and re-layouts  12.5 us (5%)
  between operations  2.74 us (1%)
    ppermute x8, starting transfers between devices, halving_scatter(): lax.ppermute(send.astype(jnp.bfloat16), axis, [(i, i ^ 1 << bit) for i in...  42.1 us
    ppermute x7, starting transfers between devices, ring_pieces(): behind = lax.ppermute(behind, axis, backward)  35.3 us
    ppermute x7, starting transfers between devices, per_device(): behind = lax.ppermute(behind, 'ctx', backward)  31.4 us
    ppermute x8, waiting for transfers between devices, ring_pieces(): ahead = lax.ppermute(ahead, axis, forward)  18 us
    ppermute x8, starting transfers between devices, per_device(): ahead = lax.ppermute(ahead, 'ctx', forward)  17.4 us
    ppermute x8, starting transfers between devices, ring_pieces(): ahead = lax.ppermute(ahead, axis, forward)  16.9 us
    ppermute x8, waiting for transfers between devices, per_device(): ahead = lax.ppermute(ahead, 'ctx', forward)  12 us
    dot_general x16, matrix products, attend_piece(): jnp.einsum('nhe,mhe->nhm', queries, key_part, preferred_element_type=jnp....  7.03 us
  transfers between devices with their start and end apart: 41, of which 22 were waited for; matrix products, arithmetic and copies ran while one was open for 12% of the time, Pallas kernels for 0%

profile of v12, /device:TPU:1, one launch (start us, length us, event | category | flops | bytes accessed | tf_op | source)
XLA Modules:
  0.0 251.8 jit_solution(1448728646943917325)
XLA Ops:
  2.3 5.7 %collective-permute-start = (bf16[104,512]{1,0:T(8,128)(2,1)S(1)}, bf16[104,512]{1,0:T(8,128)(2,1)S(1)}, u32[]{:S(2)}, u32[]{:S(2)}) collective-permute-start(bf16[104,512]{1,0:T(8,128)(2,1)S(1)} %get-tuple-element.157), channel_id=1, source_target_pairs={{0,256},{16,272},{32,288},{48,304},{64,320},{80,336},{96,352},{112... | collective-permute-start | bytes 319496 | tf_op jit(solution)/shard_map/ppermute | solution.py:34
  9.1 3.6 %collective-permute-start.40 = (bf16[320,192]{1,0:T(8,128)(2,1)S(1)}, bf16[320,192]{1,0:T(8,128)(2,1)S(1)}, u32[]{:S(2)}, u32[]{:S(2)}) collective-permute-start(bf16[320,192]{1,0:T(8,128)(2,1)S(1)} %constant_dynamic-slice_fusion), channel_id=1, source_target_pairs={{0,16},{16,32},{32,48},{48,64},{64,80},{80,96},{96,112},{112,128},... | collective-permute-start | bytes 368648 | tf_op jit(solution)/shard_map/ppermute | solution.py:19
  12.9 2.9 %copy.34 = bf16[320,3072]{0,1:T(8,128)(2,1)S(1)} copy(bf16[320,3072]{1,0:T(8,128)(2,1)} %param.10) | data formatting | bytes 3932160 | tf_op args[0]
  18.4 2.6 %fusion = f32[320,3072]{0,1:T(8,128)} fusion(bf16[320,3072]{0,1:T(8,128)(2,1)S(1)} %copy.34, f32[320]{0:T(512)S(1)} %add_rsqrt_fusion, f32[320]{0:T(512)S(1)} %broadcast_multiply_fusion), kind=kLoop, calls=%fused_computation.2 | loop fusion | flops 2949120 | bytes 5900800 | tf_op jit(solution)/shard_map/mul | solution.py:117
  22.7 3.5 %collective-permute-start.1 = (bf16[2,104,512]{2,1,0:T(8,128)(2,1)S(1)}, bf16[2,104,512]{2,1,0:T(8,128)(2,1)S(1)}, u32[]{:S(2)}, u32[]{:S(2)}) collective-permute-start(bf16[2,104,512]{2,1,0:T(8,128)(2,1)S(1)} %maximum_select_fusion.2), channel_id=1, source_target_pairs={{0,16},{16,32},{32,48},{48,64},{64,80},{80,96},{96,112},{112,128},... | collective-permute-start | bytes 638984 | tf_op jit(solution)/shard_map/ppermute | solution.py:45
  26.3 7.9 %collective-permute-start.2 = (bf16[2,104,512]{2,1,0:T(8,128)(2,1)S(1)}, bf16[2,104,512]{2,1,0:T(8,128)(2,1)S(1)}, u32[]{:S(2)}, u32[]{:S(2)}) collective-permute-start(bf16[2,104,512]{2,1,0:T(8,128)(2,1)S(1)} %maximum_select_fusion.2), channel_id=1, source_target_pairs={{0,240},{16,0},{32,16},{48,32},{64,48},{80,64},{96,80},{112,96},{1... | collective-permute-start | bytes 638984 | tf_op jit(solution)/shard_map/ppermute | solution.py:48
  38.8 4.6 %collective-permute-start.4 = (bf16[2,104,512]{2,1,0:T(8,128)(2,1)S(1)}, bf16[2,104,512]{2,1,0:T(8,128)(2,1)S(1)}, u32[]{:S(2)}, u32[]{:S(2)}) collective-permute-start(bf16[2,104,512]{2,1,0:T(8,128)(2,1)S(1)} %collective-permute-done.2), channel_id=1, source_target_pairs={{0,240},{16,0},{32,16},{48,32},{64,48},{80,64},{96,80},{112,96},{1... | collective-permute-start | bytes 638984 | tf_op jit(solution)/shard_map/ppermute | solution.py:48
  47.1 4.6 %collective-permute-start.6 = (bf16[2,104,512]{2,1,0:T(8,128)(2,1)S(1)}, bf16[2,104,512]{2,1,0:T(8,128)(2,1)S(1)}, u32[]{:S(2)}, u32[]{:S(2)}) collective-permute-start(bf16[2,104,512]{2,1,0:T(8,128)(2,1)S(1)} %collective-permute-done.4), channel_id=1, source_target_pairs={{0,240},{16,0},{32,16},{48,32},{64,48},{80,64},{96,80},{112,96},{1... | collective-permute-start | bytes 638984 | tf_op jit(solution)/shard_map/ppermute | solution.py:48
  54.9 4.6 %collective-permute-start.8 = (bf16[2,104,512]{2,1,0:T(8,128)(2,1)S(1)}, bf16[2,104,512]{2,1,0:T(8,128)(2,1)S(1)}, u32[]{:S(2)}, u32[]{:S(2)}) collective-permute-start(bf16[2,104,512]{2,1,0:T(8,128)(2,1)S(1)} %collective-permute-done.6), channel_id=1, source_target_pairs={{0,240},{16,0},{32,16},{48,32},{64,48},{80,64},{96,80},{112,96},{1... | collective-permute-start | bytes 638984 | tf_op jit(solution)/shard_map/ppermute | solution.py:48
  62.7 4.6 %collective-permute-start.10 = (bf16[2,104,512]{2,1,0:T(8,128)(2,1)S(1)}, bf16[2,104,512]{2,1,0:T(8,128)(2,1)S(1)}, u32[]{:S(2)}, u32[]{:S(2)}) collective-permute-start(bf16[2,104,512]{2,1,0:T(8,128)(2,1)S(1)} %collective-permute-done.8), channel_id=1, source_target_pairs={{0,240},{16,0},{32,16},{48,32},{64,48},{80,64},{96,80},{112,96},{1... | collective-permute-start | bytes 638984 | tf_op jit(solution)/shard_map/ppermute | solution.py:48
  70.4 4.6 %collective-permute-start.12 = (bf16[2,104,512]{2,1,0:T(8,128)(2,1)S(1)}, bf16[2,104,512]{2,1,0:T(8,128)(2,1)S(1)}, u32[]{:S(2)}, u32[]{:S(2)}) collective-permute-start(bf16[2,104,512]{2,1,0:T(8,128)(2,1)S(1)} %collective-permute-done.10), channel_id=1, source_target_pairs={{0,240},{16,0},{32,16},{48,32},{64,48},{80,64},{96,80},{112,96},{1... | collective-permute-start | bytes 638984 | tf_op jit(solution)/shard_map/ppermute | solution.py:48
  78.2 4.6 %collective-permute-start.14 = (bf16[2,104,512]{2,1,0:T(8,128)(2,1)S(1)}, bf16[2,104,512]{2,1,0:T(8,128)(2,1)S(1)}, u32[]{:S(2)}, u32[]{:S(2)}) collective-permute-start(bf16[2,104,512]{2,1,0:T(8,128)(2,1)S(1)} %collective-permute-done.12), channel_id=1, source_target_pairs={{0,240},{16,0},{32,16},{48,32},{64,48},{80,64},{96,80},{112,96},{1... | collective-permute-start | bytes 638984 | tf_op jit(solution)/shard_map/ppermute | solution.py:48
  86.9 7.8 %collective-permute-done.15 = bf16[2,104,512]{2,1,0:T(8,128)(2,1)S(1)} collective-permute-done((bf16[2,104,512]{2,1,0:T(8,128)(2,1)S(1)}, bf16[2,104,512]{2,1,0:T(8,128)(2,1)S(1)}, u32[]{:S(2)}, u32[]{:S(2)}) %collective-permute-start.15) | collective-permute-done | bytes 213024 | tf_op jit(solution)/shard_map/ppermute | solution.py:45
  99.6 3.1 %fusion.4 = bf16[320,16,2,96]{0,3,2,1:T(8,128)(2,1)S(1)} fusion(f32[320,2,16,96]{0,3,2,1:T(8,128)} %bitcast.576, f32[16,2,96]{2,1,0:T(2,128)S(1)} %copy.54, f32[16,2,96]{2,1,0:T(2,128)S(1)} %copy.53), kind=kLoop, calls=%fused_computation.31 | loop fusion | flops 2949120 | bytes 5922816 | tf_op jit(solution)/shard_map/convert_element_type | solution.py:163
  107.9 4.3 %collective-permute-done.16 = bf16[320,1,256]{2,0,1:T(8,128)(2,1)S(1)} collective-permute-done((bf16[320,1,256]{2,0,1:T(8,128)(2,1)S(1)}, bf16[320,1,256]{2,0,1:T(8,128)(2,1)S(1)}, u32[]{:S(2)}, u32[]{:S(2)}) %collective-permute-start.16) | collective-permute-done | bytes 163872 | tf_op jit(solution)/shard_map/ppermute | solution.py:185
  114.1 3.4 %collective-permute-start.17 = (bf16[2,320,1,256]{3,1,2,0:T(8,128)(2,1)S(1)}, bf16[2,320,1,256]{3,1,2,0:T(8,128)(2,1)S(1)}, u32[]{:S(2)}, u32[]{:S(2)}) collective-permute-start(bf16[2,320,1,256]{3,1,2,0:T(8,128)(2,1)S(1)} %maximum_select_fusion), channel_id=1, source_target_pairs={{0,16},{16,32},{32,48},{48,64},{64,80},{80,96},{96,112},{112,128},... | collective-permute-start | bytes 983048 | tf_op jit(solution)/shard_map/ppermute | solution.py:213
  118.8 4.3 %collective-permute-done.17 = bf16[2,320,1,256]{3,1,2,0:T(8,128)(2,1)S(1)} collective-permute-done((bf16[2,320,1,256]{3,1,2,0:T(8,128)(2,1)S(1)}, bf16[2,320,1,256]{3,1,2,0:T(8,128)(2,1)S(1)}, u32[]{:S(2)}, u32[]{:S(2)}) %collective-permute-start.17) | collective-permute-done | bytes 327712 | tf_op jit(solution)/shard_map/ppermute | solution.py:213
  123.1 2.3 collective-permute-start.18
  127.8 4.3 %collective-permute-start.21 = (bf16[2,320,1,256]{3,1,2,0:T(8,128)(2,1)S(1)}, bf16[2,320,1,256]{3,1,2,0:T(8,128)(2,1)S(1)}, u32[]{:S(2)}, u32[]{:S(2)}) collective-permute-start(bf16[2,320,1,256]{3,1,2,0:T(8,128)(2,1)S(1)} %collective-permute-done.19), channel_id=1, source_target_pairs={{0,240},{16,0},{32,16},{48,32},{64,48},{80,64},{96,80},{112,96},{1... | collective-permute-start | bytes 983048 | tf_op jit(solution)/shard_map/ppermute | solution.py:216
  138.3 4.8 %collective-permute-start.23 = (bf16[2,320,1,256]{3,1,2,0:T(8,128)(2,1)S(1)}, bf16[2,320,1,256]{3,1,2,0:T(8,128)(2,1)S(1)}, u32[]{:S(2)}, u32[]{:S(2)}) collective-permute-start(bf16[2,320,1,256]{3,1,2,0:T(8,128)(2,1)S(1)} %collective-permute-done.21), channel_id=1, source_target_pairs={{0,240},{16,0},{32,16},{48,32},{64,48},{80,64},{96,80},{112,96},{1... | collective-permute-start | bytes 983048 | tf_op jit(solution)/shard_map/ppermute | solution.py:216
  149.4 5.3 %collective-permute-start.25 = (bf16[2,320,1,256]{3,1,2,0:T(8,128)(2,1)S(1)}, bf16[2,320,1,256]{3,1,2,0:T(8,128)(2,1)S(1)}, u32[]{:S(2)}, u32[]{:S(2)}) collective-permute-start(bf16[2,320,1,256]{3,1,2,0:T(8,128)(2,1)S(1)} %collective-permute-done.23), channel_id=1, source_target_pairs={{0,240},{16,0},{32,16},{48,32},{64,48},{80,64},{96,80},{112,96},{1... | collective-permute-start | bytes 983048 | tf_op jit(solution)/shard_map/ppermute | solution.py:216
  160.6 5.0 %collective-permute-start.27 = (bf16[2,320,1,256]{3,1,2,0:T(8,128)(2,1)S(1)}, bf16[2,320,1,256]{3,1,2,0:T(8,128)(2,1)S(1)}, u32[]{:S(2)}, u32[]{:S(2)}) collective-permute-start(bf16[2,320,1,256]{3,1,2,0:T(8,128)(2,1)S(1)} %collective-permute-done.25), channel_id=1, source_target_pairs={{0,240},{16,0},{32,16},{48,32},{64,48},{80,64},{96,80},{112,96},{1... | collective-permute-start | bytes 983048 | tf_op jit(solution)/shard_map/ppermute | solution.py:216
  171.5 5.0 %collective-permute-start.29 = (bf16[2,320,1,256]{3,1,2,0:T(8,128)(2,1)S(1)}, bf16[2,320,1,256]{3,1,2,0:T(8,128)(2,1)S(1)}, u32[]{:S(2)}, u32[]{:S(2)}) collective-permute-start(bf16[2,320,1,256]{3,1,2,0:T(8,128)(2,1)S(1)} %collective-permute-done.27), channel_id=1, source_target_pairs={{0,240},{16,0},{32,16},{48,32},{64,48},{80,64},{96,80},{112,96},{1... | collective-permute-start | bytes 983048 | tf_op jit(solution)/shard_map/ppermute | solution.py:216
  182.0 5.0 %collective-permute-start.30 = (bf16[2,320,1,256]{3,1,2,0:T(8,128)(2,1)S(1)}, bf16[2,320,1,256]{3,1,2,0:T(8,128)(2,1)S(1)}, u32[]{:S(2)}, u32[]{:S(2)}) collective-permute-start(bf16[2,320,1,256]{3,1,2,0:T(8,128)(2,1)S(1)} %collective-permute-done.29), channel_id=1, source_target_pairs={{0,240},{16,0},{32,16},{48,32},{64,48},{80,64},{96,80},{112,96},{1... | collective-permute-start | bytes 983048 | tf_op jit(solution)/shard_map/ppermute | solution.py:216
  191.5 5.0 %collective-permute-done.31 = bf16[2,320,1,256]{3,1,2,0:T(8,128)(2,1)S(1)} collective-permute-done((bf16[2,320,1,256]{3,1,2,0:T(8,128)(2,1)S(1)}, bf16[2,320,1,256]{3,1,2,0:T(8,128)(2,1)S(1)}, u32[]{:S(2)}, u32[]{:S(2)}) %collective-permute-start.31) | collective-permute-done | bytes 327712 | tf_op jit(solution)/shard_map/ppermute | solution.py:213
  199.3 22.4 %collective-permute-start.32 = (bf16[160,1536]{1,0:T(8,128)(2,1)S(1)}, bf16[160,1536]{1,0:T(8,128)(2,1)S(1)}, u32[]{:S(2)}, u32[]{:S(2)}) collective-permute-start(bf16[160,1536]{1,0:T(8,128)(2,1)S(1)} %dynamic-slice_convert_fusion.1), channel_id=1, source_target_pairs={{0,1},{1,0},{2,3},{3,2},{4,5},{5,4},{6,7},{7,6},{8,9},{9,8},{10,11... | collective-permute-start | bytes 1474568 | tf_op jit(solution)/shard_map/ppermute | solution.py:70
  224.2 2.3 collective-permute-start.33
  226.7 3.1 %collective-permute-start.37 = (bf16[160,768]{1,0:T(8,128)(2,1)S(1)}, bf16[160,768]{1,0:T(8,128)(2,1)S(1)}, u32[]{:S(2)}, u32[]{:S(2)}) collective-permute-start(bf16[160,768]{1,0:T(8,128)(2,1)S(1)} %dynamic-slice_convert_fusion.2), channel_id=1, source_target_pairs={{0,2},{1,3},{2,0},{3,1},{4,6},{5,7},{6,4},{7,5},{8,10},{9,11},{10,... | collective-permute-start | bytes 737288 | tf_op jit(solution)/shard_map/ppermute | solution.py:70
  229.9 3.3 %collective-permute-done.33 = bf16[160,768]{1,0:T(8,128)(2,1)S(1)} collective-permute-done((bf16[160,768]{1,0:T(8,128)(2,1)S(1)}, bf16[160,768]{1,0:T(8,128)(2,1)S(1)}, u32[]{:S(2)}, u32[]{:S(2)}) %collective-permute-start.33) | collective-permute-done | bytes 245792 | tf_op jit(solution)/shard_map/ppermute | solution.py:70
  233.3 3.1 %collective-permute-start.34 = (bf16[160,384]{1,0:T(8,128)(2,1)S(1)}, bf16[160,384]{1,0:T(8,128)(2,1)S(1)}, u32[]{:S(2)}, u32[]{:S(2)}) collective-permute-start(bf16[160,384]{1,0:T(8,128)(2,1)S(1)} %dynamic-slice_convert_fusion.5), channel_id=1, source_target_pairs={{0,2},{1,3},{2,0},{3,1},{4,6},{5,7},{6,4},{7,5},{8,10},{9,11},{10,... | collective-permute-start | bytes 368648 | tf_op jit(solution)/shard_map/ppermute | solution.py:70
  236.5 4.3 %collective-permute-start.38 = (bf16[160,384]{1,0:T(8,128)(2,1)S(1)}, bf16[160,384]{1,0:T(8,128)(2,1)S(1)}, u32[]{:S(2)}, u32[]{:S(2)}) collective-permute-start(bf16[160,384]{1,0:T(8,128)(2,1)S(1)} %dynamic-slice_convert_fusion.4), channel_id=1, source_target_pairs={{0,4},{1,5},{2,6},{3,7},{4,0},{5,1},{6,2},{7,3},{8,12},{9,13},{10,... | collective-permute-start | bytes 368648 | tf_op jit(solution)/shard_map/ppermute | solution.py:70
  241.0 2.7 %collective-permute-start.35 = (bf16[160,192]{1,0:T(8,128)(2,1)S(1)}, bf16[160,192]{1,0:T(8,128)(2,1)S(1)}, u32[]{:S(2)}, u32[]{:S(2)}) collective-permute-start(bf16[160,192]{1,0:T(8,128)(2,1)S(1)} %dynamic-slice_convert_fusion.7), channel_id=1, source_target_pairs={{0,4},{1,5},{2,6},{3,7},{4,0},{5,1},{6,2},{7,3},{8,12},{9,13},{10,... | collective-permute-start | bytes 184328 | tf_op jit(solution)/shard_map/ppermute | solution.py:70
  (279 shorter events, 94.7 us)
Async XLA Ops:
  2.3 20.3 %collective-permute-start = (bf16[104,512]{1,0:T(8,128)(2,1)S(1)}, bf16[104,512]{1,0:T(8,128)(2,1)S(1)}, u32[]{:S(2)}, u32[]{:S(2)}) collective-permute-start(bf16[104,512]{1,0:T(8,128)(2,1)S(1)} %get-tuple-element.157), channel_id=1, source_target_pairs={{0,256},{16,272},{32,288},{48,304},{64,320},{80,336},{96,352},{112... | collective-permute-start | bytes 319496 | tf_op jit(solution)/shard_map/ppermute | solution.py:34
  9.1 25.4 %collective-permute-start.40 = (bf16[320,192]{1,0:T(8,128)(2,1)S(1)}, bf16[320,192]{1,0:T(8,128)(2,1)S(1)}, u32[]{:S(2)}, u32[]{:S(2)}) collective-permute-start(bf16[320,192]{1,0:T(8,128)(2,1)S(1)} %constant_dynamic-slice_fusion), channel_id=1, source_target_pairs={{0,16},{16,32},{32,48},{48,64},{64,80},{80,96},{96,112},{112,128},... | collective-permute-start | bytes 368648 | tf_op jit(solution)/shard_map/ppermute | solution.py:19
  22.7 14.1 %collective-permute-start.1 = (bf16[2,104,512]{2,1,0:T(8,128)(2,1)S(1)}, bf16[2,104,512]{2,1,0:T(8,128)(2,1)S(1)}, u32[]{:S(2)}, u32[]{:S(2)}) collective-permute-start(bf16[2,104,512]{2,1,0:T(8,128)(2,1)S(1)} %maximum_select_fusion.2), channel_id=1, source_target_pairs={{0,16},{16,32},{32,48},{48,64},{64,80},{80,96},{96,112},{112,128},... | collective-permute-start | bytes 638984 | tf_op jit(solution)/shard_map/ppermute | solution.py:45
  26.3 12.5 %collective-permute-start.2 = (bf16[2,104,512]{2,1,0:T(8,128)(2,1)S(1)}, bf16[2,104,512]{2,1,0:T(8,128)(2,1)S(1)}, u32[]{:S(2)}, u32[]{:S(2)}) collective-permute-start(bf16[2,104,512]{2,1,0:T(8,128)(2,1)S(1)} %maximum_select_fusion.2), channel_id=1, source_target_pairs={{0,240},{16,0},{32,16},{48,32},{64,48},{80,64},{96,80},{112,96},{1... | collective-permute-start | bytes 638984 | tf_op jit(solution)/shard_map/ppermute | solution.py:48
  36.9 8.3 %collective-permute-start.3 = (bf16[2,104,512]{2,1,0:T(8,128)(2,1)S(1)}, bf16[2,104,512]{2,1,0:T(8,128)(2,1)S(1)}, u32[]{:S(2)}, u32[]{:S(2)}) collective-permute-start(bf16[2,104,512]{2,1,0:T(8,128)(2,1)S(1)} %collective-permute-done.1), channel_id=1, source_target_pairs={{0,16},{16,32},{32,48},{48,64},{64,80},{80,96},{96,112},{112,128},... | collective-permute-start | bytes 638984 | tf_op jit(solution)/shard_map/ppermute | solution.py:45
  38.8 8.3 %collective-permute-start.4 = (bf16[2,104,512]{2,1,0:T(8,128)(2,1)S(1)}, bf16[2,104,512]{2,1,0:T(8,128)(2,1)S(1)}, u32[]{:S(2)}, u32[]{:S(2)}) collective-permute-start(bf16[2,104,512]{2,1,0:T(8,128)(2,1)S(1)} %collective-permute-done.2), channel_id=1, source_target_pairs={{0,240},{16,0},{32,16},{48,32},{64,48},{80,64},{96,80},{112,96},{1... | collective-permute-start | bytes 638984 | tf_op jit(solution)/shard_map/ppermute | solution.py:48
  45.1 7.8 %collective-permute-start.5 = (bf16[2,104,512]{2,1,0:T(8,128)(2,1)S(1)}, bf16[2,104,512]{2,1,0:T(8,128)(2,1)S(1)}, u32[]{:S(2)}, u32[]{:S(2)}) collective-permute-start(bf16[2,104,512]{2,1,0:T(8,128)(2,1)S(1)} %collective-permute-done.3), channel_id=1, source_target_pairs={{0,16},{16,32},{32,48},{48,64},{64,80},{80,96},{96,112},{112,128},... | collective-permute-start | bytes 638984 | tf_op jit(solution)/shard_map/ppermute | solution.py:45
  47.1 7.8 %collective-permute-start.6 = (bf16[2,104,512]{2,1,0:T(8,128)(2,1)S(1)}, bf16[2,104,512]{2,1,0:T(8,128)(2,1)S(1)}, u32[]{:S(2)}, u32[]{:S(2)}) collective-permute-start(bf16[2,104,512]{2,1,0:T(8,128)(2,1)S(1)} %collective-permute-done.4), channel_id=1, source_target_pairs={{0,240},{16,0},{32,16},{48,32},{64,48},{80,64},{96,80},{112,96},{1... | collective-permute-start | bytes 638984 | tf_op jit(solution)/shard_map/ppermute | solution.py:48
  52.9 7.8 %collective-permute-start.7 = (bf16[2,104,512]{2,1,0:T(8,128)(2,1)S(1)}, bf16[2,104,512]{2,1,0:T(8,128)(2,1)S(1)}, u32[]{:S(2)}, u32[]{:S(2)}) collective-permute-start(bf16[2,104,512]{2,1,0:T(8,128)(2,1)S(1)} %collective-permute-done.5), channel_id=1, source_target_pairs={{0,16},{16,32},{32,48},{48,64},{64,80},{80,96},{96,112},{112,128},... | collective-permute-start | bytes 638984 | tf_op jit(solution)/shard_map/ppermute | solution.py:45
  60.7 7.8 %collective-permute-start.9 = (bf16[2,104,512]{2,1,0:T(8,128)(2,1)S(1)}, bf16[2,104,512]{2,1,0:T(8,128)(2,1)S(1)}, u32[]{:S(2)}, u32[]{:S(2)}) collective-permute-start(bf16[2,104,512]{2,1,0:T(8,128)(2,1)S(1)} %collective-permute-done.7), channel_id=1, source_target_pairs={{0,16},{16,32},{32,48},{48,64},{64,80},{80,96},{96,112},{112,128},... | collective-permute-start | bytes 638984 | tf_op jit(solution)/shard_map/ppermute | solution.py:45
  68.5 7.8 %collective-permute-start.11 = (bf16[2,104,512]{2,1,0:T(8,128)(2,1)S(1)}, bf16[2,104,512]{2,1,0:T(8,128)(2,1)S(1)}, u32[]{:S(2)}, u32[]{:S(2)}) collective-permute-start(bf16[2,104,512]{2,1,0:T(8,128)(2,1)S(1)} %collective-permute-done.9), channel_id=1, source_target_pairs={{0,16},{16,32},{32,48},{48,64},{64,80},{80,96},{96,112},{112,128},... | collective-permute-start | bytes 638984 | tf_op jit(solution)/shard_map/ppermute | solution.py:45
  76.3 8.7 %collective-permute-start.13 = (bf16[2,104,512]{2,1,0:T(8,128)(2,1)S(1)}, bf16[2,104,512]{2,1,0:T(8,128)(2,1)S(1)}, u32[]{:S(2)}, u32[]{:S(2)}) collective-permute-start(bf16[2,104,512]{2,1,0:T(8,128)(2,1)S(1)} %collective-permute-done.11), channel_id=1, source_target_pairs={{0,16},{16,32},{32,48},{48,64},{64,80},{80,96},{96,112},{112,128},... | collective-permute-start | bytes 638984 | tf_op jit(solution)/shard_map/ppermute | solution.py:45
  78.2 8.7 %collective-permute-start.14 = (bf16[2,104,512]{2,1,0:T(8,128)(2,1)S(1)}, bf16[2,104,512]{2,1,0:T(8,128)(2,1)S(1)}, u32[]{:S(2)}, u32[]{:S(2)}) collective-permute-start(bf16[2,104,512]{2,1,0:T(8,128)(2,1)S(1)} %collective-permute-done.12), channel_id=1, source_target_pairs={{0,240},{16,0},{32,16},{48,32},{64,48},{80,64},{96,80},{112,96},{1... | collective-permute-start | bytes 638984 | tf_op jit(solution)/shard_map/ppermute | solution.py:48
  85.0 9.8 %collective-permute-start.15 = (bf16[2,104,512]{2,1,0:T(8,128)(2,1)S(1)}, bf16[2,104,512]{2,1,0:T(8,128)(2,1)S(1)}, u32[]{:S(2)}, u32[]{:S(2)}) collective-permute-start(bf16[2,104,512]{2,1,0:T(8,128)(2,1)S(1)} %collective-permute-done.13), channel_id=1, source_target_pairs={{0,16},{16,32},{32,48},{48,64},{64,80},{80,96},{96,112},{112,128},... | collective-permute-start | bytes 638984 | tf_op jit(solution)/shard_map/ppermute | solution.py:45
  112.2 13.7 %collective-permute-start.19 = (bf16[2,320,1,256]{3,1,2,0:T(8,128)(2,1)S(1)}, bf16[2,320,1,256]{3,1,2,0:T(8,128)(2,1)S(1)}, u32[]{:S(2)}, u32[]{:S(2)}) collective-permute-start(bf16[2,320,1,256]{3,1,2,0:T(8,128)(2,1)S(1)} %maximum_select_fusion), channel_id=1, source_target_pairs={{0,240},{16,0},{32,16},{48,32},{64,48},{80,64},{96,80},{112,96},{1... | collective-permute-start | bytes 983048 | tf_op jit(solution)/shard_map/ppermute | solution.py:216
  114.1 9.0 %collective-permute-start.17 = (bf16[2,320,1,256]{3,1,2,0:T(8,128)(2,1)S(1)}, bf16[2,320,1,256]{3,1,2,0:T(8,128)(2,1)S(1)}, u32[]{:S(2)}, u32[]{:S(2)}) collective-permute-start(bf16[2,320,1,256]{3,1,2,0:T(8,128)(2,1)S(1)} %maximum_select_fusion), channel_id=1, source_target_pairs={{0,16},{16,32},{32,48},{48,64},{64,80},{80,96},{96,112},{112,128},... | collective-permute-start | bytes 983048 | tf_op jit(solution)/shard_map/ppermute | solution.py:213
  123.1 10.9 %collective-permute-start.18 = (bf16[2,320,1,256]{3,1,2,0:T(8,128)(2,1)S(1)}, bf16[2,320,1,256]{3,1,2,0:T(8,128)(2,1)S(1)}, u32[]{:S(2)}, u32[]{:S(2)}) collective-permute-start(bf16[2,320,1,256]{3,1,2,0:T(8,128)(2,1)S(1)} %collective-permute-done.17), channel_id=1, source_target_pairs={{0,16},{16,32},{32,48},{48,64},{64,80},{80,96},{96,112},{112,128},... | collective-permute-start | bytes 983048 | tf_op jit(solution)/shard_map/ppermute | solution.py:213
  127.8 8.5 %collective-permute-start.21 = (bf16[2,320,1,256]{3,1,2,0:T(8,128)(2,1)S(1)}, bf16[2,320,1,256]{3,1,2,0:T(8,128)(2,1)S(1)}, u32[]{:S(2)}, u32[]{:S(2)}) collective-permute-start(bf16[2,320,1,256]{3,1,2,0:T(8,128)(2,1)S(1)} %collective-permute-done.19), channel_id=1, source_target_pairs={{0,240},{16,0},{32,16},{48,32},{64,48},{80,64},{96,80},{112,96},{1... | collective-permute-start | bytes 983048 | tf_op jit(solution)/shard_map/ppermute | solution.py:216
  134.0 9.9 %collective-permute-start.20 = (bf16[2,320,1,256]{3,1,2,0:T(8,128)(2,1)S(1)}, bf16[2,320,1,256]{3,1,2,0:T(8,128)(2,1)S(1)}, u32[]{:S(2)}, u32[]{:S(2)}) collective-permute-start(bf16[2,320,1,256]{3,1,2,0:T(8,128)(2,1)S(1)} %collective-permute-done.18), channel_id=1, source_target_pairs={{0,16},{16,32},{32,48},{48,64},{64,80},{80,96},{96,112},{112,128},... | collective-permute-start | bytes 983048 | tf_op jit(solution)/shard_map/ppermute | solution.py:213
  138.3 9.2 %collective-permute-start.23 = (bf16[2,320,1,256]{3,1,2,0:T(8,128)(2,1)S(1)}, bf16[2,320,1,256]{3,1,2,0:T(8,128)(2,1)S(1)}, u32[]{:S(2)}, u32[]{:S(2)}) collective-permute-start(bf16[2,320,1,256]{3,1,2,0:T(8,128)(2,1)S(1)} %collective-permute-done.21), channel_id=1, source_target_pairs={{0,240},{16,0},{32,16},{48,32},{64,48},{80,64},{96,80},{112,96},{1... | collective-permute-start | bytes 983048 | tf_op jit(solution)/shard_map/ppermute | solution.py:216
  143.9 10.8 %collective-permute-start.22 = (bf16[2,320,1,256]{3,1,2,0:T(8,128)(2,1)S(1)}, bf16[2,320,1,256]{3,1,2,0:T(8,128)(2,1)S(1)}, u32[]{:S(2)}, u32[]{:S(2)}) collective-permute-start(bf16[2,320,1,256]{3,1,2,0:T(8,128)(2,1)S(1)} %collective-permute-done.20), channel_id=1, source_target_pairs={{0,16},{16,32},{32,48},{48,64},{64,80},{80,96},{96,112},{112,128},... | collective-permute-start | bytes 983048 | tf_op jit(solution)/shard_map/ppermute | solution.py:213
  149.4 9.3 %collective-permute-start.25 = (bf16[2,320,1,256]{3,1,2,0:T(8,128)(2,1)S(1)}, bf16[2,320,1,256]{3,1,2,0:T(8,128)(2,1)S(1)}, u32[]{:S(2)}, u32[]{:S(2)}) collective-permute-start(bf16[2,320,1,256]{3,1,2,0:T(8,128)(2,1)S(1)} %collective-permute-done.23), channel_id=1, source_target_pairs={{0,240},{16,0},{32,16},{48,32},{64,48},{80,64},{96,80},{112,96},{1... | collective-permute-start | bytes 983048 | tf_op jit(solution)/shard_map/ppermute | solution.py:216
  154.7 10.9 %collective-permute-start.24 = (bf16[2,320,1,256]{3,1,2,0:T(8,128)(2,1)S(1)}, bf16[2,320,1,256]{3,1,2,0:T(8,128)(2,1)S(1)}, u32[]{:S(2)}, u32[]{:S(2)}) collective-permute-start(bf16[2,320,1,256]{3,1,2,0:T(8,128)(2,1)S(1)} %collective-permute-done.22), channel_id=1, source_target_pairs={{0,16},{16,32},{32,48},{48,64},{64,80},{80,96},{96,112},{112,128},... | collective-permute-start | bytes 983048 | tf_op jit(solution)/shard_map/ppermute | solution.py:213
  160.6 9.0 %collective-permute-start.27 = (bf16[2,320,1,256]{3,1,2,0:T(8,128)(2,1)S(1)}, bf16[2,320,1,256]{3,1,2,0:T(8,128)(2,1)S(1)}, u32[]{:S(2)}, u32[]{:S(2)}) collective-permute-start(bf16[2,320,1,256]{3,1,2,0:T(8,128)(2,1)S(1)} %collective-permute-done.25), channel_id=1, source_target_pairs={{0,240},{16,0},{32,16},{48,32},{64,48},{80,64},{96,80},{112,96},{1... | collective-permute-start | bytes 983048 | tf_op jit(solution)/shard_map/ppermute | solution.py:216
  165.7 10.9 %collective-permute-start.26 = (bf16[2,320,1,256]{3,1,2,0:T(8,128)(2,1)S(1)}, bf16[2,320,1,256]{3,1,2,0:T(8,128)(2,1)S(1)}, u32[]{:S(2)}, u32[]{:S(2)}) collective-permute-start(bf16[2,320,1,256]{3,1,2,0:T(8,128)(2,1)S(1)} %collective-permute-done.24), channel_id=1, source_target_pairs={{0,16},{16,32},{32,48},{48,64},{64,80},{80,96},{96,112},{112,128},... | collective-permute-start | bytes 983048 | tf_op jit(solution)/shard_map/ppermute | solution.py:213
  171.5 9.0 %collective-permute-start.29 = (bf16[2,320,1,256]{3,1,2,0:T(8,128)(2,1)S(1)}, bf16[2,320,1,256]{3,1,2,0:T(8,128)(2,1)S(1)}, u32[]{:S(2)}, u32[]{:S(2)}) collective-permute-start(bf16[2,320,1,256]{3,1,2,0:T(8,128)(2,1)S(1)} %collective-permute-done.27), channel_id=1, source_target_pairs={{0,240},{16,0},{32,16},{48,32},{64,48},{80,64},{96,80},{112,96},{1... | collective-permute-start | bytes 983048 | tf_op jit(solution)/shard_map/ppermute | solution.py:216
  176.6 10.9 %collective-permute-start.28 = (bf16[2,320,1,256]{3,1,2,0:T(8,128)(2,1)S(1)}, bf16[2,320,1,256]{3,1,2,0:T(8,128)(2,1)S(1)}, u32[]{:S(2)}, u32[]{:S(2)}) collective-permute-start(bf16[2,320,1,256]{3,1,2,0:T(8,128)(2,1)S(1)} %collective-permute-done.26), channel_id=1, source_target_pairs={{0,16},{16,32},{32,48},{48,64},{64,80},{80,96},{96,112},{112,128},... | collective-permute-start | bytes 983048 | tf_op jit(solution)/shard_map/ppermute | solution.py:213
  182.0 9.0 %collective-permute-start.30 = (bf16[2,320,1,256]{3,1,2,0:T(8,128)(2,1)S(1)}, bf16[2,320,1,256]{3,1,2,0:T(8,128)(2,1)S(1)}, u32[]{:S(2)}, u32[]{:S(2)}) collective-permute-start(bf16[2,320,1,256]{3,1,2,0:T(8,128)(2,1)S(1)} %collective-permute-done.29), channel_id=1, source_target_pairs={{0,240},{16,0},{32,16},{48,32},{64,48},{80,64},{96,80},{112,96},{1... | collective-permute-start | bytes 983048 | tf_op jit(solution)/shard_map/ppermute | solution.py:216
  187.5 9.0 %collective-permute-start.31 = (bf16[2,320,1,256]{3,1,2,0:T(8,128)(2,1)S(1)}, bf16[2,320,1,256]{3,1,2,0:T(8,128)(2,1)S(1)}, u32[]{:S(2)}, u32[]{:S(2)}) collective-permute-start(bf16[2,320,1,256]{3,1,2,0:T(8,128)(2,1)S(1)} %collective-permute-done.28), channel_id=1, source_target_pairs={{0,16},{16,32},{32,48},{48,64},{64,80},{80,96},{96,112},{112,128},... | collective-permute-start | bytes 983048 | tf_op jit(solution)/shard_map/ppermute | solution.py:213
  199.3 24.8 %collective-permute-start.32 = (bf16[160,1536]{1,0:T(8,128)(2,1)S(1)}, bf16[160,1536]{1,0:T(8,128)(2,1)S(1)}, u32[]{:S(2)}, u32[]{:S(2)}) collective-permute-start(bf16[160,1536]{1,0:T(8,128)(2,1)S(1)} %dynamic-slice_convert_fusion.1), channel_id=1, source_target_pairs={{0,1},{1,0},{2,3},{3,2},{4,5},{5,4},{6,7},{7,6},{8,9},{9,8},{10,11... | collective-permute-start | bytes 1474568 | tf_op jit(solution)/shard_map/ppermute | solution.py:70
  224.2 8.9 %collective-permute-start.33 = (bf16[160,768]{1,0:T(8,128)(2,1)S(1)}, bf16[160,768]{1,0:T(8,128)(2,1)S(1)}, u32[]{:S(2)}, u32[]{:S(2)}) collective-permute-start(bf16[160,768]{1,0:T(8,128)(2,1)S(1)} %dynamic-slice_convert_fusion.3), channel_id=1, source_target_pairs={{0,8},{1,9},{2,10},{3,11},{4,12},{5,13},{6,14},{7,15},{8,0},{9,1},... | collective-permute-start | bytes 737288 | tf_op jit(solution)/shard_map/ppermute | solution.py:70
  226.7 9.6 %collective-permute-start.37 = (bf16[160,768]{1,0:T(8,128)(2,1)S(1)}, bf16[160,768]{1,0:T(8,128)(2,1)S(1)}, u32[]{:S(2)}, u32[]{:S(2)}) collective-permute-start(bf16[160,768]{1,0:T(8,128)(2,1)S(1)} %dynamic-slice_convert_fusion.2), channel_id=1, source_target_pairs={{0,2},{1,3},{2,0},{3,1},{4,6},{5,7},{6,4},{7,5},{8,10},{9,11},{10,... | collective-permute-start | bytes 737288 | tf_op jit(solution)/shard_map/ppermute | solution.py:70
  (50 other events, 284.9 us)

commit v13 on v11

--- a/solution.py
+++ b/solution.py
@@ -220,7 +220,7 @@
     bits = size.bit_length() - 1
     middle = list(range(1, bits - 1))
     half_rows = tok_rows // 2
-    orders = [[0, bits - 1] + middle, [0] + middle + [bits - 1]]
+    orders = [[0, bits - 1] + middle, [0] + middle[:1] + [bits - 1] + middle[1:]]
     head_parts = []
     for part, order in enumerate(orders):
         by_bit = o_piece.reshape((2,) * bits + (full_rows // size,) + o_piece.shape[1:])

time: 245 us -> 244 us (level)
  no operation moved by 1% of the time
where the time goes in v13:
time: 244 us; the launch traced here: 241 us
  starting transfers between devices  154 us (63%)
  waiting for transfers between devices  47.1 us (19%)
  matrix products  15.6 us (6%)
  other arithmetic  12.8 us (5%)
  local copies, waits for them, and re-layouts  9.32 us (4%)
    ppermute x8, starting transfers between devices, halving_scatter(): lax.ppermute(send.astype(jnp.bfloat16), axis, [(i, i ^ 1 << bit) for i in...  41.7 us
    ppermute x7, starting transfers between devices, ring_pieces(): behind = lax.ppermute(behind, axis, backward)  35.3 us
    ppermute x7, starting transfers between devices, per_device(): behind = lax.ppermute(behind, 'ctx', backward)  31.4 us
    ppermute x8, waiting for transfers between devices, ring_pieces(): ahead = lax.ppermute(ahead, axis, forward)  18.7 us
    ppermute x8, starting transfers between devices, per_device(): ahead = lax.ppermute(ahead, 'ctx', forward)  17.4 us
    ppermute x8, starting transfers between devices, ring_pieces(): ahead = lax.ppermute(ahead, axis, forward)  16.9 us
    ppermute x8, waiting for transfers between devices, per_device(): ahead = lax.ppermute(ahead, 'ctx', forward)  12.3 us
    ppermute x8, waiting for transfers between devices, halving_scatter(): lax.ppermute(send.astype(jnp.bfloat16), axis, [(i, i ^ 1 << bit) for i in...  7.93 us
  transfers between devices with their start and end apart: 41, of which 22 were waited for; matrix products, arithmetic and copies ran while one was open for 10% of the time, Pallas kernels for 0%

profile of v13, /device:TPU:1, one launch (start us, length us, event | category | flops | bytes accessed | tf_op | source)
XLA Modules:
  0.0 241.0 jit_solution(8373978118363967324)
XLA Ops:
  2.3 5.7 %collective-permute-start = (bf16[104,512]{1,0:T(8,128)(2,1)S(1)}, bf16[104,512]{1,0:T(8,128)(2,1)S(1)}, u32[]{:S(2)}, u32[]{:S(2)}) collective-permute-start(bf16[104,512]{1,0:T(8,128)(2,1)S(1)} %get-tuple-element.157), channel_id=1, source_target_pairs={{0,256},{16,272},{32,288},{48,304},{64,320},{80,336},{96,352},{112... | collective-permute-start | bytes 319496 | tf_op jit(solution)/shard_map/ppermute | solution.py:34
  9.1 3.6 %collective-permute-start.40 = (bf16[320,192]{1,0:T(8,128)(2,1)S(1)}, bf16[320,192]{1,0:T(8,128)(2,1)S(1)}, u32[]{:S(2)}, u32[]{:S(2)}) collective-permute-start(bf16[320,192]{1,0:T(8,128)(2,1)S(1)} %constant_dynamic-slice_fusion), channel_id=1, source_target_pairs={{0,16},{16,32},{32,48},{48,64},{64,80},{80,96},{96,112},{112,128},... | collective-permute-start | bytes 368648 | tf_op jit(solution)/shard_map/ppermute | solution.py:19
  16.3 3.5 %collective-permute-start.1 = (bf16[2,104,512]{2,1,0:T(8,128)(2,1)S(1)}, bf16[2,104,512]{2,1,0:T(8,128)(2,1)S(1)}, u32[]{:S(2)}, u32[]{:S(2)}) collective-permute-start(bf16[2,104,512]{2,1,0:T(8,128)(2,1)S(1)} %maximum_select_fusion.2), channel_id=1, source_target_pairs={{0,16},{16,32},{32,48},{48,64},{64,80},{80,96},{96,112},{112,128},... | collective-permute-start | bytes 638984 | tf_op jit(solution)/shard_map/ppermute | solution.py:45
  19.8 7.9 %collective-permute-start.2 = (bf16[2,104,512]{2,1,0:T(8,128)(2,1)S(1)}, bf16[2,104,512]{2,1,0:T(8,128)(2,1)S(1)}, u32[]{:S(2)}, u32[]{:S(2)}) collective-permute-start(bf16[2,104,512]{2,1,0:T(8,128)(2,1)S(1)} %maximum_select_fusion.2), channel_id=1, source_target_pairs={{0,240},{16,0},{32,16},{48,32},{64,48},{80,64},{96,80},{112,96},{1... | collective-permute-start | bytes 638984 | tf_op jit(solution)/shard_map/ppermute | solution.py:48
  28.1 2.3 collective-permute-done.1
  32.3 4.6 %collective-permute-start.4 = (bf16[2,104,512]{2,1,0:T(8,128)(2,1)S(1)}, bf16[2,104,512]{2,1,0:T(8,128)(2,1)S(1)}, u32[]{:S(2)}, u32[]{:S(2)}) collective-permute-start(bf16[2,104,512]{2,1,0:T(8,128)(2,1)S(1)} %collective-permute-done.2), channel_id=1, source_target_pairs={{0,240},{16,0},{32,16},{48,32},{64,48},{80,64},{96,80},{112,96},{1... | collective-permute-start | bytes 638984 | tf_op jit(solution)/shard_map/ppermute | solution.py:48
  40.6 4.6 %collective-permute-start.6 = (bf16[2,104,512]{2,1,0:T(8,128)(2,1)S(1)}, bf16[2,104,512]{2,1,0:T(8,128)(2,1)S(1)}, u32[]{:S(2)}, u32[]{:S(2)}) collective-permute-start(bf16[2,104,512]{2,1,0:T(8,128)(2,1)S(1)} %collective-permute-done.4), channel_id=1, source_target_pairs={{0,240},{16,0},{32,16},{48,32},{64,48},{80,64},{96,80},{112,96},{1... | collective-permute-start | bytes 638984 | tf_op jit(solution)/shard_map/ppermute | solution.py:48
  48.4 4.6 %collective-permute-start.8 = (bf16[2,104,512]{2,1,0:T(8,128)(2,1)S(1)}, bf16[2,104,512]{2,1,0:T(8,128)(2,1)S(1)}, u32[]{:S(2)}, u32[]{:S(2)}) collective-permute-start(bf16[2,104,512]{2,1,0:T(8,128)(2,1)S(1)} %collective-permute-done.6), channel_id=1, source_target_pairs={{0,240},{16,0},{32,16},{48,32},{64,48},{80,64},{96,80},{112,96},{1... | collective-permute-start | bytes 638984 | tf_op jit(solution)/shard_map/ppermute | solution.py:48
  56.2 4.6 %collective-permute-start.10 = (bf16[2,104,512]{2,1,0:T(8,128)(2,1)S(1)}, bf16[2,104,512]{2,1,0:T(8,128)(2,1)S(1)}, u32[]{:S(2)}, u32[]{:S(2)}) collective-permute-start(bf16[2,104,512]{2,1,0:T(8,128)(2,1)S(1)} %collective-permute-done.8), channel_id=1, source_target_pairs={{0,240},{16,0},{32,16},{48,32},{64,48},{80,64},{96,80},{112,96},{1... | collective-permute-start | bytes 638984 | tf_op jit(solution)/shard_map/ppermute | solution.py:48
  64.0 4.6 %collective-permute-start.12 = (bf16[2,104,512]{2,1,0:T(8,128)(2,1)S(1)}, bf16[2,104,512]{2,1,0:T(8,128)(2,1)S(1)}, u32[]{:S(2)}, u32[]{:S(2)}) collective-permute-start(bf16[2,104,512]{2,1,0:T(8,128)(2,1)S(1)} %collective-permute-done.10), channel_id=1, source_target_pairs={{0,240},{16,0},{32,16},{48,32},{64,48},{80,64},{96,80},{112,96},{1... | collective-permute-start | bytes 638984 | tf_op jit(solution)/shard_map/ppermute | solution.py:48
  71.8 4.6 %collective-permute-start.14 = (bf16[2,104,512]{2,1,0:T(8,128)(2,1)S(1)}, bf16[2,104,512]{2,1,0:T(8,128)(2,1)S(1)}, u32[]{:S(2)}, u32[]{:S(2)}) collective-permute-start(bf16[2,104,512]{2,1,0:T(8,128)(2,1)S(1)} %collective-permute-done.12), channel_id=1, source_target_pairs={{0,240},{16,0},{32,16},{48,32},{64,48},{80,64},{96,80},{112,96},{1... | collective-permute-start | bytes 638984 | tf_op jit(solution)/shard_map/ppermute | solution.py:48
  80.5 7.8 %collective-permute-done.15 = bf16[2,104,512]{2,1,0:T(8,128)(2,1)S(1)} collective-permute-done((bf16[2,104,512]{2,1,0:T(8,128)(2,1)S(1)}, bf16[2,104,512]{2,1,0:T(8,128)(2,1)S(1)}, u32[]{:S(2)}, u32[]{:S(2)}) %collective-permute-start.15) | collective-permute-done | bytes 213024 | tf_op jit(solution)/shard_map/ppermute | solution.py:45
  100.0 3.5 %collective-permute-done.16 = bf16[320,1,256]{2,0,1:T(8,128)(2,1)S(1)} collective-permute-done((bf16[320,1,256]{2,0,1:T(8,128)(2,1)S(1)}, bf16[320,1,256]{2,0,1:T(8,128)(2,1)S(1)}, u32[]{:S(2)}, u32[]{:S(2)}) %collective-permute-start.16) | collective-permute-done | bytes 163872 | tf_op jit(solution)/shard_map/ppermute | solution.py:179
  105.5 3.4 %collective-permute-start.17 = (bf16[2,320,1,256]{3,1,2,0:T(8,128)(2,1)S(1)}, bf16[2,320,1,256]{3,1,2,0:T(8,128)(2,1)S(1)}, u32[]{:S(2)}, u32[]{:S(2)}) collective-permute-start(bf16[2,320,1,256]{3,1,2,0:T(8,128)(2,1)S(1)} %maximum_select_fusion), channel_id=1, source_target_pairs={{0,16},{16,32},{32,48},{48,64},{64,80},{80,96},{96,112},{112,128},... | collective-permute-start | bytes 983048 | tf_op jit(solution)/shard_map/ppermute | solution.py:207
  110.2 4.4 %collective-permute-done.17 = bf16[2,320,1,256]{3,1,2,0:T(8,128)(2,1)S(1)} collective-permute-done((bf16[2,320,1,256]{3,1,2,0:T(8,128)(2,1)S(1)}, bf16[2,320,1,256]{3,1,2,0:T(8,128)(2,1)S(1)}, u32[]{:S(2)}, u32[]{:S(2)}) %collective-permute-start.17) | collective-permute-done | bytes 327712 | tf_op jit(solution)/shard_map/ppermute | solution.py:207
  114.5 2.3 collective-permute-start.18
  118.4 4.3 %collective-permute-start.21 = (bf16[2,320,1,256]{3,1,2,0:T(8,128)(2,1)S(1)}, bf16[2,320,1,256]{3,1,2,0:T(8,128)(2,1)S(1)}, u32[]{:S(2)}, u32[]{:S(2)}) collective-permute-start(bf16[2,320,1,256]{3,1,2,0:T(8,128)(2,1)S(1)} %collective-permute-done.19), channel_id=1, source_target_pairs={{0,240},{16,0},{32,16},{48,32},{64,48},{80,64},{96,80},{112,96},{1... | collective-permute-start | bytes 983048 | tf_op jit(solution)/shard_map/ppermute | solution.py:210
  128.9 4.6 %collective-permute-start.23 = (bf16[2,320,1,256]{3,1,2,0:T(8,128)(2,1)S(1)}, bf16[2,320,1,256]{3,1,2,0:T(8,128)(2,1)S(1)}, u32[]{:S(2)}, u32[]{:S(2)}) collective-permute-start(bf16[2,320,1,256]{3,1,2,0:T(8,128)(2,1)S(1)} %collective-permute-done.21), channel_id=1, source_target_pairs={{0,240},{16,0},{32,16},{48,32},{64,48},{80,64},{96,80},{112,96},{1... | collective-permute-start | bytes 983048 | tf_op jit(solution)/shard_map/ppermute | solution.py:210
  139.0 5.5 %collective-permute-start.25 = (bf16[2,320,1,256]{3,1,2,0:T(8,128)(2,1)S(1)}, bf16[2,320,1,256]{3,1,2,0:T(8,128)(2,1)S(1)}, u32[]{:S(2)}, u32[]{:S(2)}) collective-permute-start(bf16[2,320,1,256]{3,1,2,0:T(8,128)(2,1)S(1)} %collective-permute-done.23), channel_id=1, source_target_pairs={{0,240},{16,0},{32,16},{48,32},{64,48},{80,64},{96,80},{112,96},{1... | collective-permute-start | bytes 983048 | tf_op jit(solution)/shard_map/ppermute | solution.py:210
  150.0 5.0 %collective-permute-start.27 = (bf16[2,320,1,256]{3,1,2,0:T(8,128)(2,1)S(1)}, bf16[2,320,1,256]{3,1,2,0:T(8,128)(2,1)S(1)}, u32[]{:S(2)}, u32[]{:S(2)}) collective-permute-start(bf16[2,320,1,256]{3,1,2,0:T(8,128)(2,1)S(1)} %collective-permute-done.25), channel_id=1, source_target_pairs={{0,240},{16,0},{32,16},{48,32},{64,48},{80,64},{96,80},{112,96},{1... | collective-permute-start | bytes 983048 | tf_op jit(solution)/shard_map/ppermute | solution.py:210
  160.6 5.0 %collective-permute-start.29 = (bf16[2,320,1,256]{3,1,2,0:T(8,128)(2,1)S(1)}, bf16[2,320,1,256]{3,1,2,0:T(8,128)(2,1)S(1)}, u32[]{:S(2)}, u32[]{:S(2)}) collective-permute-start(bf16[2,320,1,256]{3,1,2,0:T(8,128)(2,1)S(1)} %collective-permute-done.27), channel_id=1, source_target_pairs={{0,240},{16,0},{32,16},{48,32},{64,48},{80,64},{96,80},{112,96},{1... | collective-permute-start | bytes 983048 | tf_op jit(solution)/shard_map/ppermute | solution.py:210
  171.6 5.0 %collective-permute-start.30 = (bf16[2,320,1,256]{3,1,2,0:T(8,128)(2,1)S(1)}, bf16[2,320,1,256]{3,1,2,0:T(8,128)(2,1)S(1)}, u32[]{:S(2)}, u32[]{:S(2)}) collective-permute-start(bf16[2,320,1,256]{3,1,2,0:T(8,128)(2,1)S(1)} %collective-permute-done.29), channel_id=1, source_target_pairs={{0,240},{16,0},{32,16},{48,32},{64,48},{80,64},{96,80},{112,96},{1... | collective-permute-start | bytes 983048 | tf_op jit(solution)/shard_map/ppermute | solution.py:210
  181.0 5.0 %collective-permute-done.31 = bf16[2,320,1,256]{3,1,2,0:T(8,128)(2,1)S(1)} collective-permute-done((bf16[2,320,1,256]{3,1,2,0:T(8,128)(2,1)S(1)}, bf16[2,320,1,256]{3,1,2,0:T(8,128)(2,1)S(1)}, u32[]{:S(2)}, u32[]{:S(2)}) %collective-permute-start.31) | collective-permute-done | bytes 327712 | tf_op jit(solution)/shard_map/ppermute | solution.py:207
  188.8 22.3 %collective-permute-start.36 = (bf16[160,1536]{1,0:T(8,128)(2,1)S(1)}, bf16[160,1536]{1,0:T(8,128)(2,1)S(1)}, u32[]{:S(2)}, u32[]{:S(2)}) collective-permute-start(bf16[160,1536]{1,0:T(8,128)(2,1)S(1)} %dynamic-slice_convert_fusion), channel_id=1, source_target_pairs={{0,1},{1,0},{2,3},{3,2},{4,5},{5,4},{6,7},{7,6},{8,9},{9,8},{10,11... | collective-permute-start | bytes 1474568 | tf_op jit(solution)/shard_map/ppermute | solution.py:71
  213.7 3.1 %collective-permute-start.37 = (bf16[160,768]{1,0:T(8,128)(2,1)S(1)}, bf16[160,768]{1,0:T(8,128)(2,1)S(1)}, u32[]{:S(2)}, u32[]{:S(2)}) collective-permute-start(bf16[160,768]{1,0:T(8,128)(2,1)S(1)} %dynamic-slice_convert_fusion.2), channel_id=1, source_target_pairs={{0,2},{1,3},{2,0},{3,1},{4,6},{5,7},{6,4},{7,5},{8,10},{9,11},{10,... | collective-permute-start | bytes 737288 | tf_op jit(solution)/shard_map/ppermute | solution.py:71
  217.0 2.3 collective-permute-start.33
  219.3 3.3 %collective-permute-done.37 = bf16[160,768]{1,0:T(8,128)(2,1)S(1)} collective-permute-done((bf16[160,768]{1,0:T(8,128)(2,1)S(1)}, bf16[160,768]{1,0:T(8,128)(2,1)S(1)}, u32[]{:S(2)}, u32[]{:S(2)}) %collective-permute-start.37) | collective-permute-done | bytes 245792 | tf_op jit(solution)/shard_map/ppermute | solution.py:71
  222.7 2.3 collective-permute-start.38
  225.6 2.6 %collective-permute-start.34 = (bf16[160,384]{1,0:T(8,128)(2,1)S(1)}, bf16[160,384]{1,0:T(8,128)(2,1)S(1)}, u32[]{:S(2)}, u32[]{:S(2)}) collective-permute-start(bf16[160,384]{1,0:T(8,128)(2,1)S(1)} %dynamic-slice_convert_fusion.5), channel_id=1, source_target_pairs={{0,2},{1,3},{2,0},{3,1},{4,6},{5,7},{6,4},{7,5},{8,10},{9,11},{10,... | collective-permute-start | bytes 368648 | tf_op jit(solution)/shard_map/ppermute | solution.py:71
  228.4 4.7 %collective-permute-start.39 = (bf16[160,192]{1,0:T(8,128)(2,1)S(1)}, bf16[160,192]{1,0:T(8,128)(2,1)S(1)}, u32[]{:S(2)}, u32[]{:S(2)}) collective-permute-start(bf16[160,192]{1,0:T(8,128)(2,1)S(1)} %dynamic-slice_convert_fusion.6), channel_id=1, source_target_pairs={{0,4},{1,5},{2,6},{3,7},{4,0},{5,1},{6,2},{7,3},{8,12},{9,13},{10,... | collective-permute-start | bytes 184328 | tf_op jit(solution)/shard_map/ppermute | solution.py:71
  233.2 2.5 %collective-permute-start.35 = (bf16[160,192]{1,0:T(8,128)(2,1)S(1)}, bf16[160,192]{1,0:T(8,128)(2,1)S(1)}, u32[]{:S(2)}, u32[]{:S(2)}) collective-permute-start(bf16[160,192]{1,0:T(8,128)(2,1)S(1)} %dynamic-slice_convert_fusion.7), channel_id=1, source_target_pairs={{0,4},{1,5},{2,6},{3,7},{4,0},{5,1},{6,2},{7,3},{8,12},{9,13},{10,... | collective-permute-start | bytes 184328 | tf_op jit(solution)/shard_map/ppermute | solution.py:71
  235.9 4.0 %collective-permute-done.35 = bf16[160,192]{1,0:T(8,128)(2,1)S(1)} collective-permute-done((bf16[160,192]{1,0:T(8,128)(2,1)S(1)}, bf16[160,192]{1,0:T(8,128)(2,1)S(1)}, u32[]{:S(2)}, u32[]{:S(2)}) %collective-permute-start.35) | collective-permute-done | bytes 61472 | tf_op jit(solution)/shard_map/ppermute | solution.py:71
  (208 shorter events, 85.5 us)
Async XLA Ops:
  2.3 13.9 %collective-permute-start = (bf16[104,512]{1,0:T(8,128)(2,1)S(1)}, bf16[104,512]{1,0:T(8,128)(2,1)S(1)}, u32[]{:S(2)}, u32[]{:S(2)}) collective-permute-start(bf16[104,512]{1,0:T(8,128)(2,1)S(1)} %get-tuple-element.157), channel_id=1, source_target_pairs={{0,256},{16,272},{32,288},{48,304},{64,320},{80,336},{96,352},{112... | collective-permute-start | bytes 319496 | tf_op jit(solution)/shard_map/ppermute | solution.py:34
  9.1 18.9 %collective-permute-start.40 = (bf16[320,192]{1,0:T(8,128)(2,1)S(1)}, bf16[320,192]{1,0:T(8,128)(2,1)S(1)}, u32[]{:S(2)}, u32[]{:S(2)}) collective-permute-start(bf16[320,192]{1,0:T(8,128)(2,1)S(1)} %constant_dynamic-slice_fusion), channel_id=1, source_target_pairs={{0,16},{16,32},{32,48},{48,64},{64,80},{80,96},{96,112},{112,128},... | collective-permute-start | bytes 368648 | tf_op jit(solution)/shard_map/ppermute | solution.py:19
  16.3 14.1 %collective-permute-start.1 = (bf16[2,104,512]{2,1,0:T(8,128)(2,1)S(1)}, bf16[2,104,512]{2,1,0:T(8,128)(2,1)S(1)}, u32[]{:S(2)}, u32[]{:S(2)}) collective-permute-start(bf16[2,104,512]{2,1,0:T(8,128)(2,1)S(1)} %maximum_select_fusion.2), channel_id=1, source_target_pairs={{0,16},{16,32},{32,48},{48,64},{64,80},{80,96},{96,112},{112,128},... | collective-permute-start | bytes 638984 | tf_op jit(solution)/shard_map/ppermute | solution.py:45
  19.8 12.5 %collective-permute-start.2 = (bf16[2,104,512]{2,1,0:T(8,128)(2,1)S(1)}, bf16[2,104,512]{2,1,0:T(8,128)(2,1)S(1)}, u32[]{:S(2)}, u32[]{:S(2)}) collective-permute-start(bf16[2,104,512]{2,1,0:T(8,128)(2,1)S(1)} %maximum_select_fusion.2), channel_id=1, source_target_pairs={{0,240},{16,0},{32,16},{48,32},{64,48},{80,64},{96,80},{112,96},{1... | collective-permute-start | bytes 638984 | tf_op jit(solution)/shard_map/ppermute | solution.py:48
  30.4 8.3 %collective-permute-start.3 = (bf16[2,104,512]{2,1,0:T(8,128)(2,1)S(1)}, bf16[2,104,512]{2,1,0:T(8,128)(2,1)S(1)}, u32[]{:S(2)}, u32[]{:S(2)}) collective-permute-start(bf16[2,104,512]{2,1,0:T(8,128)(2,1)S(1)} %collective-permute-done.1), channel_id=1, source_target_pairs={{0,16},{16,32},{32,48},{48,64},{64,80},{80,96},{96,112},{112,128},... | collective-permute-start | bytes 638984 | tf_op jit(solution)/shard_map/ppermute | solution.py:45
  32.3 8.3 %collective-permute-start.4 = (bf16[2,104,512]{2,1,0:T(8,128)(2,1)S(1)}, bf16[2,104,512]{2,1,0:T(8,128)(2,1)S(1)}, u32[]{:S(2)}, u32[]{:S(2)}) collective-permute-start(bf16[2,104,512]{2,1,0:T(8,128)(2,1)S(1)} %collective-permute-done.2), channel_id=1, source_target_pairs={{0,240},{16,0},{32,16},{48,32},{64,48},{80,64},{96,80},{112,96},{1... | collective-permute-start | bytes 638984 | tf_op jit(solution)/shard_map/ppermute | solution.py:48
  38.7 7.8 %collective-permute-start.5 = (bf16[2,104,512]{2,1,0:T(8,128)(2,1)S(1)}, bf16[2,104,512]{2,1,0:T(8,128)(2,1)S(1)}, u32[]{:S(2)}, u32[]{:S(2)}) collective-permute-start(bf16[2,104,512]{2,1,0:T(8,128)(2,1)S(1)} %collective-permute-done.3), channel_id=1, source_target_pairs={{0,16},{16,32},{32,48},{48,64},{64,80},{80,96},{96,112},{112,128},... | collective-permute-start | bytes 638984 | tf_op jit(solution)/shard_map/ppermute | solution.py:45
  40.6 7.8 %collective-permute-start.6 = (bf16[2,104,512]{2,1,0:T(8,128)(2,1)S(1)}, bf16[2,104,512]{2,1,0:T(8,128)(2,1)S(1)}, u32[]{:S(2)}, u32[]{:S(2)}) collective-permute-start(bf16[2,104,512]{2,1,0:T(8,128)(2,1)S(1)} %collective-permute-done.4), channel_id=1, source_target_pairs={{0,240},{16,0},{32,16},{48,32},{64,48},{80,64},{96,80},{112,96},{1... | collective-permute-start | bytes 638984 | tf_op jit(solution)/shard_map/ppermute | solution.py:48
  46.5 7.8 %collective-permute-start.7 = (bf16[2,104,512]{2,1,0:T(8,128)(2,1)S(1)}, bf16[2,104,512]{2,1,0:T(8,128)(2,1)S(1)}, u32[]{:S(2)}, u32[]{:S(2)}) collective-permute-start(bf16[2,104,512]{2,1,0:T(8,128)(2,1)S(1)} %collective-permute-done.5), channel_id=1, source_target_pairs={{0,16},{16,32},{32,48},{48,64},{64,80},{80,96},{96,112},{112,128},... | collective-permute-start | bytes 638984 | tf_op jit(solution)/shard_map/ppermute | solution.py:45
  54.3 7.8 %collective-permute-start.9 = (bf16[2,104,512]{2,1,0:T(8,128)(2,1)S(1)}, bf16[2,104,512]{2,1,0:T(8,128)(2,1)S(1)}, u32[]{:S(2)}, u32[]{:S(2)}) collective-permute-start(bf16[2,104,512]{2,1,0:T(8,128)(2,1)S(1)} %collective-permute-done.7), channel_id=1, source_target_pairs={{0,16},{16,32},{32,48},{48,64},{64,80},{80,96},{96,112},{112,128},... | collective-permute-start | bytes 638984 | tf_op jit(solution)/shard_map/ppermute | solution.py:45
  62.1 7.8 %collective-permute-start.11 = (bf16[2,104,512]{2,1,0:T(8,128)(2,1)S(1)}, bf16[2,104,512]{2,1,0:T(8,128)(2,1)S(1)}, u32[]{:S(2)}, u32[]{:S(2)}) collective-permute-start(bf16[2,104,512]{2,1,0:T(8,128)(2,1)S(1)} %collective-permute-done.9), channel_id=1, source_target_pairs={{0,16},{16,32},{32,48},{48,64},{64,80},{80,96},{96,112},{112,128},... | collective-permute-start | bytes 638984 | tf_op jit(solution)/shard_map/ppermute | solution.py:45
  69.9 8.7 %collective-permute-start.13 = (bf16[2,104,512]{2,1,0:T(8,128)(2,1)S(1)}, bf16[2,104,512]{2,1,0:T(8,128)(2,1)S(1)}, u32[]{:S(2)}, u32[]{:S(2)}) collective-permute-start(bf16[2,104,512]{2,1,0:T(8,128)(2,1)S(1)} %collective-permute-done.11), channel_id=1, source_target_pairs={{0,16},{16,32},{32,48},{48,64},{64,80},{80,96},{96,112},{112,128},... | collective-permute-start | bytes 638984 | tf_op jit(solution)/shard_map/ppermute | solution.py:45
  71.8 8.7 %collective-permute-start.14 = (bf16[2,104,512]{2,1,0:T(8,128)(2,1)S(1)}, bf16[2,104,512]{2,1,0:T(8,128)(2,1)S(1)}, u32[]{:S(2)}, u32[]{:S(2)}) collective-permute-start(bf16[2,104,512]{2,1,0:T(8,128)(2,1)S(1)} %collective-permute-done.12), channel_id=1, source_target_pairs={{0,240},{16,0},{32,16},{48,32},{64,48},{80,64},{96,80},{112,96},{1... | collective-permute-start | bytes 638984 | tf_op jit(solution)/shard_map/ppermute | solution.py:48
  78.5 9.8 %collective-permute-start.15 = (bf16[2,104,512]{2,1,0:T(8,128)(2,1)S(1)}, bf16[2,104,512]{2,1,0:T(8,128)(2,1)S(1)}, u32[]{:S(2)}, u32[]{:S(2)}) collective-permute-start(bf16[2,104,512]{2,1,0:T(8,128)(2,1)S(1)} %collective-permute-done.13), channel_id=1, source_target_pairs={{0,16},{16,32},{32,48},{48,64},{64,80},{80,96},{96,112},{112,128},... | collective-permute-start | bytes 638984 | tf_op jit(solution)/shard_map/ppermute | solution.py:45
  103.6 13.3 %collective-permute-start.19 = (bf16[2,320,1,256]{3,1,2,0:T(8,128)(2,1)S(1)}, bf16[2,320,1,256]{3,1,2,0:T(8,128)(2,1)S(1)}, u32[]{:S(2)}, u32[]{:S(2)}) collective-permute-start(bf16[2,320,1,256]{3,1,2,0:T(8,128)(2,1)S(1)} %maximum_select_fusion), channel_id=1, source_target_pairs={{0,240},{16,0},{32,16},{48,32},{64,48},{80,64},{96,80},{112,96},{1... | collective-permute-start | bytes 983048 | tf_op jit(solution)/shard_map/ppermute | solution.py:210
  105.5 9.0 %collective-permute-start.17 = (bf16[2,320,1,256]{3,1,2,0:T(8,128)(2,1)S(1)}, bf16[2,320,1,256]{3,1,2,0:T(8,128)(2,1)S(1)}, u32[]{:S(2)}, u32[]{:S(2)}) collective-permute-start(bf16[2,320,1,256]{3,1,2,0:T(8,128)(2,1)S(1)} %maximum_select_fusion), channel_id=1, source_target_pairs={{0,16},{16,32},{32,48},{48,64},{64,80},{80,96},{96,112},{112,128},... | collective-permute-start | bytes 983048 | tf_op jit(solution)/shard_map/ppermute | solution.py:207
  114.5 10.9 %collective-permute-start.18 = (bf16[2,320,1,256]{3,1,2,0:T(8,128)(2,1)S(1)}, bf16[2,320,1,256]{3,1,2,0:T(8,128)(2,1)S(1)}, u32[]{:S(2)}, u32[]{:S(2)}) collective-permute-start(bf16[2,320,1,256]{3,1,2,0:T(8,128)(2,1)S(1)} %collective-permute-done.17), channel_id=1, source_target_pairs={{0,16},{16,32},{32,48},{48,64},{64,80},{80,96},{96,112},{112,128},... | collective-permute-start | bytes 983048 | tf_op jit(solution)/shard_map/ppermute | solution.py:207
  118.4 8.9 %collective-permute-start.21 = (bf16[2,320,1,256]{3,1,2,0:T(8,128)(2,1)S(1)}, bf16[2,320,1,256]{3,1,2,0:T(8,128)(2,1)S(1)}, u32[]{:S(2)}, u32[]{:S(2)}) collective-permute-start(bf16[2,320,1,256]{3,1,2,0:T(8,128)(2,1)S(1)} %collective-permute-done.19), channel_id=1, source_target_pairs={{0,240},{16,0},{32,16},{48,32},{64,48},{80,64},{96,80},{112,96},{1... | collective-permute-start | bytes 983048 | tf_op jit(solution)/shard_map/ppermute | solution.py:210
  125.4 9.9 %collective-permute-start.20 = (bf16[2,320,1,256]{3,1,2,0:T(8,128)(2,1)S(1)}, bf16[2,320,1,256]{3,1,2,0:T(8,128)(2,1)S(1)}, u32[]{:S(2)}, u32[]{:S(2)}) collective-permute-start(bf16[2,320,1,256]{3,1,2,0:T(8,128)(2,1)S(1)} %collective-permute-done.18), channel_id=1, source_target_pairs={{0,16},{16,32},{32,48},{48,64},{64,80},{80,96},{96,112},{112,128},... | collective-permute-start | bytes 983048 | tf_op jit(solution)/shard_map/ppermute | solution.py:207
  128.9 8.6 %collective-permute-start.23 = (bf16[2,320,1,256]{3,1,2,0:T(8,128)(2,1)S(1)}, bf16[2,320,1,256]{3,1,2,0:T(8,128)(2,1)S(1)}, u32[]{:S(2)}, u32[]{:S(2)}) collective-permute-start(bf16[2,320,1,256]{3,1,2,0:T(8,128)(2,1)S(1)} %collective-permute-done.21), channel_id=1, source_target_pairs={{0,240},{16,0},{32,16},{48,32},{64,48},{80,64},{96,80},{112,96},{1... | collective-permute-start | bytes 983048 | tf_op jit(solution)/shard_map/ppermute | solution.py:210
  135.3 9.9 %collective-permute-start.22 = (bf16[2,320,1,256]{3,1,2,0:T(8,128)(2,1)S(1)}, bf16[2,320,1,256]{3,1,2,0:T(8,128)(2,1)S(1)}, u32[]{:S(2)}, u32[]{:S(2)}) collective-permute-start(bf16[2,320,1,256]{3,1,2,0:T(8,128)(2,1)S(1)} %collective-permute-done.20), channel_id=1, source_target_pairs={{0,16},{16,32},{32,48},{48,64},{64,80},{80,96},{96,112},{112,128},... | collective-permute-start | bytes 983048 | tf_op jit(solution)/shard_map/ppermute | solution.py:207
  139.0 9.5 %collective-permute-start.25 = (bf16[2,320,1,256]{3,1,2,0:T(8,128)(2,1)S(1)}, bf16[2,320,1,256]{3,1,2,0:T(8,128)(2,1)S(1)}, u32[]{:S(2)}, u32[]{:S(2)}) collective-permute-start(bf16[2,320,1,256]{3,1,2,0:T(8,128)(2,1)S(1)} %collective-permute-done.23), channel_id=1, source_target_pairs={{0,240},{16,0},{32,16},{48,32},{64,48},{80,64},{96,80},{112,96},{1... | collective-permute-start | bytes 983048 | tf_op jit(solution)/shard_map/ppermute | solution.py:210
  145.3 10.6 %collective-permute-start.24 = (bf16[2,320,1,256]{3,1,2,0:T(8,128)(2,1)S(1)}, bf16[2,320,1,256]{3,1,2,0:T(8,128)(2,1)S(1)}, u32[]{:S(2)}, u32[]{:S(2)}) collective-permute-start(bf16[2,320,1,256]{3,1,2,0:T(8,128)(2,1)S(1)} %collective-permute-done.22), channel_id=1, source_target_pairs={{0,16},{16,32},{32,48},{48,64},{64,80},{80,96},{96,112},{112,128},... | collective-permute-start | bytes 983048 | tf_op jit(solution)/shard_map/ppermute | solution.py:207
  150.0 9.0 %collective-permute-start.27 = (bf16[2,320,1,256]{3,1,2,0:T(8,128)(2,1)S(1)}, bf16[2,320,1,256]{3,1,2,0:T(8,128)(2,1)S(1)}, u32[]{:S(2)}, u32[]{:S(2)}) collective-permute-start(bf16[2,320,1,256]{3,1,2,0:T(8,128)(2,1)S(1)} %collective-permute-done.25), channel_id=1, source_target_pairs={{0,240},{16,0},{32,16},{48,32},{64,48},{80,64},{96,80},{112,96},{1... | collective-permute-start | bytes 983048 | tf_op jit(solution)/shard_map/ppermute | solution.py:210
  155.8 10.6 %collective-permute-start.26 = (bf16[2,320,1,256]{3,1,2,0:T(8,128)(2,1)S(1)}, bf16[2,320,1,256]{3,1,2,0:T(8,128)(2,1)S(1)}, u32[]{:S(2)}, u32[]{:S(2)}) collective-permute-start(bf16[2,320,1,256]{3,1,2,0:T(8,128)(2,1)S(1)} %collective-permute-done.24), channel_id=1, source_target_pairs={{0,16},{16,32},{32,48},{48,64},{64,80},{80,96},{96,112},{112,128},... | collective-permute-start | bytes 983048 | tf_op jit(solution)/shard_map/ppermute | solution.py:207
  160.6 9.0 %collective-permute-start.29 = (bf16[2,320,1,256]{3,1,2,0:T(8,128)(2,1)S(1)}, bf16[2,320,1,256]{3,1,2,0:T(8,128)(2,1)S(1)}, u32[]{:S(2)}, u32[]{:S(2)}) collective-permute-start(bf16[2,320,1,256]{3,1,2,0:T(8,128)(2,1)S(1)} %collective-permute-done.27), channel_id=1, source_target_pairs={{0,240},{16,0},{32,16},{48,32},{64,48},{80,64},{96,80},{112,96},{1... | collective-permute-start | bytes 983048 | tf_op jit(solution)/shard_map/ppermute | solution.py:210
  166.4 10.6 %collective-permute-start.28 = (bf16[2,320,1,256]{3,1,2,0:T(8,128)(2,1)S(1)}, bf16[2,320,1,256]{3,1,2,0:T(8,128)(2,1)S(1)}, u32[]{:S(2)}, u32[]{:S(2)}) collective-permute-start(bf16[2,320,1,256]{3,1,2,0:T(8,128)(2,1)S(1)} %collective-permute-done.26), channel_id=1, source_target_pairs={{0,16},{16,32},{32,48},{48,64},{64,80},{80,96},{96,112},{112,128},... | collective-permute-start | bytes 983048 | tf_op jit(solution)/shard_map/ppermute | solution.py:207
  171.6 9.0 %collective-permute-start.30 = (bf16[2,320,1,256]{3,1,2,0:T(8,128)(2,1)S(1)}, bf16[2,320,1,256]{3,1,2,0:T(8,128)(2,1)S(1)}, u32[]{:S(2)}, u32[]{:S(2)}) collective-permute-start(bf16[2,320,1,256]{3,1,2,0:T(8,128)(2,1)S(1)} %collective-permute-done.29), channel_id=1, source_target_pairs={{0,240},{16,0},{32,16},{48,32},{64,48},{80,64},{96,80},{112,96},{1... | collective-permute-start | bytes 983048 | tf_op jit(solution)/shard_map/ppermute | solution.py:210
  177.0 9.0 %collective-permute-start.31 = (bf16[2,320,1,256]{3,1,2,0:T(8,128)(2,1)S(1)}, bf16[2,320,1,256]{3,1,2,0:T(8,128)(2,1)S(1)}, u32[]{:S(2)}, u32[]{:S(2)}) collective-permute-start(bf16[2,320,1,256]{3,1,2,0:T(8,128)(2,1)S(1)} %collective-permute-done.28), channel_id=1, source_target_pairs={{0,16},{16,32},{32,48},{48,64},{64,80},{80,96},{96,112},{112,128},... | collective-permute-start | bytes 983048 | tf_op jit(solution)/shard_map/ppermute | solution.py:207
  188.8 24.7 %collective-permute-start.36 = (bf16[160,1536]{1,0:T(8,128)(2,1)S(1)}, bf16[160,1536]{1,0:T(8,128)(2,1)S(1)}, u32[]{:S(2)}, u32[]{:S(2)}) collective-permute-start(bf16[160,1536]{1,0:T(8,128)(2,1)S(1)} %dynamic-slice_convert_fusion), channel_id=1, source_target_pairs={{0,1},{1,0},{2,3},{3,2},{4,5},{5,4},{6,7},{7,6},{8,9},{9,8},{10,11... | collective-permute-start | bytes 1474568 | tf_op jit(solution)/shard_map/ppermute | solution.py:71
  213.7 8.9 %collective-permute-start.37 = (bf16[160,768]{1,0:T(8,128)(2,1)S(1)}, bf16[160,768]{1,0:T(8,128)(2,1)S(1)}, u32[]{:S(2)}, u32[]{:S(2)}) collective-permute-start(bf16[160,768]{1,0:T(8,128)(2,1)S(1)} %dynamic-slice_convert_fusion.2), channel_id=1, source_target_pairs={{0,2},{1,3},{2,0},{3,1},{4,6},{5,7},{6,4},{7,5},{8,10},{9,11},{10,... | collective-permute-start | bytes 737288 | tf_op jit(solution)/shard_map/ppermute | solution.py:71
  217.0 8.6 %collective-permute-start.33 = (bf16[160,768]{1,0:T(8,128)(2,1)S(1)}, bf16[160,768]{1,0:T(8,128)(2,1)S(1)}, u32[]{:S(2)}, u32[]{:S(2)}) collective-permute-start(bf16[160,768]{1,0:T(8,128)(2,1)S(1)} %dynamic-slice_convert_fusion.3), channel_id=1, source_target_pairs={{0,8},{1,9},{2,10},{3,11},{4,12},{5,13},{6,14},{7,15},{8,0},{9,1},... | collective-permute-start | bytes 737288 | tf_op jit(solution)/shard_map/ppermute | solution.py:71
  (17 other events, 132.1 us)
